TPU v7x, 32 devices: a whole 2x2x4 slice. The times are simulated.
32 devices in a mesh: graph: 16 (over z, y, core), head: 2 (over x).
Axes of the slice: x: 2, y: 2, z: 4, core: 2. Of those that a mesh axis runs over, the one named last changes fastest.
Arguments:
- nodes: bfloat16 [2048, 1024], P('graph'), may hold values from -6 to 6
- gain: float32 [1024], replicated, may hold values from 0.1 to 1.9
- w_query: bfloat16 [1024, 1024], P(None, 'head'), may hold values from -3 to 3
- w_key: bfloat16 [1024, 1024], P(None, 'head'), may hold values from -0.1875 to 0.1875
- w_value: bfloat16 [1024, 1024], P(None, 'head'), may hold values from -0.1875 to 0.1875
- w_out: bfloat16 [1024, 1024], P('head'), may hold values from -0.5 to 0.5
- links: int32 [16, 4], P('graph'), may hold values 0 or 1
- cotangent: bfloat16 [2048, 1024], P('graph'), may hold values from -6 to 6
Outputs:
- mixed: bfloat16 [2048, 1024], P('graph', 'head')
- nodes_grad: bfloat16 [2048, 1024], P('graph')
- gain_grad: float32 [1024], replicated
- w_query_grad: float32 [1024, 1024], P('graph', 'head')
- w_key_grad: float32 [1024, 1024], P('graph', 'head')
- w_value_grad: float32 [1024, 1024], P('graph', 'head')
- w_out_grad: float32 [1024, 1024], P('head', 'graph')
All inputs are finite; a program needn't handle non-finite values. No bound on the sum of `links` on one device may be relied on, other than what follows from the above.
Results may differ from a plain program's by a relative error of at most 0.019.
The roundings to bfloat16 on the way count: a program that leaves them out, or rounds other values in their place, can miss the bound.
Values may be sent and summed in bfloat16 or wider, within the bound.
No kernel may reach another device: no remote copies, remote signals or barrier semaphores. Data moves between devices by JAX's collectives and lax.ppermute only.
A program may use at most 64 MiB of HBM per device.

v0:
```python
import jax
import jax.numpy as jnp
from jax import lax
from jax.sharding import PartitionSpec as P

HEAD_DIM = 64


EPS = 1e-05
NEG = -1e30


def from_partner(value, axis, apart):
    mask = 2**apart
    pairs = [(source, source ^ mask) for source in range(lax.axis_size(axis))]
    return lax.ppermute(value, axis, pairs)


def flip_blocks(array, level):
    step = 1 << level
    shaped = array.reshape((array.shape[0] // (2 * step), 2, step) + array.shape[1:])
    return jnp.flip(shaped, axis=1).reshape(array.shape)


def shards(nodes, gain, w_query, w_key, w_value, w_out, links, cotangent):
    blocks_dev = links.shape[0]
    local_levels = blocks_dev.bit_length() - 1
    graph_levels = lax.axis_size("graph").bit_length() - 1
    node_rows, width = nodes.shape
    block_len = node_rows // blocks_dev
    columns = w_query.shape[1]
    local_heads = columns // HEAD_DIM
    score_scale = HEAD_DIM ** (-0.5)
    contract_rows = (((0,), (0,)), ((), ()))
    wide_nodes = nodes.astype(jnp.float32)
    inverse = lax.rsqrt(jnp.mean(wide_nodes * wide_nodes, axis=1, keepdims=True) + EPS)
    normed = (wide_nodes * inverse * gain).astype(jnp.bfloat16)
    query = jnp.dot(normed, w_query, preferred_element_type=jnp.float32).astype(jnp.bfloat16)
    keys = jnp.dot(normed, w_key, preferred_element_type=jnp.float32).astype(jnp.bfloat16)
    values = jnp.dot(normed, w_value, preferred_element_type=jnp.float32).astype(jnp.bfloat16)
    key_blocks = keys.reshape(blocks_dev, block_len, columns)
    value_blocks = values.reshape(blocks_dev, block_len, columns)
    bit_order = list(range(graph_levels))
    remote = {}
    for bit in bit_order:
        remote[bit] = from_partner((key_blocks, value_blocks), "graph", bit)
    key_slots = (
        [key_blocks]
        + [flip_blocks(key_blocks, level) for level in range(local_levels)]
        + [remote[bit][0] for bit in range(graph_levels)]
    )
    value_slots = (
        [value_blocks]
        + [flip_blocks(value_blocks, level) for level in range(local_levels)]
        + [remote[bit][1] for bit in range(graph_levels)]
    )
    slot_count = len(key_slots)
    head_shape = (blocks_dev, block_len, local_heads, HEAD_DIM)
    keys_all = jnp.stack(key_slots).reshape((slot_count,) + head_shape)
    values_all = jnp.stack(value_slots).reshape((slot_count,) + head_shape)
    query_heads = query.reshape(head_shape)
    active = jnp.concatenate([jnp.ones((blocks_dev, 1), jnp.int32), links], axis=1)
    allowed = active[:, None, None, :, None] > 0
    scores = (
        jnp.einsum("bqhe,sbkhe->bhqsk", query_heads, keys_all, preferred_element_type=jnp.float32)
        * score_scale
    )
    scores = jnp.where(allowed, scores, NEG)
    top = jnp.max(scores, axis=(3, 4), keepdims=True)
    raised = jnp.exp(scores - top)
    total = jnp.sum(raised, axis=(3, 4), keepdims=True)
    probs = raised / total
    probs_low = probs.astype(jnp.bfloat16)
    attended = jnp.einsum(
        "bhqsk,sbkhe->bqhe", probs_low, values_all, preferred_element_type=jnp.float32
    )
    attended = attended.astype(jnp.bfloat16).reshape(node_rows, columns)
    mixed_terms = jnp.dot(attended, w_out, preferred_element_type=jnp.float32)
    mixed = lax.psum_scatter(
        mixed_terms.astype(jnp.bfloat16), "head", scatter_dimension=1, tiled=True
    )
    grad_attended = jnp.dot(cotangent, w_out.T, preferred_element_type=jnp.float32).astype(
        jnp.bfloat16
    )
    out_terms = lax.dot_general(
        attended, cotangent, contract_rows, preferred_element_type=jnp.float32
    )
    w_out_grad = lax.psum_scatter(out_terms, "graph", scatter_dimension=1, tiled=True)
    grad_heads = grad_attended.reshape(head_shape)
    grad_probs = jnp.einsum(
        "bqhe,sbkhe->bhqsk", grad_heads, values_all, preferred_element_type=jnp.float32
    )
    delta = jnp.sum(probs * grad_probs, axis=(3, 4), keepdims=True)
    grad_scores = probs * (grad_probs - delta) * score_scale
    grad_query = jnp.einsum("bhqsk,sbkhe->bqhe", grad_scores, keys_all.astype(jnp.float32))
    grad_query = grad_query.astype(jnp.bfloat16).reshape(node_rows, columns)
    slot_block_shape = (slot_count, blocks_dev, block_len, columns)
    key_terms = jnp.einsum("bhqsk,bqhe->sbkhe", grad_scores, query_heads.astype(jnp.float32))
    key_terms = key_terms.astype(jnp.bfloat16).reshape(slot_block_shape)
    value_terms = jnp.einsum(
        "bhqsk,bqhe->sbkhe", probs_low, grad_heads, preferred_element_type=jnp.float32
    )
    value_terms = value_terms.astype(jnp.bfloat16).reshape(slot_block_shape)
    grad_key = key_terms[0].astype(jnp.float32)
    grad_value = value_terms[0].astype(jnp.float32)
    returned = {}
    for bit in bit_order:
        slot = 1 + local_levels + bit
        returned[bit] = from_partner((key_terms[slot], value_terms[slot]), "graph", bit)
    for bit in range(graph_levels):
        grad_key = grad_key + returned[bit][0].astype(jnp.float32)
        grad_value = grad_value + returned[bit][1].astype(jnp.float32)
    grad_key = grad_key.astype(jnp.bfloat16).reshape(node_rows, columns)
    grad_value = grad_value.astype(jnp.bfloat16).reshape(node_rows, columns)
    joined_rows = lax.psum_scatter(
        lax.dot_general(
            normed,
            jnp.concatenate([grad_query, grad_key, grad_value], axis=1),
            contract_rows,
            preferred_element_type=jnp.float32,
        ),
        "graph",
        scatter_dimension=0,
        tiled=True,
    )
    w_query_grad = joined_rows[:, :columns]
    w_key_grad = joined_rows[:, columns : 2 * columns]
    w_value_grad = joined_rows[:, 2 * columns :]
    feature_terms = (
        jnp.dot(grad_query, w_query.T, preferred_element_type=jnp.float32)
        + jnp.dot(grad_key, w_key.T, preferred_element_type=jnp.float32)
        + jnp.dot(grad_value, w_value.T, preferred_element_type=jnp.float32)
    )
    grad_normed = lax.psum(feature_terms.astype(jnp.bfloat16), "head").astype(jnp.float32)
    gain_grad = lax.psum(jnp.sum(grad_normed * wide_nodes * inverse, axis=0), "graph")
    scaled = grad_normed * gain
    nodes_grad = (
        inverse
        * (
            scaled
            - wide_nodes * inverse * inverse * jnp.mean(scaled * wide_nodes, axis=1, keepdims=True)
        )
    ).astype(jnp.bfloat16)
    return (mixed, nodes_grad, gain_grad, w_query_grad, w_key_grad, w_value_grad, w_out_grad)


def solution(mesh):
    in_specs = (
        P("graph", None),
        P(),
        P(None, "head"),
        P(None, "head"),
        P(None, "head"),
        P("head", None),
        P("graph", None),
        P("graph", None),
    )
    out_specs = (
        P("graph", "head"),
        P("graph", None),
        P(),
        P("graph", "head"),
        P("graph", "head"),
        P("graph", "head"),
        P("head", "graph"),
    )
    return jax.shard_map(shards, mesh=mesh, in_specs=in_specs, out_specs=out_specs, check_vma=False)
```

profile of v0, /device:TPU:0, one launch (start us, length us, event | category | flops | bytes accessed | tf_op | source)
XLA Modules:
  0.0 256.6 jit_solution(6664184992313538055)
XLA Ops:
  9.3 2.4 convolution_convert_fusion.6
  12.2 2.5 collective-permute-start.1
  16.3 2.3 convolution_convert_fusion.4
  25.2 1.7 copy.60
  27.1 1.7 copy.50
  29.7 2.9 %collective-permute-start.7 = (bf16[1,128,512]{2,1,0:T(8,128)(2,1)}, bf16[1,128,512]{2,1,0:T(8,128)(2,1)}, u32[]{:S(2)}, u32[]{:S(2)}) collective-permute-start(bf16[1,128,512]{2,1,0:T(8,128)(2,1)} %bitcast.2), channel_id=1, source_target_pairs={{0,16},{2,18},{4,20},{6,22},{8,24},{10,26},{12,28},{14,30},{16,0},... | collective-permute-start | bytes 393224 | tf_op jit(solution)/shard_map/ppermute | solution.py:16
  35.4 1.7 copy.52
  38.0 4.6 %collective-permute-done.7 = bf16[1,128,512]{2,1,0:T(8,128)(2,1)} collective-permute-done((bf16[1,128,512]{2,1,0:T(8,128)(2,1)}, bf16[1,128,512]{2,1,0:T(8,128)(2,1)}, u32[]{:S(2)}, u32[]{:S(2)}) %collective-permute-start.7) | collective-permute-done | bytes 131104 | tf_op jit(solution)/shard_map/ppermute | solution.py:16
  42.6 1.7 copy.53
  55.6 3.1 %multiply_reduce_fusion = (f32[8,128]{1,0:T(8,128)S(1)}, f32[8,128,5,128]{1,3,2,0:T(8,128)S(1)}) fusion(f32[8,128]{1,0:T(8,128)S(1)} %fusion.2, f32[8,128]{1,0:T(8,128)S(1)} %get-tuple-element.22, f32[8,128,5,128]{1,3,2,0:T(8,128)} %copy-done.2, pred[5]{0:T(512)(128)(4,1)} %copy-done.13, bf16[128,8,64,1]{0,2,3,1:T(8,128)(2,1)} %bitcast.166, ...), kind=kOutput, calls=%fused_computation.1 | convolution fusion | flops 87817216 | bytes 6041605 | tf_op jit(solution)/shard_map/bqhe,sbkhe->bhqsk/dot_general | solution.py:90
  62.8 3.7 %collective-permute-start.10 = (bf16[1,128,512]{1,2,0:T(8,128)(2,1)S(1)}, bf16[1,128,512]{1,2,0:T(8,128)(2,1)S(1)}, u32[]{:S(2)}, u32[]{:S(2)}) collective-permute-start(bf16[1,128,512]{1,2,0:T(8,128)(2,1)S(1)} %bitcast.164), channel_id=1, source_target_pairs={{0,8},{2,10},{4,12},{6,14},{8,0},{10,2},{12,4},{14,6},{16,24},{18,... | collective-permute-start | bytes 393224 | tf_op jit(solution)/shard_map/ppermute | solution.py:16
  68.2 2.8 %collective-permute-done.11 = bf16[1,128,512]{1,2,0:T(8,128)(2,1)S(1)} collective-permute-done((bf16[1,128,512]{1,2,0:T(8,128)(2,1)S(1)}, bf16[1,128,512]{1,2,0:T(8,128)(2,1)S(1)}, u32[]{:S(2)}, u32[]{:S(2)}) %collective-permute-start.11) | collective-permute-done | bytes 131104 | tf_op jit(solution)/shard_map/ppermute | solution.py:16
  71.1 2.4 collective-permute-start.13
  74.1 3.4 %collective-permute-done.15 = bf16[1,128,512]{1,2,0:T(8,128)(2,1)S(1)} collective-permute-done((bf16[1,128,512]{1,2,0:T(8,128)(2,1)S(1)}, bf16[1,128,512]{1,2,0:T(8,128)(2,1)S(1)}, u32[]{:S(2)}, u32[]{:S(2)}) %collective-permute-start.15) | collective-permute-done | bytes 131104 | tf_op jit(solution)/shard_map/ppermute | solution.py:16
  79.6 4.7 %fusion.25 = f32[1024,1536]{1,0:T(8,128)} fusion(bf16[128,512]{0,1:T(8,128)(2,1)S(1)} %fusion.40, bf16[128,512]{0,1:T(8,128)(2,1)S(1)} %fusion.39, bf16[128,512]{0,1:T(8,128)(2,1)} %bitcast.148, bf16[128,1024]{1,0:T(8,128)(2,1)S(1)} %copy-done.1, f32[1024]{0:T(1024)S(1)} %copy-done.11, f32[128]{0:T(128)S(1)} %add_rsqrt_fusion), kind=kOutput, calls=%fused_computation.45 | convolution fusion | flops 404357120 | bytes 6951424 | tf_op jit(solution)/shard_map/dot_general | solution.py:116
  84.9 2.6 %fusion.7 = bf16[8,64,128]{2,1,0:T(8,128)(2,1)S(1)} fusion(bf16[5,1,128,8,64]{2,4,0,3,1:T(8,128)(2,1)S(1)} %constant_dynamic-update-slice_fusion, f32[8,128,5,128]{1,3,2,0:T(8,128)} %copy-done.2, f32[8,128]{1,0:T(8,128)S(1)} %fusion.2, f32[8,128]{1,0:T(8,128)S(1)} %get-tuple-element.22, pred[5]{0:T(512)(128)(4,1)S(1)} %copy-done.15), kind=kOutput, calls=%fused_computation.22 | convolution fusion | flops 87228416 | bytes 3416069 | tf_op jit(solution)/shard_map/bhqsk,sbkhe->bqhe/dot_general | solution.py:74
  88.7 1.8 fusion.56
  90.5 12.1 %all-reduce.2.cloned.1.call-done = bf16[128,1024]{1,0:T(8,128)(2,1)} async-done(((bf16[128,1024]{1,0:T(8,128)(2,1)}), bf16[128,1024]{1,0:T(8,128)(2,1)}) %all-reduce.2.cloned.1.call-update) | async-done | bytes 262160 | tf_op jit(solution)/shard_map/psum | solution.py:134
  103.9 34.3 %psum.15 = f32[1024]{0:T(1024)} all-reduce(f32[1024]{0:T(1024)S(1)} %get-tuple-element.7), channel_id=1, replica_groups=mesh['graph'=16,'head'=2] {'graph'}, use_global_device_ids=true, to_apply=%region_8.9 | all-reduce | flops 1024 | bytes 8192 | tf_op jit(solution)/shard_map/psum | solution.py:135
  138.2 1.8 fusion.20
  140.0 29.4 %reduce-scatter.6.cloned.1.call-done = f32[64,1536]{1,0:T(8,128)} async-done(((f32[1024,1536]{1,0:T(8,128)}), f32[64,1536]{1,0:T(8,128)}) %reduce-scatter.6.cloned.1.call-update) | async-done | bytes 393232 | tf_op jit(solution)/shard_map/reduce_scatter | solution.py:115
  169.4 1.8 fusion.54
  171.2 11.6 %reduce-scatter.4.cloned.1.call-done = bf16[128,512]{1,0:T(8,128)(2,1)} async-done(((bf16[128,1024]{1,0:T(8,128)(2,1)}), bf16[128,512]{1,0:T(8,128)(2,1)}) %reduce-scatter.4.cloned.1.call-update) | async-done | bytes 131088 | tf_op jit(solution)/shard_map/reduce_scatter | solution.py:79
  182.8 66.2 %reduce-scatter.8.cloned.1.call-done = f32[512,64]{0,1:T(8,128)} async-done(((f32[512,1024]{0,1:T(8,128)}), f32[512,64]{0,1:T(8,128)}) %reduce-scatter.8.cloned.1.call-update) | async-done | bytes 131088 | tf_op jit(solution)/shard_map/reduce_scatter | solution.py:88
  (110 shorter events, 37.3 us)
Async XLA Ops:
  8.0 13.2 %copy-start = (bf16[1024,512]{1,0:T(8,128)(2,1)S(1)}, bf16[1024,512]{1,0:T(8,128)(2,1)}, u32[]{:S(2)}) copy-start(bf16[1024,512]{1,0:T(8,128)(2,1)} %param.10) | copy-start | bytes 3145732
  8.0 13.2 %copy-start.1 = (bf16[128,1024]{1,0:T(8,128)(2,1)S(1)}, bf16[128,1024]{1,0:T(8,128)(2,1)}, u32[]{:S(2)}) copy-start(bf16[128,1024]{1,0:T(8,128)(2,1)} %param.8) | copy-start | bytes 786436
  8.0 94.6 %all-reduce.2.cloned.1.call-start = ((), (), s32[]{:S(2)}) async-start(), calls=%async_computation.4 | async-start | bytes 524288 | tf_op jit(solution)/shard_map/psum | solution.py:134
  11.7 37.0 %collective-permute-start = (bf16[1,128,512]{2,1,0:T(8,128)(2,1)}, bf16[1,128,512]{2,1,0:T(8,128)(2,1)}, u32[]{:S(2)}, u32[]{:S(2)}) collective-permute-start(bf16[1,128,512]{2,1,0:T(8,128)(2,1)} %bitcast.15), channel_id=1, source_target_pairs={{0,2},{2,0},{4,6},{6,4},{8,10},{10,8},{12,14},{14,12},{16,18},{18,... | collective-permute-start | bytes 393224 | tf_op jit(solution)/shard_map/ppermute | solution.py:16
  12.2 38.3 %collective-permute-start.1 = (bf16[1,128,512]{2,1,0:T(8,128)(2,1)}, bf16[1,128,512]{2,1,0:T(8,128)(2,1)}, u32[]{:S(2)}, u32[]{:S(2)}) collective-permute-start(bf16[1,128,512]{2,1,0:T(8,128)(2,1)} %bitcast.15), channel_id=1, source_target_pairs={{0,4},{2,6},{4,0},{6,2},{8,12},{10,14},{12,8},{14,10},{16,20},{18,... | collective-permute-start | bytes 393224 | tf_op jit(solution)/shard_map/ppermute | solution.py:16
  14.7 37.5 %collective-permute-start.2 = (bf16[1,128,512]{2,1,0:T(8,128)(2,1)}, bf16[1,128,512]{2,1,0:T(8,128)(2,1)}, u32[]{:S(2)}, u32[]{:S(2)}) collective-permute-start(bf16[1,128,512]{2,1,0:T(8,128)(2,1)} %bitcast.15), channel_id=1, source_target_pairs={{0,8},{2,10},{4,12},{6,14},{8,0},{10,2},{12,4},{14,6},{16,24},{18,... | collective-permute-start | bytes 393224 | tf_op jit(solution)/shard_map/ppermute | solution.py:16
  18.6 8.3 %collective-permute-start.4 = (bf16[1,128,512]{2,1,0:T(8,128)(2,1)}, bf16[1,128,512]{2,1,0:T(8,128)(2,1)}, u32[]{:S(2)}, u32[]{:S(2)}) collective-permute-start(bf16[1,128,512]{2,1,0:T(8,128)(2,1)} %bitcast.2), channel_id=1, source_target_pairs={{0,2},{2,0},{4,6},{6,4},{8,10},{10,8},{12,14},{14,12},{16,18},{18,... | collective-permute-start | bytes 393224 | tf_op jit(solution)/shard_map/ppermute | solution.py:16
  18.6 11.1 %collective-permute-start.5 = (bf16[1,128,512]{2,1,0:T(8,128)(2,1)}, bf16[1,128,512]{2,1,0:T(8,128)(2,1)}, u32[]{:S(2)}, u32[]{:S(2)}) collective-permute-start(bf16[1,128,512]{2,1,0:T(8,128)(2,1)} %bitcast.2), channel_id=1, source_target_pairs={{0,4},{2,6},{4,0},{6,2},{8,12},{10,14},{12,8},{14,10},{16,20},{18,... | collective-permute-start | bytes 393224 | tf_op jit(solution)/shard_map/ppermute | solution.py:16
  24.2 21.7 %copy-start.13 = (pred[5]{0:T(512)(128)(4,1)}, pred[5]{0:T(512)(128)(4,1)S(1)}, u32[]{:S(2)}) copy-start(pred[5]{0:T(512)(128)(4,1)S(1)} %compare_bitcast_fusion) | copy-start | bytes 19
  26.9 8.3 %collective-permute-start.6 = (bf16[1,128,512]{2,1,0:T(8,128)(2,1)}, bf16[1,128,512]{2,1,0:T(8,128)(2,1)}, u32[]{:S(2)}, u32[]{:S(2)}) collective-permute-start(bf16[1,128,512]{2,1,0:T(8,128)(2,1)} %bitcast.2), channel_id=1, source_target_pairs={{0,8},{2,10},{4,12},{6,14},{8,0},{10,2},{12,4},{14,6},{16,24},{18,... | collective-permute-start | bytes 393224 | tf_op jit(solution)/shard_map/ppermute | solution.py:16
  29.7 12.9 %collective-permute-start.7 = (bf16[1,128,512]{2,1,0:T(8,128)(2,1)}, bf16[1,128,512]{2,1,0:T(8,128)(2,1)}, u32[]{:S(2)}, u32[]{:S(2)}) collective-permute-start(bf16[1,128,512]{2,1,0:T(8,128)(2,1)} %bitcast.2), channel_id=1, source_target_pairs={{0,16},{2,18},{4,20},{6,22},{8,24},{10,26},{12,28},{14,30},{16,0},... | collective-permute-start | bytes 393224 | tf_op jit(solution)/shard_map/ppermute | solution.py:16
  35.2 18.7 %collective-permute-start.3 = (bf16[1,128,512]{2,1,0:T(8,128)(2,1)}, bf16[1,128,512]{2,1,0:T(8,128)(2,1)}, u32[]{:S(2)}, u32[]{:S(2)}) collective-permute-start(bf16[1,128,512]{2,1,0:T(8,128)(2,1)} %bitcast.15), channel_id=1, source_target_pairs={{0,16},{2,18},{4,20},{6,22},{8,24},{10,26},{12,28},{14,30},{16,0},... | collective-permute-start | bytes 393224 | tf_op jit(solution)/shard_map/ppermute | solution.py:16
  62.7 15.6 %copy-start.6 = (bf16[1024,512]{1,0:T(8,128)(2,1)S(1)}, bf16[1024,512]{1,0:T(8,128)(2,1)}, u32[]{:S(2)}) copy-start(bf16[1024,512]{1,0:T(8,128)(2,1)} %param.12) | copy-start | bytes 3145732
  62.7 8.3 %collective-permute-start.11 = (bf16[1,128,512]{1,2,0:T(8,128)(2,1)S(1)}, bf16[1,128,512]{1,2,0:T(8,128)(2,1)S(1)}, u32[]{:S(2)}, u32[]{:S(2)}) collective-permute-start(bf16[1,128,512]{1,2,0:T(8,128)(2,1)S(1)} %bitcast.165), channel_id=1, source_target_pairs={{0,16},{2,18},{4,20},{6,22},{8,24},{10,26},{12,28},{14,30},{16,0},... | collective-permute-start | bytes 393224 | tf_op jit(solution)/shard_map/ppermute | solution.py:16
  62.8 8.4 %collective-permute-start.10 = (bf16[1,128,512]{1,2,0:T(8,128)(2,1)S(1)}, bf16[1,128,512]{1,2,0:T(8,128)(2,1)S(1)}, u32[]{:S(2)}, u32[]{:S(2)}) collective-permute-start(bf16[1,128,512]{1,2,0:T(8,128)(2,1)S(1)} %bitcast.164), channel_id=1, source_target_pairs={{0,8},{2,10},{4,12},{6,14},{8,0},{10,2},{12,4},{14,6},{16,24},{18,... | collective-permute-start | bytes 393224 | tf_op jit(solution)/shard_map/ppermute | solution.py:16
  66.4 7.1 %collective-permute-start.9 = (bf16[1,128,512]{1,2,0:T(8,128)(2,1)S(1)}, bf16[1,128,512]{1,2,0:T(8,128)(2,1)S(1)}, u32[]{:S(2)}, u32[]{:S(2)}) collective-permute-start(bf16[1,128,512]{1,2,0:T(8,128)(2,1)S(1)} %bitcast.162), channel_id=1, source_target_pairs={{0,4},{2,6},{4,0},{6,2},{8,12},{10,14},{12,8},{14,10},{16,20},{18,... | collective-permute-start | bytes 393224 | tf_op jit(solution)/shard_map/ppermute | solution.py:16
  68.0 5.6 %collective-permute-start.8 = (bf16[1,128,512]{1,2,0:T(8,128)(2,1)S(1)}, bf16[1,128,512]{1,2,0:T(8,128)(2,1)S(1)}, u32[]{:S(2)}, u32[]{:S(2)}) collective-permute-start(bf16[1,128,512]{1,2,0:T(8,128)(2,1)S(1)} %bitcast.159), channel_id=1, source_target_pairs={{0,2},{2,0},{4,6},{6,4},{8,10},{10,8},{12,14},{14,12},{16,18},{18,... | collective-permute-start | bytes 393224 | tf_op jit(solution)/shard_map/ppermute | solution.py:16
  68.0 9.5 %collective-permute-start.15 = (bf16[1,128,512]{1,2,0:T(8,128)(2,1)S(1)}, bf16[1,128,512]{1,2,0:T(8,128)(2,1)S(1)}, u32[]{:S(2)}, u32[]{:S(2)}) collective-permute-start(bf16[1,128,512]{1,2,0:T(8,128)(2,1)S(1)} %bitcast.163), channel_id=1, source_target_pairs={{0,16},{2,18},{4,20},{6,22},{8,24},{10,26},{12,28},{14,30},{16,0},... | collective-permute-start | bytes 393224 | tf_op jit(solution)/shard_map/ppermute | solution.py:16
  71.0 7.3 %collective-permute-start.14 = (bf16[1,128,512]{1,2,0:T(8,128)(2,1)S(1)}, bf16[1,128,512]{1,2,0:T(8,128)(2,1)S(1)}, u32[]{:S(2)}, u32[]{:S(2)}) collective-permute-start(bf16[1,128,512]{1,2,0:T(8,128)(2,1)S(1)} %bitcast.161), channel_id=1, source_target_pairs={{0,8},{2,10},{4,12},{6,14},{8,0},{10,2},{12,4},{14,6},{16,24},{18,... | collective-permute-start | bytes 393224 | tf_op jit(solution)/shard_map/ppermute | solution.py:16
  71.1 7.1 %collective-permute-start.13 = (bf16[1,128,512]{1,2,0:T(8,128)(2,1)S(1)}, bf16[1,128,512]{1,2,0:T(8,128)(2,1)S(1)}, u32[]{:S(2)}, u32[]{:S(2)}) collective-permute-start(bf16[1,128,512]{1,2,0:T(8,128)(2,1)S(1)} %bitcast.160), channel_id=1, source_target_pairs={{0,4},{2,6},{4,0},{6,2},{8,12},{10,14},{12,8},{14,10},{16,20},{18,... | collective-permute-start | bytes 393224 | tf_op jit(solution)/shard_map/ppermute | solution.py:16
  73.5 4.7 %collective-permute-start.12 = (bf16[1,128,512]{1,2,0:T(8,128)(2,1)S(1)}, bf16[1,128,512]{1,2,0:T(8,128)(2,1)S(1)}, u32[]{:S(2)}, u32[]{:S(2)}) collective-permute-start(bf16[1,128,512]{1,2,0:T(8,128)(2,1)S(1)} %bitcast.158), channel_id=1, source_target_pairs={{0,2},{2,0},{4,6},{6,4},{8,10},{10,8},{12,14},{14,12},{16,18},{18,... | collective-permute-start | bytes 393224 | tf_op jit(solution)/shard_map/ppermute | solution.py:16
  79.5 89.9 %reduce-scatter.6.cloned.1.call-start = ((), (), s32[]{:S(2)}) async-start(), calls=%async_computation.5 | async-start | bytes 6684672 | tf_op jit(solution)/shard_map/reduce_scatter | solution.py:115
  84.3 98.6 %reduce-scatter.4.cloned.1.call-start = ((), (), s32[]{:S(2)}) async-start(), calls=%async_computation.3 | async-start | bytes 393216 | tf_op jit(solution)/shard_map/reduce_scatter | solution.py:79
  88.6 160.4 %reduce-scatter.8.cloned.1.call-start = ((), (), s32[]{:S(2)}) async-start(), calls=%async_computation.6 | async-start | bytes 2228224 | tf_op jit(solution)/shard_map/reduce_scatter | solution.py:88
  (13 other events, 81.6 us)
Sparse Core Ops, SparseCore 0:
  79.7 22.9 all-reduce.1
Sparse Core Ops, SparseCore 1:
  84.4 85.0 reduce-scatter.5
  172.2 10.6 reduce-scatter.3
  187.5 61.5 reduce-scatter.7
where the time goes:
time: 257 us
  waiting for transfers between devices  131 us (51%)
  blocking collectives  34.3 us (13%)
  local copies, waits for them, and re-layouts  26.6 us (10%)
  matrix products  26.3 us (10%)
  starting transfers between devices  16.4 us (6%)
  between operations  16.1 us (6%)
  other arithmetic  5.75 us (2%)
    reduce_scatter x1, waiting for transfers between devices, shards(): lax.psum_scatter(out_terms, 'graph', scatter_dimension=1, tiled=True)  66.2 us
    psum x1, blocking collectives, shards(): lax.psum(jnp.sum(grad_normed * wide_nodes * inverse, axis=0), 'graph')  34.3 us
    reduce_scatter x1, waiting for transfers between devices, shards(): lax.psum_scatter(lax.dot_general(normed, jnp.concatenate([grad_query, gra...  29.4 us
    ppermute x16, starting transfers between devices, from_partner(): return lax.ppermute(value, axis, pairs)  16.2 us
    psum x1, waiting for transfers between devices, shards(): lax.psum(feature_terms.astype(jnp.bfloat16), 'head').astype(jnp.float32)  12.1 us
    ppermute x16, waiting for transfers between devices, from_partner(): return lax.ppermute(value, axis, pairs)  11.7 us
    reduce_scatter x1, waiting for transfers between devices, shards(): lax.psum_scatter(mixed_terms.astype(jnp.bfloat16), 'head', scatter_dimens...  11.6 us
    ppermute x8, local copies, waits for them, and re-layouts, from_partner(): return lax.ppermute(value, axis, pairs)  10.7 us
  transfers between devices with their start and end apart: 20, of which 9 were waited for; matrix products, arithmetic and copies ran while one was open for 17% of the time, Pallas kernels for 0%

commit v1 on v0

--- a/solution.py
+++ b/solution.py
@@ -14,6 +14,36 @@
     mask = 2**apart
     pairs = [(source, source ^ mask) for source in range(lax.axis_size(axis))]
     return lax.ppermute(value, axis, pairs)
+
+
+def bit_major_rows(matrix, levels):
+    rows, width = matrix.shape
+    inner = width >> levels
+    shaped = matrix.reshape((rows,) + (2,) * levels + (inner,))
+    order = (0,) + tuple(range(levels, 0, -1)) + (levels + 1,)
+    return shaped.transpose(order).reshape(rows, width)
+
+
+def halving_sum(partial, axis, levels):
+    me = lax.axis_index(axis)
+    for bit in range(levels):
+        half = partial.shape[0] // 2
+        mine = (me >> bit) & 1
+        keep = lax.dynamic_slice_in_dim(partial, mine * half, half, 0)
+        send = lax.dynamic_slice_in_dim(partial, (1 - mine) * half, half, 0)
+        got = from_partner(send.astype(jnp.bfloat16), axis, bit)
+        partial = keep + got.astype(jnp.float32)
+    return partial
+
+
+def doubling_sum(value, axis, levels):
+    for bit in range(levels):
+        value = value + from_partner(value, axis, bit)
+    return value
+
+
+def head_swap(value):
+    return lax.ppermute(value, "head", [(0, 1), (1, 0)])
 
 
 def flip_blocks(array, level):
@@ -75,17 +105,19 @@
         "bhqsk,sbkhe->bqhe", probs_low, values_all, preferred_element_type=jnp.float32
     )
     attended = attended.astype(jnp.bfloat16).reshape(node_rows, columns)
+    head_me = lax.axis_index("head")
     mixed_terms = jnp.dot(attended, w_out, preferred_element_type=jnp.float32)
-    mixed = lax.psum_scatter(
-        mixed_terms.astype(jnp.bfloat16), "head", scatter_dimension=1, tiled=True
-    )
+    own_mixed = lax.dynamic_slice_in_dim(mixed_terms, head_me * columns, columns, 1)
+    other_mixed = lax.dynamic_slice_in_dim(mixed_terms, (1 - head_me) * columns, columns, 1)
+    mixed = (own_mixed + head_swap(other_mixed)).astype(jnp.bfloat16)
     grad_attended = jnp.dot(cotangent, w_out.T, preferred_element_type=jnp.float32).astype(
         jnp.bfloat16
     )
     out_terms = lax.dot_general(
-        attended, cotangent, contract_rows, preferred_element_type=jnp.float32
-    )
-    w_out_grad = lax.psum_scatter(out_terms, "graph", scatter_dimension=1, tiled=True)
+        bit_major_rows(cotangent, graph_levels), attended, contract_rows,
+        preferred_element_type=jnp.float32,
+    )
+    w_out_grad = halving_sum(out_terms, "graph", graph_levels).T
     grad_heads = grad_attended.reshape(head_shape)
     grad_probs = jnp.einsum(
         "bqhe,sbkhe->bhqsk", grad_heads, values_all, preferred_element_type=jnp.float32
@@ -112,16 +144,15 @@
         grad_value = grad_value + returned[bit][1].astype(jnp.float32)
     grad_key = grad_key.astype(jnp.bfloat16).reshape(node_rows, columns)
     grad_value = grad_value.astype(jnp.bfloat16).reshape(node_rows, columns)
-    joined_rows = lax.psum_scatter(
+    joined_rows = halving_sum(
         lax.dot_general(
-            normed,
+            bit_major_rows(normed, graph_levels),
             jnp.concatenate([grad_query, grad_key, grad_value], axis=1),
             contract_rows,
             preferred_element_type=jnp.float32,
         ),
         "graph",
-        scatter_dimension=0,
-        tiled=True,
+        graph_levels,
     )
     w_query_grad = joined_rows[:, :columns]
     w_key_grad = joined_rows[:, columns : 2 * columns]
@@ -131,8 +162,10 @@
         + jnp.dot(grad_key, w_key.T, preferred_element_type=jnp.float32)
         + jnp.dot(grad_value, w_value.T, preferred_element_type=jnp.float32)
     )
-    grad_normed = lax.psum(feature_terms.astype(jnp.bfloat16), "head").astype(jnp.float32)
-    gain_grad = lax.psum(jnp.sum(grad_normed * wide_nodes * inverse, axis=0), "graph")
+    grad_normed = feature_terms + head_swap(feature_terms)
+    gain_grad = doubling_sum(
+        jnp.sum(grad_normed * wide_nodes * inverse, axis=0), "graph", graph_levels
+    )
     scaled = grad_normed * gain
     nodes_grad = (
         inverse

time: 257 us -> 142 us (0.55)
  waiting for transfers between devices: 131 us -> 62.3 us
  blocking collectives: 34.3 us -> 0 us
  between operations: 16.1 us -> 1.27 us
  starting transfers between devices: 16.4 us -> 30.4 us
  matrix products: 26.3 us -> 18.9 us
  local copies, waits for them, and re-layouts: 26.6 us -> 21.6 us
    reduce_scatter x3 -> x0, waiting for transfers between devices: 107 us -> none  [the longest x1 66.2 us: shards(): lax.psum_scatter(out_terms, 'graph', scatter_dimension=1, tiled=True)]
    ppermute x16 -> x28, waiting for transfers between devices: 11.7 us -> 49.8 us  [from_partner(): return lax.ppermute(value, axis, pairs)]
    psum x1 -> x0, blocking collectives: 34.3 us -> none  [shards(): lax.psum(jnp.sum(grad_normed * wide_nodes * inverse, axis=0), 'graph')]
    ppermute x0 -> x2, waiting for transfers between devices: none -> 12.5 us  [head_swap(): return lax.ppermute(value, 'head', [(0, 1), (1, 0)])]
    psum x1 -> x0, waiting for transfers between devices: 12.1 us -> none  [shards(): lax.psum(feature_terms.astype(jnp.bfloat16), 'head').astype(jnp.float32)]
    ppermute x16 -> x28, starting transfers between devices: 16.2 us -> 28.3 us  [from_partner(): return lax.ppermute(value, axis, pairs)]
    dot_general x2, matrix products: 6.49 us -> 1.42 us  [the longest x1 0.99 us: shards(): lax.dot_general(bit_major_rows(normed, graph_levels), jnp.concatenate([gr...]
    ppermute x8, local copies, waits for them, and re-layouts: 10.7 us -> 7.25 us  [from_partner(): return lax.ppermute(value, axis, pairs)]
  transfers between devices with their start and end apart: 20 -> 30, of which waited for: 9 -> 14; matrix products, arithmetic and copies ran while one was open for 17% -> 21% of each run, Pallas kernels for 0% -> 0%
where the time goes in v1:
time: 142 us; the launch traced here: 141 us
  waiting for transfers between devices  62.3 us (44%)
  starting transfers between devices  30.4 us (21%)
  local copies, waits for them, and re-layouts  21.6 us (15%)
  matrix products  18.9 us (13%)
  other arithmetic  6.69 us (5%)
    ppermute x28, waiting for transfers between devices, from_partner(): return lax.ppermute(value, axis, pairs)  49.8 us
    ppermute x28, starting transfers between devices, from_partner(): return lax.ppermute(value, axis, pairs)  28.3 us
    ppermute x2, waiting for transfers between devices, head_swap(): return lax.ppermute(value, 'head', [(0, 1), (1, 0)])  12.5 us
    ppermute x8, local copies, waits for them, and re-layouts, from_partner(): return lax.ppermute(value, axis, pairs)  7.25 us
    unnamed x44, local copies, waits for them, and re-layouts  6.54 us
    dot_general x1, matrix products, shards(): jnp.einsum('bqhe,sbkhe->bhqsk', grad_heads, values_all, preferred_element...  3.07 us
  transfers between devices with their start and end apart: 30, of which 14 were waited for; matrix products, arithmetic and copies ran while one was open for 21% of the time, Pallas kernels for 0%

profile of v1, /device:TPU:0, one launch (start us, length us, event | category | flops | bytes accessed | tf_op | source)
XLA Modules:
  0.0 141.1 jit_solution(5971279494777936642)
XLA Ops:
  2.9 2.3 %convolution_convert_fusion.5 = bf16[128,512]{1,0:T(8,128)(2,1)} fusion(bf16[128,1024]{1,0:T(8,128)(2,1)S(1)} %fusion.15, bf16[1024,512]{1,0:T(8,128)(2,1)} %param.12), kind=kOutput, calls=%fused_computation.23 | convolution fusion | flops 134283264 | bytes 1441792 | tf_op jit(solution)/shard_map/dot_general | solution.py:70
  5.7 2.5 %collective-permute-start.1 = (bf16[1,128,512]{2,1,0:T(8,128)(2,1)}, bf16[1,128,512]{2,1,0:T(8,128)(2,1)}, u32[]{:S(2)}, u32[]{:S(2)}) collective-permute-start(bf16[1,128,512]{2,1,0:T(8,128)(2,1)} %bitcast.15), channel_id=1, source_target_pairs={{0,4},{2,6},{4,0},{6,2},{8,12},{10,14},{12,8},{14,10},{16,20},{18,... | collective-permute-start | bytes 393224 | tf_op jit(solution)/shard_map/ppermute | solution.py:16
  8.2 1.6 %collective-permute-start.2 = (bf16[1,128,512]{2,1,0:T(8,128)(2,1)}, bf16[1,128,512]{2,1,0:T(8,128)(2,1)}, u32[]{:S(2)}, u32[]{:S(2)}) collective-permute-start(bf16[1,128,512]{2,1,0:T(8,128)(2,1)} %bitcast.15), channel_id=1, source_target_pairs={{0,8},{2,10},{4,12},{6,14},{8,0},{10,2},{12,4},{14,6},{16,24},{18,... | collective-permute-start | bytes 393224 | tf_op jit(solution)/shard_map/ppermute | solution.py:16
  9.8 2.2 %convolution_convert_fusion.3 = bf16[128,512]{1,0:T(8,128)(2,1)} fusion(bf16[128,1024]{1,0:T(8,128)(2,1)S(1)} %fusion.15, bf16[1024,512]{1,0:T(8,128)(2,1)} %param.11), kind=kOutput, calls=%fused_computation.21 | convolution fusion | flops 134283264 | bytes 1441792 | tf_op jit(solution)/shard_map/dot_general | solution.py:69
  18.5 1.7 %copy.49 = bf16[128,512]{0,1:T(8,128)(2,1)} copy(bf16[128,512]{1,0:T(8,128)(2,1)} %convolution_convert_fusion.4) | data formatting | bytes 262144 | tf_op jit(solution)/shard_map/convert_element_type | solution.py:68
  20.2 1.7 %copy.61 = bf16[128,512]{0,1:T(8,128)(2,1)} copy(bf16[128,512]{1,0:T(8,128)(2,1)} %convolution_convert_fusion.2) | data formatting | bytes 262144 | tf_op jit(solution)/shard_map/convert_element_type | solution.py:113
  23.2 2.9 %collective-permute-start.7 = (bf16[1,128,512]{2,1,0:T(8,128)(2,1)}, bf16[1,128,512]{2,1,0:T(8,128)(2,1)}, u32[]{:S(2)}, u32[]{:S(2)}) collective-permute-start(bf16[1,128,512]{2,1,0:T(8,128)(2,1)} %bitcast.2), channel_id=1, source_target_pairs={{0,16},{2,18},{4,20},{6,22},{8,24},{10,26},{12,28},{14,30},{16,0},... | collective-permute-start | bytes 393224 | tf_op jit(solution)/shard_map/ppermute | solution.py:16
  27.2 3.3 %collective-permute-done.6 = bf16[1,128,512]{2,1,0:T(8,128)(2,1)} collective-permute-done((bf16[1,128,512]{2,1,0:T(8,128)(2,1)}, bf16[1,128,512]{2,1,0:T(8,128)(2,1)}, u32[]{:S(2)}, u32[]{:S(2)}) %collective-permute-start.6) | collective-permute-done | bytes 131104 | tf_op jit(solution)/shard_map/ppermute | solution.py:16
  32.3 3.5 %collective-permute-done.7 = bf16[1,128,512]{2,1,0:T(8,128)(2,1)} collective-permute-done((bf16[1,128,512]{2,1,0:T(8,128)(2,1)}, bf16[1,128,512]{2,1,0:T(8,128)(2,1)}, u32[]{:S(2)}, u32[]{:S(2)}) %collective-permute-start.7) | collective-permute-done | bytes 131104 | tf_op jit(solution)/shard_map/ppermute | solution.py:16
  36.8 1.7 %fusion = (f32[8,128]{1,0:T(8,128)S(1)}, f32[8,128,5,128]{1,3,2,0:T(8,128)S(1)}) fusion(pred[5]{0:T(512)(128)(4,1)S(1)} %compare_bitcast_fusion, bf16[128,8,64,1]{0,2,3,1:T(8,128)(2,1)} %bitcast.171, bf16[5,1,128,8,64]{2,4,0,3,1:T(8,128)(2,1)S(1)} %constant_dynamic-update-slice_fusion.5), kind=kOutput, calls=%fused_computation.6 | convolution fusion | flops 85851136 | bytes 3411973 | tf_op jit(solution)/shard_map/bqhe,sbkhe->bhqsk/dot_general | solution.py:95
  46.6 3.1 %multiply_reduce_fusion = (f32[8,128]{1,0:T(8,128)S(1)}, f32[8,128,5,128]{1,3,2,0:T(8,128)S(1)}) fusion(f32[8,128]{1,0:T(8,128)S(1)} %fusion.2, f32[8,128]{1,0:T(8,128)S(1)} %get-tuple-element.36, f32[8,128,5,128]{1,3,2,0:T(8,128)} %copy-done.1, pred[5]{0:T(512)(128)(4,1)S(1)} %compare_bitcast_fusion, bf16[128,8,64,1]{0,2,3,1:T(8,128)(2,1)S(1)} %bitcast.188, ...), kind=kOutput, calls=%fused_computation.3 | convolution fusion | flops 87817216 | bytes 6041605 | tf_op jit(solution)/shard_map/bqhe,sbkhe->bhqsk/dot_general | solution.py:122
  54.8 4.1 %collective-permute-start.11 = (bf16[1,128,512]{1,2,0:T(8,128)(2,1)S(1)}, bf16[1,128,512]{1,2,0:T(8,128)(2,1)S(1)}, u32[]{:S(2)}, u32[]{:S(2)}) collective-permute-start(bf16[1,128,512]{1,2,0:T(8,128)(2,1)S(1)} %bitcast.186), channel_id=1, source_target_pairs={{0,8},{2,10},{4,12},{6,14},{8,0},{10,2},{12,4},{14,6},{16,24},{18,... | collective-permute-start | bytes 393224 | tf_op jit(solution)/shard_map/ppermute | solution.py:16
  61.1 2.4 %collective-permute-done.12 = bf16[1,128,512]{1,2,0:T(8,128)(2,1)S(1)} collective-permute-done((bf16[1,128,512]{1,2,0:T(8,128)(2,1)S(1)}, bf16[1,128,512]{1,2,0:T(8,128)(2,1)S(1)}, u32[]{:S(2)}, u32[]{:S(2)}) %collective-permute-start.12) | collective-permute-done | bytes 131104 | tf_op jit(solution)/shard_map/ppermute | solution.py:16
  63.6 1.6 %collective-permute-start.14 = (bf16[1,128,512]{1,2,0:T(8,128)(2,1)S(1)}, bf16[1,128,512]{1,2,0:T(8,128)(2,1)S(1)}, u32[]{:S(2)}, u32[]{:S(2)}) collective-permute-start(bf16[1,128,512]{1,2,0:T(8,128)(2,1)S(1)} %bitcast.182), channel_id=1, source_target_pairs={{0,4},{2,6},{4,0},{6,2},{8,12},{10,14},{12,8},{14,10},{16,20},{18,... | collective-permute-start | bytes 393224 | tf_op jit(solution)/shard_map/ppermute | solution.py:16
  65.4 5.1 %collective-permute-done.16 = bf16[1,128,512]{1,2,0:T(8,128)(2,1)S(1)} collective-permute-done((bf16[1,128,512]{1,2,0:T(8,128)(2,1)S(1)}, bf16[1,128,512]{1,2,0:T(8,128)(2,1)S(1)}, u32[]{:S(2)}, u32[]{:S(2)}) %collective-permute-start.16) | collective-permute-done | bytes 131104 | tf_op jit(solution)/shard_map/ppermute | solution.py:16
  74.6 1.6 %collective-permute-start.17 = (f32[128,1024]{1,0:T(8,128)S(1)}, f32[128,1024]{1,0:T(8,128)S(1)}, u32[]{:S(2)}, u32[]{:S(2)}) collective-permute-start(f32[128,1024]{1,0:T(8,128)S(1)} %convolution_add_fusion), channel_id=1, source_target_pairs={{0,1},{1,0},{2,3},{3,2},{4,5},{5,4},{6,7},{7,6},{8,9},{9,8},{10,11... | collective-permute-start | bytes 1572872 | tf_op jit(solution)/shard_map/ppermute | solution.py:46
  77.3 12.2 %collective-permute-done.17 = f32[128,1024]{1,0:T(8,128)S(1)} collective-permute-done((f32[128,1024]{1,0:T(8,128)S(1)}, f32[128,1024]{1,0:T(8,128)S(1)}, u32[]{:S(2)}, u32[]{:S(2)}) %collective-permute-start.17) | collective-permute-done | bytes 524320 | tf_op jit(solution)/shard_map/ppermute | solution.py:46
  94.5 4.5 %collective-permute-done.19 = f32[1024]{0:T(1024)S(1)} collective-permute-done((f32[1024]{0:T(1024)S(1)}, f32[1024]{0:T(1024)S(1)}, u32[]{:S(2)}, u32[]{:S(2)}) %collective-permute-start.19) | collective-permute-done | bytes 4128 | tf_op jit(solution)/shard_map/ppermute | solution.py:16
  99.1 3.6 %collective-permute-done.20 = f32[1024]{0:T(1024)S(1)} collective-permute-done((f32[1024]{0:T(1024)S(1)}, f32[1024]{0:T(1024)S(1)}, u32[]{:S(2)}, u32[]{:S(2)}) %collective-permute-start.20) | collective-permute-done | bytes 4128 | tf_op jit(solution)/shard_map/ppermute | solution.py:16
  104.1 2.1 %collective-permute-start.28 = (bf16[128,512]{0,1:T(8,128)(2,1)S(1)}, bf16[128,512]{0,1:T(8,128)(2,1)S(1)}, u32[]{:S(2)}, u32[]{:S(2)}) collective-permute-start(bf16[128,512]{0,1:T(8,128)(2,1)S(1)} %dynamic-slice_convert_fusion.7), channel_id=1, source_target_pairs={{0,8},{2,10},{4,12},{6,14},{8,0},{10,2},{12,4},{14,6},{16,24},{18,... | collective-permute-start | bytes 393224 | tf_op jit(solution)/shard_map/ppermute | solution.py:16
  106.1 9.4 %collective-permute-done.23 = bf16[256,1536]{1,0:T(8,128)(2,1)S(1)} collective-permute-done((bf16[256,1536]{1,0:T(8,128)(2,1)S(1)}, bf16[256,1536]{1,0:T(8,128)(2,1)S(1)}, u32[]{:S(2)}, u32[]{:S(2)}) %collective-permute-start.23) | collective-permute-done | bytes 786464 | tf_op jit(solution)/shard_map/ppermute | solution.py:16
  117.5 3.5 %collective-permute-start.29 = (bf16[64,512]{0,1:T(8,128)(2,1)S(1)}, bf16[64,512]{0,1:T(8,128)(2,1)S(1)}, u32[]{:S(2)}, u32[]{:S(2)}) collective-permute-start(bf16[64,512]{0,1:T(8,128)(2,1)S(1)} %dynamic-slice_convert_fusion.6), channel_id=1, source_target_pairs={{0,16},{2,18},{4,20},{6,22},{8,24},{10,26},{12,28},{14,30},{16,0},... | collective-permute-start | bytes 196616 | tf_op jit(solution)/shard_map/ppermute | solution.py:16
  121.0 8.4 %collective-permute-done.24 = bf16[128,1536]{1,0:T(8,128)(2,1)S(1)} collective-permute-done((bf16[128,1536]{1,0:T(8,128)(2,1)S(1)}, bf16[128,1536]{1,0:T(8,128)(2,1)S(1)}, u32[]{:S(2)}, u32[]{:S(2)}) %collective-permute-start.24) | collective-permute-done | bytes 393248 | tf_op jit(solution)/shard_map/ppermute | solution.py:16
  131.7 8.6 %collective-permute-done.25 = bf16[64,1536]{1,0:T(8,128)(2,1)S(1)} collective-permute-done((bf16[64,1536]{1,0:T(8,128)(2,1)S(1)}, bf16[64,1536]{1,0:T(8,128)(2,1)S(1)}, u32[]{:S(2)}, u32[]{:S(2)}) %collective-permute-start.25) | collective-permute-done | bytes 196640 | tf_op jit(solution)/shard_map/ppermute | solution.py:16
  (149 shorter events, 46.4 us)
Async XLA Ops:
  5.2 35.4 %collective-permute-start = (bf16[1,128,512]{2,1,0:T(8,128)(2,1)}, bf16[1,128,512]{2,1,0:T(8,128)(2,1)}, u32[]{:S(2)}, u32[]{:S(2)}) collective-permute-start(bf16[1,128,512]{2,1,0:T(8,128)(2,1)} %bitcast.15), channel_id=1, source_target_pairs={{0,2},{2,0},{4,6},{6,4},{8,10},{10,8},{12,14},{14,12},{16,18},{18,... | collective-permute-start | bytes 393224 | tf_op jit(solution)/shard_map/ppermute | solution.py:16
  5.7 36.6 %collective-permute-start.1 = (bf16[1,128,512]{2,1,0:T(8,128)(2,1)}, bf16[1,128,512]{2,1,0:T(8,128)(2,1)}, u32[]{:S(2)}, u32[]{:S(2)}) collective-permute-start(bf16[1,128,512]{2,1,0:T(8,128)(2,1)} %bitcast.15), channel_id=1, source_target_pairs={{0,4},{2,6},{4,0},{6,2},{8,12},{10,14},{12,8},{14,10},{16,20},{18,... | collective-permute-start | bytes 393224 | tf_op jit(solution)/shard_map/ppermute | solution.py:16
  8.2 35.9 %collective-permute-start.2 = (bf16[1,128,512]{2,1,0:T(8,128)(2,1)}, bf16[1,128,512]{2,1,0:T(8,128)(2,1)}, u32[]{:S(2)}, u32[]{:S(2)}) collective-permute-start(bf16[1,128,512]{2,1,0:T(8,128)(2,1)} %bitcast.15), channel_id=1, source_target_pairs={{0,8},{2,10},{4,12},{6,14},{8,0},{10,2},{12,4},{14,6},{16,24},{18,... | collective-permute-start | bytes 393224 | tf_op jit(solution)/shard_map/ppermute | solution.py:16
  12.0 9.9 %collective-permute-start.4 = (bf16[1,128,512]{2,1,0:T(8,128)(2,1)}, bf16[1,128,512]{2,1,0:T(8,128)(2,1)}, u32[]{:S(2)}, u32[]{:S(2)}) collective-permute-start(bf16[1,128,512]{2,1,0:T(8,128)(2,1)} %bitcast.2), channel_id=1, source_target_pairs={{0,2},{2,0},{4,6},{6,4},{8,10},{10,8},{12,14},{14,12},{16,18},{18,... | collective-permute-start | bytes 393224 | tf_op jit(solution)/shard_map/ppermute | solution.py:16
  12.0 11.3 %collective-permute-start.5 = (bf16[1,128,512]{2,1,0:T(8,128)(2,1)}, bf16[1,128,512]{2,1,0:T(8,128)(2,1)}, u32[]{:S(2)}, u32[]{:S(2)}) collective-permute-start(bf16[1,128,512]{2,1,0:T(8,128)(2,1)} %bitcast.2), channel_id=1, source_target_pairs={{0,4},{2,6},{4,0},{6,2},{8,12},{10,14},{12,8},{14,10},{16,20},{18,... | collective-permute-start | bytes 393224 | tf_op jit(solution)/shard_map/ppermute | solution.py:16
  21.9 8.5 %collective-permute-start.6 = (bf16[1,128,512]{2,1,0:T(8,128)(2,1)}, bf16[1,128,512]{2,1,0:T(8,128)(2,1)}, u32[]{:S(2)}, u32[]{:S(2)}) collective-permute-start(bf16[1,128,512]{2,1,0:T(8,128)(2,1)} %bitcast.2), channel_id=1, source_target_pairs={{0,8},{2,10},{4,12},{6,14},{8,0},{10,2},{12,4},{14,6},{16,24},{18,... | collective-permute-start | bytes 393224 | tf_op jit(solution)/shard_map/ppermute | solution.py:16
  23.2 12.5 %collective-permute-start.7 = (bf16[1,128,512]{2,1,0:T(8,128)(2,1)}, bf16[1,128,512]{2,1,0:T(8,128)(2,1)}, u32[]{:S(2)}, u32[]{:S(2)}) collective-permute-start(bf16[1,128,512]{2,1,0:T(8,128)(2,1)} %bitcast.2), channel_id=1, source_target_pairs={{0,16},{2,18},{4,20},{6,22},{8,24},{10,26},{12,28},{14,30},{16,0},... | collective-permute-start | bytes 393224 | tf_op jit(solution)/shard_map/ppermute | solution.py:16
  30.4 15.4 %collective-permute-start.3 = (bf16[1,128,512]{2,1,0:T(8,128)(2,1)}, bf16[1,128,512]{2,1,0:T(8,128)(2,1)S(1)}, u32[]{:S(2)}, u32[]{:S(2)}) collective-permute-start(bf16[1,128,512]{2,1,0:T(8,128)(2,1)} %bitcast.15), channel_id=1, source_target_pairs={{0,16},{2,18},{4,20},{6,22},{8,24},{10,26},{12,28},{14,30},{16,0},... | collective-permute-start | bytes 393224 | tf_op jit(solution)/shard_map/ppermute | solution.py:16
  54.7 8.7 %collective-permute-start.12 = (bf16[1,128,512]{1,2,0:T(8,128)(2,1)S(1)}, bf16[1,128,512]{1,2,0:T(8,128)(2,1)S(1)}, u32[]{:S(2)}, u32[]{:S(2)}) collective-permute-start(bf16[1,128,512]{1,2,0:T(8,128)(2,1)S(1)} %bitcast.187), channel_id=1, source_target_pairs={{0,16},{2,18},{4,20},{6,22},{8,24},{10,26},{12,28},{14,30},{16,0},... | collective-permute-start | bytes 393224 | tf_op jit(solution)/shard_map/ppermute | solution.py:16
  54.8 8.8 %collective-permute-start.11 = (bf16[1,128,512]{1,2,0:T(8,128)(2,1)S(1)}, bf16[1,128,512]{1,2,0:T(8,128)(2,1)S(1)}, u32[]{:S(2)}, u32[]{:S(2)}) collective-permute-start(bf16[1,128,512]{1,2,0:T(8,128)(2,1)S(1)} %bitcast.186), channel_id=1, source_target_pairs={{0,8},{2,10},{4,12},{6,14},{8,0},{10,2},{12,4},{14,6},{16,24},{18,... | collective-permute-start | bytes 393224 | tf_op jit(solution)/shard_map/ppermute | solution.py:16
  60.9 9.5 %collective-permute-start.16 = (bf16[1,128,512]{1,2,0:T(8,128)(2,1)S(1)}, bf16[1,128,512]{1,2,0:T(8,128)(2,1)S(1)}, u32[]{:S(2)}, u32[]{:S(2)}) collective-permute-start(bf16[1,128,512]{1,2,0:T(8,128)(2,1)S(1)} %bitcast.185), channel_id=1, source_target_pairs={{0,16},{2,18},{4,20},{6,22},{8,24},{10,26},{12,28},{14,30},{16,0},... | collective-permute-start | bytes 393224 | tf_op jit(solution)/shard_map/ppermute | solution.py:16
  63.5 7.6 %collective-permute-start.15 = (bf16[1,128,512]{1,2,0:T(8,128)(2,1)S(1)}, bf16[1,128,512]{1,2,0:T(8,128)(2,1)S(1)}, u32[]{:S(2)}, u32[]{:S(2)}) collective-permute-start(bf16[1,128,512]{1,2,0:T(8,128)(2,1)S(1)} %bitcast.184), channel_id=1, source_target_pairs={{0,8},{2,10},{4,12},{6,14},{8,0},{10,2},{12,4},{14,6},{16,24},{18,... | collective-permute-start | bytes 393224 | tf_op jit(solution)/shard_map/ppermute | solution.py:16
  63.6 7.5 %collective-permute-start.14 = (bf16[1,128,512]{1,2,0:T(8,128)(2,1)S(1)}, bf16[1,128,512]{1,2,0:T(8,128)(2,1)S(1)}, u32[]{:S(2)}, u32[]{:S(2)}) collective-permute-start(bf16[1,128,512]{1,2,0:T(8,128)(2,1)S(1)} %bitcast.182), channel_id=1, source_target_pairs={{0,4},{2,6},{4,0},{6,2},{8,12},{10,14},{12,8},{14,10},{16,20},{18,... | collective-permute-start | bytes 393224 | tf_op jit(solution)/shard_map/ppermute | solution.py:16
  72.4 19.5 %collective-permute-start.22 = (bf16[512,1536]{1,0:T(8,128)(2,1)S(1)}, bf16[512,1536]{1,0:T(8,128)(2,1)S(1)}, u32[]{:S(2)}, u32[]{:S(2)}) collective-permute-start(bf16[512,1536]{1,0:T(8,128)(2,1)S(1)} %dynamic-slice_convert_fusion), channel_id=1, source_target_pairs={{0,2},{2,0},{4,6},{6,4},{8,10},{10,8},{12,14},{14,12},{16,18},{18,... | collective-permute-start | bytes 4718600 | tf_op jit(solution)/shard_map/ppermute | solution.py:16
  74.6 14.9 %collective-permute-start.17 = (f32[128,1024]{1,0:T(8,128)S(1)}, f32[128,1024]{1,0:T(8,128)S(1)}, u32[]{:S(2)}, u32[]{:S(2)}) collective-permute-start(f32[128,1024]{1,0:T(8,128)S(1)} %convolution_add_fusion), channel_id=1, source_target_pairs={{0,1},{1,0},{2,3},{3,2},{4,5},{5,4},{6,7},{7,6},{8,9},{9,8},{10,11... | collective-permute-start | bytes 1572872 | tf_op jit(solution)/shard_map/ppermute | solution.py:46
  76.5 17.3 %collective-permute-start.8 = (f32[128,512]{1,0:T(8,128)S(1)}, f32[128,512]{1,0:T(8,128)S(1)}, u32[]{:S(2)}, u32[]{:S(2)}) collective-permute-start(f32[128,512]{1,0:T(8,128)S(1)} %constant_dynamic-slice_fusion), channel_id=1, source_target_pairs={{0,1},{1,0},{2,3},{3,2},{4,5},{5,4},{6,7},{7,6},{8,9},{9,8},{10,11... | collective-permute-start | bytes 786440 | tf_op jit(solution)/shard_map/ppermute | solution.py:46
  89.8 14.1 %collective-permute-start.27 = (bf16[256,512]{0,1:T(8,128)(2,1)S(1)}, bf16[256,512]{0,1:T(8,128)(2,1)S(1)}, u32[]{:S(2)}, u32[]{:S(2)}) collective-permute-start(bf16[256,512]{0,1:T(8,128)(2,1)S(1)} %dynamic-slice_convert_fusion.4), channel_id=1, source_target_pairs={{0,4},{2,6},{4,0},{6,2},{8,12},{10,14},{12,8},{14,10},{16,20},{18,... | collective-permute-start | bytes 786440 | tf_op jit(solution)/shard_map/ppermute | solution.py:16
  90.9 8.1 %collective-permute-start.19 = (f32[1024]{0:T(1024)S(1)}, f32[1024]{0:T(1024)S(1)}, u32[]{:S(2)}, u32[]{:S(2)}) collective-permute-start(f32[1024]{0:T(1024)S(1)} %add.137), channel_id=1, source_target_pairs={{0,4},{2,6},{4,0},{6,2},{8,12},{10,14},{12,8},{14,10},{16,20},{18,... | collective-permute-start | bytes 12296 | tf_op jit(solution)/shard_map/ppermute | solution.py:16
  92.5 23.0 %collective-permute-start.23 = (bf16[256,1536]{1,0:T(8,128)(2,1)S(1)}, bf16[256,1536]{1,0:T(8,128)(2,1)S(1)}, u32[]{:S(2)}, u32[]{:S(2)}) collective-permute-start(bf16[256,1536]{1,0:T(8,128)(2,1)S(1)} %dynamic-slice_convert_fusion.1), channel_id=1, source_target_pairs={{0,4},{2,6},{4,0},{6,2},{8,12},{10,14},{12,8},{14,10},{16,20},{18,... | collective-permute-start | bytes 2359304 | tf_op jit(solution)/shard_map/ppermute | solution.py:16
  102.7 14.1 %collective-permute-start.21 = (f32[1024]{0:T(1024)S(1)}, f32[1024]{0:T(1024)S(1)}, u32[]{:S(2)}, u32[]{:S(2)}) collective-permute-start(f32[1024]{0:T(1024)S(1)} %add.139), channel_id=1, source_target_pairs={{0,16},{2,18},{4,20},{6,22},{8,24},{10,26},{12,28},{14,30},{16,0},... | collective-permute-start | bytes 12296 | tf_op jit(solution)/shard_map/ppermute | solution.py:16
  104.1 13.3 %collective-permute-start.28 = (bf16[128,512]{0,1:T(8,128)(2,1)S(1)}, bf16[128,512]{0,1:T(8,128)(2,1)S(1)}, u32[]{:S(2)}, u32[]{:S(2)}) collective-permute-start(bf16[128,512]{0,1:T(8,128)(2,1)S(1)} %dynamic-slice_convert_fusion.7), channel_id=1, source_target_pairs={{0,8},{2,10},{4,12},{6,14},{8,0},{10,2},{12,4},{14,6},{16,24},{18,... | collective-permute-start | bytes 393224 | tf_op jit(solution)/shard_map/ppermute | solution.py:16
  115.8 13.6 %collective-permute-start.24 = (bf16[128,1536]{1,0:T(8,128)(2,1)S(1)}, bf16[128,1536]{1,0:T(8,128)(2,1)S(1)}, u32[]{:S(2)}, u32[]{:S(2)}) collective-permute-start(bf16[128,1536]{1,0:T(8,128)(2,1)S(1)} %dynamic-slice_convert_fusion.3), channel_id=1, source_target_pairs={{0,8},{2,10},{4,12},{6,14},{8,0},{10,2},{12,4},{14,6},{16,24},{18,... | collective-permute-start | bytes 1179656 | tf_op jit(solution)/shard_map/ppermute | solution.py:16
  117.5 13.3 %collective-permute-start.29 = (bf16[64,512]{0,1:T(8,128)(2,1)S(1)}, bf16[64,512]{0,1:T(8,128)(2,1)S(1)}, u32[]{:S(2)}, u32[]{:S(2)}) collective-permute-start(bf16[64,512]{0,1:T(8,128)(2,1)S(1)} %dynamic-slice_convert_fusion.6), channel_id=1, source_target_pairs={{0,16},{2,18},{4,20},{6,22},{8,24},{10,26},{12,28},{14,30},{16,0},... | collective-permute-start | bytes 196616 | tf_op jit(solution)/shard_map/ppermute | solution.py:16
  129.5 10.8 %collective-permute-start.25 = (bf16[64,1536]{1,0:T(8,128)(2,1)S(1)}, bf16[64,1536]{1,0:T(8,128)(2,1)S(1)}, u32[]{:S(2)}, u32[]{:S(2)}) collective-permute-start(bf16[64,1536]{1,0:T(8,128)(2,1)S(1)} %dynamic-slice_convert_fusion.5), channel_id=1, source_target_pairs={{0,16},{2,18},{4,20},{6,22},{8,24},{10,26},{12,28},{14,30},{16,0},... | collective-permute-start | bytes 589832 | tf_op jit(solution)/shard_map/ppermute | solution.py:16
  (21 other events, 135.0 us)

commit v2 on v1

--- a/solution.py
+++ b/solution.py
@@ -16,17 +16,18 @@
     return lax.ppermute(value, axis, pairs)
 
 
-def bit_major_rows(matrix, levels):
+def bit_major_rows(matrix, order):
     rows, width = matrix.shape
+    levels = len(order)
     inner = width >> levels
     shaped = matrix.reshape((rows,) + (2,) * levels + (inner,))
-    order = (0,) + tuple(range(levels, 0, -1)) + (levels + 1,)
-    return shaped.transpose(order).reshape(rows, width)
-
-
-def halving_sum(partial, axis, levels):
+    axes = (0,) + tuple(levels - bit for bit in order) + (levels + 1,)
+    return shaped.transpose(axes).reshape(rows, width)
+
+
+def halving_sum(partial, axis, order):
     me = lax.axis_index(axis)
-    for bit in range(levels):
+    for bit in order:
         half = partial.shape[0] // 2
         mine = (me >> bit) & 1
         keep = lax.dynamic_slice_in_dim(partial, mine * half, half, 0)
@@ -34,6 +35,39 @@
         got = from_partner(send.astype(jnp.bfloat16), axis, bit)
         partial = keep + got.astype(jnp.float32)
     return partial
+
+
+def split_orders(levels):
+    first = tuple(range(levels))
+    if levels < 3:
+        return first, first
+    return first, (0, 2, 1) + first[3:]
+
+
+def scatter_rows(pairs, axis, levels):
+    contract = (((0,), (0,)), ((), ()))
+    chunks = []
+    for index, order in enumerate(split_orders(levels)):
+        pieces = []
+        for left, right in pairs:
+            cut = right.shape[1] // 2
+            piece = right[:, index * cut : (index + 1) * cut]
+            pieces.append(
+                lax.dot_general(
+                    bit_major_rows(left, order), piece, contract,
+                    preferred_element_type=jnp.float32,
+                )
+            )
+        chunks.append(halving_sum(jnp.concatenate(pieces, axis=1), axis, order))
+    results = []
+    offset = 0
+    for left, right in pairs:
+        cut = right.shape[1] // 2
+        results.append(
+            jnp.concatenate([chunk[:, offset : offset + cut] for chunk in chunks], axis=1)
+        )
+        offset += cut
+    return results
 
 
 def doubling_sum(value, axis, levels):
@@ -113,11 +147,6 @@
     grad_attended = jnp.dot(cotangent, w_out.T, preferred_element_type=jnp.float32).astype(
         jnp.bfloat16
     )
-    out_terms = lax.dot_general(
-        bit_major_rows(cotangent, graph_levels), attended, contract_rows,
-        preferred_element_type=jnp.float32,
-    )
-    w_out_grad = halving_sum(out_terms, "graph", graph_levels).T
     grad_heads = grad_attended.reshape(head_shape)
     grad_probs = jnp.einsum(
         "bqhe,sbkhe->bhqsk", grad_heads, values_all, preferred_element_type=jnp.float32
@@ -144,25 +173,20 @@
         grad_value = grad_value + returned[bit][1].astype(jnp.float32)
     grad_key = grad_key.astype(jnp.bfloat16).reshape(node_rows, columns)
     grad_value = grad_value.astype(jnp.bfloat16).reshape(node_rows, columns)
-    joined_rows = halving_sum(
-        lax.dot_general(
-            bit_major_rows(normed, graph_levels),
-            jnp.concatenate([grad_query, grad_key, grad_value], axis=1),
-            contract_rows,
-            preferred_element_type=jnp.float32,
-        ),
-        "graph",
-        graph_levels,
-    )
-    w_query_grad = joined_rows[:, :columns]
-    w_key_grad = joined_rows[:, columns : 2 * columns]
-    w_value_grad = joined_rows[:, 2 * columns :]
+    w_out_rows, w_query_grad = scatter_rows(
+        [(cotangent, attended), (normed, grad_query)], "graph", graph_levels
+    )
+    w_out_grad = w_out_rows.T
+    w_key_grad, w_value_grad = scatter_rows(
+        [(normed, grad_key), (normed, grad_value)], "graph", graph_levels
+    )
     feature_terms = (
         jnp.dot(grad_query, w_query.T, preferred_element_type=jnp.float32)
         + jnp.dot(grad_key, w_key.T, preferred_element_type=jnp.float32)
         + jnp.dot(grad_value, w_value.T, preferred_element_type=jnp.float32)
     )
-    grad_normed = feature_terms + head_swap(feature_terms)
+    low_terms = feature_terms.astype(jnp.bfloat16)
+    grad_normed = low_terms.astype(jnp.float32) + head_swap(low_terms).astype(jnp.float32)
     gain_grad = doubling_sum(
         jnp.sum(grad_normed * wide_nodes * inverse, axis=0), "graph", graph_levels
     )

time: 142 us -> 136 us (0.958)
  waiting for transfers between devices: 62.3 us -> 41.7 us
  starting transfers between devices: 30.4 us -> 41.2 us
  local copies, waits for them, and re-layouts: 21.6 us -> 24.7 us
    ppermute x28 -> x36, waiting for transfers between devices: 49.8 us -> 34.4 us  [from_partner(): return lax.ppermute(value, axis, pairs)]
    ppermute x28 -> x36, starting transfers between devices: 28.3 us -> 39 us  [from_partner(): return lax.ppermute(value, axis, pairs)]
    ppermute x2, waiting for transfers between devices: 12.5 us -> 7.31 us  [head_swap(): return lax.ppermute(value, 'head', [(0, 1), (1, 0)])]
    unnamed x44 -> x45, local copies, waits for them, and re-layouts: 6.54 us -> 11.2 us
  transfers between devices with their start and end apart: 30 -> 38, of which waited for: 14 -> 15; matrix products, arithmetic and copies ran while one was open for 21% -> 25% of each run, Pallas kernels for 0% -> 0%
where the time goes in v2:
time: 136 us; the launch traced here: 135 us
  waiting for transfers between devices  41.7 us (31%)
  starting transfers between devices  41.2 us (30%)
  local copies, waits for them, and re-layouts  24.7 us (18%)
  matrix products  18.3 us (13%)
  other arithmetic  7.89 us (6%)
  between operations  1.46 us (1%)
    ppermute x36, starting transfers between devices, from_partner(): return lax.ppermute(value, axis, pairs)  39 us
    ppermute x36, waiting for transfers between devices, from_partner(): return lax.ppermute(value, axis, pairs)  34.4 us
    unnamed x45, local copies, waits for them, and re-layouts  11.2 us
    ppermute x2, waiting for transfers between devices, head_swap(): return lax.ppermute(value, 'head', [(0, 1), (1, 0)])  7.31 us
    ppermute x8, local copies, waits for them, and re-layouts, from_partner(): return lax.ppermute(value, axis, pairs)  7.25 us
    dot_general x1, matrix products, shards(): jnp.einsum('bqhe,sbkhe->bhqsk', grad_heads, values_all, preferred_element...  3.09 us
  transfers between devices with their start and end apart: 38, of which 15 were waited for; matrix products, arithmetic and copies ran while one was open for 25% of the time, Pallas kernels for 0%

profile of v2, /device:TPU:0, one launch (start us, length us, event | category | flops | bytes accessed | tf_op | source)
XLA Modules:
  0.0 135.2 jit_solution(5722864253743794754)
XLA Ops:
  5.1 2.6 %collective-permute-start.1 = (bf16[1,128,512]{2,1,0:T(8,128)(2,1)S(1)}, bf16[1,128,512]{2,1,0:T(8,128)(2,1)}, u32[]{:S(2)}, u32[]{:S(2)}) collective-permute-start(bf16[1,128,512]{2,1,0:T(8,128)(2,1)S(1)} %bitcast.196), channel_id=1, source_target_pairs={{0,4},{2,6},{4,0},{6,2},{8,12},{10,14},{12,8},{14,10},{16,20},{18,... | collective-permute-start | bytes 393224 | tf_op jit(solution)/shard_map/ppermute | solution.py:16
  17.4 1.7 %copy.64 = bf16[128,512]{0,1:T(8,128)(2,1)} copy(bf16[128,512]{1,0:T(8,128)(2,1)} %convolution_convert_fusion.2) | data formatting | bytes 262144 | tf_op jit(solution)/shard_map/convert_element_type | solution.py:147
  21.8 2.9 %collective-permute-start.7 = (bf16[1,128,512]{2,1,0:T(8,128)(2,1)S(1)}, bf16[1,128,512]{2,1,0:T(8,128)(2,1)}, u32[]{:S(2)}, u32[]{:S(2)}) collective-permute-start(bf16[1,128,512]{2,1,0:T(8,128)(2,1)S(1)} %bitcast.202), channel_id=1, source_target_pairs={{0,16},{2,18},{4,20},{6,22},{8,24},{10,26},{12,28},{14,30},{16,0},... | collective-permute-start | bytes 393224 | tf_op jit(solution)/shard_map/ppermute | solution.py:16
  26.4 2.5 %collective-permute-start.3 = (bf16[1,128,512]{2,1,0:T(8,128)(2,1)S(1)}, bf16[1,128,512]{2,1,0:T(8,128)(2,1)}, u32[]{:S(2)}, u32[]{:S(2)}) collective-permute-start(bf16[1,128,512]{2,1,0:T(8,128)(2,1)S(1)} %bitcast.198), channel_id=1, source_target_pairs={{0,16},{2,18},{4,20},{6,22},{8,24},{10,26},{12,28},{14,30},{16,0},... | collective-permute-start | bytes 393224 | tf_op jit(solution)/shard_map/ppermute | solution.py:16
  29.7 4.8 %collective-permute-done.7 = bf16[1,128,512]{2,1,0:T(8,128)(2,1)} collective-permute-done((bf16[1,128,512]{2,1,0:T(8,128)(2,1)S(1)}, bf16[1,128,512]{2,1,0:T(8,128)(2,1)}, u32[]{:S(2)}, u32[]{:S(2)}) %collective-permute-start.7) | collective-permute-done | bytes 131104 | tf_op jit(solution)/shard_map/ppermute | solution.py:16
  36.3 1.7 %fusion = (f32[8,128]{1,0:T(8,128)S(1)}, f32[8,128,5,128]{1,3,2,0:T(8,128)S(1)}) fusion(pred[5]{0:T(512)(128)(4,1)S(1)} %compare_bitcast_fusion, bf16[128,8,64,1]{0,2,3,1:T(8,128)(2,1)S(1)} %bitcast.188, bf16[5,1,128,8,64]{2,4,0,3,1:T(8,128)(2,1)} %constant_dynamic-update-slice_fusion.5), kind=kOutput, calls=%fused_computation.20 | convolution fusion | flops 85851136 | bytes 3411973 | tf_op jit(solution)/shard_map/bqhe,sbkhe->bhqsk/dot_general | solution.py:129
  47.0 3.1 %multiply_reduce_fusion = (f32[8,128]{1,0:T(8,128)S(1)}, f32[8,128,5,128]{1,3,2,0:T(8,128)S(1)}) fusion(f32[8,128]{1,0:T(8,128)S(1)} %fusion.2, f32[8,128]{1,0:T(8,128)S(1)} %get-tuple-element.41, f32[8,128,5,128]{1,3,2,0:T(8,128)} %copy-done.1, pred[5]{0:T(512)(128)(4,1)S(1)} %compare_bitcast_fusion, bf16[128,8,64,1]{0,2,3,1:T(8,128)(2,1)} %bitcast.217, ...), kind=kOutput, calls=%fused_computation.1 | convolution fusion | flops 87817216 | bytes 6041605 | tf_op jit(solution)/shard_map/bqhe,sbkhe->bhqsk/dot_general | solution.py:151
  57.2 3.5 %collective-permute-start.11 = (bf16[1,128,512]{1,2,0:T(8,128)(2,1)S(1)}, bf16[1,128,512]{1,2,0:T(8,128)(2,1)S(1)}, u32[]{:S(2)}, u32[]{:S(2)}) collective-permute-start(bf16[1,128,512]{1,2,0:T(8,128)(2,1)S(1)} %bitcast.215), channel_id=1, source_target_pairs={{0,8},{2,10},{4,12},{6,14},{8,0},{10,2},{12,4},{14,6},{16,24},{18,... | collective-permute-start | bytes 393224 | tf_op jit(solution)/shard_map/ppermute | solution.py:16
  65.1 2.3 %collective-permute-start.15 = (bf16[1,128,512]{1,2,0:T(8,128)(2,1)S(1)}, bf16[1,128,512]{1,2,0:T(8,128)(2,1)S(1)}, u32[]{:S(2)}, u32[]{:S(2)}) collective-permute-start(bf16[1,128,512]{1,2,0:T(8,128)(2,1)S(1)} %bitcast.211), channel_id=1, source_target_pairs={{0,8},{2,10},{4,12},{6,14},{8,0},{10,2},{12,4},{14,6},{16,24},{18,... | collective-permute-start | bytes 393224 | tf_op jit(solution)/shard_map/ppermute | solution.py:16
  70.2 2.7 %collective-permute-done.16 = bf16[1,128,512]{1,2,0:T(8,128)(2,1)S(1)} collective-permute-done((bf16[1,128,512]{1,2,0:T(8,128)(2,1)S(1)}, bf16[1,128,512]{1,2,0:T(8,128)(2,1)S(1)}, u32[]{:S(2)}, u32[]{:S(2)}) %collective-permute-start.16) | collective-permute-done | bytes 131104 | tf_op jit(solution)/shard_map/ppermute | solution.py:16
  75.5 7.3 %collective-permute-done.17 = bf16[128,1024]{1,0:T(8,128)(2,1)S(1)} collective-permute-done((bf16[128,1024]{1,0:T(8,128)(2,1)S(1)}, bf16[128,1024]{1,0:T(8,128)(2,1)S(1)}, u32[]{:S(2)}, u32[]{:S(2)}) %collective-permute-start.17) | collective-permute-done | bytes 262176 | tf_op jit(solution)/shard_map/ppermute | solution.py:80
  86.3 1.8 %collective-permute-done.19 = f32[1024]{0:T(1024)S(1)} collective-permute-done((f32[1024]{0:T(1024)S(1)}, f32[1024]{0:T(1024)S(1)}, u32[]{:S(2)}, u32[]{:S(2)}) %collective-permute-start.19) | collective-permute-done | bytes 4128 | tf_op jit(solution)/shard_map/ppermute | solution.py:16
  88.1 3.6 %collective-permute-done.20 = f32[1024]{0:T(1024)S(1)} collective-permute-done((f32[1024]{0:T(1024)S(1)}, f32[1024]{0:T(1024)S(1)}, u32[]{:S(2)}, u32[]{:S(2)}) %collective-permute-start.20) | collective-permute-done | bytes 4128 | tf_op jit(solution)/shard_map/ppermute | solution.py:16
  93.6 2.6 %collective-permute-done.21 = f32[1024]{0:T(1024)S(1)} collective-permute-done((f32[1024]{0:T(1024)S(1)}, f32[1024]{0:T(1024)S(1)}, u32[]{:S(2)}, u32[]{:S(2)}) %collective-permute-start.21) | collective-permute-done | bytes 4128 | tf_op jit(solution)/shard_map/ppermute | solution.py:16
  99.0 1.9 %collective-permute-start.35 = (bf16[256,512]{0,1:T(8,128)(2,1)S(1)}, bf16[256,512]{0,1:T(8,128)(2,1)S(1)}, u32[]{:S(2)}, u32[]{:S(2)}) collective-permute-start(bf16[256,512]{0,1:T(8,128)(2,1)S(1)} %dynamic-slice_convert_fusion), channel_id=1, source_target_pairs={{0,8},{2,10},{4,12},{6,14},{8,0},{10,2},{12,4},{14,6},{16,24},{18,... | collective-permute-start | bytes 786440 | tf_op jit(solution)/shard_map/ppermute | solution.py:16
  102.1 4.2 %collective-permute-done.27 = bf16[256,512]{0,1:T(8,128)(2,1)S(1)} collective-permute-done((bf16[256,512]{0,1:T(8,128)(2,1)S(1)}, bf16[256,512]{0,1:T(8,128)(2,1)S(1)}, u32[]{:S(2)}, u32[]{:S(2)}) %collective-permute-start.27) | collective-permute-done | bytes 262176 | tf_op jit(solution)/shard_map/ppermute | solution.py:16
  108.7 2.8 %collective-permute-done.28 = bf16[128,512]{0,1:T(8,128)(2,1)S(1)} collective-permute-done((bf16[128,512]{0,1:T(8,128)(2,1)S(1)}, bf16[128,512]{0,1:T(8,128)(2,1)S(1)}, u32[]{:S(2)}, u32[]{:S(2)}) %collective-permute-start.28) | collective-permute-done | bytes 131104 | tf_op jit(solution)/shard_map/ppermute | solution.py:16
  111.6 2.3 %collective-permute-start.29 = (bf16[64,512]{0,1:T(8,128)(2,1)S(1)}, bf16[64,512]{0,1:T(8,128)(2,1)S(1)}, u32[]{:S(2)}, u32[]{:S(2)}) collective-permute-start(bf16[64,512]{0,1:T(8,128)(2,1)S(1)} %dynamic-slice_convert_fusion.8), channel_id=1, source_target_pairs={{0,16},{2,18},{4,20},{6,22},{8,24},{10,26},{12,28},{14,30},{16,0},... | collective-permute-start | bytes 196616 | tf_op jit(solution)/shard_map/ppermute | solution.py:16
  114.1 2.2 %collective-permute-start.25 = (bf16[64,512]{0,1:T(8,128)(2,1)S(1)}, bf16[64,512]{0,1:T(8,128)(2,1)S(1)}, u32[]{:S(2)}, u32[]{:S(2)}) collective-permute-start(bf16[64,512]{0,1:T(8,128)(2,1)S(1)} %dynamic-slice_convert_fusion.10), channel_id=1, source_target_pairs={{0,16},{2,18},{4,20},{6,22},{8,24},{10,26},{12,28},{14,30},{16,0},... | collective-permute-start | bytes 196616 | tf_op jit(solution)/shard_map/ppermute | solution.py:16
  118.8 1.9 %collective-permute-done.29 = bf16[64,512]{0,1:T(8,128)(2,1)S(1)} collective-permute-done((bf16[64,512]{0,1:T(8,128)(2,1)S(1)}, bf16[64,512]{0,1:T(8,128)(2,1)S(1)}, u32[]{:S(2)}, u32[]{:S(2)}) %collective-permute-start.29) | collective-permute-done | bytes 65568 | tf_op jit(solution)/shard_map/ppermute | solution.py:16
  120.9 1.9 %collective-permute-done.25 = bf16[64,512]{0,1:T(8,128)(2,1)S(1)} collective-permute-done((bf16[64,512]{0,1:T(8,128)(2,1)S(1)}, bf16[64,512]{0,1:T(8,128)(2,1)S(1)}, u32[]{:S(2)}, u32[]{:S(2)}) %collective-permute-start.25) | collective-permute-done | bytes 65568 | tf_op jit(solution)/shard_map/ppermute | solution.py:16
  125.0 3.0 %collective-permute-start.33 = (bf16[64,512]{0,1:T(8,128)(2,1)S(1)}, bf16[64,512]{0,1:T(8,128)(2,1)S(1)}, u32[]{:S(2)}, u32[]{:S(2)}) collective-permute-start(bf16[64,512]{0,1:T(8,128)(2,1)S(1)} %dynamic-slice_convert_fusion.6), channel_id=1, source_target_pairs={{0,16},{2,18},{4,20},{6,22},{8,24},{10,26},{12,28},{14,30},{16,0},... | collective-permute-start | bytes 196616 | tf_op jit(solution)/shard_map/ppermute | solution.py:16
  127.9 2.7 %collective-permute-done.37 = bf16[64,512]{0,1:T(8,128)(2,1)S(1)} collective-permute-done((bf16[64,512]{0,1:T(8,128)(2,1)S(1)}, bf16[64,512]{0,1:T(8,128)(2,1)S(1)}, u32[]{:S(2)}, u32[]{:S(2)}) %collective-permute-start.37) | collective-permute-done | bytes 65568 | tf_op jit(solution)/shard_map/ppermute | solution.py:16
  130.8 2.6 %collective-permute-done.33 = bf16[64,512]{0,1:T(8,128)(2,1)S(1)} collective-permute-done((bf16[64,512]{0,1:T(8,128)(2,1)S(1)}, bf16[64,512]{0,1:T(8,128)(2,1)S(1)}, u32[]{:S(2)}, u32[]{:S(2)}) %collective-permute-start.33) | collective-permute-done | bytes 65568 | tf_op jit(solution)/shard_map/ppermute | solution.py:16
  (195 shorter events, 65.0 us)
Async XLA Ops:
  4.6 35.5 %collective-permute-start = (bf16[1,128,512]{2,1,0:T(8,128)(2,1)S(1)}, bf16[1,128,512]{2,1,0:T(8,128)(2,1)}, u32[]{:S(2)}, u32[]{:S(2)}) collective-permute-start(bf16[1,128,512]{2,1,0:T(8,128)(2,1)S(1)} %bitcast.195), channel_id=1, source_target_pairs={{0,2},{2,0},{4,6},{6,4},{8,10},{10,8},{12,14},{14,12},{16,18},{18,... | collective-permute-start | bytes 393224 | tf_op jit(solution)/shard_map/ppermute | solution.py:16
  5.1 36.7 %collective-permute-start.1 = (bf16[1,128,512]{2,1,0:T(8,128)(2,1)S(1)}, bf16[1,128,512]{2,1,0:T(8,128)(2,1)}, u32[]{:S(2)}, u32[]{:S(2)}) collective-permute-start(bf16[1,128,512]{2,1,0:T(8,128)(2,1)S(1)} %bitcast.196), channel_id=1, source_target_pairs={{0,4},{2,6},{4,0},{6,2},{8,12},{10,14},{12,8},{14,10},{16,20},{18,... | collective-permute-start | bytes 393224 | tf_op jit(solution)/shard_map/ppermute | solution.py:16
  7.7 35.8 %collective-permute-start.2 = (bf16[1,128,512]{2,1,0:T(8,128)(2,1)S(1)}, bf16[1,128,512]{2,1,0:T(8,128)(2,1)}, u32[]{:S(2)}, u32[]{:S(2)}) collective-permute-start(bf16[1,128,512]{2,1,0:T(8,128)(2,1)S(1)} %bitcast.197), channel_id=1, source_target_pairs={{0,8},{2,10},{4,12},{6,14},{8,0},{10,2},{12,4},{14,6},{16,24},{18,... | collective-permute-start | bytes 393224 | tf_op jit(solution)/shard_map/ppermute | solution.py:16
  10.8 9.1 %collective-permute-start.4 = (bf16[1,128,512]{2,1,0:T(8,128)(2,1)S(1)}, bf16[1,128,512]{2,1,0:T(8,128)(2,1)}, u32[]{:S(2)}, u32[]{:S(2)}) collective-permute-start(bf16[1,128,512]{2,1,0:T(8,128)(2,1)S(1)} %bitcast.199), channel_id=1, source_target_pairs={{0,2},{2,0},{4,6},{6,4},{8,10},{10,8},{12,14},{14,12},{16,18},{18,... | collective-permute-start | bytes 393224 | tf_op jit(solution)/shard_map/ppermute | solution.py:16
  10.9 10.9 %collective-permute-start.5 = (bf16[1,128,512]{2,1,0:T(8,128)(2,1)S(1)}, bf16[1,128,512]{2,1,0:T(8,128)(2,1)}, u32[]{:S(2)}, u32[]{:S(2)}) collective-permute-start(bf16[1,128,512]{2,1,0:T(8,128)(2,1)S(1)} %bitcast.200), channel_id=1, source_target_pairs={{0,4},{2,6},{4,0},{6,2},{8,12},{10,14},{12,8},{14,10},{16,20},{18,... | collective-permute-start | bytes 393224 | tf_op jit(solution)/shard_map/ppermute | solution.py:16
  21.8 12.8 %collective-permute-start.7 = (bf16[1,128,512]{2,1,0:T(8,128)(2,1)S(1)}, bf16[1,128,512]{2,1,0:T(8,128)(2,1)}, u32[]{:S(2)}, u32[]{:S(2)}) collective-permute-start(bf16[1,128,512]{2,1,0:T(8,128)(2,1)S(1)} %bitcast.202), channel_id=1, source_target_pairs={{0,16},{2,18},{4,20},{6,22},{8,24},{10,26},{12,28},{14,30},{16,0},... | collective-permute-start | bytes 393224 | tf_op jit(solution)/shard_map/ppermute | solution.py:16
  26.4 18.8 %collective-permute-start.3 = (bf16[1,128,512]{2,1,0:T(8,128)(2,1)S(1)}, bf16[1,128,512]{2,1,0:T(8,128)(2,1)}, u32[]{:S(2)}, u32[]{:S(2)}) collective-permute-start(bf16[1,128,512]{2,1,0:T(8,128)(2,1)S(1)} %bitcast.198), channel_id=1, source_target_pairs={{0,16},{2,18},{4,20},{6,22},{8,24},{10,26},{12,28},{14,30},{16,0},... | collective-permute-start | bytes 393224 | tf_op jit(solution)/shard_map/ppermute | solution.py:16
  54.9 29.5 %collective-permute-start.8 = (f32[128,512]{1,0:T(8,128)S(1)}, f32[128,512]{1,0:T(8,128)S(1)}, u32[]{:S(2)}, u32[]{:S(2)}) collective-permute-start(f32[128,512]{1,0:T(8,128)S(1)} %constant_dynamic-slice_fusion), channel_id=1, source_target_pairs={{0,1},{1,0},{2,3},{3,2},{4,5},{5,4},{6,7},{7,6},{8,9},{9,8},{10,11... | collective-permute-start | bytes 786440 | tf_op jit(solution)/shard_map/ppermute | solution.py:80
  57.1 7.9 %collective-permute-start.12 = (bf16[1,128,512]{1,2,0:T(8,128)(2,1)S(1)}, bf16[1,128,512]{1,2,0:T(8,128)(2,1)S(1)}, u32[]{:S(2)}, u32[]{:S(2)}) collective-permute-start(bf16[1,128,512]{1,2,0:T(8,128)(2,1)S(1)} %bitcast.216), channel_id=1, source_target_pairs={{0,16},{2,18},{4,20},{6,22},{8,24},{10,26},{12,28},{14,30},{16,0},... | collective-permute-start | bytes 393224 | tf_op jit(solution)/shard_map/ppermute | solution.py:16
  57.2 8.0 %collective-permute-start.11 = (bf16[1,128,512]{1,2,0:T(8,128)(2,1)S(1)}, bf16[1,128,512]{1,2,0:T(8,128)(2,1)S(1)}, u32[]{:S(2)}, u32[]{:S(2)}) collective-permute-start(bf16[1,128,512]{1,2,0:T(8,128)(2,1)S(1)} %bitcast.215), channel_id=1, source_target_pairs={{0,8},{2,10},{4,12},{6,14},{8,0},{10,2},{12,4},{14,6},{16,24},{18,... | collective-permute-start | bytes 393224 | tf_op jit(solution)/shard_map/ppermute | solution.py:16
  65.0 7.9 %collective-permute-start.16 = (bf16[1,128,512]{1,2,0:T(8,128)(2,1)S(1)}, bf16[1,128,512]{1,2,0:T(8,128)(2,1)S(1)}, u32[]{:S(2)}, u32[]{:S(2)}) collective-permute-start(bf16[1,128,512]{1,2,0:T(8,128)(2,1)S(1)} %bitcast.213), channel_id=1, source_target_pairs={{0,16},{2,18},{4,20},{6,22},{8,24},{10,26},{12,28},{14,30},{16,0},... | collective-permute-start | bytes 393224 | tf_op jit(solution)/shard_map/ppermute | solution.py:16
  72.9 23.9 %collective-permute-start.26 = (bf16[512,512]{0,1:T(8,128)(2,1)S(1)}, bf16[512,512]{0,1:T(8,128)(2,1)S(1)}, u32[]{:S(2)}, u32[]{:S(2)}) collective-permute-start(bf16[512,512]{0,1:T(8,128)(2,1)S(1)} %fusion.17), channel_id=1, source_target_pairs={{0,2},{2,0},{4,6},{6,4},{8,10},{10,8},{12,14},{14,12},{16,18},{18,... | collective-permute-start | bytes 1572872 | tf_op jit(solution)/shard_map/ppermute | solution.py:16
  72.9 24.3 %collective-permute-start.22 = (bf16[512,512]{0,1:T(8,128)(2,1)S(1)}, bf16[512,512]{0,1:T(8,128)(2,1)S(1)}, u32[]{:S(2)}, u32[]{:S(2)}) collective-permute-start(bf16[512,512]{0,1:T(8,128)(2,1)S(1)} %fusion.21), channel_id=1, source_target_pairs={{0,2},{2,0},{4,6},{6,4},{8,10},{10,8},{12,14},{14,12},{16,18},{18,... | collective-permute-start | bytes 1572872 | tf_op jit(solution)/shard_map/ppermute | solution.py:16
  74.5 8.3 %collective-permute-start.17 = (bf16[128,1024]{1,0:T(8,128)(2,1)S(1)}, bf16[128,1024]{1,0:T(8,128)(2,1)S(1)}, u32[]{:S(2)}, u32[]{:S(2)}) collective-permute-start(bf16[128,1024]{1,0:T(8,128)(2,1)S(1)} %fusion.5), channel_id=1, source_target_pairs={{0,1},{1,0},{2,3},{3,2},{4,5},{5,4},{6,7},{7,6},{8,9},{9,8},{10,11... | collective-permute-start | bytes 786440 | tf_op jit(solution)/shard_map/ppermute | solution.py:80
  75.1 23.6 %collective-permute-start.34 = (bf16[512,512]{0,1:T(8,128)(2,1)S(1)}, bf16[512,512]{0,1:T(8,128)(2,1)S(1)}, u32[]{:S(2)}, u32[]{:S(2)}) collective-permute-start(bf16[512,512]{0,1:T(8,128)(2,1)S(1)} %fusion.9), channel_id=1, source_target_pairs={{0,2},{2,0},{4,6},{6,4},{8,10},{10,8},{12,14},{14,12},{16,18},{18,... | collective-permute-start | bytes 1572872 | tf_op jit(solution)/shard_map/ppermute | solution.py:16
  84.3 16.6 %collective-permute-start.30 = (bf16[512,512]{0,1:T(8,128)(2,1)S(1)}, bf16[512,512]{0,1:T(8,128)(2,1)S(1)}, u32[]{:S(2)}, u32[]{:S(2)}) collective-permute-start(bf16[512,512]{0,1:T(8,128)(2,1)S(1)} %fusion.13), channel_id=1, source_target_pairs={{0,2},{2,0},{4,6},{6,4},{8,10},{10,8},{12,14},{14,12},{16,18},{18,... | collective-permute-start | bytes 1572872 | tf_op jit(solution)/shard_map/ppermute | solution.py:16
  97.0 9.3 %collective-permute-start.27 = (bf16[256,512]{0,1:T(8,128)(2,1)S(1)}, bf16[256,512]{0,1:T(8,128)(2,1)S(1)}, u32[]{:S(2)}, u32[]{:S(2)}) collective-permute-start(bf16[256,512]{0,1:T(8,128)(2,1)S(1)} %dynamic-slice_convert_fusion.2), channel_id=1, source_target_pairs={{0,8},{2,10},{4,12},{6,14},{8,0},{10,2},{12,4},{14,6},{16,24},{18,... | collective-permute-start | bytes 786440 | tf_op jit(solution)/shard_map/ppermute | solution.py:16
  97.5 10.2 %collective-permute-start.23 = (bf16[256,512]{0,1:T(8,128)(2,1)S(1)}, bf16[256,512]{0,1:T(8,128)(2,1)S(1)}, u32[]{:S(2)}, u32[]{:S(2)}) collective-permute-start(bf16[256,512]{0,1:T(8,128)(2,1)S(1)} %dynamic-slice_convert_fusion.3), channel_id=1, source_target_pairs={{0,4},{2,6},{4,0},{6,2},{8,12},{10,14},{12,8},{14,10},{16,20},{18,... | collective-permute-start | bytes 786440 | tf_op jit(solution)/shard_map/ppermute | solution.py:16
  99.0 17.3 %collective-permute-start.35 = (bf16[256,512]{0,1:T(8,128)(2,1)S(1)}, bf16[256,512]{0,1:T(8,128)(2,1)S(1)}, u32[]{:S(2)}, u32[]{:S(2)}) collective-permute-start(bf16[256,512]{0,1:T(8,128)(2,1)S(1)} %dynamic-slice_convert_fusion), channel_id=1, source_target_pairs={{0,8},{2,10},{4,12},{6,14},{8,0},{10,2},{12,4},{14,6},{16,24},{18,... | collective-permute-start | bytes 786440 | tf_op jit(solution)/shard_map/ppermute | solution.py:16
  101.2 16.1 %collective-permute-start.31 = (bf16[256,512]{0,1:T(8,128)(2,1)S(1)}, bf16[256,512]{0,1:T(8,128)(2,1)S(1)}, u32[]{:S(2)}, u32[]{:S(2)}) collective-permute-start(bf16[256,512]{0,1:T(8,128)(2,1)S(1)} %dynamic-slice_convert_fusion.1), channel_id=1, source_target_pairs={{0,4},{2,6},{4,0},{6,2},{8,12},{10,14},{12,8},{14,10},{16,20},{18,... | collective-permute-start | bytes 786440 | tf_op jit(solution)/shard_map/ppermute | solution.py:16
  111.6 9.1 %collective-permute-start.29 = (bf16[64,512]{0,1:T(8,128)(2,1)S(1)}, bf16[64,512]{0,1:T(8,128)(2,1)S(1)}, u32[]{:S(2)}, u32[]{:S(2)}) collective-permute-start(bf16[64,512]{0,1:T(8,128)(2,1)S(1)} %dynamic-slice_convert_fusion.8), channel_id=1, source_target_pairs={{0,16},{2,18},{4,20},{6,22},{8,24},{10,26},{12,28},{14,30},{16,0},... | collective-permute-start | bytes 196616 | tf_op jit(solution)/shard_map/ppermute | solution.py:16
  114.1 8.7 %collective-permute-start.25 = (bf16[64,512]{0,1:T(8,128)(2,1)S(1)}, bf16[64,512]{0,1:T(8,128)(2,1)S(1)}, u32[]{:S(2)}, u32[]{:S(2)}) collective-permute-start(bf16[64,512]{0,1:T(8,128)(2,1)S(1)} %dynamic-slice_convert_fusion.10), channel_id=1, source_target_pairs={{0,16},{2,18},{4,20},{6,22},{8,24},{10,26},{12,28},{14,30},{16,0},... | collective-permute-start | bytes 196616 | tf_op jit(solution)/shard_map/ppermute | solution.py:16
  116.4 8.2 %collective-permute-start.36 = (bf16[128,512]{0,1:T(8,128)(2,1)S(1)}, bf16[128,512]{0,1:T(8,128)(2,1)S(1)}, u32[]{:S(2)}, u32[]{:S(2)}) collective-permute-start(bf16[128,512]{0,1:T(8,128)(2,1)S(1)} %dynamic-slice_convert_fusion.5), channel_id=1, source_target_pairs={{0,4},{2,6},{4,0},{6,2},{8,12},{10,14},{12,8},{14,10},{16,20},{18,... | collective-permute-start | bytes 393224 | tf_op jit(solution)/shard_map/ppermute | solution.py:16
  125.0 8.5 %collective-permute-start.33 = (bf16[64,512]{0,1:T(8,128)(2,1)S(1)}, bf16[64,512]{0,1:T(8,128)(2,1)S(1)}, u32[]{:S(2)}, u32[]{:S(2)}) collective-permute-start(bf16[64,512]{0,1:T(8,128)(2,1)S(1)} %dynamic-slice_convert_fusion.6), channel_id=1, source_target_pairs={{0,16},{2,18},{4,20},{6,22},{8,24},{10,26},{12,28},{14,30},{16,0},... | collective-permute-start | bytes 196616 | tf_op jit(solution)/shard_map/ppermute | solution.py:16
  (28 other events, 168.8 us)

commit v3 on v2

--- a/solution.py
+++ b/solution.py
@@ -25,16 +25,14 @@
     return shaped.transpose(axes).reshape(rows, width)
 
 
-def halving_sum(partial, axis, order):
+def halving_step(partial, axis, bit):
     me = lax.axis_index(axis)
-    for bit in order:
-        half = partial.shape[0] // 2
-        mine = (me >> bit) & 1
-        keep = lax.dynamic_slice_in_dim(partial, mine * half, half, 0)
-        send = lax.dynamic_slice_in_dim(partial, (1 - mine) * half, half, 0)
-        got = from_partner(send.astype(jnp.bfloat16), axis, bit)
-        partial = keep + got.astype(jnp.float32)
-    return partial
+    half = partial.shape[0] // 2
+    mine = (me >> bit) & 1
+    keep = lax.dynamic_slice_in_dim(partial, mine * half, half, 0)
+    send = lax.dynamic_slice_in_dim(partial, (1 - mine) * half, half, 0)
+    got = from_partner(send.astype(jnp.bfloat16), axis, bit)
+    return keep + got.astype(jnp.float32)
 
 
 def split_orders(levels):
@@ -44,7 +42,7 @@
     return first, (0, 2, 1) + first[3:]
 
 
-def scatter_rows(pairs, axis, levels):
+def scatter_begin(pairs, levels):
     contract = (((0,), (0,)), ((), ()))
     chunks = []
     for index, order in enumerate(split_orders(levels)):
@@ -58,7 +56,22 @@
                     preferred_element_type=jnp.float32,
                 )
             )
-        chunks.append(halving_sum(jnp.concatenate(pieces, axis=1), axis, order))
+        chunks.append(jnp.concatenate(pieces, axis=1))
+    return chunks, 0
+
+
+def scatter_step(state, axis, levels):
+    chunks, done = state
+    if done == levels:
+        return state
+    orders = split_orders(levels)
+    return [halving_step(c, axis, o[done]) for c, o in zip(chunks, orders)], done + 1
+
+
+def scatter_end(state, pairs, axis, levels):
+    while state[1] < levels:
+        state = scatter_step(state, axis, levels)
+    chunks = state[0]
     results = []
     offset = 0
     for left, right in pairs:
@@ -164,6 +177,12 @@
     value_terms = value_terms.astype(jnp.bfloat16).reshape(slot_block_shape)
     grad_key = key_terms[0].astype(jnp.float32)
     grad_value = value_terms[0].astype(jnp.float32)
+    out_pairs = [(cotangent, attended), (normed, grad_query)]
+    early = scatter_step(scatter_begin(out_pairs, graph_levels), "graph", graph_levels)
+    early_chunks, key_terms, value_terms = lax.optimization_barrier(
+        (early[0], key_terms, value_terms)
+    )
+    early = scatter_step((early_chunks, early[1]), "graph", graph_levels)
     returned = {}
     for bit in bit_order:
         slot = 1 + local_levels + bit
@@ -173,13 +192,15 @@
         grad_value = grad_value + returned[bit][1].astype(jnp.float32)
     grad_key = grad_key.astype(jnp.bfloat16).reshape(node_rows, columns)
     grad_value = grad_value.astype(jnp.bfloat16).reshape(node_rows, columns)
-    w_out_rows, w_query_grad = scatter_rows(
-        [(cotangent, attended), (normed, grad_query)], "graph", graph_levels
-    )
+    early_chunks, grad_key, grad_value = lax.optimization_barrier(
+        (early[0], grad_key, grad_value)
+    )
+    early = scatter_step((early_chunks, early[1]), "graph", graph_levels)
+    kv_pairs = [(normed, grad_key), (normed, grad_value)]
+    late = scatter_step(scatter_begin(kv_pairs, graph_levels), "graph", graph_levels)
+    w_out_rows, w_query_grad = scatter_end(early, out_pairs, "graph", graph_levels)
     w_out_grad = w_out_rows.T
-    w_key_grad, w_value_grad = scatter_rows(
-        [(normed, grad_key), (normed, grad_value)], "graph", graph_levels
-    )
+    late = scatter_step(late, "graph", graph_levels)
     feature_terms = (
         jnp.dot(grad_query, w_query.T, preferred_element_type=jnp.float32)
         + jnp.dot(grad_key, w_key.T, preferred_element_type=jnp.float32)
@@ -187,9 +208,10 @@
     )
     low_terms = feature_terms.astype(jnp.bfloat16)
     grad_normed = low_terms.astype(jnp.float32) + head_swap(low_terms).astype(jnp.float32)
-    gain_grad = doubling_sum(
-        jnp.sum(grad_normed * wide_nodes * inverse, axis=0), "graph", graph_levels
-    )
+    gain_terms = jnp.sum(grad_normed * wide_nodes * inverse, axis=0)
+    gain_terms, late_chunks = lax.optimization_barrier((gain_terms, late[0]))
+    w_key_grad, w_value_grad = scatter_end((late_chunks, late[1]), kv_pairs, "graph", graph_levels)
+    gain_grad = doubling_sum(gain_terms, "graph", graph_levels)
     scaled = grad_normed * gain
     nodes_grad = (
         inverse

time: 136 us -> 148 us (1.088)
  other arithmetic: 7.89 us -> 14.4 us
  starting transfers between devices: 41.2 us -> 43.6 us
  waiting for transfers between devices: 41.7 us -> 44.1 us
    ppermute x36, waiting for transfers between devices: 34.4 us -> 38.1 us  [from_partner(): return lax.ppermute(value, axis, pairs)]
    add x16, other arithmetic: 1.69 us -> 4.05 us  [halving_step(): return keep + got.astype(jnp.float32)]
    unnamed x45 -> x55, local copies, waits for them, and re-layouts: 11.2 us -> 13.3 us
    convert_element_type x4, other arithmetic: 0.31 us -> 1.93 us  [halving_step(): got = from_partner(send.astype(jnp.bfloat16), axis, bit)]
  transfers between devices with their start and end apart: 38 -> 38, of which waited for: 15 -> 18; matrix products, arithmetic and copies ran while one was open for 25% -> 25% of each run, Pallas kernels for 0% -> 0%
where the time goes in v3:
time: 148 us; the launch traced here: 147 us
  waiting for transfers between devices  44.1 us (30%)
  starting transfers between devices  43.6 us (29%)
  local copies, waits for them, and re-layouts  25.7 us (17%)
  matrix products  17.6 us (12%)
  other arithmetic  14.4 us (10%)
  between operations  1.51 us (1%)
    ppermute x36, starting transfers between devices, from_partner(): return lax.ppermute(value, axis, pairs)  40.1 us
    ppermute x36, waiting for transfers between devices, from_partner(): return lax.ppermute(value, axis, pairs)  38.1 us
    unnamed x55, local copies, waits for them, and re-layouts  13.3 us
    ppermute x8, local copies, waits for them, and re-layouts, from_partner(): return lax.ppermute(value, axis, pairs)  6.35 us
    ppermute x2, waiting for transfers between devices, head_swap(): return lax.ppermute(value, 'head', [(0, 1), (1, 0)])  6.03 us
    add x16, other arithmetic, halving_step(): return keep + got.astype(jnp.float32)  4.05 us
    ppermute x2, starting transfers between devices, head_swap(): return lax.ppermute(value, 'head', [(0, 1), (1, 0)])  3.45 us
    dot_general x1, matrix products, shards(): jnp.einsum('bqhe,sbkhe->bhqsk', grad_heads, values_all, preferred_element...  3.08 us
  transfers between devices with their start and end apart: 38, of which 18 were waited for; matrix products, arithmetic and copies ran while one was open for 25% of the time, Pallas kernels for 0%

profile of v3, /device:TPU:0, one launch (start us, length us, event | category | flops | bytes accessed | tf_op | source)
XLA Modules:
  0.0 146.9 jit_solution(1078244212928474533)
XLA Ops:
  3.0 2.2 %convolution_convert_fusion.3 = bf16[128,512]{1,0:T(8,128)(2,1)} fusion(bf16[128,1024]{1,0:T(8,128)(2,1)S(1)} %fusion.32, bf16[1024,512]{1,0:T(8,128)(2,1)} %param.11), kind=kOutput, calls=%fused_computation.36 | convolution fusion | flops 134283264 | bytes 1441792 | tf_op jit(solution)/shard_map/dot_general | solution.py:116
  5.7 2.5 %collective-permute-start.5 = (bf16[1,128,512]{2,1,0:T(8,128)(2,1)}, bf16[1,128,512]{2,1,0:T(8,128)(2,1)}, u32[]{:S(2)}, u32[]{:S(2)}) collective-permute-start(bf16[1,128,512]{2,1,0:T(8,128)(2,1)} %bitcast.2), channel_id=1, source_target_pairs={{0,4},{2,6},{4,0},{6,2},{8,12},{10,14},{12,8},{14,10},{16,20},{18,... | collective-permute-start | bytes 393224 | tf_op jit(solution)/shard_map/ppermute | solution.py:16
  9.8 2.6 %collective-permute-start.7 = (bf16[1,128,512]{2,1,0:T(8,128)(2,1)}, bf16[1,128,512]{2,1,0:T(8,128)(2,1)}, u32[]{:S(2)}, u32[]{:S(2)}) collective-permute-start(bf16[1,128,512]{2,1,0:T(8,128)(2,1)} %bitcast.2), channel_id=1, source_target_pairs={{0,16},{2,18},{4,20},{6,22},{8,24},{10,26},{12,28},{14,30},{16,0},... | collective-permute-start | bytes 393224 | tf_op jit(solution)/shard_map/ppermute | solution.py:16
  28.8 1.7 %fusion = (f32[8,128]{1,0:T(8,128)S(1)}, f32[8,128,5,128]{1,3,2,0:T(8,128)S(1)}) fusion(pred[5]{0:T(512)(128)(4,1)S(1)} %compare_bitcast_fusion, bf16[128,8,64,1]{0,2,3,1:T(8,128)(2,1)S(1)} %bitcast.208, bf16[5,1,128,8,64]{2,4,0,3,1:T(8,128)(2,1)} %constant_dynamic-update-slice_fusion.5), kind=kOutput, calls=%fused_computation.20 | convolution fusion | flops 85851136 | bytes 3411973 | tf_op jit(solution)/shard_map/bqhe,sbkhe->bhqsk/dot_general | solution.py:142
  37.6 3.1 %multiply_reduce_fusion = (f32[8,128]{1,0:T(8,128)S(1)}, f32[8,128,5,128]{1,3,2,0:T(8,128)S(1)}) fusion(f32[8,128]{1,0:T(8,128)S(1)} %fusion.2, f32[8,128]{1,0:T(8,128)S(1)} %get-tuple-element.59, f32[8,128,5,128]{1,3,2,0:T(8,128)} %copy-done.1, pred[5]{0:T(512)(128)(4,1)S(1)} %compare_bitcast_fusion, bf16[128,8,64,1]{0,2,3,1:T(8,128)(2,1)S(1)} %bitcast.225, ...), kind=kOutput, calls=%fused_computation.1 | convolution fusion | flops 87817216 | bytes 6041605 | tf_op jit(solution)/shard_map/bqhe,sbkhe->bhqsk/dot_general | solution.py:164
  47.6 1.9 %collective-permute-start.8 = (f32[128,512]{1,0:T(8,128)S(1)}, f32[128,512]{1,0:T(8,128)S(1)}, u32[]{:S(2)}, u32[]{:S(2)}) collective-permute-start(f32[128,512]{1,0:T(8,128)S(1)} %constant_dynamic-slice_fusion), channel_id=1, source_target_pairs={{0,1},{1,0},{2,3},{3,2},{4,5},{5,4},{6,7},{7,6},{8,9},{9,8},{10,11... | collective-permute-start | bytes 786440 | tf_op jit(solution)/shard_map/ppermute | solution.py:93
  50.1 6.0 %collective-permute-done.8 = f32[128,512]{1,0:T(8,128)S(1)} collective-permute-done((f32[128,512]{1,0:T(8,128)S(1)}, f32[128,512]{1,0:T(8,128)S(1)}, u32[]{:S(2)}, u32[]{:S(2)}) %collective-permute-start.8) | collective-permute-done | bytes 262176 | tf_op jit(solution)/shard_map/ppermute | solution.py:93
  57.4 1.8 %collective-permute-start.18 = (bf16[1,128,512]{1,2,0:T(8,128)(2,1)S(1)}, bf16[1,128,512]{1,2,0:T(8,128)(2,1)S(1)}, u32[]{:S(2)}, u32[]{:S(2)}) collective-permute-start(bf16[1,128,512]{1,2,0:T(8,128)(2,1)S(1)} %get-tuple-element.47), channel_id=1, source_target_pairs={{0,4},{2,6},{4,0},{6,2},{8,12},{10,14},{12,8},{14,10},{16,20},{18,... | collective-permute-start | bytes 393224 | tf_op jit(solution)/shard_map/ppermute | solution.py:16
  60.8 2.6 %collective-permute-start.20 = (bf16[1,128,512]{1,2,0:T(8,128)(2,1)S(1)}, bf16[1,128,512]{1,2,0:T(8,128)(2,1)S(1)}, u32[]{:S(2)}, u32[]{:S(2)}) collective-permute-start(bf16[1,128,512]{1,2,0:T(8,128)(2,1)S(1)} %slice_bitcast_fusion.6), channel_id=1, source_target_pairs={{0,16},{2,18},{4,20},{6,22},{8,24},{10,26},{12,28},{14,30},{16,0},... | collective-permute-start | bytes 393224 | tf_op jit(solution)/shard_map/ppermute | solution.py:16
  65.1 2.1 %collective-permute-done.19 = bf16[1,128,512]{1,2,0:T(8,128)(2,1)S(1)} collective-permute-done((bf16[1,128,512]{1,2,0:T(8,128)(2,1)S(1)}, bf16[1,128,512]{1,2,0:T(8,128)(2,1)S(1)}, u32[]{:S(2)}, u32[]{:S(2)}) %collective-permute-start.19) | collective-permute-done | bytes 131104 | tf_op jit(solution)/shard_map/ppermute | solution.py:16
  72.6 3.1 %collective-permute-done.16 = bf16[1,128,512]{1,2,0:T(8,128)(2,1)S(1)} collective-permute-done((bf16[1,128,512]{1,2,0:T(8,128)(2,1)S(1)}, bf16[1,128,512]{1,2,0:T(8,128)(2,1)S(1)}, u32[]{:S(2)}, u32[]{:S(2)}) %collective-permute-start.16) | collective-permute-done | bytes 131104 | tf_op jit(solution)/shard_map/ppermute | solution.py:16
  75.8 3.1 %collective-permute-done.12 = bf16[256,512]{0,1:T(8,128)(2,1)S(1)} collective-permute-done((bf16[256,512]{0,1:T(8,128)(2,1)S(1)}, bf16[256,512]{0,1:T(8,128)(2,1)S(1)}, u32[]{:S(2)}, u32[]{:S(2)}) %collective-permute-start.12) | collective-permute-done | bytes 262176 | tf_op jit(solution)/shard_map/ppermute | solution.py:16
  83.1 1.7 %collective-permute-start.30 = (bf16[128,512]{0,1:T(8,128)(2,1)S(1)}, bf16[128,512]{0,1:T(8,128)(2,1)S(1)}, u32[]{:S(2)}, u32[]{:S(2)}) collective-permute-start(bf16[128,512]{0,1:T(8,128)(2,1)S(1)} %dynamic-slice_convert_fusion.11), channel_id=1, source_target_pairs={{0,8},{2,10},{4,12},{6,14},{8,0},{10,2},{12,4},{14,6},{16,24},{18,... | collective-permute-start | bytes 393224 | tf_op jit(solution)/shard_map/ppermute | solution.py:16
  88.7 2.7 %collective-permute-start.31 = (bf16[64,512]{0,1:T(8,128)(2,1)S(1)}, bf16[64,512]{0,1:T(8,128)(2,1)S(1)}, u32[]{:S(2)}, u32[]{:S(2)}) collective-permute-start(bf16[64,512]{0,1:T(8,128)(2,1)S(1)} %dynamic-slice_convert_fusion.10), channel_id=1, source_target_pairs={{0,16},{2,18},{4,20},{6,22},{8,24},{10,26},{12,28},{14,30},{16,0},... | collective-permute-start | bytes 196616 | tf_op jit(solution)/shard_map/ppermute | solution.py:16
  92.0 2.6 %collective-permute-start.33 = (bf16[64,512]{0,1:T(8,128)(2,1)S(1)}, bf16[64,512]{0,1:T(8,128)(2,1)S(1)}, u32[]{:S(2)}, u32[]{:S(2)}) collective-permute-start(bf16[64,512]{0,1:T(8,128)(2,1)S(1)} %dynamic-slice_convert_fusion.8), channel_id=1, source_target_pairs={{0,16},{2,18},{4,20},{6,22},{8,24},{10,26},{12,28},{14,30},{16,0},... | collective-permute-start | bytes 196616 | tf_op jit(solution)/shard_map/ppermute | solution.py:16
  94.6 6.5 %collective-permute-done.31 = bf16[64,512]{0,1:T(8,128)(2,1)S(1)} collective-permute-done((bf16[64,512]{0,1:T(8,128)(2,1)S(1)}, bf16[64,512]{0,1:T(8,128)(2,1)S(1)}, u32[]{:S(2)}, u32[]{:S(2)}) %collective-permute-start.31) | collective-permute-done | bytes 65568 | tf_op jit(solution)/shard_map/ppermute | solution.py:16
  103.7 1.7 %copy.92 = f32[64,512]{1,0:T(8,128)} copy(f32[64,512]{0,1:T(8,128)} %get-tuple-element.63) | data formatting | bytes 262144
  113.0 2.8 %collective-permute-done.25 = bf16[256,512]{0,1:T(8,128)(2,1)S(1)} collective-permute-done((bf16[256,512]{0,1:T(8,128)(2,1)S(1)}, bf16[256,512]{0,1:T(8,128)(2,1)S(1)}, u32[]{:S(2)}, u32[]{:S(2)}) %collective-permute-start.25) | collective-permute-done | bytes 262176 | tf_op jit(solution)/shard_map/ppermute | solution.py:16
  115.9 2.5 %collective-permute-done.23 = bf16[256,512]{0,1:T(8,128)(2,1)S(1)} collective-permute-done((bf16[256,512]{0,1:T(8,128)(2,1)S(1)}, bf16[256,512]{0,1:T(8,128)(2,1)S(1)}, u32[]{:S(2)}, u32[]{:S(2)}) %collective-permute-start.23) | collective-permute-done | bytes 262176 | tf_op jit(solution)/shard_map/ppermute | solution.py:16
  121.4 1.9 %collective-permute-done.27 = f32[1024]{0:T(1024)S(1)} collective-permute-done((f32[1024]{0:T(1024)S(1)}, f32[1024]{0:T(1024)S(1)}, u32[]{:S(2)}, u32[]{:S(2)}) %collective-permute-start.27) | collective-permute-done | bytes 4128 | tf_op jit(solution)/shard_map/ppermute | solution.py:16
  123.9 1.9 %fusion.36 = bf16[128,1024]{1,0:T(8,128)(2,1)} fusion(bf16[128,1024]{1,0:T(8,128)(2,1)S(1)} %copy-done.5, bf16[128,1024]{1,0:T(8,128)(2,1)} %collective-permute-done.21, bf16[128,1024]{1,0:T(8,128)(2,1)S(1)} %fusion.5, f32[128]{0:T(128)S(1)} %broadcast_multiply_fusion, f32[1024]{0:T(1024)S(1)} %copy-done.16, f32[128]{0:T(128)S(1)} %add_rsqrt_fusion), kind=kLoop, calls=%fused_computation.72 | loop fusion | flops 1441792 | bytes 1053696 | tf_op jit(solution)/shard_map/convert_element_type | solution.py:222
  126.9 3.4 %collective-permute-start.29 = (f32[1024]{0:T(1024)S(1)}, f32[1024]{0:T(1024)S(1)}, u32[]{:S(2)}, u32[]{:S(2)}) collective-permute-start(f32[1024]{0:T(1024)S(1)} %add.201), channel_id=1, source_target_pairs={{0,16},{2,18},{4,20},{6,22},{8,24},{10,26},{12,28},{14,30},{16,0},... | collective-permute-start | bytes 12296 | tf_op jit(solution)/shard_map/ppermute | solution.py:16
  132.7 3.0 %collective-permute-start.35 = (bf16[64,512]{0,1:T(8,128)(2,1)S(1)}, bf16[64,512]{0,1:T(8,128)(2,1)S(1)}, u32[]{:S(2)}, u32[]{:S(2)}) collective-permute-start(bf16[64,512]{0,1:T(8,128)(2,1)S(1)} %dynamic-slice_convert_fusion.6), channel_id=1, source_target_pairs={{0,16},{2,18},{4,20},{6,22},{8,24},{10,26},{12,28},{14,30},{16,0},... | collective-permute-start | bytes 196616 | tf_op jit(solution)/shard_map/ppermute | solution.py:16
  135.9 7.7 %collective-permute-done.35 = bf16[64,512]{0,1:T(8,128)(2,1)S(1)} collective-permute-done((bf16[64,512]{0,1:T(8,128)(2,1)S(1)}, bf16[64,512]{0,1:T(8,128)(2,1)S(1)}, u32[]{:S(2)}, u32[]{:S(2)}) %collective-permute-start.35) | collective-permute-done | bytes 65568 | tf_op jit(solution)/shard_map/ppermute | solution.py:16
  (213 shorter events, 74.3 us)
Async XLA Ops:
  5.2 15.7 %collective-permute-start.4 = (bf16[1,128,512]{2,1,0:T(8,128)(2,1)}, bf16[1,128,512]{2,1,0:T(8,128)(2,1)}, u32[]{:S(2)}, u32[]{:S(2)}) collective-permute-start(bf16[1,128,512]{2,1,0:T(8,128)(2,1)} %bitcast.2), channel_id=1, source_target_pairs={{0,2},{2,0},{4,6},{6,4},{8,10},{10,8},{12,14},{14,12},{16,18},{18,... | collective-permute-start | bytes 393224 | tf_op jit(solution)/shard_map/ppermute | solution.py:16
  5.7 17.5 %collective-permute-start.5 = (bf16[1,128,512]{2,1,0:T(8,128)(2,1)}, bf16[1,128,512]{2,1,0:T(8,128)(2,1)}, u32[]{:S(2)}, u32[]{:S(2)}) collective-permute-start(bf16[1,128,512]{2,1,0:T(8,128)(2,1)} %bitcast.2), channel_id=1, source_target_pairs={{0,4},{2,6},{4,0},{6,2},{8,12},{10,14},{12,8},{14,10},{16,20},{18,... | collective-permute-start | bytes 393224 | tf_op jit(solution)/shard_map/ppermute | solution.py:16
  8.2 17.1 %collective-permute-start.6 = (bf16[1,128,512]{2,1,0:T(8,128)(2,1)}, bf16[1,128,512]{2,1,0:T(8,128)(2,1)}, u32[]{:S(2)}, u32[]{:S(2)}) collective-permute-start(bf16[1,128,512]{2,1,0:T(8,128)(2,1)} %bitcast.2), channel_id=1, source_target_pairs={{0,8},{2,10},{4,12},{6,14},{8,0},{10,2},{12,4},{14,6},{16,24},{18,... | collective-permute-start | bytes 393224 | tf_op jit(solution)/shard_map/ppermute | solution.py:16
  9.8 17.2 %collective-permute-start.7 = (bf16[1,128,512]{2,1,0:T(8,128)(2,1)}, bf16[1,128,512]{2,1,0:T(8,128)(2,1)}, u32[]{:S(2)}, u32[]{:S(2)}) collective-permute-start(bf16[1,128,512]{2,1,0:T(8,128)(2,1)} %bitcast.2), channel_id=1, source_target_pairs={{0,16},{2,18},{4,20},{6,22},{8,24},{10,26},{12,28},{14,30},{16,0},... | collective-permute-start | bytes 393224 | tf_op jit(solution)/shard_map/ppermute | solution.py:16
  13.9 18.7 %collective-permute-start = (bf16[1,128,512]{2,1,0:T(8,128)(2,1)S(1)}, bf16[1,128,512]{2,1,0:T(8,128)(2,1)}, u32[]{:S(2)}, u32[]{:S(2)}) collective-permute-start(bf16[1,128,512]{2,1,0:T(8,128)(2,1)S(1)} %bitcast.215), channel_id=1, source_target_pairs={{0,2},{2,0},{4,6},{6,4},{8,10},{10,8},{12,14},{14,12},{16,18},{18,... | collective-permute-start | bytes 393224 | tf_op jit(solution)/shard_map/ppermute | solution.py:16
  20.9 13.4 %collective-permute-start.1 = (bf16[1,128,512]{2,1,0:T(8,128)(2,1)S(1)}, bf16[1,128,512]{2,1,0:T(8,128)(2,1)S(1)}, u32[]{:S(2)}, u32[]{:S(2)}) collective-permute-start(bf16[1,128,512]{2,1,0:T(8,128)(2,1)S(1)} %bitcast.216), channel_id=1, source_target_pairs={{0,4},{2,6},{4,0},{6,2},{8,12},{10,14},{12,8},{14,10},{16,20},{18,... | collective-permute-start | bytes 393224 | tf_op jit(solution)/shard_map/ppermute | solution.py:16
  23.2 12.0 %collective-permute-start.2 = (bf16[1,128,512]{2,1,0:T(8,128)(2,1)S(1)}, bf16[1,128,512]{2,1,0:T(8,128)(2,1)S(1)}, u32[]{:S(2)}, u32[]{:S(2)}) collective-permute-start(bf16[1,128,512]{2,1,0:T(8,128)(2,1)S(1)} %bitcast.217), channel_id=1, source_target_pairs={{0,8},{2,10},{4,12},{6,14},{8,0},{10,2},{12,4},{14,6},{16,24},{18,... | collective-permute-start | bytes 393224 | tf_op jit(solution)/shard_map/ppermute | solution.py:16
  25.3 10.6 %collective-permute-start.3 = (bf16[1,128,512]{2,1,0:T(8,128)(2,1)S(1)}, bf16[1,128,512]{2,1,0:T(8,128)(2,1)}, u32[]{:S(2)}, u32[]{:S(2)}) collective-permute-start(bf16[1,128,512]{2,1,0:T(8,128)(2,1)S(1)} %bitcast.218), channel_id=1, source_target_pairs={{0,16},{2,18},{4,20},{6,22},{8,24},{10,26},{12,28},{14,30},{16,0},... | collective-permute-start | bytes 393224 | tf_op jit(solution)/shard_map/ppermute | solution.py:16
  46.2 10.6 %collective-permute-start.10 = (bf16[512,512]{0,1:T(8,128)(2,1)S(1)}, bf16[512,512]{0,1:T(8,128)(2,1)S(1)}, u32[]{:S(2)}, u32[]{:S(2)}) collective-permute-start(bf16[512,512]{0,1:T(8,128)(2,1)S(1)} %fusion.17), channel_id=1, source_target_pairs={{0,2},{2,0},{4,6},{6,4},{8,10},{10,8},{12,14},{14,12},{16,18},{18,... | collective-permute-start | bytes 1572872 | tf_op jit(solution)/shard_map/ppermute | solution.py:16
  47.2 9.9 %collective-permute-start.9 = (bf16[512,512]{0,1:T(8,128)(2,1)S(1)}, bf16[512,512]{0,1:T(8,128)(2,1)S(1)}, u32[]{:S(2)}, u32[]{:S(2)}) collective-permute-start(bf16[512,512]{0,1:T(8,128)(2,1)S(1)} %fusion.21), channel_id=1, source_target_pairs={{0,2},{2,0},{4,6},{6,4},{8,10},{10,8},{12,14},{14,12},{16,18},{18,... | collective-permute-start | bytes 1572872 | tf_op jit(solution)/shard_map/ppermute | solution.py:16
  47.6 8.5 %collective-permute-start.8 = (f32[128,512]{1,0:T(8,128)S(1)}, f32[128,512]{1,0:T(8,128)S(1)}, u32[]{:S(2)}, u32[]{:S(2)}) collective-permute-start(f32[128,512]{1,0:T(8,128)S(1)} %constant_dynamic-slice_fusion), channel_id=1, source_target_pairs={{0,1},{1,0},{2,3},{3,2},{4,5},{5,4},{6,7},{7,6},{8,9},{9,8},{10,11... | collective-permute-start | bytes 786440 | tf_op jit(solution)/shard_map/ppermute | solution.py:93
  60.8 8.5 %collective-permute-start.20 = (bf16[1,128,512]{1,2,0:T(8,128)(2,1)S(1)}, bf16[1,128,512]{1,2,0:T(8,128)(2,1)S(1)}, u32[]{:S(2)}, u32[]{:S(2)}) collective-permute-start(bf16[1,128,512]{1,2,0:T(8,128)(2,1)S(1)} %slice_bitcast_fusion.6), channel_id=1, source_target_pairs={{0,16},{2,18},{4,20},{6,22},{8,24},{10,26},{12,28},{14,30},{16,0},... | collective-permute-start | bytes 393224 | tf_op jit(solution)/shard_map/ppermute | solution.py:16
  63.7 8.2 %collective-permute-start.14 = (bf16[1,128,512]{1,2,0:T(8,128)(2,1)S(1)}, bf16[1,128,512]{1,2,0:T(8,128)(2,1)S(1)}, u32[]{:S(2)}, u32[]{:S(2)}) collective-permute-start(bf16[1,128,512]{1,2,0:T(8,128)(2,1)S(1)} %get-tuple-element.50), channel_id=1, source_target_pairs={{0,4},{2,6},{4,0},{6,2},{8,12},{10,14},{12,8},{14,10},{16,20},{18,... | collective-permute-start | bytes 393224 | tf_op jit(solution)/shard_map/ppermute | solution.py:16
  64.2 8.4 %collective-permute-start.15 = (bf16[1,128,512]{1,2,0:T(8,128)(2,1)S(1)}, bf16[1,128,512]{1,2,0:T(8,128)(2,1)S(1)}, u32[]{:S(2)}, u32[]{:S(2)}) collective-permute-start(bf16[1,128,512]{1,2,0:T(8,128)(2,1)S(1)} %get-tuple-element.49), channel_id=1, source_target_pairs={{0,8},{2,10},{4,12},{6,14},{8,0},{10,2},{12,4},{14,6},{16,24},{18,... | collective-permute-start | bytes 393224 | tf_op jit(solution)/shard_map/ppermute | solution.py:16
  67.2 8.4 %collective-permute-start.16 = (bf16[1,128,512]{1,2,0:T(8,128)(2,1)S(1)}, bf16[1,128,512]{1,2,0:T(8,128)(2,1)S(1)}, u32[]{:S(2)}, u32[]{:S(2)}) collective-permute-start(bf16[1,128,512]{1,2,0:T(8,128)(2,1)S(1)} %slice_bitcast_fusion.7), channel_id=1, source_target_pairs={{0,16},{2,18},{4,20},{6,22},{8,24},{10,26},{12,28},{14,30},{16,0},... | collective-permute-start | bytes 393224 | tf_op jit(solution)/shard_map/ppermute | solution.py:16
  69.3 9.5 %collective-permute-start.12 = (bf16[256,512]{0,1:T(8,128)(2,1)S(1)}, bf16[256,512]{0,1:T(8,128)(2,1)S(1)}, u32[]{:S(2)}, u32[]{:S(2)}) collective-permute-start(bf16[256,512]{0,1:T(8,128)(2,1)S(1)} %dynamic-slice_convert_fusion.2), channel_id=1, source_target_pairs={{0,8},{2,10},{4,12},{6,14},{8,0},{10,2},{12,4},{14,6},{16,24},{18,... | collective-permute-start | bytes 786440 | tf_op jit(solution)/shard_map/ppermute | solution.py:16
  81.2 26.0 %collective-permute-start.24 = (bf16[512,512]{0,1:T(8,128)(2,1)}, bf16[512,512]{0,1:T(8,128)(2,1)}, u32[]{:S(2)}, u32[]{:S(2)}) collective-permute-start(bf16[512,512]{0,1:T(8,128)(2,1)} %fusion.9), channel_id=1, source_target_pairs={{0,2},{2,0},{4,6},{6,4},{8,10},{10,8},{12,14},{14,12},{16,18},{18,... | collective-permute-start | bytes 1572872 | tf_op jit(solution)/shard_map/ppermute | solution.py:16
  82.0 27.5 %collective-permute-start.22 = (bf16[512,512]{0,1:T(8,128)(2,1)}, bf16[512,512]{0,1:T(8,128)(2,1)}, u32[]{:S(2)}, u32[]{:S(2)}) collective-permute-start(bf16[512,512]{0,1:T(8,128)(2,1)} %fusion.13), channel_id=1, source_target_pairs={{0,2},{2,0},{4,6},{6,4},{8,10},{10,8},{12,14},{14,12},{16,18},{18,... | collective-permute-start | bytes 1572872 | tf_op jit(solution)/shard_map/ppermute | solution.py:16
  85.3 26.5 %collective-permute-start.21 = (bf16[128,1024]{1,0:T(8,128)(2,1)S(1)}, bf16[128,1024]{1,0:T(8,128)(2,1)}, u32[]{:S(2)}, u32[]{:S(2)}) collective-permute-start(bf16[128,1024]{1,0:T(8,128)(2,1)S(1)} %fusion.5), channel_id=1, source_target_pairs={{0,1},{1,0},{2,3},{3,2},{4,5},{5,4},{6,7},{7,6},{8,9},{9,8},{10,11... | collective-permute-start | bytes 786440 | tf_op jit(solution)/shard_map/ppermute | solution.py:93
  88.7 12.4 %collective-permute-start.31 = (bf16[64,512]{0,1:T(8,128)(2,1)S(1)}, bf16[64,512]{0,1:T(8,128)(2,1)S(1)}, u32[]{:S(2)}, u32[]{:S(2)}) collective-permute-start(bf16[64,512]{0,1:T(8,128)(2,1)S(1)} %dynamic-slice_convert_fusion.10), channel_id=1, source_target_pairs={{0,16},{2,18},{4,20},{6,22},{8,24},{10,26},{12,28},{14,30},{16,0},... | collective-permute-start | bytes 196616 | tf_op jit(solution)/shard_map/ppermute | solution.py:16
  92.0 10.6 %collective-permute-start.33 = (bf16[64,512]{0,1:T(8,128)(2,1)S(1)}, bf16[64,512]{0,1:T(8,128)(2,1)S(1)}, u32[]{:S(2)}, u32[]{:S(2)}) collective-permute-start(bf16[64,512]{0,1:T(8,128)(2,1)S(1)} %dynamic-slice_convert_fusion.8), channel_id=1, source_target_pairs={{0,16},{2,18},{4,20},{6,22},{8,24},{10,26},{12,28},{14,30},{16,0},... | collective-permute-start | bytes 196616 | tf_op jit(solution)/shard_map/ppermute | solution.py:16
  121.1 11.5 %collective-permute-start.34 = (bf16[128,512]{0,1:T(8,128)(2,1)S(1)}, bf16[128,512]{0,1:T(8,128)(2,1)S(1)}, u32[]{:S(2)}, u32[]{:S(2)}) collective-permute-start(bf16[128,512]{0,1:T(8,128)(2,1)S(1)} %dynamic-slice_convert_fusion.7), channel_id=1, source_target_pairs={{0,8},{2,10},{4,12},{6,14},{8,0},{10,2},{12,4},{14,6},{16,24},{18,... | collective-permute-start | bytes 393224 | tf_op jit(solution)/shard_map/ppermute | solution.py:16
  132.7 10.9 %collective-permute-start.35 = (bf16[64,512]{0,1:T(8,128)(2,1)S(1)}, bf16[64,512]{0,1:T(8,128)(2,1)S(1)}, u32[]{:S(2)}, u32[]{:S(2)}) collective-permute-start(bf16[64,512]{0,1:T(8,128)(2,1)S(1)} %dynamic-slice_convert_fusion.6), channel_id=1, source_target_pairs={{0,16},{2,18},{4,20},{6,22},{8,24},{10,26},{12,28},{14,30},{16,0},... | collective-permute-start | bytes 196616 | tf_op jit(solution)/shard_map/ppermute | solution.py:16
  135.8 9.4 %collective-permute-start.37 = (bf16[64,512]{0,1:T(8,128)(2,1)S(1)}, bf16[64,512]{0,1:T(8,128)(2,1)S(1)}, u32[]{:S(2)}, u32[]{:S(2)}) collective-permute-start(bf16[64,512]{0,1:T(8,128)(2,1)S(1)} %dynamic-slice_convert_fusion.4), channel_id=1, source_target_pairs={{0,16},{2,18},{4,20},{6,22},{8,24},{10,26},{12,28},{14,30},{16,0},... | collective-permute-start | bytes 196616 | tf_op jit(solution)/shard_map/ppermute | solution.py:16
  (35 other events, 217.8 us)

commit v4 on v2

--- a/solution.py
+++ b/solution.py
@@ -104,10 +104,12 @@
     values = jnp.dot(normed, w_value, preferred_element_type=jnp.float32).astype(jnp.bfloat16)
     key_blocks = keys.reshape(blocks_dev, block_len, columns)
     value_blocks = values.reshape(blocks_dev, block_len, columns)
-    bit_order = list(range(graph_levels))
+    bit_order = list(range(graph_levels))[::-1]
+    joined_blocks = jnp.concatenate([key_blocks, value_blocks], axis=2)
     remote = {}
     for bit in bit_order:
-        remote[bit] = from_partner((key_blocks, value_blocks), "graph", bit)
+        got = from_partner(joined_blocks, "graph", bit)
+        remote[bit] = (got[:, :, :columns], got[:, :, columns:])
     key_slots = (
         [key_blocks]
         + [flip_blocks(key_blocks, level) for level in range(local_levels)]
@@ -167,7 +169,10 @@
     returned = {}
     for bit in bit_order:
         slot = 1 + local_levels + bit
-        returned[bit] = from_partner((key_terms[slot], value_terms[slot]), "graph", bit)
+        got = from_partner(
+            jnp.concatenate([key_terms[slot], value_terms[slot]], axis=2), "graph", bit
+        )
+        returned[bit] = (got[:, :, :columns], got[:, :, columns:])
     for bit in range(graph_levels):
         grad_key = grad_key + returned[bit][0].astype(jnp.float32)
         grad_value = grad_value + returned[bit][1].astype(jnp.float32)
@@ -187,9 +192,8 @@
     )
     low_terms = feature_terms.astype(jnp.bfloat16)
     grad_normed = low_terms.astype(jnp.float32) + head_swap(low_terms).astype(jnp.float32)
-    gain_grad = doubling_sum(
-        jnp.sum(grad_normed * wide_nodes * inverse, axis=0), "graph", graph_levels
-    )
+    gain_terms = jnp.sum(low_terms.astype(jnp.float32) * wide_nodes * inverse, axis=0)
+    gain_grad = doubling_sum(gain_terms + head_swap(gain_terms), "graph", graph_levels)
     scaled = grad_normed * gain
     nodes_grad = (
         inverse

time: 136 us -> 137 us (level)
  starting transfers between devices: 41.2 us -> 26.3 us
  local copies, waits for them, and re-layouts: 24.7 us -> 33.1 us
  waiting for transfers between devices: 41.7 us -> 48.3 us
  other arithmetic: 7.89 us -> 11.1 us
  matrix products: 18.3 us -> 15.8 us
    ppermute x36 -> x28, starting transfers between devices: 39 us -> 23.5 us  [from_partner(): return lax.ppermute(value, axis, pairs)]
    slice x1 -> x12, local copies, waits for them, and re-layouts: 0.05 us -> 14.6 us  [shards(): remote[bit] = (got[:, :, :columns], got[:, :, columns:])]
    ppermute x8 -> x0, local copies, waits for them, and re-layouts: 7.25 us -> none  [from_partner(): return lax.ppermute(value, axis, pairs)]
    ppermute x36 -> x28, waiting for transfers between devices: 34.4 us -> 39.2 us  [from_partner(): return lax.ppermute(value, axis, pairs)]
    dot_general x1, matrix products: 3.09 us -> 1.01 us  [shards(): jnp.einsum('bqhe,sbkhe->bhqsk', grad_heads, values_all, preferred_element...]
    add x16, other arithmetic: 1.69 us -> 3.58 us  [halving_sum(): partial = keep + got.astype(jnp.float32)]
    ppermute x2 -> x3, waiting for transfers between devices: 7.31 us -> 9.05 us  [head_swap(): return lax.ppermute(value, 'head', [(0, 1), (1, 0)])]
    convert_element_type x12, local copies, waits for them, and re-layouts: 0.71 us -> 2.11 us  [halving_sum(): got = from_partner(send.astype(jnp.bfloat16), axis, bit)]
  transfers between devices with their start and end apart: 38 -> 31, of which waited for: 15 -> 15; matrix products, arithmetic and copies ran while one was open for 25% -> 21% of each run, Pallas kernels for 0% -> 0%
where the time goes in v4:
time: 137 us; the launch traced here: 136 us
  waiting for transfers between devices  48.3 us (35%)
  local copies, waits for them, and re-layouts  33.1 us (24%)
  starting transfers between devices  26.3 us (19%)
  matrix products  15.8 us (12%)
  other arithmetic  11.1 us (8%)
  between operations  1.42 us (1%)
    ppermute x28, waiting for transfers between devices, from_partner(): return lax.ppermute(value, axis, pairs)  39.2 us
    ppermute x28, starting transfers between devices, from_partner(): return lax.ppermute(value, axis, pairs)  23.5 us
    slice x12, local copies, waits for them, and re-layouts, shards(): remote[bit] = (got[:, :, :columns], got[:, :, columns:])  14.6 us
    unnamed x43, local copies, waits for them, and re-layouts  11.6 us
    ppermute x3, waiting for transfers between devices, head_swap(): return lax.ppermute(value, 'head', [(0, 1), (1, 0)])  9.05 us
    add x16, other arithmetic, halving_sum(): partial = keep + got.astype(jnp.float32)  3.58 us
    ppermute x3, starting transfers between devices, head_swap(): return lax.ppermute(value, 'head', [(0, 1), (1, 0)])  2.76 us
  transfers between devices with their start and end apart: 31, of which 15 were waited for; matrix products, arithmetic and copies ran while one was open for 21% of the time, Pallas kernels for 0%

profile of v4, /device:TPU:0, one launch (start us, length us, event | category | flops | bytes accessed | tf_op | source)
XLA Modules:
  0.0 136.0 jit_solution(14618586825831093063)
XLA Ops:
  7.3 2.5 %collective-permute-start.1 = (bf16[1,128,1024]{2,1,0:T(8,128)(2,1)}, bf16[1,128,1024]{2,1,0:T(8,128)(2,1)}, u32[]{:S(2)}, u32[]{:S(2)}) collective-permute-start(bf16[1,128,1024]{2,1,0:T(8,128)(2,1)} %pad_maximum_fusion), channel_id=1, source_target_pairs={{0,4},{2,6},{4,0},{6,2},{8,12},{10,14},{12,8},{14,10},{16,20},{18,... | collective-permute-start | bytes 786440 | tf_op jit(solution)/shard_map/ppermute | solution.py:16
  11.4 2.6 %collective-permute-start.3 = (bf16[1,128,1024]{2,1,0:T(8,128)(2,1)}, bf16[1,128,1024]{2,1,0:T(8,128)(2,1)}, u32[]{:S(2)}, u32[]{:S(2)}) collective-permute-start(bf16[1,128,1024]{2,1,0:T(8,128)(2,1)} %pad_maximum_fusion), channel_id=1, source_target_pairs={{0,16},{2,18},{4,20},{6,22},{8,24},{10,26},{12,28},{14,30},{16,0},... | collective-permute-start | bytes 786440 | tf_op jit(solution)/shard_map/ppermute | solution.py:16
  20.8 1.6 %fusion.81 = (bf16[1,128,512]{2,1,0:T(8,128)(2,1)}, bf16[1,128,512]{2,1,0:T(8,128)(2,1)S(1)}) fusion(bf16[1,128,1024]{2,1,0:T(8,128)(2,1)} %collective-permute-done), kind=kLoop, calls=%fused_computation.169 | loop fusion | bytes 524288 | tf_op jit(solution)/shard_map/slice | solution.py:112
  24.3 1.6 %fusion.79 = (bf16[1,128,512]{2,1,0:T(8,128)(2,1)}, bf16[1,128,512]{2,1,0:T(8,128)(2,1)S(1)}) fusion(bf16[1,128,1024]{2,1,0:T(8,128)(2,1)} %collective-permute-done.2), kind=kLoop, calls=%fused_computation.167 | loop fusion | bytes 524288 | tf_op jit(solution)/shard_map/slice | solution.py:112
  26.5 1.7 %fusion.78 = (bf16[1,128,512]{2,1,0:T(8,128)(2,1)}, bf16[1,128,512]{2,1,0:T(8,128)(2,1)}) fusion(bf16[1,128,1024]{2,1,0:T(8,128)(2,1)} %collective-permute-done.3), kind=kLoop, calls=%fused_computation.166 | loop fusion | bytes 524288 | tf_op jit(solution)/shard_map/slice | solution.py:112
  29.2 1.7 %copy.54 = bf16[1,128,512]{1,2,0:T(8,128)(2,1)} copy(bf16[1,128,512]{2,1,0:T(8,128)(2,1)} %get-tuple-element.49) | data formatting | bytes 262144 | tf_op jit(solution)/shard_map/slice | solution.py:112
  30.9 1.7 %copy.55 = bf16[1,128,512]{1,2,0:T(8,128)(2,1)} copy(bf16[1,128,512]{2,1,0:T(8,128)(2,1)} %get-tuple-element.47) | data formatting | bytes 262144 | tf_op jit(solution)/shard_map/slice | solution.py:112
  32.5 1.7 %copy.56 = bf16[1,128,512]{1,2,0:T(8,128)(2,1)} copy(bf16[1,128,512]{2,1,0:T(8,128)(2,1)} %get-tuple-element.45) | data formatting | bytes 262144 | tf_op jit(solution)/shard_map/slice | solution.py:112
  34.2 1.7 %copy.57 = bf16[1,128,512]{1,2,0:T(8,128)(2,1)} copy(bf16[1,128,512]{2,1,0:T(8,128)(2,1)} %get-tuple-element.43) | data formatting | bytes 262144 | tf_op jit(solution)/shard_map/slice | solution.py:112
  42.2 1.8 %fusion = (f32[8,128]{1,0:T(8,128)S(1)}, f32[8,128,5,128]{1,3,2,0:T(8,128)S(1)}) fusion(pred[5]{0:T(512)(128)(4,1)S(1)} %compare_bitcast_fusion, bf16[128,8,64,1]{0,2,3,1:T(8,128)(2,1)S(1)} %bitcast.190, bf16[5,1,128,8,64]{2,4,0,3,1:T(8,128)(2,1)} %constant_dynamic-update-slice_fusion.5), kind=kOutput, calls=%fused_computation.20 | convolution fusion | flops 85851136 | bytes 3411973 | tf_op jit(solution)/shard_map/bqhe,sbkhe->bhqsk/dot_general | solution.py:131
  52.8 2.8 %collective-permute-start.7 = (bf16[1,128,1024]{1,2,0:T(8,128)(2,1)S(1)}, bf16[1,128,1024]{1,2,0:T(8,128)(2,1)S(1)}, u32[]{:S(2)}, u32[]{:S(2)}) collective-permute-start(bf16[1,128,1024]{1,2,0:T(8,128)(2,1)S(1)} %pad_maximum_fusion.3), channel_id=1, source_target_pairs={{0,8},{2,10},{4,12},{6,14},{8,0},{10,2},{12,4},{14,6},{16,24},{18,... | collective-permute-start | bytes 786440 | tf_op jit(solution)/shard_map/ppermute | solution.py:16
  58.1 8.1 %collective-permute-done.8 = bf16[1,128,1024]{1,2,0:T(8,128)(2,1)S(1)} collective-permute-done((bf16[1,128,1024]{1,2,0:T(8,128)(2,1)S(1)}, bf16[1,128,1024]{1,2,0:T(8,128)(2,1)S(1)}, u32[]{:S(2)}, u32[]{:S(2)}) %collective-permute-start.8) | collective-permute-done | bytes 262176 | tf_op jit(solution)/shard_map/ppermute | solution.py:16
  71.5 6.2 %collective-permute-done.9 = bf16[128,1024]{1,0:T(8,128)(2,1)S(1)} collective-permute-done((bf16[128,1024]{1,0:T(8,128)(2,1)S(1)}, bf16[128,1024]{1,0:T(8,128)(2,1)S(1)}, u32[]{:S(2)}, u32[]{:S(2)}) %collective-permute-start.9) | collective-permute-done | bytes 262176 | tf_op jit(solution)/shard_map/ppermute | solution.py:80
  78.8 2.9 %collective-permute-done.10 = f32[1024]{0:T(1024)S(1)} collective-permute-done((f32[1024]{0:T(1024)S(1)}, f32[1024]{0:T(1024)S(1)}, u32[]{:S(2)}, u32[]{:S(2)}) %collective-permute-start.10) | collective-permute-done | bytes 4128 | tf_op jit(solution)/shard_map/ppermute | solution.py:80
  83.5 2.9 %collective-permute-done.12 = f32[1024]{0:T(1024)S(1)} collective-permute-done((f32[1024]{0:T(1024)S(1)}, f32[1024]{0:T(1024)S(1)}, u32[]{:S(2)}, u32[]{:S(2)}) %collective-permute-start.12) | collective-permute-done | bytes 4128 | tf_op jit(solution)/shard_map/ppermute | solution.py:16
  88.0 2.5 %collective-permute-done.13 = f32[1024]{0:T(1024)S(1)} collective-permute-done((f32[1024]{0:T(1024)S(1)}, f32[1024]{0:T(1024)S(1)}, u32[]{:S(2)}, u32[]{:S(2)}) %collective-permute-start.13) | collective-permute-done | bytes 4128 | tf_op jit(solution)/shard_map/ppermute | solution.py:16
  92.2 2.9 %collective-permute-done.14 = f32[1024]{0:T(1024)S(1)} collective-permute-done((f32[1024]{0:T(1024)S(1)}, f32[1024]{0:T(1024)S(1)}, u32[]{:S(2)}, u32[]{:S(2)}) %collective-permute-start.14) | collective-permute-done | bytes 4128 | tf_op jit(solution)/shard_map/ppermute | solution.py:16
  103.1 2.2 %collective-permute-start.18 = (bf16[64,512]{0,1:T(8,128)(2,1)S(1)}, bf16[64,512]{0,1:T(8,128)(2,1)S(1)}, u32[]{:S(2)}, u32[]{:S(2)}) collective-permute-start(bf16[64,512]{0,1:T(8,128)(2,1)S(1)} %dynamic-slice_convert_fusion.10), channel_id=1, source_target_pairs={{0,16},{2,18},{4,20},{6,22},{8,24},{10,26},{12,28},{14,30},{16,0},... | collective-permute-start | bytes 196616 | tf_op jit(solution)/shard_map/ppermute | solution.py:16
  105.3 7.7 %collective-permute-done.22 = bf16[64,512]{0,1:T(8,128)(2,1)S(1)} collective-permute-done((bf16[64,512]{0,1:T(8,128)(2,1)S(1)}, bf16[64,512]{0,1:T(8,128)(2,1)S(1)}, u32[]{:S(2)}, u32[]{:S(2)}) %collective-permute-start.22) | collective-permute-done | bytes 65568 | tf_op jit(solution)/shard_map/ppermute | solution.py:16
  115.4 1.7 %copy.84 = f32[64,512]{1,0:T(8,128)} copy(f32[64,512]{0,1:T(8,128)} %get-tuple-element.60) | data formatting | bytes 262144
  121.2 2.7 %collective-permute-done.29 = bf16[128,512]{0,1:T(8,128)(2,1)S(1)} collective-permute-done((bf16[128,512]{0,1:T(8,128)(2,1)S(1)}, bf16[128,512]{0,1:T(8,128)(2,1)S(1)}, u32[]{:S(2)}, u32[]{:S(2)}) %collective-permute-start.29) | collective-permute-done | bytes 131104 | tf_op jit(solution)/shard_map/ppermute | solution.py:16
  124.2 3.5 %collective-permute-done.25 = bf16[128,512]{0,1:T(8,128)(2,1)S(1)} collective-permute-done((bf16[128,512]{0,1:T(8,128)(2,1)S(1)}, bf16[128,512]{0,1:T(8,128)(2,1)S(1)}, u32[]{:S(2)}, u32[]{:S(2)}) %collective-permute-start.25) | collective-permute-done | bytes 131104 | tf_op jit(solution)/shard_map/ppermute | solution.py:16
  128.0 2.5 %collective-permute-done.30 = bf16[64,512]{0,1:T(8,128)(2,1)S(1)} collective-permute-done((bf16[64,512]{0,1:T(8,128)(2,1)S(1)}, bf16[64,512]{0,1:T(8,128)(2,1)S(1)}, u32[]{:S(2)}, u32[]{:S(2)}) %collective-permute-start.30) | collective-permute-done | bytes 65568 | tf_op jit(solution)/shard_map/ppermute | solution.py:16
  130.7 3.6 %collective-permute-done.26 = bf16[64,512]{0,1:T(8,128)(2,1)S(1)} collective-permute-done((bf16[64,512]{0,1:T(8,128)(2,1)S(1)}, bf16[64,512]{0,1:T(8,128)(2,1)S(1)}, u32[]{:S(2)}, u32[]{:S(2)}) %collective-permute-start.26) | collective-permute-done | bytes 65568 | tf_op jit(solution)/shard_map/ppermute | solution.py:16
  (188 shorter events, 63.8 us)
Async XLA Ops:
  6.9 13.9 %collective-permute-start = (bf16[1,128,1024]{2,1,0:T(8,128)(2,1)}, bf16[1,128,1024]{2,1,0:T(8,128)(2,1)}, u32[]{:S(2)}, u32[]{:S(2)}) collective-permute-start(bf16[1,128,1024]{2,1,0:T(8,128)(2,1)} %pad_maximum_fusion), channel_id=1, source_target_pairs={{0,2},{2,0},{4,6},{6,4},{8,10},{10,8},{12,14},{14,12},{16,18},{18,... | collective-permute-start | bytes 786440 | tf_op jit(solution)/shard_map/ppermute | solution.py:16
  7.3 15.1 %collective-permute-start.1 = (bf16[1,128,1024]{2,1,0:T(8,128)(2,1)}, bf16[1,128,1024]{2,1,0:T(8,128)(2,1)}, u32[]{:S(2)}, u32[]{:S(2)}) collective-permute-start(bf16[1,128,1024]{2,1,0:T(8,128)(2,1)} %pad_maximum_fusion), channel_id=1, source_target_pairs={{0,4},{2,6},{4,0},{6,2},{8,12},{10,14},{12,8},{14,10},{16,20},{18,... | collective-permute-start | bytes 786440 | tf_op jit(solution)/shard_map/ppermute | solution.py:16
  9.8 14.5 %collective-permute-start.2 = (bf16[1,128,1024]{2,1,0:T(8,128)(2,1)}, bf16[1,128,1024]{2,1,0:T(8,128)(2,1)}, u32[]{:S(2)}, u32[]{:S(2)}) collective-permute-start(bf16[1,128,1024]{2,1,0:T(8,128)(2,1)} %pad_maximum_fusion), channel_id=1, source_target_pairs={{0,8},{2,10},{4,12},{6,14},{8,0},{10,2},{12,4},{14,6},{16,24},{18,... | collective-permute-start | bytes 786440 | tf_op jit(solution)/shard_map/ppermute | solution.py:16
  11.4 15.1 %collective-permute-start.3 = (bf16[1,128,1024]{2,1,0:T(8,128)(2,1)}, bf16[1,128,1024]{2,1,0:T(8,128)(2,1)}, u32[]{:S(2)}, u32[]{:S(2)}) collective-permute-start(bf16[1,128,1024]{2,1,0:T(8,128)(2,1)} %pad_maximum_fusion), channel_id=1, source_target_pairs={{0,16},{2,18},{4,20},{6,22},{8,24},{10,26},{12,28},{14,30},{16,0},... | collective-permute-start | bytes 786440 | tf_op jit(solution)/shard_map/ppermute | solution.py:16
  50.7 19.6 %collective-permute-start.4 = (f32[128,512]{1,0:T(8,128)S(1)}, f32[128,512]{1,0:T(8,128)S(1)}, u32[]{:S(2)}, u32[]{:S(2)}) collective-permute-start(f32[128,512]{1,0:T(8,128)S(1)} %constant_dynamic-slice_fusion), channel_id=1, source_target_pairs={{0,1},{1,0},{2,3},{3,2},{4,5},{5,4},{6,7},{7,6},{8,9},{9,8},{10,11... | collective-permute-start | bytes 786440 | tf_op jit(solution)/shard_map/ppermute | solution.py:80
  52.4 13.8 %collective-permute-start.8 = (bf16[1,128,1024]{1,2,0:T(8,128)(2,1)S(1)}, bf16[1,128,1024]{1,2,0:T(8,128)(2,1)S(1)}, u32[]{:S(2)}, u32[]{:S(2)}) collective-permute-start(bf16[1,128,1024]{1,2,0:T(8,128)(2,1)S(1)} %pad_maximum_fusion.4), channel_id=1, source_target_pairs={{0,16},{2,18},{4,20},{6,22},{8,24},{10,26},{12,28},{14,30},{16,0},... | collective-permute-start | bytes 786440 | tf_op jit(solution)/shard_map/ppermute | solution.py:16
  52.8 13.4 %collective-permute-start.7 = (bf16[1,128,1024]{1,2,0:T(8,128)(2,1)S(1)}, bf16[1,128,1024]{1,2,0:T(8,128)(2,1)S(1)}, u32[]{:S(2)}, u32[]{:S(2)}) collective-permute-start(bf16[1,128,1024]{1,2,0:T(8,128)(2,1)S(1)} %pad_maximum_fusion.3), channel_id=1, source_target_pairs={{0,8},{2,10},{4,12},{6,14},{8,0},{10,2},{12,4},{14,6},{16,24},{18,... | collective-permute-start | bytes 786440 | tf_op jit(solution)/shard_map/ppermute | solution.py:16
  55.6 11.2 %collective-permute-start.6 = (bf16[1,128,1024]{1,2,0:T(8,128)(2,1)S(1)}, bf16[1,128,1024]{1,2,0:T(8,128)(2,1)S(1)}, u32[]{:S(2)}, u32[]{:S(2)}) collective-permute-start(bf16[1,128,1024]{1,2,0:T(8,128)(2,1)S(1)} %pad_maximum_fusion.2), channel_id=1, source_target_pairs={{0,4},{2,6},{4,0},{6,2},{8,12},{10,14},{12,8},{14,10},{16,20},{18,... | collective-permute-start | bytes 786440 | tf_op jit(solution)/shard_map/ppermute | solution.py:16
  56.2 10.6 %collective-permute-start.5 = (bf16[1,128,1024]{1,2,0:T(8,128)(2,1)S(1)}, bf16[1,128,1024]{1,2,0:T(8,128)(2,1)S(1)}, u32[]{:S(2)}, u32[]{:S(2)}) collective-permute-start(bf16[1,128,1024]{1,2,0:T(8,128)(2,1)S(1)} %pad_maximum_fusion.1), channel_id=1, source_target_pairs={{0,2},{2,0},{4,6},{6,4},{8,10},{10,8},{12,14},{14,12},{16,18},{18,... | collective-permute-start | bytes 786440 | tf_op jit(solution)/shard_map/ppermute | solution.py:16
  66.2 12.3 %collective-permute-start.19 = (bf16[512,512]{0,1:T(8,128)(2,1)S(1)}, bf16[512,512]{0,1:T(8,128)(2,1)S(1)}, u32[]{:S(2)}, u32[]{:S(2)}) collective-permute-start(bf16[512,512]{0,1:T(8,128)(2,1)S(1)} %fusion.17), channel_id=1, source_target_pairs={{0,2},{2,0},{4,6},{6,4},{8,10},{10,8},{12,14},{14,12},{16,18},{18,... | collective-permute-start | bytes 1572872 | tf_op jit(solution)/shard_map/ppermute | solution.py:16
  66.2 17.1 %collective-permute-start.15 = (bf16[512,512]{0,1:T(8,128)(2,1)S(1)}, bf16[512,512]{0,1:T(8,128)(2,1)S(1)}, u32[]{:S(2)}, u32[]{:S(2)}) collective-permute-start(bf16[512,512]{0,1:T(8,128)(2,1)S(1)} %fusion.21), channel_id=1, source_target_pairs={{0,2},{2,0},{4,6},{6,4},{8,10},{10,8},{12,14},{14,12},{16,18},{18,... | collective-permute-start | bytes 1572872 | tf_op jit(solution)/shard_map/ppermute | solution.py:16
  69.4 8.3 %collective-permute-start.9 = (bf16[128,1024]{1,0:T(8,128)(2,1)S(1)}, bf16[128,1024]{1,0:T(8,128)(2,1)S(1)}, u32[]{:S(2)}, u32[]{:S(2)}) collective-permute-start(bf16[128,1024]{1,0:T(8,128)(2,1)S(1)} %fusion.5), channel_id=1, source_target_pairs={{0,1},{1,0},{2,3},{3,2},{4,5},{5,4},{6,7},{7,6},{8,9},{9,8},{10,11... | collective-permute-start | bytes 786440 | tf_op jit(solution)/shard_map/ppermute | solution.py:80
  70.1 26.9 %collective-permute-start.27 = (bf16[512,512]{0,1:T(8,128)(2,1)S(1)}, bf16[512,512]{0,1:T(8,128)(2,1)S(1)}, u32[]{:S(2)}, u32[]{:S(2)}) collective-permute-start(bf16[512,512]{0,1:T(8,128)(2,1)S(1)} %fusion.9), channel_id=1, source_target_pairs={{0,2},{2,0},{4,6},{6,4},{8,10},{10,8},{12,14},{14,12},{16,18},{18,... | collective-permute-start | bytes 1572872 | tf_op jit(solution)/shard_map/ppermute | solution.py:16
  70.3 29.2 %collective-permute-start.23 = (bf16[512,512]{0,1:T(8,128)(2,1)S(1)}, bf16[512,512]{0,1:T(8,128)(2,1)S(1)}, u32[]{:S(2)}, u32[]{:S(2)}) collective-permute-start(bf16[512,512]{0,1:T(8,128)(2,1)S(1)} %fusion.13), channel_id=1, source_target_pairs={{0,2},{2,0},{4,6},{6,4},{8,10},{10,8},{12,14},{14,12},{16,18},{18,... | collective-permute-start | bytes 1572872 | tf_op jit(solution)/shard_map/ppermute | solution.py:16
  81.7 14.0 %collective-permute-start.20 = (bf16[256,512]{0,1:T(8,128)(2,1)S(1)}, bf16[256,512]{0,1:T(8,128)(2,1)S(1)}, u32[]{:S(2)}, u32[]{:S(2)}) collective-permute-start(bf16[256,512]{0,1:T(8,128)(2,1)S(1)} %dynamic-slice_convert_fusion.2), channel_id=1, source_target_pairs={{0,8},{2,10},{4,12},{6,14},{8,0},{10,2},{12,4},{14,6},{16,24},{18,... | collective-permute-start | bytes 786440 | tf_op jit(solution)/shard_map/ppermute | solution.py:16
  87.4 8.9 %collective-permute-start.16 = (bf16[256,512]{0,1:T(8,128)(2,1)S(1)}, bf16[256,512]{0,1:T(8,128)(2,1)S(1)}, u32[]{:S(2)}, u32[]{:S(2)}) collective-permute-start(bf16[256,512]{0,1:T(8,128)(2,1)S(1)} %dynamic-slice_convert_fusion.3), channel_id=1, source_target_pairs={{0,4},{2,6},{4,0},{6,2},{8,12},{10,14},{12,8},{14,10},{16,20},{18,... | collective-permute-start | bytes 786440 | tf_op jit(solution)/shard_map/ppermute | solution.py:16
  96.5 6.5 %collective-permute-start.17 = (bf16[128,512]{0,1:T(8,128)(2,1)S(1)}, bf16[128,512]{0,1:T(8,128)(2,1)S(1)}, u32[]{:S(2)}, u32[]{:S(2)}) collective-permute-start(bf16[128,512]{0,1:T(8,128)(2,1)S(1)} %dynamic-slice_convert_fusion.11), channel_id=1, source_target_pairs={{0,8},{2,10},{4,12},{6,14},{8,0},{10,2},{12,4},{14,6},{16,24},{18,... | collective-permute-start | bytes 393224 | tf_op jit(solution)/shard_map/ppermute | solution.py:16
  97.9 19.9 %collective-permute-start.28 = (bf16[256,512]{0,1:T(8,128)(2,1)}, bf16[256,512]{0,1:T(8,128)(2,1)}, u32[]{:S(2)}, u32[]{:S(2)}) collective-permute-start(bf16[256,512]{0,1:T(8,128)(2,1)} %dynamic-slice_convert_fusion), channel_id=1, source_target_pairs={{0,8},{2,10},{4,12},{6,14},{8,0},{10,2},{12,4},{14,6},{16,24},{18,... | collective-permute-start | bytes 786440 | tf_op jit(solution)/shard_map/ppermute | solution.py:16
  100.5 19.6 %collective-permute-start.24 = (bf16[256,512]{0,1:T(8,128)(2,1)}, bf16[256,512]{0,1:T(8,128)(2,1)}, u32[]{:S(2)}, u32[]{:S(2)}) collective-permute-start(bf16[256,512]{0,1:T(8,128)(2,1)} %dynamic-slice_convert_fusion.1), channel_id=1, source_target_pairs={{0,4},{2,6},{4,0},{6,2},{8,12},{10,14},{12,8},{14,10},{16,20},{18,... | collective-permute-start | bytes 786440 | tf_op jit(solution)/shard_map/ppermute | solution.py:16
  102.1 10.9 %collective-permute-start.22 = (bf16[64,512]{0,1:T(8,128)(2,1)S(1)}, bf16[64,512]{0,1:T(8,128)(2,1)S(1)}, u32[]{:S(2)}, u32[]{:S(2)}) collective-permute-start(bf16[64,512]{0,1:T(8,128)(2,1)S(1)} %dynamic-slice_convert_fusion.8), channel_id=1, source_target_pairs={{0,16},{2,18},{4,20},{6,22},{8,24},{10,26},{12,28},{14,30},{16,0},... | collective-permute-start | bytes 196616 | tf_op jit(solution)/shard_map/ppermute | solution.py:16
  103.1 11.4 %collective-permute-start.18 = (bf16[64,512]{0,1:T(8,128)(2,1)S(1)}, bf16[64,512]{0,1:T(8,128)(2,1)S(1)}, u32[]{:S(2)}, u32[]{:S(2)}) collective-permute-start(bf16[64,512]{0,1:T(8,128)(2,1)S(1)} %dynamic-slice_convert_fusion.10), channel_id=1, source_target_pairs={{0,16},{2,18},{4,20},{6,22},{8,24},{10,26},{12,28},{14,30},{16,0},... | collective-permute-start | bytes 196616 | tf_op jit(solution)/shard_map/ppermute | solution.py:16
  121.2 6.5 %collective-permute-start.25 = (bf16[128,512]{0,1:T(8,128)(2,1)S(1)}, bf16[128,512]{0,1:T(8,128)(2,1)S(1)}, u32[]{:S(2)}, u32[]{:S(2)}) collective-permute-start(bf16[128,512]{0,1:T(8,128)(2,1)S(1)} %dynamic-slice_convert_fusion.7), channel_id=1, source_target_pairs={{0,8},{2,10},{4,12},{6,14},{8,0},{10,2},{12,4},{14,6},{16,24},{18,... | collective-permute-start | bytes 393224 | tf_op jit(solution)/shard_map/ppermute | solution.py:16
  124.1 6.4 %collective-permute-start.30 = (bf16[64,512]{0,1:T(8,128)(2,1)S(1)}, bf16[64,512]{0,1:T(8,128)(2,1)S(1)}, u32[]{:S(2)}, u32[]{:S(2)}) collective-permute-start(bf16[64,512]{0,1:T(8,128)(2,1)S(1)} %dynamic-slice_convert_fusion.4), channel_id=1, source_target_pairs={{0,16},{2,18},{4,20},{6,22},{8,24},{10,26},{12,28},{14,30},{16,0},... | collective-permute-start | bytes 196616 | tf_op jit(solution)/shard_map/ppermute | solution.py:16
  127.8 6.4 %collective-permute-start.26 = (bf16[64,512]{0,1:T(8,128)(2,1)S(1)}, bf16[64,512]{0,1:T(8,128)(2,1)S(1)}, u32[]{:S(2)}, u32[]{:S(2)}) collective-permute-start(bf16[64,512]{0,1:T(8,128)(2,1)S(1)} %dynamic-slice_convert_fusion.6), channel_id=1, source_target_pairs={{0,16},{2,18},{4,20},{6,22},{8,24},{10,26},{12,28},{14,30},{16,0},... | collective-permute-start | bytes 196616 | tf_op jit(solution)/shard_map/ppermute | solution.py:16
  (20 other events, 121.7 us)

commit v5 on v4

--- a/solution.py
+++ b/solution.py
@@ -2,6 +2,9 @@
 import jax.numpy as jnp
 from jax import lax
 from jax.sharding import PartitionSpec as P
+import functools
+from jax.experimental import pallas as pl
+from jax.experimental.pallas import tpu as pltpu
 
 HEAD_DIM = 64
 
@@ -86,6 +89,98 @@
     return jnp.flip(shaped, axis=1).reshape(array.shape)
 
 
+def attention_kernel(slots, pairs, active_ref, q_ref, g_ref, *refs):
+    key_refs = refs[:slots]
+    value_refs = refs[slots : 2 * slots]
+    att_ref, gq_ref = refs[2 * slots], refs[2 * slots + 1]
+    term_refs = refs[2 * slots + 2 : 3 * slots + 2]
+    block = pl.program_id(0)
+    scale = HEAD_DIM ** (-0.5)
+    width = 2 * HEAD_DIM
+    lane = lax.broadcasted_iota(jnp.int32, (q_ref.shape[0], width), 1)
+    low_lanes = lane < HEAD_DIM
+    flags = [active_ref[block * slots + s] > 0 for s in range(slots)]
+    contract_last = (((1,), (1,)), ((), ()))
+    contract_first = (((0,), (0,)), ((), ()))
+    highest = lax.Precision.HIGHEST
+    for pair in range(pairs):
+        cols = pl.ds(pair * width, width)
+        q2 = q_ref[:, cols]
+        g2 = g_ref[:, cols]
+        keys = [key_refs[s][:, cols] for s in range(slots)]
+        values = [value_refs[s][:, cols] for s in range(slots)]
+        outs = []
+        for half in range(2):
+            sel = low_lanes if half == 0 else jnp.logical_not(low_lanes)
+            qm = jnp.where(sel, q2, jnp.zeros_like(q2))
+            gm = jnp.where(sel, g2, jnp.zeros_like(g2))
+            scores = []
+            for s in range(slots):
+                raw = lax.dot_general(qm, keys[s], contract_last, preferred_element_type=jnp.float32) * scale
+                scores.append(jnp.where(flags[s], raw, NEG))
+            top = functools.reduce(jnp.maximum, [jnp.max(x, axis=1, keepdims=True) for x in scores])
+            raised = [jnp.exp(x - top) for x in scores]
+            total = functools.reduce(jnp.add, [jnp.sum(x, axis=1, keepdims=True) for x in raised])
+            probs = [x / total for x in raised]
+            probs_low = [x.astype(jnp.bfloat16) for x in probs]
+            attended = functools.reduce(jnp.add, [
+                jnp.dot(probs_low[s], values[s], preferred_element_type=jnp.float32) for s in range(slots)
+            ])
+            grad_probs = [
+                lax.dot_general(gm, values[s], contract_last, preferred_element_type=jnp.float32)
+                for s in range(slots)
+            ]
+            delta = functools.reduce(jnp.add, [
+                jnp.sum(probs[s] * grad_probs[s], axis=1, keepdims=True) for s in range(slots)
+            ])
+            grad_scores = [probs[s] * (grad_probs[s] - delta) * scale for s in range(slots)]
+            grad_query = functools.reduce(jnp.add, [
+                jnp.dot(grad_scores[s], keys[s].astype(jnp.float32), precision=highest,
+                        preferred_element_type=jnp.float32)
+                for s in range(slots)
+            ])
+            key_terms = [
+                lax.dot_general(grad_scores[s], q2.astype(jnp.float32), contract_first,
+                                precision=highest, preferred_element_type=jnp.float32)
+                for s in range(slots)
+            ]
+            value_terms = [
+                lax.dot_general(probs_low[s], g2, contract_first, preferred_element_type=jnp.float32)
+                for s in range(slots)
+            ]
+            outs.append((attended, grad_query, key_terms, value_terms))
+        (att_a, gq_a, kt_a, vt_a), (att_b, gq_b, kt_b, vt_b) = outs
+        att_ref[:, cols] = jnp.where(low_lanes, att_a, att_b).astype(att_ref.dtype)
+        gq_ref[:, cols] = jnp.where(low_lanes, gq_a, gq_b).astype(gq_ref.dtype)
+        for s in range(slots):
+            term_refs[s][:, cols] = jnp.where(low_lanes, kt_a[s], kt_b[s]).astype(jnp.bfloat16)
+            term_refs[s][:, pl.ds(q_ref.shape[1] + pair * width, width)] = jnp.where(
+                low_lanes, vt_a[s], vt_b[s]
+            ).astype(jnp.bfloat16)
+
+
+def block_attention(active, query, grad, joined_slots):
+    blocks, rows, columns = query.shape
+    slots = len(joined_slots)
+    pairs = columns // (2 * HEAD_DIM)
+    spec = pl.BlockSpec((None, rows, columns), lambda b, act: (b, 0, 0))
+    value_spec = pl.BlockSpec((None, rows, columns), lambda b, act: (b, 0, 1))
+    wide_spec = pl.BlockSpec((None, rows, 2 * columns), lambda b, act: (b, 0, 0))
+    shape = jax.ShapeDtypeStruct((blocks, rows, columns), jnp.bfloat16)
+    wide = jax.ShapeDtypeStruct((blocks, rows, 2 * columns), jnp.bfloat16)
+    outs = pl.pallas_call(
+        functools.partial(attention_kernel, slots, pairs),
+        grid_spec=pltpu.PrefetchScalarGridSpec(
+            num_scalar_prefetch=1,
+            grid=(blocks,),
+            in_specs=[spec] * (2 + slots) + [value_spec] * slots,
+            out_specs=[spec] * 2 + [wide_spec] * slots,
+        ),
+        out_shape=[shape] * 2 + [wide] * slots,
+    )(active.reshape(-1), query, grad, *joined_slots, *joined_slots)
+    return outs[0], outs[1], outs[2:]
+
+
 def shards(nodes, gain, w_query, w_key, w_value, w_out, links, cotangent):
     blocks_dev = links.shape[0]
     local_levels = blocks_dev.bit_length() - 1
@@ -108,70 +203,35 @@
     joined_blocks = jnp.concatenate([key_blocks, value_blocks], axis=2)
     remote = {}
     for bit in bit_order:
-        got = from_partner(joined_blocks, "graph", bit)
-        remote[bit] = (got[:, :, :columns], got[:, :, columns:])
-    key_slots = (
-        [key_blocks]
-        + [flip_blocks(key_blocks, level) for level in range(local_levels)]
-        + [remote[bit][0] for bit in range(graph_levels)]
-    )
-    value_slots = (
-        [value_blocks]
-        + [flip_blocks(value_blocks, level) for level in range(local_levels)]
-        + [remote[bit][1] for bit in range(graph_levels)]
-    )
-    slot_count = len(key_slots)
-    head_shape = (blocks_dev, block_len, local_heads, HEAD_DIM)
-    keys_all = jnp.stack(key_slots).reshape((slot_count,) + head_shape)
-    values_all = jnp.stack(value_slots).reshape((slot_count,) + head_shape)
-    query_heads = query.reshape(head_shape)
+        remote[bit] = from_partner(joined_blocks, "graph", bit)
+    joined_slots = (
+        [joined_blocks]
+        + [flip_blocks(joined_blocks, level) for level in range(local_levels)]
+        + [remote[bit] for bit in range(graph_levels)]
+    )
     active = jnp.concatenate([jnp.ones((blocks_dev, 1), jnp.int32), links], axis=1)
-    allowed = active[:, None, None, :, None] > 0
-    scores = (
-        jnp.einsum("bqhe,sbkhe->bhqsk", query_heads, keys_all, preferred_element_type=jnp.float32)
-        * score_scale
-    )
-    scores = jnp.where(allowed, scores, NEG)
-    top = jnp.max(scores, axis=(3, 4), keepdims=True)
-    raised = jnp.exp(scores - top)
-    total = jnp.sum(raised, axis=(3, 4), keepdims=True)
-    probs = raised / total
-    probs_low = probs.astype(jnp.bfloat16)
-    attended = jnp.einsum(
-        "bhqsk,sbkhe->bqhe", probs_low, values_all, preferred_element_type=jnp.float32
-    )
-    attended = attended.astype(jnp.bfloat16).reshape(node_rows, columns)
+    grad_attended = jnp.dot(cotangent, w_out.T, preferred_element_type=jnp.float32).astype(
+        jnp.bfloat16
+    )
+    attended, grad_query, term_slots = block_attention(
+        active,
+        query.reshape(blocks_dev, block_len, columns),
+        grad_attended.reshape(blocks_dev, block_len, columns),
+        joined_slots,
+    )
+    attended = attended.reshape(node_rows, columns)
+    grad_query = grad_query.reshape(node_rows, columns)
     head_me = lax.axis_index("head")
     mixed_terms = jnp.dot(attended, w_out, preferred_element_type=jnp.float32)
     own_mixed = lax.dynamic_slice_in_dim(mixed_terms, head_me * columns, columns, 1)
     other_mixed = lax.dynamic_slice_in_dim(mixed_terms, (1 - head_me) * columns, columns, 1)
     mixed = (own_mixed + head_swap(other_mixed)).astype(jnp.bfloat16)
-    grad_attended = jnp.dot(cotangent, w_out.T, preferred_element_type=jnp.float32).astype(
-        jnp.bfloat16
-    )
-    grad_heads = grad_attended.reshape(head_shape)
-    grad_probs = jnp.einsum(
-        "bqhe,sbkhe->bhqsk", grad_heads, values_all, preferred_element_type=jnp.float32
-    )
-    delta = jnp.sum(probs * grad_probs, axis=(3, 4), keepdims=True)
-    grad_scores = probs * (grad_probs - delta) * score_scale
-    grad_query = jnp.einsum("bhqsk,sbkhe->bqhe", grad_scores, keys_all.astype(jnp.float32))
-    grad_query = grad_query.astype(jnp.bfloat16).reshape(node_rows, columns)
-    slot_block_shape = (slot_count, blocks_dev, block_len, columns)
-    key_terms = jnp.einsum("bhqsk,bqhe->sbkhe", grad_scores, query_heads.astype(jnp.float32))
-    key_terms = key_terms.astype(jnp.bfloat16).reshape(slot_block_shape)
-    value_terms = jnp.einsum(
-        "bhqsk,bqhe->sbkhe", probs_low, grad_heads, preferred_element_type=jnp.float32
-    )
-    value_terms = value_terms.astype(jnp.bfloat16).reshape(slot_block_shape)
-    grad_key = key_terms[0].astype(jnp.float32)
-    grad_value = value_terms[0].astype(jnp.float32)
+    grad_key = term_slots[0][:, :, :columns].astype(jnp.float32)
+    grad_value = term_slots[0][:, :, columns:].astype(jnp.float32)
     returned = {}
     for bit in bit_order:
         slot = 1 + local_levels + bit
-        got = from_partner(
-            jnp.concatenate([key_terms[slot], value_terms[slot]], axis=2), "graph", bit
-        )
+        got = from_partner(term_slots[slot], "graph", bit)
         returned[bit] = (got[:, :, :columns], got[:, :, columns:])
     for bit in range(graph_levels):
         grad_key = grad_key + returned[bit][0].astype(jnp.float32)

time: 137 us -> 135 us (0.985)
  local copies, waits for them, and re-layouts: 33.1 us -> 14.7 us
  Pallas kernels: 0 us -> 14.5 us
  starting transfers between devices: 26.3 us -> 33.7 us
  matrix products: 15.8 us -> 10.2 us
    slice x13 -> x0, local copies, waits for them, and re-layouts: 14.7 us -> none  [the longest x12 14.6 us: shards(): remote[bit] = (got[:, :, :columns], got[:, :, columns:])]
    pallas_call x0 -> x1, Pallas kernels: none -> 14.5 us  [block_attention(): pl.pallas_call(functools.partial(attention_kernel, slots, pairs), grid_sp...]
    dot_general x6 -> x0, matrix products: 6.96 us -> none  [the longest x1 1.81 us: shards(): jnp.einsum('bqhe,sbkhe->bhqsk', query_heads, keys_all, preferred_element_...]
    ppermute x28, starting transfers between devices: 23.5 us -> 29.1 us  [from_partner(): return lax.ppermute(value, axis, pairs)]
    unnamed x43 -> x33, local copies, waits for them, and re-layouts: 11.6 us -> 7.55 us
    ppermute x28, waiting for transfers between devices: 39.2 us -> 43 us  [from_partner(): return lax.ppermute(value, axis, pairs)]
    transpose x4, local copies, waits for them, and re-layouts: 0.79 us -> 4.09 us  [bit_major_rows(): return shaped.transpose(axes).reshape(rows, width)]
    ppermute x3, waiting for transfers between devices: 9.05 us -> 6.43 us  [head_swap(): return lax.ppermute(value, 'head', [(0, 1), (1, 0)])]
  transfers between devices with their start and end apart: 31 -> 31, of which waited for: 15 -> 16; matrix products, arithmetic and copies ran while one was open for 21% -> 20% of each run, Pallas kernels for 0% -> 0%
where the time goes in v5:
time: 135 us
  waiting for transfers between devices  49.4 us (37%)
  starting transfers between devices  33.7 us (25%)
  local copies, waits for them, and re-layouts  14.7 us (11%)
  Pallas kernels  14.5 us (11%)
  other arithmetic  10.9 us (8%)
  matrix products  10.2 us (8%)
    ppermute x28, waiting for transfers between devices, from_partner(): return lax.ppermute(value, axis, pairs)  43 us
    ppermute x28, starting transfers between devices, from_partner(): return lax.ppermute(value, axis, pairs)  29.1 us
    pallas_call x1, Pallas kernels, block_attention(): pl.pallas_call(functools.partial(attention_kernel, slots, pairs), grid_sp...  14.5 us
    unnamed x33, local copies, waits for them, and re-layouts  7.55 us
    ppermute x3, waiting for transfers between devices, head_swap(): return lax.ppermute(value, 'head', [(0, 1), (1, 0)])  6.43 us
    ppermute x3, starting transfers between devices, head_swap(): return lax.ppermute(value, 'head', [(0, 1), (1, 0)])  4.61 us
    transpose x4, local copies, waits for them, and re-layouts, bit_major_rows(): return shaped.transpose(axes).reshape(rows, width)  4.09 us
    add x16, other arithmetic, halving_sum(): partial = keep + got.astype(jnp.float32)  3.55 us
  transfers between devices with their start and end apart: 31, of which 16 were waited for; matrix products, arithmetic and copies ran while one was open for 20% of the time, Pallas kernels for 0%

profile of v5, /device:TPU:0, one launch (start us, length us, event | category | flops | bytes accessed | tf_op | source)
XLA Modules:
  0.0 134.6 jit_solution(6654713247520772131)
XLA Ops:
  6.1 2.5 %collective-permute-start.1 = (bf16[1,128,1024]{2,1,0:T(8,128)(2,1)}, bf16[1,128,1024]{2,1,0:T(8,128)(2,1)}, u32[]{:S(2)}, u32[]{:S(2)}) collective-permute-start(bf16[1,128,1024]{2,1,0:T(8,128)(2,1)} %pad_maximum_fusion.refs_0_.refs_5_), channel_id=1, source_target_pairs={{0,4},{2,6},{4,0},{6,2},{8,12},{10,14},{12,8},{14,10},{16,20},{18,... | collective-permute-start | bytes 786440 | tf_op jit(solution)/shard_map/ppermute | solution.py:19
  10.2 2.6 %collective-permute-start.3 = (bf16[1,128,1024]{2,1,0:T(8,128)(2,1)}, bf16[1,128,1024]{2,1,0:T(8,128)(2,1)}, u32[]{:S(2)}, u32[]{:S(2)}) collective-permute-start(bf16[1,128,1024]{2,1,0:T(8,128)(2,1)} %pad_maximum_fusion.refs_0_.refs_5_), channel_id=1, source_target_pairs={{0,16},{2,18},{4,20},{6,22},{8,24},{10,26},{12,28},{14,30},{16,0},... | collective-permute-start | bytes 786440 | tf_op jit(solution)/shard_map/ppermute | solution.py:19
  15.3 1.8 %copy.19 = bf16[128,1024]{0,1:T(8,128)(2,1)} copy(bf16[128,1024]{1,0:T(8,128)(2,1)} %param.15) | data formatting | bytes 524288 | tf_op args[7]
  17.1 1.7 %copy.20 = bf16[128,2,2,2,2,64]{0,5,4,3,2,1:T(8,128)(2,1)} copy(bf16[128,2,2,2,2,64]{0,5,1,2,3,4:T(8,128)(2,1)} %bitcast.70) | data formatting | bytes 524288 | tf_op jit(solution)/shard_map/transpose | solution.py:28
  18.8 1.7 %copy.23 = bf16[128,2,2,2,2,64]{0,5,4,3,2,1:T(8,128)(2,1)} copy(bf16[128,2,2,2,2,64]{0,5,1,3,2,4:T(8,128)(2,1)} %bitcast.71) | data formatting | bytes 524288 | tf_op jit(solution)/shard_map/transpose | solution.py:28
  21.1 2.1 %fusion.3.g_ref = bf16[1,128,512]{2,1,0:T(8,128)(2,1)} fusion(bf16[128,1024]{1,0:T(8,128)(2,1)} %param.15, bf16[512,1024]{1,0:T(8,128)(2,1)S(1)} %copy-done), kind=kOutput, calls=%fused_computation.26 | convolution fusion | flops 134283264 | bytes 1441792 | tf_op jit(solution)/shard_map/dot_general | solution.py:213
  23.2 2.1 %collective-permute-done.3.refs_4_.refs_9_ = bf16[1,128,1024]{2,1,0:T(8,128)(2,1)} collective-permute-done((bf16[1,128,1024]{2,1,0:T(8,128)(2,1)}, bf16[1,128,1024]{2,1,0:T(8,128)(2,1)}, u32[]{:S(2)}, u32[]{:S(2)}) %collective-permute-start.3) | collective-permute-done | bytes 262176 | tf_op jit(solution)/shard_map/ppermute | solution.py:19
  25.2 14.5 %shard_map.135 = (bf16[1,128,512]{2,1,0:T(8,128)(2,1)}, bf16[1,128,512]{2,1,0:T(8,128)(2,1)}, bf16[1,128,1024]{2,1,0:T(8,128)(2,1)}, bf16[1,128,1024]{2,1,0:T(8,...) custom-call(s32[5]{0:T(128)} %add_bitcast_fusion.active_ref, ...), custom_call_target="tpu_custom_call" | custom-call | tf_op jit(solution)/shard_map/pallas_call | solution.py:171
  40.8 2.6 %collective-permute-start.8 = (bf16[1,128,1024]{2,1,0:T(8,128)(2,1)}, bf16[1,128,1024]{2,1,0:T(8,128)(2,1)S(1)}, u32[]{:S(2)}, u32[]{:S(2)}) collective-permute-start(bf16[1,128,1024]{2,1,0:T(8,128)(2,1)} %get-tuple-element.20), channel_id=1, source_target_pairs={{0,16},{2,18},{4,20},{6,22},{8,24},{10,26},{12,28},{14,30},{16,0},... | collective-permute-start | bytes 786440 | tf_op jit(solution)/shard_map/ppermute | solution.py:19
  50.2 4.1 %collective-permute-done.7 = bf16[1,128,1024]{2,1,0:T(8,128)(2,1)S(1)} collective-permute-done((bf16[1,128,1024]{2,1,0:T(8,128)(2,1)}, bf16[1,128,1024]{2,1,0:T(8,128)(2,1)S(1)}, u32[]{:S(2)}, u32[]{:S(2)}) %collective-permute-start.7) | collective-permute-done | bytes 262176 | tf_op jit(solution)/shard_map/ppermute | solution.py:19
  62.0 6.2 %collective-permute-done.9 = bf16[128,1024]{1,0:T(8,128)(2,1)S(1)} collective-permute-done((bf16[128,1024]{1,0:T(8,128)(2,1)S(1)}, bf16[128,1024]{1,0:T(8,128)(2,1)S(1)}, u32[]{:S(2)}, u32[]{:S(2)}) %collective-permute-start.9) | collective-permute-done | bytes 262176 | tf_op jit(solution)/shard_map/ppermute | solution.py:83
  75.2 2.8 %collective-permute-done.12 = f32[1024]{0:T(1024)S(1)} collective-permute-done((f32[1024]{0:T(1024)S(1)}, f32[1024]{0:T(1024)S(1)}, u32[]{:S(2)}, u32[]{:S(2)}) %collective-permute-start.12) | collective-permute-done | bytes 4128 | tf_op jit(solution)/shard_map/ppermute | solution.py:19
  78.3 4.8 %collective-permute-done.13 = f32[1024]{0:T(1024)S(1)} collective-permute-done((f32[1024]{0:T(1024)S(1)}, f32[1024]{0:T(1024)S(1)}, u32[]{:S(2)}, u32[]{:S(2)}) %collective-permute-start.13) | collective-permute-done | bytes 4128 | tf_op jit(solution)/shard_map/ppermute | solution.py:19
  85.1 2.5 %collective-permute-done.14 = f32[1024]{0:T(1024)S(1)} collective-permute-done((f32[1024]{0:T(1024)S(1)}, f32[1024]{0:T(1024)S(1)}, u32[]{:S(2)}, u32[]{:S(2)}) %collective-permute-start.14) | collective-permute-done | bytes 4128 | tf_op jit(solution)/shard_map/ppermute | solution.py:19
  90.9 1.8 %collective-permute-start.17 = (bf16[128,512]{0,1:T(8,128)(2,1)S(1)}, bf16[128,512]{0,1:T(8,128)(2,1)S(1)}, u32[]{:S(2)}, u32[]{:S(2)}) collective-permute-start(bf16[128,512]{0,1:T(8,128)(2,1)S(1)} %dynamic-slice_convert_fusion.11), channel_id=1, source_target_pairs={{0,8},{2,10},{4,12},{6,14},{8,0},{10,2},{12,4},{14,6},{16,24},{18,... | collective-permute-start | bytes 393224 | tf_op jit(solution)/shard_map/ppermute | solution.py:19
  92.9 1.6 %collective-permute-start.21 = (bf16[128,512]{0,1:T(8,128)(2,1)S(1)}, bf16[128,512]{0,1:T(8,128)(2,1)S(1)}, u32[]{:S(2)}, u32[]{:S(2)}) collective-permute-start(bf16[128,512]{0,1:T(8,128)(2,1)S(1)} %dynamic-slice_convert_fusion.9), channel_id=1, source_target_pairs={{0,4},{2,6},{4,0},{6,2},{8,12},{10,14},{12,8},{14,10},{16,20},{18,... | collective-permute-start | bytes 393224 | tf_op jit(solution)/shard_map/ppermute | solution.py:19
  94.5 4.9 %collective-permute-done.17 = bf16[128,512]{0,1:T(8,128)(2,1)S(1)} collective-permute-done((bf16[128,512]{0,1:T(8,128)(2,1)S(1)}, bf16[128,512]{0,1:T(8,128)(2,1)S(1)}, u32[]{:S(2)}, u32[]{:S(2)}) %collective-permute-start.17) | collective-permute-done | bytes 131104 | tf_op jit(solution)/shard_map/ppermute | solution.py:19
  99.5 2.1 %collective-permute-start.18 = (bf16[64,512]{0,1:T(8,128)(2,1)S(1)}, bf16[64,512]{0,1:T(8,128)(2,1)S(1)}, u32[]{:S(2)}, u32[]{:S(2)}) collective-permute-start(bf16[64,512]{0,1:T(8,128)(2,1)S(1)} %dynamic-slice_convert_fusion.10), channel_id=1, source_target_pairs={{0,16},{2,18},{4,20},{6,22},{8,24},{10,26},{12,28},{14,30},{16,0},... | collective-permute-start | bytes 196616 | tf_op jit(solution)/shard_map/ppermute | solution.py:19
  102.7 6.7 %collective-permute-done.18 = bf16[64,512]{0,1:T(8,128)(2,1)S(1)} collective-permute-done((bf16[64,512]{0,1:T(8,128)(2,1)S(1)}, bf16[64,512]{0,1:T(8,128)(2,1)S(1)}, u32[]{:S(2)}, u32[]{:S(2)}) %collective-permute-start.18) | collective-permute-done | bytes 65568 | tf_op jit(solution)/shard_map/ppermute | solution.py:19
  111.9 1.7 %copy.25 = f32[64,512]{1,0:T(8,128)} copy(f32[64,512]{0,1:T(8,128)} %get-tuple-element.47) | data formatting | bytes 262144
  116.6 1.6 %collective-permute-start.29 = (bf16[128,512]{0,1:T(8,128)(2,1)S(1)}, bf16[128,512]{0,1:T(8,128)(2,1)S(1)}, u32[]{:S(2)}, u32[]{:S(2)}) collective-permute-start(bf16[128,512]{0,1:T(8,128)(2,1)S(1)} %dynamic-slice_convert_fusion.5), channel_id=1, source_target_pairs={{0,4},{2,6},{4,0},{6,2},{8,12},{10,14},{12,8},{14,10},{16,20},{18,... | collective-permute-start | bytes 393224 | tf_op jit(solution)/shard_map/ppermute | solution.py:19
  118.2 2.3 %collective-permute-done.25 = bf16[128,512]{0,1:T(8,128)(2,1)S(1)} collective-permute-done((bf16[128,512]{0,1:T(8,128)(2,1)S(1)}, bf16[128,512]{0,1:T(8,128)(2,1)S(1)}, u32[]{:S(2)}, u32[]{:S(2)}) %collective-permute-start.25) | collective-permute-done | bytes 131104 | tf_op jit(solution)/shard_map/ppermute | solution.py:19
  121.8 3.0 %collective-permute-start.30 = (bf16[64,512]{0,1:T(8,128)(2,1)S(1)}, bf16[64,512]{0,1:T(8,128)(2,1)S(1)}, u32[]{:S(2)}, u32[]{:S(2)}) collective-permute-start(bf16[64,512]{0,1:T(8,128)(2,1)S(1)} %dynamic-slice_convert_fusion.4), channel_id=1, source_target_pairs={{0,16},{2,18},{4,20},{6,22},{8,24},{10,26},{12,28},{14,30},{16,0},... | collective-permute-start | bytes 196616 | tf_op jit(solution)/shard_map/ppermute | solution.py:19
  124.8 6.6 %collective-permute-done.26 = bf16[64,512]{0,1:T(8,128)(2,1)S(1)} collective-permute-done((bf16[64,512]{0,1:T(8,128)(2,1)S(1)}, bf16[64,512]{0,1:T(8,128)(2,1)S(1)}, u32[]{:S(2)}, u32[]{:S(2)}) %collective-permute-start.26) | collective-permute-done | bytes 65568 | tf_op jit(solution)/shard_map/ppermute | solution.py:19
  (147 shorter events, 49.3 us)
Async XLA Ops:
  5.6 17.5 %collective-permute-start = (bf16[1,128,1024]{2,1,0:T(8,128)(2,1)}, bf16[1,128,1024]{2,1,0:T(8,128)(2,1)}, u32[]{:S(2)}, u32[]{:S(2)}) collective-permute-start(bf16[1,128,1024]{2,1,0:T(8,128)(2,1)} %pad_maximum_fusion.refs_0_.refs_5_), channel_id=1, source_target_pairs={{0,2},{2,0},{4,6},{6,4},{8,10},{10,8},{12,14},{14,12},{16,18},{18,... | collective-permute-start | bytes 786440 | tf_op jit(solution)/shard_map/ppermute | solution.py:19
  6.1 17.1 %collective-permute-start.1 = (bf16[1,128,1024]{2,1,0:T(8,128)(2,1)}, bf16[1,128,1024]{2,1,0:T(8,128)(2,1)}, u32[]{:S(2)}, u32[]{:S(2)}) collective-permute-start(bf16[1,128,1024]{2,1,0:T(8,128)(2,1)} %pad_maximum_fusion.refs_0_.refs_5_), channel_id=1, source_target_pairs={{0,4},{2,6},{4,0},{6,2},{8,12},{10,14},{12,8},{14,10},{16,20},{18,... | collective-permute-start | bytes 786440 | tf_op jit(solution)/shard_map/ppermute | solution.py:19
  8.6 14.6 %collective-permute-start.2 = (bf16[1,128,1024]{2,1,0:T(8,128)(2,1)}, bf16[1,128,1024]{2,1,0:T(8,128)(2,1)}, u32[]{:S(2)}, u32[]{:S(2)}) collective-permute-start(bf16[1,128,1024]{2,1,0:T(8,128)(2,1)} %pad_maximum_fusion.refs_0_.refs_5_), channel_id=1, source_target_pairs={{0,8},{2,10},{4,12},{6,14},{8,0},{10,2},{12,4},{14,6},{16,24},{18,... | collective-permute-start | bytes 786440 | tf_op jit(solution)/shard_map/ppermute | solution.py:19
  10.2 15.1 %collective-permute-start.3 = (bf16[1,128,1024]{2,1,0:T(8,128)(2,1)}, bf16[1,128,1024]{2,1,0:T(8,128)(2,1)}, u32[]{:S(2)}, u32[]{:S(2)}) collective-permute-start(bf16[1,128,1024]{2,1,0:T(8,128)(2,1)} %pad_maximum_fusion.refs_0_.refs_5_), channel_id=1, source_target_pairs={{0,16},{2,18},{4,20},{6,22},{8,24},{10,26},{12,28},{14,30},{16,0},... | collective-permute-start | bytes 786440 | tf_op jit(solution)/shard_map/ppermute | solution.py:19
  39.7 7.7 %collective-permute-start.5 = (bf16[1,128,1024]{2,1,0:T(8,128)(2,1)}, bf16[1,128,1024]{2,1,0:T(8,128)(2,1)S(1)}, u32[]{:S(2)}, u32[]{:S(2)}) collective-permute-start(bf16[1,128,1024]{2,1,0:T(8,128)(2,1)} %get-tuple-element.17), channel_id=1, source_target_pairs={{0,2},{2,0},{4,6},{6,4},{8,10},{10,8},{12,14},{14,12},{16,18},{18,... | collective-permute-start | bytes 786440 | tf_op jit(solution)/shard_map/ppermute | solution.py:19
  39.8 8.9 %collective-permute-start.6 = (bf16[1,128,1024]{2,1,0:T(8,128)(2,1)}, bf16[1,128,1024]{2,1,0:T(8,128)(2,1)S(1)}, u32[]{:S(2)}, u32[]{:S(2)}) collective-permute-start(bf16[1,128,1024]{2,1,0:T(8,128)(2,1)} %get-tuple-element.18), channel_id=1, source_target_pairs={{0,4},{2,6},{4,0},{6,2},{8,12},{10,14},{12,8},{14,10},{16,20},{18,... | collective-permute-start | bytes 786440 | tf_op jit(solution)/shard_map/ppermute | solution.py:19
  40.4 13.9 %collective-permute-start.7 = (bf16[1,128,1024]{2,1,0:T(8,128)(2,1)}, bf16[1,128,1024]{2,1,0:T(8,128)(2,1)S(1)}, u32[]{:S(2)}, u32[]{:S(2)}) collective-permute-start(bf16[1,128,1024]{2,1,0:T(8,128)(2,1)} %get-tuple-element.19), channel_id=1, source_target_pairs={{0,8},{2,10},{4,12},{6,14},{8,0},{10,2},{12,4},{14,6},{16,24},{18,... | collective-permute-start | bytes 786440 | tf_op jit(solution)/shard_map/ppermute | solution.py:19
  40.8 14.9 %collective-permute-start.8 = (bf16[1,128,1024]{2,1,0:T(8,128)(2,1)}, bf16[1,128,1024]{2,1,0:T(8,128)(2,1)S(1)}, u32[]{:S(2)}, u32[]{:S(2)}) collective-permute-start(bf16[1,128,1024]{2,1,0:T(8,128)(2,1)} %get-tuple-element.20), channel_id=1, source_target_pairs={{0,16},{2,18},{4,20},{6,22},{8,24},{10,26},{12,28},{14,30},{16,0},... | collective-permute-start | bytes 786440 | tf_op jit(solution)/shard_map/ppermute | solution.py:19
  46.0 23.9 %collective-permute-start.15 = (bf16[512,512]{0,1:T(8,128)(2,1)S(1)}, bf16[512,512]{0,1:T(8,128)(2,1)S(1)}, u32[]{:S(2)}, u32[]{:S(2)}) collective-permute-start(bf16[512,512]{0,1:T(8,128)(2,1)S(1)} %fusion.19), channel_id=1, source_target_pairs={{0,2},{2,0},{4,6},{6,4},{8,10},{10,8},{12,14},{14,12},{16,18},{18,... | collective-permute-start | bytes 1572872 | tf_op jit(solution)/shard_map/ppermute | solution.py:19
  47.4 24.7 %collective-permute-start.19 = (bf16[512,512]{0,1:T(8,128)(2,1)S(1)}, bf16[512,512]{0,1:T(8,128)(2,1)S(1)}, u32[]{:S(2)}, u32[]{:S(2)}) collective-permute-start(bf16[512,512]{0,1:T(8,128)(2,1)S(1)} %fusion.15), channel_id=1, source_target_pairs={{0,2},{2,0},{4,6},{6,4},{8,10},{10,8},{12,14},{14,12},{16,18},{18,... | collective-permute-start | bytes 1572872 | tf_op jit(solution)/shard_map/ppermute | solution.py:19
  48.7 12.3 %collective-permute-start.4 = (f32[128,512]{1,0:T(8,128)S(1)}, f32[128,512]{1,0:T(8,128)S(1)}, u32[]{:S(2)}, u32[]{:S(2)}) collective-permute-start(f32[128,512]{1,0:T(8,128)S(1)} %constant_dynamic-slice_fusion), channel_id=1, source_target_pairs={{0,1},{1,0},{2,3},{3,2},{4,5},{5,4},{6,7},{7,6},{8,9},{9,8},{10,11... | collective-permute-start | bytes 786440 | tf_op jit(solution)/shard_map/ppermute | solution.py:83
  58.8 29.4 %collective-permute-start.23 = (bf16[512,512]{0,1:T(8,128)(2,1)S(1)}, bf16[512,512]{0,1:T(8,128)(2,1)S(1)}, u32[]{:S(2)}, u32[]{:S(2)}) collective-permute-start(bf16[512,512]{0,1:T(8,128)(2,1)S(1)} %fusion.11), channel_id=1, source_target_pairs={{0,2},{2,0},{4,6},{6,4},{8,10},{10,8},{12,14},{14,12},{16,18},{18,... | collective-permute-start | bytes 1572872 | tf_op jit(solution)/shard_map/ppermute | solution.py:19
  59.4 8.8 %collective-permute-start.9 = (bf16[128,1024]{1,0:T(8,128)(2,1)S(1)}, bf16[128,1024]{1,0:T(8,128)(2,1)S(1)}, u32[]{:S(2)}, u32[]{:S(2)}) collective-permute-start(bf16[128,1024]{1,0:T(8,128)(2,1)S(1)} %fusion.1), channel_id=1, source_target_pairs={{0,1},{1,0},{2,3},{3,2},{4,5},{5,4},{6,7},{7,6},{8,9},{9,8},{10,11... | collective-permute-start | bytes 786440 | tf_op jit(solution)/shard_map/ppermute | solution.py:83
  61.0 28.6 %collective-permute-start.27 = (bf16[512,512]{0,1:T(8,128)(2,1)S(1)}, bf16[512,512]{0,1:T(8,128)(2,1)S(1)}, u32[]{:S(2)}, u32[]{:S(2)}) collective-permute-start(bf16[512,512]{0,1:T(8,128)(2,1)S(1)} %fusion.7), channel_id=1, source_target_pairs={{0,2},{2,0},{4,6},{6,4},{8,10},{10,8},{12,14},{14,12},{16,18},{18,... | collective-permute-start | bytes 1572872 | tf_op jit(solution)/shard_map/ppermute | solution.py:19
  70.2 20.6 %collective-permute-start.16 = (bf16[256,512]{0,1:T(8,128)(2,1)S(1)}, bf16[256,512]{0,1:T(8,128)(2,1)S(1)}, u32[]{:S(2)}, u32[]{:S(2)}) collective-permute-start(bf16[256,512]{0,1:T(8,128)(2,1)S(1)} %dynamic-slice_convert_fusion.3), channel_id=1, source_target_pairs={{0,4},{2,6},{4,0},{6,2},{8,12},{10,14},{12,8},{14,10},{16,20},{18,... | collective-permute-start | bytes 786440 | tf_op jit(solution)/shard_map/ppermute | solution.py:19
  74.8 17.9 %collective-permute-start.20 = (bf16[256,512]{0,1:T(8,128)(2,1)S(1)}, bf16[256,512]{0,1:T(8,128)(2,1)S(1)}, u32[]{:S(2)}, u32[]{:S(2)}) collective-permute-start(bf16[256,512]{0,1:T(8,128)(2,1)S(1)} %dynamic-slice_convert_fusion.2), channel_id=1, source_target_pairs={{0,8},{2,10},{4,12},{6,14},{8,0},{10,2},{12,4},{14,6},{16,24},{18,... | collective-permute-start | bytes 786440 | tf_op jit(solution)/shard_map/ppermute | solution.py:19
  89.1 25.3 %collective-permute-start.24 = (bf16[256,512]{0,1:T(8,128)(2,1)}, bf16[256,512]{0,1:T(8,128)(2,1)}, u32[]{:S(2)}, u32[]{:S(2)}) collective-permute-start(bf16[256,512]{0,1:T(8,128)(2,1)} %dynamic-slice_convert_fusion.1), channel_id=1, source_target_pairs={{0,4},{2,6},{4,0},{6,2},{8,12},{10,14},{12,8},{14,10},{16,20},{18,... | collective-permute-start | bytes 786440 | tf_op jit(solution)/shard_map/ppermute | solution.py:19
  90.5 25.0 %collective-permute-start.28 = (bf16[256,512]{0,1:T(8,128)(2,1)}, bf16[256,512]{0,1:T(8,128)(2,1)}, u32[]{:S(2)}, u32[]{:S(2)}) collective-permute-start(bf16[256,512]{0,1:T(8,128)(2,1)} %dynamic-slice_convert_fusion), channel_id=1, source_target_pairs={{0,8},{2,10},{4,12},{6,14},{8,0},{10,2},{12,4},{14,6},{16,24},{18,... | collective-permute-start | bytes 786440 | tf_op jit(solution)/shard_map/ppermute | solution.py:19
  90.9 8.4 %collective-permute-start.17 = (bf16[128,512]{0,1:T(8,128)(2,1)S(1)}, bf16[128,512]{0,1:T(8,128)(2,1)S(1)}, u32[]{:S(2)}, u32[]{:S(2)}) collective-permute-start(bf16[128,512]{0,1:T(8,128)(2,1)S(1)} %dynamic-slice_convert_fusion.11), channel_id=1, source_target_pairs={{0,8},{2,10},{4,12},{6,14},{8,0},{10,2},{12,4},{14,6},{16,24},{18,... | collective-permute-start | bytes 393224 | tf_op jit(solution)/shard_map/ppermute | solution.py:19
  92.9 8.8 %collective-permute-start.21 = (bf16[128,512]{0,1:T(8,128)(2,1)S(1)}, bf16[128,512]{0,1:T(8,128)(2,1)S(1)}, u32[]{:S(2)}, u32[]{:S(2)}) collective-permute-start(bf16[128,512]{0,1:T(8,128)(2,1)S(1)} %dynamic-slice_convert_fusion.9), channel_id=1, source_target_pairs={{0,4},{2,6},{4,0},{6,2},{8,12},{10,14},{12,8},{14,10},{16,20},{18,... | collective-permute-start | bytes 393224 | tf_op jit(solution)/shard_map/ppermute | solution.py:19
  99.5 9.9 %collective-permute-start.18 = (bf16[64,512]{0,1:T(8,128)(2,1)S(1)}, bf16[64,512]{0,1:T(8,128)(2,1)S(1)}, u32[]{:S(2)}, u32[]{:S(2)}) collective-permute-start(bf16[64,512]{0,1:T(8,128)(2,1)S(1)} %dynamic-slice_convert_fusion.10), channel_id=1, source_target_pairs={{0,16},{2,18},{4,20},{6,22},{8,24},{10,26},{12,28},{14,30},{16,0},... | collective-permute-start | bytes 196616 | tf_op jit(solution)/shard_map/ppermute | solution.py:19
  101.8 9.2 %collective-permute-start.22 = (bf16[64,512]{0,1:T(8,128)(2,1)S(1)}, bf16[64,512]{0,1:T(8,128)(2,1)S(1)}, u32[]{:S(2)}, u32[]{:S(2)}) collective-permute-start(bf16[64,512]{0,1:T(8,128)(2,1)S(1)} %dynamic-slice_convert_fusion.8), channel_id=1, source_target_pairs={{0,16},{2,18},{4,20},{6,22},{8,24},{10,26},{12,28},{14,30},{16,0},... | collective-permute-start | bytes 196616 | tf_op jit(solution)/shard_map/ppermute | solution.py:19
  120.6 10.7 %collective-permute-start.26 = (bf16[64,512]{0,1:T(8,128)(2,1)S(1)}, bf16[64,512]{0,1:T(8,128)(2,1)S(1)}, u32[]{:S(2)}, u32[]{:S(2)}) collective-permute-start(bf16[64,512]{0,1:T(8,128)(2,1)S(1)} %dynamic-slice_convert_fusion.6), channel_id=1, source_target_pairs={{0,16},{2,18},{4,20},{6,22},{8,24},{10,26},{12,28},{14,30},{16,0},... | collective-permute-start | bytes 196616 | tf_op jit(solution)/shard_map/ppermute | solution.py:19
  121.8 11.1 %collective-permute-start.30 = (bf16[64,512]{0,1:T(8,128)(2,1)S(1)}, bf16[64,512]{0,1:T(8,128)(2,1)S(1)}, u32[]{:S(2)}, u32[]{:S(2)}) collective-permute-start(bf16[64,512]{0,1:T(8,128)(2,1)S(1)} %dynamic-slice_convert_fusion.4), channel_id=1, source_target_pairs={{0,16},{2,18},{4,20},{6,22},{8,24},{10,26},{12,28},{14,30},{16,0},... | collective-permute-start | bytes 196616 | tf_op jit(solution)/shard_map/ppermute | solution.py:19
  (21 other events, 107.5 us)

commit v6 on v5

--- a/solution.py
+++ b/solution.py
@@ -28,16 +28,36 @@
     return shaped.transpose(axes).reshape(rows, width)
 
 
-def halving_sum(partial, axis, order):
+def as_pairs(vector):
+    high = vector.astype(jnp.bfloat16)
+    low = (vector - high.astype(jnp.float32)).astype(jnp.bfloat16)
+    return high, low
+
+
+def from_pairs(high, low):
+    return high.astype(jnp.float32) + low.astype(jnp.float32)
+
+
+def halving_sum(partial, axis, order, extra=None):
     me = lax.axis_index(axis)
+    width = partial.shape[1]
     for bit in order:
         half = partial.shape[0] // 2
         mine = (me >> bit) & 1
         keep = lax.dynamic_slice_in_dim(partial, mine * half, half, 0)
         send = lax.dynamic_slice_in_dim(partial, (1 - mine) * half, half, 0)
-        got = from_partner(send.astype(jnp.bfloat16), axis, bit)
+        send = send.astype(jnp.bfloat16)
+        if extra is not None:
+            high, low = as_pairs(extra)
+            code = jnp.concatenate([high, low]).reshape(-1, width)
+            send = jnp.concatenate([send, code], axis=0)
+        got = from_partner(send, axis, bit)
+        if extra is not None:
+            code = got[half:].reshape(2, -1)
+            extra = from_pairs(high, low) + from_pairs(code[0], code[1])
+            got = got[:half]
         partial = keep + got.astype(jnp.float32)
-    return partial
+    return partial, extra
 
 
 def split_orders(levels):
@@ -47,7 +67,7 @@
     return first, (0, 2, 1) + first[3:]
 
 
-def scatter_rows(pairs, axis, levels):
+def scatter_rows(pairs, axis, levels, extra):
     contract = (((0,), (0,)), ((), ()))
     chunks = []
     for index, order in enumerate(split_orders(levels)):
@@ -61,7 +81,12 @@
                     preferred_element_type=jnp.float32,
                 )
             )
-        chunks.append(halving_sum(jnp.concatenate(pieces, axis=1), axis, order))
+        chunk, summed = halving_sum(
+            jnp.concatenate(pieces, axis=1), axis, order, extra if index == 0 else None
+        )
+        chunks.append(chunk)
+        if index == 0:
+            extra = summed
     results = []
     offset = 0
     for left, right in pairs:
@@ -70,7 +95,7 @@
             jnp.concatenate([chunk[:, offset : offset + cut] for chunk in chunks], axis=1)
         )
         offset += cut
-    return results
+    return results, extra
 
 
 def doubling_sum(value, axis, levels):
@@ -238,22 +263,20 @@
         grad_value = grad_value + returned[bit][1].astype(jnp.float32)
     grad_key = grad_key.astype(jnp.bfloat16).reshape(node_rows, columns)
     grad_value = grad_value.astype(jnp.bfloat16).reshape(node_rows, columns)
-    w_out_rows, w_query_grad = scatter_rows(
-        [(cotangent, attended), (normed, grad_query)], "graph", graph_levels
-    )
-    w_out_grad = w_out_rows.T
-    w_key_grad, w_value_grad = scatter_rows(
-        [(normed, grad_key), (normed, grad_value)], "graph", graph_levels
-    )
     feature_terms = (
         jnp.dot(grad_query, w_query.T, preferred_element_type=jnp.float32)
         + jnp.dot(grad_key, w_key.T, preferred_element_type=jnp.float32)
         + jnp.dot(grad_value, w_value.T, preferred_element_type=jnp.float32)
     )
     low_terms = feature_terms.astype(jnp.bfloat16)
+    gain_terms = jnp.sum(low_terms.astype(jnp.float32) * wide_nodes * inverse, axis=0)
+    (w_out_rows, w_query_grad, w_key_grad, w_value_grad), gain_part = scatter_rows(
+        [(cotangent, attended), (normed, grad_query), (normed, grad_key), (normed, grad_value)],
+        "graph", graph_levels, gain_terms,
+    )
+    w_out_grad = w_out_rows.T
+    gain_grad = gain_part + head_swap(gain_part)
     grad_normed = low_terms.astype(jnp.float32) + head_swap(low_terms).astype(jnp.float32)
-    gain_terms = jnp.sum(low_terms.astype(jnp.float32) * wide_nodes * inverse, axis=0)
-    gain_grad = doubling_sum(gain_terms + head_swap(gain_terms), "graph", graph_levels)
     scaled = grad_normed * gain
     nodes_grad = (
         inverse

time: 135 us -> 162 us (1.20)
  local copies, waits for them, and re-layouts: 14.7 us -> 33.4 us
  other arithmetic: 10.9 us -> 25.5 us
  starting transfers between devices: 33.7 us -> 22 us
  waiting for transfers between devices: 49.4 us -> 51.6 us
  matrix products: 10.2 us -> 12.2 us
    ppermute x28 -> x16, starting transfers between devices: 29.1 us -> 17.4 us  [from_partner(): return lax.ppermute(value, axis, pairs)]
    add x16 -> x7, other arithmetic: 3.55 us -> 10.7 us  [halving_sum(): partial = keep + got.astype(jnp.float32)]
    unnamed x33 -> x67, local copies, waits for them, and re-layouts: 7.55 us -> 14.1 us
    ppermute x3, waiting for transfers between devices: 6.43 us -> 11.6 us  [head_swap(): return lax.ppermute(value, 'head', [(0, 1), (1, 0)])]
    concatenate x0 -> x10, other arithmetic: none -> 4.68 us  [the longest x4 3.52 us: halving_sum(): send = jnp.concatenate([send, code], axis=0)]
    convert_element_type x12 -> x8, local copies, waits for them, and re-layouts: 2.12 us -> 6.36 us  [halving_sum(): send = send.astype(jnp.bfloat16)]
    concatenate x0 -> x2, local copies, waits for them, and re-layouts: none -> 3.62 us  [halving_sum(): send = jnp.concatenate([send, code], axis=0)]
    ppermute x28 -> x16, waiting for transfers between devices: 43 us -> 40 us  [from_partner(): return lax.ppermute(value, axis, pairs)]
  transfers between devices with their start and end apart: 31 -> 19, of which waited for: 16 -> 10; matrix products, arithmetic and copies ran while one was open for 20% -> 34% of each run, Pallas kernels for 0% -> 0%
where the time goes in v6:
time: 162 us; the launch traced here: 161 us
  waiting for transfers between devices  51.6 us (32%)
  local copies, waits for them, and re-layouts  33.4 us (21%)
  other arithmetic  25.5 us (16%)
  starting transfers between devices  22 us (14%)
  Pallas kernels  14.5 us (9%)
  matrix products  12.2 us (8%)
    ppermute x16, waiting for transfers between devices, from_partner(): return lax.ppermute(value, axis, pairs)  40 us
    ppermute x16, starting transfers between devices, from_partner(): return lax.ppermute(value, axis, pairs)  17.4 us
    pallas_call x1, Pallas kernels, block_attention(): pl.pallas_call(functools.partial(attention_kernel, slots, pairs), grid_sp...  14.5 us
    unnamed x67, local copies, waits for them, and re-layouts  14.1 us
    ppermute x3, waiting for transfers between devices, head_swap(): return lax.ppermute(value, 'head', [(0, 1), (1, 0)])  11.6 us
    add x7, other arithmetic, halving_sum(): partial = keep + got.astype(jnp.float32)  10.7 us
    convert_element_type x8, local copies, waits for them, and re-layouts, halving_sum(): send = send.astype(jnp.bfloat16)  6.36 us
    transpose x4, local copies, waits for them, and re-layouts, bit_major_rows(): return shaped.transpose(axes).reshape(rows, width)  6 us
  transfers between devices with their start and end apart: 19, of which 10 were waited for; matrix products, arithmetic and copies ran while one was open for 34% of the time, Pallas kernels for 0%

profile of v6, /device:TPU:0, one launch (start us, length us, event | category | flops | bytes accessed | tf_op | source)
XLA Modules:
  0.0 160.5 jit_solution(4142159324506613985)
XLA Ops:
  6.1 2.5 %collective-permute-start.1 = (bf16[1,128,1024]{2,1,0:T(8,128)(2,1)}, bf16[1,128,1024]{2,1,0:T(8,128)(2,1)}, u32[]{:S(2)}, u32[]{:S(2)}) collective-permute-start(bf16[1,128,1024]{2,1,0:T(8,128)(2,1)} %pad_maximum_fusion.5.refs_0_.refs_5_), channel_id=1, source_target_pairs={{0,4},{2,6},{4,0},{6,2},{8,12},{10,14},{12,8},{14,10},{16,20},{18,... | collective-permute-start | bytes 786440 | tf_op jit(solution)/shard_map/ppermute | solution.py:19
  10.2 2.6 %collective-permute-start.3 = (bf16[1,128,1024]{2,1,0:T(8,128)(2,1)}, bf16[1,128,1024]{2,1,0:T(8,128)(2,1)}, u32[]{:S(2)}, u32[]{:S(2)}) collective-permute-start(bf16[1,128,1024]{2,1,0:T(8,128)(2,1)} %pad_maximum_fusion.5.refs_0_.refs_5_), channel_id=1, source_target_pairs={{0,16},{2,18},{4,20},{6,22},{8,24},{10,26},{12,28},{14,30},{16,0},... | collective-permute-start | bytes 786440 | tf_op jit(solution)/shard_map/ppermute | solution.py:19
  15.5 1.8 %copy.33 = bf16[128,1024]{0,1:T(8,128)(2,1)} copy(bf16[128,1024]{1,0:T(8,128)(2,1)} %param.15) | data formatting | bytes 524288 | tf_op args[7]
  17.3 1.7 %copy.45 = bf16[128,2,2,2,2,64]{0,5,4,3,2,1:T(8,128)(2,1)} copy(bf16[128,2,2,2,2,64]{0,5,1,3,2,4:T(8,128)(2,1)} %bitcast.72) | data formatting | bytes 524288 | tf_op jit(solution)/shard_map/transpose | solution.py:28
  19.0 1.7 %copy.36 = bf16[128,2,2,2,2,64]{0,5,4,3,2,1:T(8,128)(2,1)} copy(bf16[128,2,2,2,2,64]{0,5,1,2,3,4:T(8,128)(2,1)} %bitcast.71) | data formatting | bytes 524288 | tf_op jit(solution)/shard_map/transpose | solution.py:28
  20.7 1.7 %copy.34 = bf16[128,2,2,2,2,64]{0,5,4,3,2,1:T(8,128)(2,1)} copy(bf16[128,2,2,2,2,64]{0,5,1,2,3,4:T(8,128)(2,1)} %bitcast.73) | data formatting | bytes 524288 | tf_op jit(solution)/shard_map/transpose | solution.py:28
  22.9 2.1 %fusion.3.g_ref = bf16[1,128,512]{2,1,0:T(8,128)(2,1)} fusion(bf16[128,1024]{1,0:T(8,128)(2,1)} %param.15, bf16[512,1024]{1,0:T(8,128)(2,1)S(1)} %copy-done.7), kind=kOutput, calls=%fused_computation.17 | convolution fusion | flops 134283264 | bytes 1441792 | tf_op jit(solution)/shard_map/dot_general | solution.py:238
  25.2 14.5 %shard_map.135 = (bf16[1,128,512]{2,1,0:T(8,128)(2,1)}, bf16[1,128,512]{2,1,0:T(8,128)(2,1)}, bf16[1,128,1024]{2,1,0:T(8,128)(2,1)}, bf16[1,128,1024]{2,1,0:T(8,...) custom-call(s32[5]{0:T(128)} %add_bitcast_fusion.active_ref, ...), custom_call_target="tpu_custom_call" | custom-call | tf_op jit(solution)/shard_map/pallas_call | solution.py:196
  40.8 2.6 %collective-permute-start.8 = (bf16[1,128,1024]{2,1,0:T(8,128)(2,1)}, bf16[1,128,1024]{2,1,0:T(8,128)(2,1)S(1)}, u32[]{:S(2)}, u32[]{:S(2)}) collective-permute-start(bf16[1,128,1024]{2,1,0:T(8,128)(2,1)} %get-tuple-element.20), channel_id=1, source_target_pairs={{0,16},{2,18},{4,20},{6,22},{8,24},{10,26},{12,28},{14,30},{16,0},... | collective-permute-start | bytes 786440 | tf_op jit(solution)/shard_map/ppermute | solution.py:19
  46.5 2.2 %collective-permute-done.6 = bf16[1,128,1024]{2,1,0:T(8,128)(2,1)S(1)} collective-permute-done((bf16[1,128,1024]{2,1,0:T(8,128)(2,1)}, bf16[1,128,1024]{2,1,0:T(8,128)(2,1)S(1)}, u32[]{:S(2)}, u32[]{:S(2)}) %collective-permute-start.6) | collective-permute-done | bytes 262176 | tf_op jit(solution)/shard_map/ppermute | solution.py:19
  48.7 5.6 %collective-permute-done.7 = bf16[1,128,1024]{2,1,0:T(8,128)(2,1)S(1)} collective-permute-done((bf16[1,128,1024]{2,1,0:T(8,128)(2,1)}, bf16[1,128,1024]{2,1,0:T(8,128)(2,1)S(1)}, u32[]{:S(2)}, u32[]{:S(2)}) %collective-permute-start.7) | collective-permute-done | bytes 262176 | tf_op jit(solution)/shard_map/ppermute | solution.py:19
  65.1 4.3 %collective-permute-done.9 = bf16[128,1024]{1,0:T(8,128)(2,1)S(1)} collective-permute-done((bf16[128,1024]{1,0:T(8,128)(2,1)S(1)}, bf16[128,1024]{1,0:T(8,128)(2,1)S(1)}, u32[]{:S(2)}, u32[]{:S(2)}) %collective-permute-start.9) | collective-permute-done | bytes 262176 | tf_op jit(solution)/shard_map/ppermute | solution.py:108
  76.9 7.2 %collective-permute-done.4 = f32[128,512]{1,0:T(8,128)S(1)} collective-permute-done((f32[128,512]{1,0:T(8,128)S(1)}, f32[128,512]{1,0:T(8,128)S(1)}, u32[]{:S(2)}, u32[]{:S(2)}) %collective-permute-start.4) | collective-permute-done | bytes 262176 | tf_op jit(solution)/shard_map/ppermute | solution.py:108
  84.8 2.2 %convert_add_fusion = f32[512,1024]{0,1:T(8,128)S(1)} fusion(bf16[512,1024]{0,1:T(8,128)(2,1)} %collective-permute-done.15, f32[1024,1024]{0,1:T(8,128)} %copy-done.1, s32[]{:T(128)S(6)} %select_n.49), kind=kLoop, calls=%fused_computation.2 | loop fusion | flops 1048576 | bytes 5242884 | tf_op jit(solution)/shard_map/add | solution.py:59
  91.9 2.3 %convert_add_fusion.1 = f32[512,1024]{0,1:T(8,128)S(1)} fusion(bf16[512,1024]{0,1:T(8,128)(2,1)} %copy.51, f32[1024,1024]{0,1:T(8,128)} %copy-done.2, s32[]{:T(128)S(6)} %select_n.49), kind=kLoop, calls=%fused_computation.4 | loop fusion | flops 1048576 | bytes 5242884 | tf_op jit(solution)/shard_map/add | solution.py:59
  96.0 1.9 %pad_maximum_fusion.3 = bf16[258,1024]{0,1:T(8,128)(2,1)} fusion(bf16[2,1024]{0,1:T(8,128)(2,1)} %copy.40, bf16[256,1024]{0,1:T(8,128)(2,1)S(1)} %dynamic-slice_convert_fusion.3), kind=kLoop, calls=%fused_computation.28 | loop fusion | flops 1056768 | bytes 1056768 | tf_op jit(solution)/shard_map/concatenate | solution.py:53
  98.0 2.2 %copy.41 = bf16[258,1024]{1,0:T(8,128)(2,1)} copy(bf16[258,1024]{0,1:T(8,128)(2,1)} %pad_maximum_fusion.3) | data formatting | bytes 1056768 | tf_op jit(solution)/shard_map/concatenate | solution.py:53
  107.9 7.7 %collective-permute-done.11 = bf16[258,1024]{1,0:T(8,128)(2,1)S(1)} collective-permute-done((bf16[258,1024]{1,0:T(8,128)(2,1)}, bf16[258,1024]{1,0:T(8,128)(2,1)S(1)}, u32[]{:S(2)}, u32[]{:S(2)}) %collective-permute-start.11) | collective-permute-done | bytes 528416 | tf_op jit(solution)/shard_map/ppermute | solution.py:19
  117.2 2.1 %copy.52 = bf16[256,1024]{0,1:T(8,128)(2,1)} copy(bf16[256,1024]{1,0:T(8,128)(2,1)} %slice.181) | data formatting | bytes 1048576
  120.1 2.2 %convert_add_fusion.3 = f32[256,1024]{0,1:T(8,128)} fusion(bf16[256,1024]{0,1:T(8,128)(2,1)} %copy.52, f32[512,1024]{0,1:T(8,128)S(1)} %convert_add_fusion.1, s32[]{:T(128)S(6)} %select_n.51), kind=kLoop, calls=%fused_computation.22 | loop fusion | flops 524288 | bytes 2621444 | tf_op jit(solution)/shard_map/add | solution.py:59
  123.8 1.8 %collective-permute-start.12 = (bf16[130,1024]{0,1:T(8,128)(2,1)S(1)}, bf16[130,1024]{0,1:T(8,128)(2,1)S(1)}, u32[]{:S(2)}, u32[]{:S(2)}) collective-permute-start(bf16[130,1024]{0,1:T(8,128)(2,1)S(1)} %pad_maximum_fusion.4), channel_id=1, source_target_pairs={{0,8},{2,10},{4,12},{6,14},{8,0},{10,2},{12,4},{14,6},{16,24},{18,... | collective-permute-start | bytes 798728 | tf_op jit(solution)/shard_map/ppermute | solution.py:19
  128.5 12.0 %collective-permute-done.12 = bf16[130,1024]{0,1:T(8,128)(2,1)S(1)} collective-permute-done((bf16[130,1024]{0,1:T(8,128)(2,1)S(1)}, bf16[130,1024]{0,1:T(8,128)(2,1)S(1)}, u32[]{:S(2)}, u32[]{:S(2)}) %collective-permute-start.12) | collective-permute-done | bytes 266272 | tf_op jit(solution)/shard_map/ppermute | solution.py:19
  141.9 1.9 %fusion.12 = bf16[128,1024]{1,0:T(8,128)(2,1)} fusion(bf16[128,1024]{1,0:T(8,128)(2,1)S(1)} %copy-done.4, bf16[128,1024]{1,0:T(8,128)(2,1)} %copy-done.13, bf16[128,1024]{1,0:T(8,128)(2,1)} %copy-done.11, f32[128]{0:T(128)S(1)} %broadcast_multiply_fusion, f32[1024]{0:T(1024)S(1)} %copy-done.21, f32[128]{0:T(128)S(1)} %copy-done.27), kind=kLoop, calls=%fused_computation.36 | loop fusion | flops 1441792 | bytes 1053696 | tf_op jit(solution)/shard_map/convert_element_type | solution.py:287
  143.9 9.5 %collective-permute-done.13 = bf16[66,1024]{0,1:T(8,128)(2,1)S(1)} collective-permute-done((bf16[66,1024]{0,1:T(8,128)(2,1)S(1)}, bf16[66,1024]{0,1:T(8,128)(2,1)S(1)}, u32[]{:S(2)}, u32[]{:S(2)}) %collective-permute-start.13) | collective-permute-done | bytes 135200 | tf_op jit(solution)/shard_map/ppermute | solution.py:19
  (167 shorter events, 63.1 us)
Async XLA Ops:
  1.9 67.5 %copy-start.26 = (f32[128]{0:T(128)}, f32[128]{0:T(128)S(1)}, u32[]{:S(2)}) copy-start(f32[128]{0:T(128)S(1)} %add_rsqrt_fusion) | copy-start | bytes 1540
  5.6 19.4 %collective-permute-start = (bf16[1,128,1024]{2,1,0:T(8,128)(2,1)}, bf16[1,128,1024]{2,1,0:T(8,128)(2,1)}, u32[]{:S(2)}, u32[]{:S(2)}) collective-permute-start(bf16[1,128,1024]{2,1,0:T(8,128)(2,1)} %pad_maximum_fusion.5.refs_0_.refs_5_), channel_id=1, source_target_pairs={{0,2},{2,0},{4,6},{6,4},{8,10},{10,8},{12,14},{14,12},{16,18},{18,... | collective-permute-start | bytes 786440 | tf_op jit(solution)/shard_map/ppermute | solution.py:19
  6.1 19.0 %collective-permute-start.1 = (bf16[1,128,1024]{2,1,0:T(8,128)(2,1)}, bf16[1,128,1024]{2,1,0:T(8,128)(2,1)}, u32[]{:S(2)}, u32[]{:S(2)}) collective-permute-start(bf16[1,128,1024]{2,1,0:T(8,128)(2,1)} %pad_maximum_fusion.5.refs_0_.refs_5_), channel_id=1, source_target_pairs={{0,4},{2,6},{4,0},{6,2},{8,12},{10,14},{12,8},{14,10},{16,20},{18,... | collective-permute-start | bytes 786440 | tf_op jit(solution)/shard_map/ppermute | solution.py:19
  8.6 16.5 %collective-permute-start.2 = (bf16[1,128,1024]{2,1,0:T(8,128)(2,1)}, bf16[1,128,1024]{2,1,0:T(8,128)(2,1)}, u32[]{:S(2)}, u32[]{:S(2)}) collective-permute-start(bf16[1,128,1024]{2,1,0:T(8,128)(2,1)} %pad_maximum_fusion.5.refs_0_.refs_5_), channel_id=1, source_target_pairs={{0,8},{2,10},{4,12},{6,14},{8,0},{10,2},{12,4},{14,6},{16,24},{18,... | collective-permute-start | bytes 786440 | tf_op jit(solution)/shard_map/ppermute | solution.py:19
  10.2 15.1 %collective-permute-start.3 = (bf16[1,128,1024]{2,1,0:T(8,128)(2,1)}, bf16[1,128,1024]{2,1,0:T(8,128)(2,1)}, u32[]{:S(2)}, u32[]{:S(2)}) collective-permute-start(bf16[1,128,1024]{2,1,0:T(8,128)(2,1)} %pad_maximum_fusion.5.refs_0_.refs_5_), channel_id=1, source_target_pairs={{0,16},{2,18},{4,20},{6,22},{8,24},{10,26},{12,28},{14,30},{16,0},... | collective-permute-start | bytes 786440 | tf_op jit(solution)/shard_map/ppermute | solution.py:19
  25.0 19.6 %copy-start.8 = (bf16[128,2,2,2,2,64]{0,5,4,3,2,1:T(8,128)(2,1)S(1)}, bf16[128,2,2,2,2,64]{0,5,4,3,2,1:T(8,128)(2,1)}, u32[]{:S(2)}) copy-start(bf16[128,2,2,2,2,64]{0,5,4,3,2,1:T(8,128)(2,1)} %copy.36) | copy-start | bytes 786436
  25.0 20.8 %copy-start.14 = (bf16[128,2,2,2,2,64]{0,5,4,3,2,1:T(8,128)(2,1)S(1)}, bf16[128,2,2,2,2,64]{0,5,4,3,2,1:T(8,128)(2,1)}, u32[]{:S(2)}) copy-start(bf16[128,2,2,2,2,64]{0,5,4,3,2,1:T(8,128)(2,1)} %copy.45) | copy-start | bytes 786436
  39.7 6.8 %collective-permute-start.5 = (bf16[1,128,1024]{2,1,0:T(8,128)(2,1)}, bf16[1,128,1024]{2,1,0:T(8,128)(2,1)S(1)}, u32[]{:S(2)}, u32[]{:S(2)}) collective-permute-start(bf16[1,128,1024]{2,1,0:T(8,128)(2,1)} %get-tuple-element.17), channel_id=1, source_target_pairs={{0,2},{2,0},{4,6},{6,4},{8,10},{10,8},{12,14},{14,12},{16,18},{18,... | collective-permute-start | bytes 786440 | tf_op jit(solution)/shard_map/ppermute | solution.py:19
  39.8 8.9 %collective-permute-start.6 = (bf16[1,128,1024]{2,1,0:T(8,128)(2,1)}, bf16[1,128,1024]{2,1,0:T(8,128)(2,1)S(1)}, u32[]{:S(2)}, u32[]{:S(2)}) collective-permute-start(bf16[1,128,1024]{2,1,0:T(8,128)(2,1)} %get-tuple-element.18), channel_id=1, source_target_pairs={{0,4},{2,6},{4,0},{6,2},{8,12},{10,14},{12,8},{14,10},{16,20},{18,... | collective-permute-start | bytes 786440 | tf_op jit(solution)/shard_map/ppermute | solution.py:19
  40.4 13.9 %collective-permute-start.7 = (bf16[1,128,1024]{2,1,0:T(8,128)(2,1)}, bf16[1,128,1024]{2,1,0:T(8,128)(2,1)S(1)}, u32[]{:S(2)}, u32[]{:S(2)}) collective-permute-start(bf16[1,128,1024]{2,1,0:T(8,128)(2,1)} %get-tuple-element.19), channel_id=1, source_target_pairs={{0,8},{2,10},{4,12},{6,14},{8,0},{10,2},{12,4},{14,6},{16,24},{18,... | collective-permute-start | bytes 786440 | tf_op jit(solution)/shard_map/ppermute | solution.py:19
  40.8 14.9 %collective-permute-start.8 = (bf16[1,128,1024]{2,1,0:T(8,128)(2,1)}, bf16[1,128,1024]{2,1,0:T(8,128)(2,1)S(1)}, u32[]{:S(2)}, u32[]{:S(2)}) collective-permute-start(bf16[1,128,1024]{2,1,0:T(8,128)(2,1)} %get-tuple-element.20), channel_id=1, source_target_pairs={{0,16},{2,18},{4,20},{6,22},{8,24},{10,26},{12,28},{14,30},{16,0},... | collective-permute-start | bytes 786440 | tf_op jit(solution)/shard_map/ppermute | solution.py:19
  60.1 24.7 %collective-permute-start.15 = (bf16[512,1024]{0,1:T(8,128)(2,1)}, bf16[512,1024]{0,1:T(8,128)(2,1)}, u32[]{:S(2)}, u32[]{:S(2)}) collective-permute-start(bf16[512,1024]{0,1:T(8,128)(2,1)} %dynamic-slice_convert_fusion), channel_id=1, source_target_pairs={{0,2},{2,0},{4,6},{6,4},{8,10},{10,8},{12,14},{14,12},{16,18},{18,... | collective-permute-start | bytes 3145736 | tf_op jit(solution)/shard_map/ppermute | solution.py:19
  60.6 8.8 %collective-permute-start.9 = (bf16[128,1024]{1,0:T(8,128)(2,1)S(1)}, bf16[128,1024]{1,0:T(8,128)(2,1)S(1)}, u32[]{:S(2)}, u32[]{:S(2)}) collective-permute-start(bf16[128,1024]{1,0:T(8,128)(2,1)S(1)} %fusion.1), channel_id=1, source_target_pairs={{0,1},{1,0},{2,3},{3,2},{4,5},{5,4},{6,7},{7,6},{8,9},{9,8},{10,11... | collective-permute-start | bytes 786440 | tf_op jit(solution)/shard_map/ppermute | solution.py:108
  73.8 15.8 %collective-permute-start.10 = (bf16[514,1024]{1,0:T(8,128)(2,1)}, bf16[514,1024]{1,0:T(8,128)(2,1)S(1)}, u32[]{:S(2)}, u32[]{:S(2)}) collective-permute-start(bf16[514,1024]{1,0:T(8,128)(2,1)} %copy.38), channel_id=1, source_target_pairs={{0,2},{2,0},{4,6},{6,4},{8,10},{10,8},{12,14},{14,12},{16,18},{18,... | collective-permute-start | bytes 3158024 | tf_op jit(solution)/shard_map/ppermute | solution.py:19
  75.3 8.8 %collective-permute-start.4 = (f32[128,512]{1,0:T(8,128)S(1)}, f32[128,512]{1,0:T(8,128)S(1)}, u32[]{:S(2)}, u32[]{:S(2)}) collective-permute-start(f32[128,512]{1,0:T(8,128)S(1)} %constant_dynamic-slice_fusion), channel_id=1, source_target_pairs={{0,1},{1,0},{2,3},{3,2},{4,5},{5,4},{6,7},{7,6},{8,9},{9,8},{10,11... | collective-permute-start | bytes 786440 | tf_op jit(solution)/shard_map/ppermute | solution.py:108
  89.3 13.9 %collective-permute-start.16 = (bf16[256,1024]{0,1:T(8,128)(2,1)}, bf16[256,1024]{0,1:T(8,128)(2,1)}, u32[]{:S(2)}, u32[]{:S(2)}) collective-permute-start(bf16[256,1024]{0,1:T(8,128)(2,1)} %dynamic-slice_convert_fusion.2), channel_id=1, source_target_pairs={{0,8},{2,10},{4,12},{6,14},{8,0},{10,2},{12,4},{14,6},{16,24},{18,... | collective-permute-start | bytes 1572872 | tf_op jit(solution)/shard_map/ppermute | solution.py:19
  100.2 15.4 %collective-permute-start.11 = (bf16[258,1024]{1,0:T(8,128)(2,1)}, bf16[258,1024]{1,0:T(8,128)(2,1)S(1)}, u32[]{:S(2)}, u32[]{:S(2)}) collective-permute-start(bf16[258,1024]{1,0:T(8,128)(2,1)} %copy.41), channel_id=1, source_target_pairs={{0,4},{2,6},{4,0},{6,2},{8,12},{10,14},{12,8},{14,10},{16,20},{18,... | collective-permute-start | bytes 1585160 | tf_op jit(solution)/shard_map/ppermute | solution.py:19
  106.4 19.2 %collective-permute-start.17 = (bf16[128,1024]{0,1:T(8,128)(2,1)}, bf16[128,1024]{0,1:T(8,128)(2,1)}, u32[]{:S(2)}, u32[]{:S(2)}) collective-permute-start(bf16[128,1024]{0,1:T(8,128)(2,1)} %dynamic-slice_convert_fusion.5), channel_id=1, source_target_pairs={{0,4},{2,6},{4,0},{6,2},{8,12},{10,14},{12,8},{14,10},{16,20},{18,... | collective-permute-start | bytes 786440 | tf_op jit(solution)/shard_map/ppermute | solution.py:19
  122.3 18.2 %copy-start.10 = (f32[256,1024]{0,1:T(8,128)S(1)}, f32[256,1024]{0,1:T(8,128)}, u32[]{:S(2)}) copy-start(f32[256,1024]{0,1:T(8,128)} %convert_add_fusion.3) | copy-start | bytes 3145732
  123.8 18.2 %copy-start.21 = (f32[1024]{0:T(1024)S(1)}, f32[1024]{0:T(1024)}, u32[]{:S(2)}) copy-start(f32[1024]{0:T(1024)} %param.9) | copy-start | bytes 12292
  123.8 16.7 %collective-permute-start.12 = (bf16[130,1024]{0,1:T(8,128)(2,1)S(1)}, bf16[130,1024]{0,1:T(8,128)(2,1)S(1)}, u32[]{:S(2)}, u32[]{:S(2)}) collective-permute-start(bf16[130,1024]{0,1:T(8,128)(2,1)S(1)} %pad_maximum_fusion.4), channel_id=1, source_target_pairs={{0,8},{2,10},{4,12},{6,14},{8,0},{10,2},{12,4},{14,6},{16,24},{18,... | collective-permute-start | bytes 798728 | tf_op jit(solution)/shard_map/ppermute | solution.py:19
  127.6 16.3 %collective-permute-start.18 = (bf16[64,1024]{0,1:T(8,128)(2,1)}, bf16[64,1024]{0,1:T(8,128)(2,1)}, u32[]{:S(2)}, u32[]{:S(2)}) collective-permute-start(bf16[64,1024]{0,1:T(8,128)(2,1)} %dynamic-slice_convert_fusion.4), channel_id=1, source_target_pairs={{0,16},{2,18},{4,20},{6,22},{8,24},{10,26},{12,28},{14,30},{16,0},... | collective-permute-start | bytes 393224 | tf_op jit(solution)/shard_map/ppermute | solution.py:19
  141.4 12.0 %collective-permute-start.13 = (bf16[66,1024]{0,1:T(8,128)(2,1)S(1)}, bf16[66,1024]{0,1:T(8,128)(2,1)S(1)}, u32[]{:S(2)}, u32[]{:S(2)}) collective-permute-start(bf16[66,1024]{0,1:T(8,128)(2,1)S(1)} %pad_maximum_fusion.6), channel_id=1, source_target_pairs={{0,16},{2,18},{4,20},{6,22},{8,24},{10,26},{12,28},{14,30},{16,0},... | collective-permute-start | bytes 405512 | tf_op jit(solution)/shard_map/ppermute | solution.py:19
  155.2 4.8 %collective-permute-start.14 = (f32[1024]{0:T(1024)S(1)}, f32[1024]{0:T(1024)S(1)}, u32[]{:S(2)}, u32[]{:S(2)}) collective-permute-start(f32[1024]{0:T(1024)S(1)} %fusion.41), channel_id=1, source_target_pairs={{0,1},{1,0},{2,3},{3,2},{4,5},{5,4},{6,7},{7,6},{8,9},{9,8},{10,11... | collective-permute-start | bytes 12296 | tf_op jit(solution)/shard_map/ppermute | solution.py:108
  (25 other events, 149.7 us)

commit v7 on v5

--- a/solution.py
+++ b/solution.py
@@ -102,7 +102,6 @@
     flags = [active_ref[block * slots + s] > 0 for s in range(slots)]
     contract_last = (((1,), (1,)), ((), ()))
     contract_first = (((0,), (0,)), ((), ()))
-    highest = lax.Precision.HIGHEST
     for pair in range(pairs):
         cols = pl.ds(pair * width, width)
         q2 = q_ref[:, cols]
@@ -121,7 +120,8 @@
             top = functools.reduce(jnp.maximum, [jnp.max(x, axis=1, keepdims=True) for x in scores])
             raised = [jnp.exp(x - top) for x in scores]
             total = functools.reduce(jnp.add, [jnp.sum(x, axis=1, keepdims=True) for x in raised])
-            probs = [x / total for x in raised]
+            spread = 1.0 / total
+            probs = [x * spread for x in raised]
             probs_low = [x.astype(jnp.bfloat16) for x in probs]
             attended = functools.reduce(jnp.add, [
                 jnp.dot(probs_low[s], values[s], preferred_element_type=jnp.float32) for s in range(slots)
@@ -133,15 +133,17 @@
             delta = functools.reduce(jnp.add, [
                 jnp.sum(probs[s] * grad_probs[s], axis=1, keepdims=True) for s in range(slots)
             ])
-            grad_scores = [probs[s] * (grad_probs[s] - delta) * scale for s in range(slots)]
+            grad_scores = [
+                (probs[s] * (grad_probs[s] - delta) * scale).astype(jnp.bfloat16)
+                for s in range(slots)
+            ]
             grad_query = functools.reduce(jnp.add, [
-                jnp.dot(grad_scores[s], keys[s].astype(jnp.float32), precision=highest,
-                        preferred_element_type=jnp.float32)
+                jnp.dot(grad_scores[s], keys[s], preferred_element_type=jnp.float32)
                 for s in range(slots)
             ])
             key_terms = [
-                lax.dot_general(grad_scores[s], q2.astype(jnp.float32), contract_first,
-                                precision=highest, preferred_element_type=jnp.float32)
+                lax.dot_general(grad_scores[s], q2, contract_first,
+                                preferred_element_type=jnp.float32)
                 for s in range(slots)
             ]
             value_terms = [

time: 135 us -> 132 us (0.978)
  Pallas kernels: 14.5 us -> 11 us
    pallas_call x1, Pallas kernels: 14.5 us -> 11 us  [block_attention(): pl.pallas_call(functools.partial(attention_kernel, slots, pairs), grid_sp...]
  transfers between devices with their start and end apart: 31 -> 31, of which waited for: 16 -> 16; matrix products, arithmetic and copies ran while one was open for 20% -> 21% of each run, Pallas kernels for 0% -> 0%
where the time goes in v7:
time: 132 us; the launch traced here: 131 us
  waiting for transfers between devices  49.4 us (37%)
  starting transfers between devices  33.7 us (26%)
  local copies, waits for them, and re-layouts  14.7 us (11%)
  other arithmetic  11.1 us (8%)
  Pallas kernels  11 us (8%)
  matrix products  10.2 us (8%)
    ppermute x28, waiting for transfers between devices, from_partner(): return lax.ppermute(value, axis, pairs)  43 us
    ppermute x28, starting transfers between devices, from_partner(): return lax.ppermute(value, axis, pairs)  29.1 us
    pallas_call x1, Pallas kernels, block_attention(): pl.pallas_call(functools.partial(attention_kernel, slots, pairs), grid_sp...  11 us
    unnamed x33, local copies, waits for them, and re-layouts  7.55 us
    ppermute x3, waiting for transfers between devices, head_swap(): return lax.ppermute(value, 'head', [(0, 1), (1, 0)])  6.43 us
    ppermute x3, starting transfers between devices, head_swap(): return lax.ppermute(value, 'head', [(0, 1), (1, 0)])  4.6 us
    transpose x4, local copies, waits for them, and re-layouts, bit_major_rows(): return shaped.transpose(axes).reshape(rows, width)  4.09 us
    add x16, other arithmetic, halving_sum(): partial = keep + got.astype(jnp.float32)  3.55 us
  transfers between devices with their start and end apart: 31, of which 16 were waited for; matrix products, arithmetic and copies ran while one was open for 21% of the time, Pallas kernels for 0%

profile of v7, /device:TPU:0, one launch (start us, length us, event | category | flops | bytes accessed | tf_op | source)
XLA Modules:
  0.0 131.3 jit_solution(934503102073542138)
XLA Ops:
  6.1 2.5 %collective-permute-start.1 = (bf16[1,128,1024]{2,1,0:T(8,128)(2,1)}, bf16[1,128,1024]{2,1,0:T(8,128)(2,1)}, u32[]{:S(2)}, u32[]{:S(2)}) collective-permute-start(bf16[1,128,1024]{2,1,0:T(8,128)(2,1)} %pad_maximum_fusion.refs_0_.refs_5_), channel_id=1, source_target_pairs={{0,4},{2,6},{4,0},{6,2},{8,12},{10,14},{12,8},{14,10},{16,20},{18,... | collective-permute-start | bytes 786440 | tf_op jit(solution)/shard_map/ppermute | solution.py:19
  10.2 2.6 %collective-permute-start.3 = (bf16[1,128,1024]{2,1,0:T(8,128)(2,1)}, bf16[1,128,1024]{2,1,0:T(8,128)(2,1)}, u32[]{:S(2)}, u32[]{:S(2)}) collective-permute-start(bf16[1,128,1024]{2,1,0:T(8,128)(2,1)} %pad_maximum_fusion.refs_0_.refs_5_), channel_id=1, source_target_pairs={{0,16},{2,18},{4,20},{6,22},{8,24},{10,26},{12,28},{14,30},{16,0},... | collective-permute-start | bytes 786440 | tf_op jit(solution)/shard_map/ppermute | solution.py:19
  15.3 1.8 %copy.19 = bf16[128,1024]{0,1:T(8,128)(2,1)} copy(bf16[128,1024]{1,0:T(8,128)(2,1)} %param.15) | data formatting | bytes 524288 | tf_op args[7]
  17.1 1.7 %copy.20 = bf16[128,2,2,2,2,64]{0,5,4,3,2,1:T(8,128)(2,1)} copy(bf16[128,2,2,2,2,64]{0,5,1,2,3,4:T(8,128)(2,1)} %bitcast.70) | data formatting | bytes 524288 | tf_op jit(solution)/shard_map/transpose | solution.py:28
  18.8 1.7 %copy.23 = bf16[128,2,2,2,2,64]{0,5,4,3,2,1:T(8,128)(2,1)} copy(bf16[128,2,2,2,2,64]{0,5,1,3,2,4:T(8,128)(2,1)} %bitcast.71) | data formatting | bytes 524288 | tf_op jit(solution)/shard_map/transpose | solution.py:28
  21.1 2.1 %fusion.3.g_ref = bf16[1,128,512]{2,1,0:T(8,128)(2,1)} fusion(bf16[128,1024]{1,0:T(8,128)(2,1)} %param.15, bf16[512,1024]{1,0:T(8,128)(2,1)S(1)} %copy-done), kind=kOutput, calls=%fused_computation.26 | convolution fusion | flops 134283264 | bytes 1441792 | tf_op jit(solution)/shard_map/dot_general | solution.py:215
  23.2 2.1 %collective-permute-done.3.refs_4_.refs_9_ = bf16[1,128,1024]{2,1,0:T(8,128)(2,1)} collective-permute-done((bf16[1,128,1024]{2,1,0:T(8,128)(2,1)}, bf16[1,128,1024]{2,1,0:T(8,128)(2,1)}, u32[]{:S(2)}, u32[]{:S(2)}) %collective-permute-start.3) | collective-permute-done | bytes 262176 | tf_op jit(solution)/shard_map/ppermute | solution.py:19
  25.2 11.0 %shard_map.135 = (bf16[1,128,512]{2,1,0:T(8,128)(2,1)}, bf16[1,128,512]{2,1,0:T(8,128)(2,1)}, bf16[1,128,1024]{2,1,0:T(8,128)(2,1)}, bf16[1,128,1024]{2,1,0:T(8,...) custom-call(s32[5]{0:T(128)} %add_bitcast_fusion.active_ref, ...), custom_call_target="tpu_custom_call" | custom-call | tf_op jit(solution)/shard_map/pallas_call | solution.py:173
  37.3 2.6 %collective-permute-start.8 = (bf16[1,128,1024]{2,1,0:T(8,128)(2,1)}, bf16[1,128,1024]{2,1,0:T(8,128)(2,1)S(1)}, u32[]{:S(2)}, u32[]{:S(2)}) collective-permute-start(bf16[1,128,1024]{2,1,0:T(8,128)(2,1)} %get-tuple-element.20), channel_id=1, source_target_pairs={{0,16},{2,18},{4,20},{6,22},{8,24},{10,26},{12,28},{14,30},{16,0},... | collective-permute-start | bytes 786440 | tf_op jit(solution)/shard_map/ppermute | solution.py:19
  46.7 4.1 %collective-permute-done.7 = bf16[1,128,1024]{2,1,0:T(8,128)(2,1)S(1)} collective-permute-done((bf16[1,128,1024]{2,1,0:T(8,128)(2,1)}, bf16[1,128,1024]{2,1,0:T(8,128)(2,1)S(1)}, u32[]{:S(2)}, u32[]{:S(2)}) %collective-permute-start.7) | collective-permute-done | bytes 262176 | tf_op jit(solution)/shard_map/ppermute | solution.py:19
  58.5 6.2 %collective-permute-done.9 = bf16[128,1024]{1,0:T(8,128)(2,1)S(1)} collective-permute-done((bf16[128,1024]{1,0:T(8,128)(2,1)S(1)}, bf16[128,1024]{1,0:T(8,128)(2,1)S(1)}, u32[]{:S(2)}, u32[]{:S(2)}) %collective-permute-start.9) | collective-permute-done | bytes 262176 | tf_op jit(solution)/shard_map/ppermute | solution.py:83
  71.8 2.8 %collective-permute-done.12 = f32[1024]{0:T(1024)S(1)} collective-permute-done((f32[1024]{0:T(1024)S(1)}, f32[1024]{0:T(1024)S(1)}, u32[]{:S(2)}, u32[]{:S(2)}) %collective-permute-start.12) | collective-permute-done | bytes 4128 | tf_op jit(solution)/shard_map/ppermute | solution.py:19
  75.0 4.8 %collective-permute-done.13 = f32[1024]{0:T(1024)S(1)} collective-permute-done((f32[1024]{0:T(1024)S(1)}, f32[1024]{0:T(1024)S(1)}, u32[]{:S(2)}, u32[]{:S(2)}) %collective-permute-start.13) | collective-permute-done | bytes 4128 | tf_op jit(solution)/shard_map/ppermute | solution.py:19
  81.8 2.5 %collective-permute-done.14 = f32[1024]{0:T(1024)S(1)} collective-permute-done((f32[1024]{0:T(1024)S(1)}, f32[1024]{0:T(1024)S(1)}, u32[]{:S(2)}, u32[]{:S(2)}) %collective-permute-start.14) | collective-permute-done | bytes 4128 | tf_op jit(solution)/shard_map/ppermute | solution.py:19
  87.6 1.8 %collective-permute-start.17 = (bf16[128,512]{0,1:T(8,128)(2,1)S(1)}, bf16[128,512]{0,1:T(8,128)(2,1)S(1)}, u32[]{:S(2)}, u32[]{:S(2)}) collective-permute-start(bf16[128,512]{0,1:T(8,128)(2,1)S(1)} %dynamic-slice_convert_fusion.11), channel_id=1, source_target_pairs={{0,8},{2,10},{4,12},{6,14},{8,0},{10,2},{12,4},{14,6},{16,24},{18,... | collective-permute-start | bytes 393224 | tf_op jit(solution)/shard_map/ppermute | solution.py:19
  89.5 1.6 %collective-permute-start.21 = (bf16[128,512]{0,1:T(8,128)(2,1)S(1)}, bf16[128,512]{0,1:T(8,128)(2,1)S(1)}, u32[]{:S(2)}, u32[]{:S(2)}) collective-permute-start(bf16[128,512]{0,1:T(8,128)(2,1)S(1)} %dynamic-slice_convert_fusion.9), channel_id=1, source_target_pairs={{0,4},{2,6},{4,0},{6,2},{8,12},{10,14},{12,8},{14,10},{16,20},{18,... | collective-permute-start | bytes 393224 | tf_op jit(solution)/shard_map/ppermute | solution.py:19
  91.1 4.9 %collective-permute-done.17 = bf16[128,512]{0,1:T(8,128)(2,1)S(1)} collective-permute-done((bf16[128,512]{0,1:T(8,128)(2,1)S(1)}, bf16[128,512]{0,1:T(8,128)(2,1)S(1)}, u32[]{:S(2)}, u32[]{:S(2)}) %collective-permute-start.17) | collective-permute-done | bytes 131104 | tf_op jit(solution)/shard_map/ppermute | solution.py:19
  96.2 2.2 %collective-permute-start.18 = (bf16[64,512]{0,1:T(8,128)(2,1)S(1)}, bf16[64,512]{0,1:T(8,128)(2,1)S(1)}, u32[]{:S(2)}, u32[]{:S(2)}) collective-permute-start(bf16[64,512]{0,1:T(8,128)(2,1)S(1)} %dynamic-slice_convert_fusion.10), channel_id=1, source_target_pairs={{0,16},{2,18},{4,20},{6,22},{8,24},{10,26},{12,28},{14,30},{16,0},... | collective-permute-start | bytes 196616 | tf_op jit(solution)/shard_map/ppermute | solution.py:19
  99.4 6.7 %collective-permute-done.18 = bf16[64,512]{0,1:T(8,128)(2,1)S(1)} collective-permute-done((bf16[64,512]{0,1:T(8,128)(2,1)S(1)}, bf16[64,512]{0,1:T(8,128)(2,1)S(1)}, u32[]{:S(2)}, u32[]{:S(2)}) %collective-permute-start.18) | collective-permute-done | bytes 65568 | tf_op jit(solution)/shard_map/ppermute | solution.py:19
  108.5 1.7 %copy.25 = f32[64,512]{1,0:T(8,128)} copy(f32[64,512]{0,1:T(8,128)} %get-tuple-element.47) | data formatting | bytes 262144
  113.2 1.6 %collective-permute-start.29 = (bf16[128,512]{0,1:T(8,128)(2,1)S(1)}, bf16[128,512]{0,1:T(8,128)(2,1)S(1)}, u32[]{:S(2)}, u32[]{:S(2)}) collective-permute-start(bf16[128,512]{0,1:T(8,128)(2,1)S(1)} %dynamic-slice_convert_fusion.5), channel_id=1, source_target_pairs={{0,4},{2,6},{4,0},{6,2},{8,12},{10,14},{12,8},{14,10},{16,20},{18,... | collective-permute-start | bytes 393224 | tf_op jit(solution)/shard_map/ppermute | solution.py:19
  114.9 2.2 %collective-permute-done.25 = bf16[128,512]{0,1:T(8,128)(2,1)S(1)} collective-permute-done((bf16[128,512]{0,1:T(8,128)(2,1)S(1)}, bf16[128,512]{0,1:T(8,128)(2,1)S(1)}, u32[]{:S(2)}, u32[]{:S(2)}) %collective-permute-start.25) | collective-permute-done | bytes 131104 | tf_op jit(solution)/shard_map/ppermute | solution.py:19
  118.5 3.0 %collective-permute-start.30 = (bf16[64,512]{0,1:T(8,128)(2,1)S(1)}, bf16[64,512]{0,1:T(8,128)(2,1)S(1)}, u32[]{:S(2)}, u32[]{:S(2)}) collective-permute-start(bf16[64,512]{0,1:T(8,128)(2,1)S(1)} %dynamic-slice_convert_fusion.4), channel_id=1, source_target_pairs={{0,16},{2,18},{4,20},{6,22},{8,24},{10,26},{12,28},{14,30},{16,0},... | collective-permute-start | bytes 196616 | tf_op jit(solution)/shard_map/ppermute | solution.py:19
  121.4 6.6 %collective-permute-done.26 = bf16[64,512]{0,1:T(8,128)(2,1)S(1)} collective-permute-done((bf16[64,512]{0,1:T(8,128)(2,1)S(1)}, bf16[64,512]{0,1:T(8,128)(2,1)S(1)}, u32[]{:S(2)}, u32[]{:S(2)}) %collective-permute-start.26) | collective-permute-done | bytes 65568 | tf_op jit(solution)/shard_map/ppermute | solution.py:19
  (147 shorter events, 49.5 us)
Async XLA Ops:
  5.6 17.5 %collective-permute-start = (bf16[1,128,1024]{2,1,0:T(8,128)(2,1)}, bf16[1,128,1024]{2,1,0:T(8,128)(2,1)}, u32[]{:S(2)}, u32[]{:S(2)}) collective-permute-start(bf16[1,128,1024]{2,1,0:T(8,128)(2,1)} %pad_maximum_fusion.refs_0_.refs_5_), channel_id=1, source_target_pairs={{0,2},{2,0},{4,6},{6,4},{8,10},{10,8},{12,14},{14,12},{16,18},{18,... | collective-permute-start | bytes 786440 | tf_op jit(solution)/shard_map/ppermute | solution.py:19
  6.1 17.1 %collective-permute-start.1 = (bf16[1,128,1024]{2,1,0:T(8,128)(2,1)}, bf16[1,128,1024]{2,1,0:T(8,128)(2,1)}, u32[]{:S(2)}, u32[]{:S(2)}) collective-permute-start(bf16[1,128,1024]{2,1,0:T(8,128)(2,1)} %pad_maximum_fusion.refs_0_.refs_5_), channel_id=1, source_target_pairs={{0,4},{2,6},{4,0},{6,2},{8,12},{10,14},{12,8},{14,10},{16,20},{18,... | collective-permute-start | bytes 786440 | tf_op jit(solution)/shard_map/ppermute | solution.py:19
  8.6 14.6 %collective-permute-start.2 = (bf16[1,128,1024]{2,1,0:T(8,128)(2,1)}, bf16[1,128,1024]{2,1,0:T(8,128)(2,1)}, u32[]{:S(2)}, u32[]{:S(2)}) collective-permute-start(bf16[1,128,1024]{2,1,0:T(8,128)(2,1)} %pad_maximum_fusion.refs_0_.refs_5_), channel_id=1, source_target_pairs={{0,8},{2,10},{4,12},{6,14},{8,0},{10,2},{12,4},{14,6},{16,24},{18,... | collective-permute-start | bytes 786440 | tf_op jit(solution)/shard_map/ppermute | solution.py:19
  10.2 15.1 %collective-permute-start.3 = (bf16[1,128,1024]{2,1,0:T(8,128)(2,1)}, bf16[1,128,1024]{2,1,0:T(8,128)(2,1)}, u32[]{:S(2)}, u32[]{:S(2)}) collective-permute-start(bf16[1,128,1024]{2,1,0:T(8,128)(2,1)} %pad_maximum_fusion.refs_0_.refs_5_), channel_id=1, source_target_pairs={{0,16},{2,18},{4,20},{6,22},{8,24},{10,26},{12,28},{14,30},{16,0},... | collective-permute-start | bytes 786440 | tf_op jit(solution)/shard_map/ppermute | solution.py:19
  36.2 7.7 %collective-permute-start.5 = (bf16[1,128,1024]{2,1,0:T(8,128)(2,1)}, bf16[1,128,1024]{2,1,0:T(8,128)(2,1)S(1)}, u32[]{:S(2)}, u32[]{:S(2)}) collective-permute-start(bf16[1,128,1024]{2,1,0:T(8,128)(2,1)} %get-tuple-element.17), channel_id=1, source_target_pairs={{0,2},{2,0},{4,6},{6,4},{8,10},{10,8},{12,14},{14,12},{16,18},{18,... | collective-permute-start | bytes 786440 | tf_op jit(solution)/shard_map/ppermute | solution.py:19
  36.3 8.9 %collective-permute-start.6 = (bf16[1,128,1024]{2,1,0:T(8,128)(2,1)}, bf16[1,128,1024]{2,1,0:T(8,128)(2,1)S(1)}, u32[]{:S(2)}, u32[]{:S(2)}) collective-permute-start(bf16[1,128,1024]{2,1,0:T(8,128)(2,1)} %get-tuple-element.18), channel_id=1, source_target_pairs={{0,4},{2,6},{4,0},{6,2},{8,12},{10,14},{12,8},{14,10},{16,20},{18,... | collective-permute-start | bytes 786440 | tf_op jit(solution)/shard_map/ppermute | solution.py:19
  36.9 13.9 %collective-permute-start.7 = (bf16[1,128,1024]{2,1,0:T(8,128)(2,1)}, bf16[1,128,1024]{2,1,0:T(8,128)(2,1)S(1)}, u32[]{:S(2)}, u32[]{:S(2)}) collective-permute-start(bf16[1,128,1024]{2,1,0:T(8,128)(2,1)} %get-tuple-element.19), channel_id=1, source_target_pairs={{0,8},{2,10},{4,12},{6,14},{8,0},{10,2},{12,4},{14,6},{16,24},{18,... | collective-permute-start | bytes 786440 | tf_op jit(solution)/shard_map/ppermute | solution.py:19
  37.3 14.9 %collective-permute-start.8 = (bf16[1,128,1024]{2,1,0:T(8,128)(2,1)}, bf16[1,128,1024]{2,1,0:T(8,128)(2,1)S(1)}, u32[]{:S(2)}, u32[]{:S(2)}) collective-permute-start(bf16[1,128,1024]{2,1,0:T(8,128)(2,1)} %get-tuple-element.20), channel_id=1, source_target_pairs={{0,16},{2,18},{4,20},{6,22},{8,24},{10,26},{12,28},{14,30},{16,0},... | collective-permute-start | bytes 786440 | tf_op jit(solution)/shard_map/ppermute | solution.py:19
  42.5 24.1 %collective-permute-start.15 = (bf16[512,512]{0,1:T(8,128)(2,1)S(1)}, bf16[512,512]{0,1:T(8,128)(2,1)S(1)}, u32[]{:S(2)}, u32[]{:S(2)}) collective-permute-start(bf16[512,512]{0,1:T(8,128)(2,1)S(1)} %fusion.19), channel_id=1, source_target_pairs={{0,2},{2,0},{4,6},{6,4},{8,10},{10,8},{12,14},{14,12},{16,18},{18,... | collective-permute-start | bytes 1572872 | tf_op jit(solution)/shard_map/ppermute | solution.py:19
  43.9 24.8 %collective-permute-start.19 = (bf16[512,512]{0,1:T(8,128)(2,1)S(1)}, bf16[512,512]{0,1:T(8,128)(2,1)S(1)}, u32[]{:S(2)}, u32[]{:S(2)}) collective-permute-start(bf16[512,512]{0,1:T(8,128)(2,1)S(1)} %fusion.15), channel_id=1, source_target_pairs={{0,2},{2,0},{4,6},{6,4},{8,10},{10,8},{12,14},{14,12},{16,18},{18,... | collective-permute-start | bytes 1572872 | tf_op jit(solution)/shard_map/ppermute | solution.py:19
  45.2 12.3 %collective-permute-start.4 = (f32[128,512]{1,0:T(8,128)S(1)}, f32[128,512]{1,0:T(8,128)S(1)}, u32[]{:S(2)}, u32[]{:S(2)}) collective-permute-start(f32[128,512]{1,0:T(8,128)S(1)} %constant_dynamic-slice_fusion), channel_id=1, source_target_pairs={{0,1},{1,0},{2,3},{3,2},{4,5},{5,4},{6,7},{7,6},{8,9},{9,8},{10,11... | collective-permute-start | bytes 786440 | tf_op jit(solution)/shard_map/ppermute | solution.py:83
  55.3 29.5 %collective-permute-start.23 = (bf16[512,512]{0,1:T(8,128)(2,1)S(1)}, bf16[512,512]{0,1:T(8,128)(2,1)S(1)}, u32[]{:S(2)}, u32[]{:S(2)}) collective-permute-start(bf16[512,512]{0,1:T(8,128)(2,1)S(1)} %fusion.11), channel_id=1, source_target_pairs={{0,2},{2,0},{4,6},{6,4},{8,10},{10,8},{12,14},{14,12},{16,18},{18,... | collective-permute-start | bytes 1572872 | tf_op jit(solution)/shard_map/ppermute | solution.py:19
  55.9 8.8 %collective-permute-start.9 = (bf16[128,1024]{1,0:T(8,128)(2,1)S(1)}, bf16[128,1024]{1,0:T(8,128)(2,1)S(1)}, u32[]{:S(2)}, u32[]{:S(2)}) collective-permute-start(bf16[128,1024]{1,0:T(8,128)(2,1)S(1)} %fusion.1), channel_id=1, source_target_pairs={{0,1},{1,0},{2,3},{3,2},{4,5},{5,4},{6,7},{7,6},{8,9},{9,8},{10,11... | collective-permute-start | bytes 786440 | tf_op jit(solution)/shard_map/ppermute | solution.py:83
  57.5 28.7 %collective-permute-start.27 = (bf16[512,512]{0,1:T(8,128)(2,1)S(1)}, bf16[512,512]{0,1:T(8,128)(2,1)S(1)}, u32[]{:S(2)}, u32[]{:S(2)}) collective-permute-start(bf16[512,512]{0,1:T(8,128)(2,1)S(1)} %fusion.7), channel_id=1, source_target_pairs={{0,2},{2,0},{4,6},{6,4},{8,10},{10,8},{12,14},{14,12},{16,18},{18,... | collective-permute-start | bytes 1572872 | tf_op jit(solution)/shard_map/ppermute | solution.py:19
  66.9 20.6 %collective-permute-start.16 = (bf16[256,512]{0,1:T(8,128)(2,1)S(1)}, bf16[256,512]{0,1:T(8,128)(2,1)S(1)}, u32[]{:S(2)}, u32[]{:S(2)}) collective-permute-start(bf16[256,512]{0,1:T(8,128)(2,1)S(1)} %dynamic-slice_convert_fusion.3), channel_id=1, source_target_pairs={{0,4},{2,6},{4,0},{6,2},{8,12},{10,14},{12,8},{14,10},{16,20},{18,... | collective-permute-start | bytes 786440 | tf_op jit(solution)/shard_map/ppermute | solution.py:19
  71.5 17.9 %collective-permute-start.20 = (bf16[256,512]{0,1:T(8,128)(2,1)S(1)}, bf16[256,512]{0,1:T(8,128)(2,1)S(1)}, u32[]{:S(2)}, u32[]{:S(2)}) collective-permute-start(bf16[256,512]{0,1:T(8,128)(2,1)S(1)} %dynamic-slice_convert_fusion.2), channel_id=1, source_target_pairs={{0,8},{2,10},{4,12},{6,14},{8,0},{10,2},{12,4},{14,6},{16,24},{18,... | collective-permute-start | bytes 786440 | tf_op jit(solution)/shard_map/ppermute | solution.py:19
  85.8 25.2 %collective-permute-start.24 = (bf16[256,512]{0,1:T(8,128)(2,1)}, bf16[256,512]{0,1:T(8,128)(2,1)}, u32[]{:S(2)}, u32[]{:S(2)}) collective-permute-start(bf16[256,512]{0,1:T(8,128)(2,1)} %dynamic-slice_convert_fusion.1), channel_id=1, source_target_pairs={{0,4},{2,6},{4,0},{6,2},{8,12},{10,14},{12,8},{14,10},{16,20},{18,... | collective-permute-start | bytes 786440 | tf_op jit(solution)/shard_map/ppermute | solution.py:19
  87.2 25.0 %collective-permute-start.28 = (bf16[256,512]{0,1:T(8,128)(2,1)}, bf16[256,512]{0,1:T(8,128)(2,1)}, u32[]{:S(2)}, u32[]{:S(2)}) collective-permute-start(bf16[256,512]{0,1:T(8,128)(2,1)} %dynamic-slice_convert_fusion), channel_id=1, source_target_pairs={{0,8},{2,10},{4,12},{6,14},{8,0},{10,2},{12,4},{14,6},{16,24},{18,... | collective-permute-start | bytes 786440 | tf_op jit(solution)/shard_map/ppermute | solution.py:19
  87.6 8.4 %collective-permute-start.17 = (bf16[128,512]{0,1:T(8,128)(2,1)S(1)}, bf16[128,512]{0,1:T(8,128)(2,1)S(1)}, u32[]{:S(2)}, u32[]{:S(2)}) collective-permute-start(bf16[128,512]{0,1:T(8,128)(2,1)S(1)} %dynamic-slice_convert_fusion.11), channel_id=1, source_target_pairs={{0,8},{2,10},{4,12},{6,14},{8,0},{10,2},{12,4},{14,6},{16,24},{18,... | collective-permute-start | bytes 393224 | tf_op jit(solution)/shard_map/ppermute | solution.py:19
  89.5 8.8 %collective-permute-start.21 = (bf16[128,512]{0,1:T(8,128)(2,1)S(1)}, bf16[128,512]{0,1:T(8,128)(2,1)S(1)}, u32[]{:S(2)}, u32[]{:S(2)}) collective-permute-start(bf16[128,512]{0,1:T(8,128)(2,1)S(1)} %dynamic-slice_convert_fusion.9), channel_id=1, source_target_pairs={{0,4},{2,6},{4,0},{6,2},{8,12},{10,14},{12,8},{14,10},{16,20},{18,... | collective-permute-start | bytes 393224 | tf_op jit(solution)/shard_map/ppermute | solution.py:19
  96.2 9.9 %collective-permute-start.18 = (bf16[64,512]{0,1:T(8,128)(2,1)S(1)}, bf16[64,512]{0,1:T(8,128)(2,1)S(1)}, u32[]{:S(2)}, u32[]{:S(2)}) collective-permute-start(bf16[64,512]{0,1:T(8,128)(2,1)S(1)} %dynamic-slice_convert_fusion.10), channel_id=1, source_target_pairs={{0,16},{2,18},{4,20},{6,22},{8,24},{10,26},{12,28},{14,30},{16,0},... | collective-permute-start | bytes 196616 | tf_op jit(solution)/shard_map/ppermute | solution.py:19
  98.5 9.2 %collective-permute-start.22 = (bf16[64,512]{0,1:T(8,128)(2,1)S(1)}, bf16[64,512]{0,1:T(8,128)(2,1)S(1)}, u32[]{:S(2)}, u32[]{:S(2)}) collective-permute-start(bf16[64,512]{0,1:T(8,128)(2,1)S(1)} %dynamic-slice_convert_fusion.8), channel_id=1, source_target_pairs={{0,16},{2,18},{4,20},{6,22},{8,24},{10,26},{12,28},{14,30},{16,0},... | collective-permute-start | bytes 196616 | tf_op jit(solution)/shard_map/ppermute | solution.py:19
  117.3 10.7 %collective-permute-start.26 = (bf16[64,512]{0,1:T(8,128)(2,1)S(1)}, bf16[64,512]{0,1:T(8,128)(2,1)S(1)}, u32[]{:S(2)}, u32[]{:S(2)}) collective-permute-start(bf16[64,512]{0,1:T(8,128)(2,1)S(1)} %dynamic-slice_convert_fusion.6), channel_id=1, source_target_pairs={{0,16},{2,18},{4,20},{6,22},{8,24},{10,26},{12,28},{14,30},{16,0},... | collective-permute-start | bytes 196616 | tf_op jit(solution)/shard_map/ppermute | solution.py:19
  118.5 11.1 %collective-permute-start.30 = (bf16[64,512]{0,1:T(8,128)(2,1)S(1)}, bf16[64,512]{0,1:T(8,128)(2,1)S(1)}, u32[]{:S(2)}, u32[]{:S(2)}) collective-permute-start(bf16[64,512]{0,1:T(8,128)(2,1)S(1)} %dynamic-slice_convert_fusion.4), channel_id=1, source_target_pairs={{0,16},{2,18},{4,20},{6,22},{8,24},{10,26},{12,28},{14,30},{16,0},... | collective-permute-start | bytes 196616 | tf_op jit(solution)/shard_map/ppermute | solution.py:19
  (21 other events, 107.5 us)

commit v8 on v7

--- a/solution.py
+++ b/solution.py
@@ -255,7 +255,8 @@
     low_terms = feature_terms.astype(jnp.bfloat16)
     grad_normed = low_terms.astype(jnp.float32) + head_swap(low_terms).astype(jnp.float32)
     gain_terms = jnp.sum(low_terms.astype(jnp.float32) * wide_nodes * inverse, axis=0)
-    gain_grad = doubling_sum(gain_terms + head_swap(gain_terms), "graph", graph_levels)
+    padded = jnp.zeros((16, width), jnp.float32).at[0].set(gain_terms)
+    gain_grad = lax.psum(padded, ("graph", "head"))[0]
     scaled = grad_normed * gain
     nodes_grad = (
         inverse

time: 132 us -> 258 us (1.95)
  waiting for transfers between devices: 49.4 us -> 165 us
  between operations: 1.19 us -> 14.7 us
  starting transfers between devices: 33.7 us -> 28.2 us
  other arithmetic: 11.1 us -> 15.8 us
    psum x0 -> x1, waiting for transfers between devices: none -> 116 us  [shards(): gain_grad = lax.psum(padded, ('graph', 'head'))[0]]
    ppermute x3 -> x2, waiting for transfers between devices: 6.43 us -> 1.62 us  [head_swap(): return lax.ppermute(value, 'head', [(0, 1), (1, 0)])]
    ppermute x28 -> x24, waiting for transfers between devices: 43 us -> 47.7 us  [from_partner(): return lax.ppermute(value, axis, pairs)]
    add x16, other arithmetic: 3.55 us -> 7.85 us  [halving_sum(): partial = keep + got.astype(jnp.float32)]
    ppermute x28 -> x24, starting transfers between devices: 29.1 us -> 25.1 us  [from_partner(): return lax.ppermute(value, axis, pairs)]
    transpose x4, local copies, waits for them, and re-layouts: 4.09 us -> 0.08 us  [bit_major_rows(): return shaped.transpose(axes).reshape(rows, width)]
    unnamed x33 -> x59, local copies, waits for them, and re-layouts: 7.55 us -> 6.89 us
  transfers between devices with their start and end apart: 31 -> 27, of which waited for: 16 -> 14; matrix products, arithmetic and copies ran while one was open for 21% -> 11% of each run, Pallas kernels for 0% -> 0%
where the time goes in v8:
time: 258 us; the launch traced here: 257 us
  waiting for transfers between devices  165 us (64%)
  starting transfers between devices  28.2 us (11%)
  other arithmetic  15.8 us (6%)
  between operations  14.7 us (6%)
  local copies, waits for them, and re-layouts  13.2 us (5%)
  Pallas kernels  11 us (4%)
  matrix products  9.21 us (4%)
    psum x1, waiting for transfers between devices, shards(): gain_grad = lax.psum(padded, ('graph', 'head'))[0]  116 us
    ppermute x24, waiting for transfers between devices, from_partner(): return lax.ppermute(value, axis, pairs)  47.7 us
    ppermute x24, starting transfers between devices, from_partner(): return lax.ppermute(value, axis, pairs)  25.1 us
    pallas_call x1, Pallas kernels, block_attention(): pl.pallas_call(functools.partial(attention_kernel, slots, pairs), grid_sp...  11 us
    add x16, other arithmetic, halving_sum(): partial = keep + got.astype(jnp.float32)  7.85 us
    unnamed x59, local copies, waits for them, and re-layouts  6.89 us
  transfers between devices with their start and end apart: 27, of which 14 were waited for; matrix products, arithmetic and copies ran while one was open for 11% of the time, Pallas kernels for 0%

profile of v8, /device:TPU:0, one launch (start us, length us, event | category | flops | bytes accessed | tf_op | source)
XLA Modules:
  0.0 257.1 jit_solution(9731609483539223565)
XLA Ops:
  9.6 1.5 fusion.4
  12.0 2.6 %collective-permute-start.1 = (bf16[1,128,1024]{2,1,0:T(8,128)(2,1)S(1)}, bf16[1,128,1024]{2,1,0:T(8,128)(2,1)}, u32[]{:S(2)}, u32[]{:S(2)}) collective-permute-start(bf16[1,128,1024]{2,1,0:T(8,128)(2,1)S(1)} %pad_maximum_fusion.refs_0_.refs_5_), channel_id=1, source_target_pairs={{0,4},{2,6},{4,0},{6,2},{8,12},{10,14},{12,8},{14,10},{16,20},{18,... | collective-permute-start | bytes 786440 | tf_op jit(solution)/shard_map/ppermute | solution.py:19
  14.6 1.6 collective-permute-start.2
  16.2 2.6 %collective-permute-start.3 = (bf16[1,128,1024]{2,1,0:T(8,128)(2,1)S(1)}, bf16[1,128,1024]{2,1,0:T(8,128)(2,1)}, u32[]{:S(2)}, u32[]{:S(2)}) collective-permute-start(bf16[1,128,1024]{2,1,0:T(8,128)(2,1)S(1)} %pad_maximum_fusion.refs_0_.refs_5_), channel_id=1, source_target_pairs={{0,16},{2,18},{4,20},{6,22},{8,24},{10,26},{12,28},{14,30},{16,0},... | collective-permute-start | bytes 786440 | tf_op jit(solution)/shard_map/ppermute | solution.py:19
  22.9 5.7 %collective-permute-done.2.refs_3_.refs_8_ = bf16[1,128,1024]{2,1,0:T(8,128)(2,1)} collective-permute-done((bf16[1,128,1024]{2,1,0:T(8,128)(2,1)S(1)}, bf16[1,128,1024]{2,1,0:T(8,128)(2,1)}, u32[]{:S(2)}, u32[]{:S(2)}) %collective-permute-start.2) | collective-permute-done | bytes 262176 | tf_op jit(solution)/shard_map/ppermute | solution.py:19
  28.6 2.4 collective-permute-done.3.refs_4_.refs_9_
  31.0 11.0 %shard_map.135 = (bf16[1,128,512]{2,1,0:T(8,128)(2,1)}, bf16[1,128,512]{2,1,0:T(8,128)(2,1)}, bf16[1,128,1024]{2,1,0:T(8,128)(2,1)}, bf16[1,128,1024]{2,1,0:T(8,...) custom-call(s32[5]{0:T(128)} %add_bitcast_fusion.active_ref, ...), custom_call_target="tpu_custom_call" | custom-call | tf_op jit(solution)/shard_map/pallas_call | solution.py:173
  43.0 2.6 %collective-permute-start.8 = (bf16[1,128,1024]{2,1,0:T(8,128)(2,1)}, bf16[1,128,1024]{2,1,0:T(8,128)(2,1)S(1)}, u32[]{:S(2)}, u32[]{:S(2)}) collective-permute-start(bf16[1,128,1024]{2,1,0:T(8,128)(2,1)} %get-tuple-element.32), channel_id=1, source_target_pairs={{0,16},{2,18},{4,20},{6,22},{8,24},{10,26},{12,28},{14,30},{16,0},... | collective-permute-start | bytes 786440 | tf_op jit(solution)/shard_map/ppermute | solution.py:19
  52.4 4.1 %collective-permute-done.7 = bf16[1,128,1024]{2,1,0:T(8,128)(2,1)S(1)} collective-permute-done((bf16[1,128,1024]{2,1,0:T(8,128)(2,1)}, bf16[1,128,1024]{2,1,0:T(8,128)(2,1)S(1)}, u32[]{:S(2)}, u32[]{:S(2)}) %collective-permute-start.7) | collective-permute-done | bytes 262176 | tf_op jit(solution)/shard_map/ppermute | solution.py:19
  64.5 1.6 collective-permute-start.9
  68.0 1.5 collective-permute-start.11
  71.2 1.6 collective-permute-done.9
  74.2 1.9 fusion.28
  76.1 115.7 %all-reduce.3.cloned.1.call-done = f32[16,1024]{1,0:T(8,128)} async-done(((f32[16,1024]{1,0:T(8,128)}), f32[16,1024]{1,0:T(8,128)}) %all-reduce.3.cloned.1.call-update) | async-done | bytes 65552 | tf_op jit(solution)/shard_map/psum | solution.py:259
  193.1 1.5 fusion.13
  199.0 2.8 %collective-permute-start.23 = (bf16[256,512]{0,1:T(8,128)(2,1)}, bf16[256,512]{0,1:T(8,128)(2,1)}, u32[]{:S(2)}, u32[]{:S(2)}) collective-permute-start(bf16[256,512]{0,1:T(8,128)(2,1)} %dynamic-slice_convert_fusion), channel_id=1, source_target_pairs={{0,8},{2,10},{4,12},{6,14},{8,0},{10,2},{12,4},{14,6},{16,24},{18,... | collective-permute-start | bytes 786440 | tf_op jit(solution)/shard_map/ppermute | solution.py:19
  204.6 6.9 %collective-permute-done.12 = bf16[128,512]{0,1:T(8,128)(2,1)S(1)} collective-permute-done((bf16[128,512]{0,1:T(8,128)(2,1)S(1)}, bf16[128,512]{0,1:T(8,128)(2,1)S(1)}, u32[]{:S(2)}, u32[]{:S(2)}) %collective-permute-start.12) | collective-permute-done | bytes 131104 | tf_op jit(solution)/shard_map/ppermute | solution.py:19
  212.9 2.0 collective-permute-start.17
  214.9 8.5 %collective-permute-done.13 = bf16[64,512]{0,1:T(8,128)(2,1)S(1)} collective-permute-done((bf16[64,512]{0,1:T(8,128)(2,1)S(1)}, bf16[64,512]{0,1:T(8,128)(2,1)S(1)}, u32[]{:S(2)}, u32[]{:S(2)}) %collective-permute-start.13) | collective-permute-done | bytes 65568 | tf_op jit(solution)/shard_map/ppermute | solution.py:19
  223.5 2.5 collective-permute-done.17
  230.7 3.7 %collective-permute-done.20 = bf16[128,512]{0,1:T(8,128)(2,1)S(1)} collective-permute-done((bf16[128,512]{0,1:T(8,128)(2,1)S(1)}, bf16[128,512]{0,1:T(8,128)(2,1)S(1)}, u32[]{:S(2)}, u32[]{:S(2)}) %collective-permute-start.20) | collective-permute-done | bytes 131104 | tf_op jit(solution)/shard_map/ppermute | solution.py:19
  235.7 2.0 collective-permute-start.25
  237.7 8.1 %collective-permute-done.21 = bf16[64,512]{0,1:T(8,128)(2,1)S(1)} collective-permute-done((bf16[64,512]{0,1:T(8,128)(2,1)S(1)}, bf16[64,512]{0,1:T(8,128)(2,1)S(1)}, u32[]{:S(2)}, u32[]{:S(2)}) %collective-permute-start.21) | collective-permute-done | bytes 65568 | tf_op jit(solution)/shard_map/ppermute | solution.py:19
  246.0 2.5 collective-permute-done.25
  (163 shorter events, 45.5 us)
Async XLA Ops:
  7.2 184.6 %all-reduce.3.cloned.1.call-start = ((), (), s32[]{:S(2)}) async-start(), calls=%async_computation | async-start | bytes 131072 | tf_op jit(solution)/shard_map/psum | solution.py:259
  11.5 11.4 %collective-permute-start = (bf16[1,128,1024]{2,1,0:T(8,128)(2,1)S(1)}, bf16[1,128,1024]{2,1,0:T(8,128)(2,1)S(1)}, u32[]{:S(2)}, u32[]{:S(2)}) collective-permute-start(bf16[1,128,1024]{2,1,0:T(8,128)(2,1)S(1)} %pad_maximum_fusion.refs_0_.refs_5_), channel_id=1, source_target_pairs={{0,2},{2,0},{4,6},{6,4},{8,10},{10,8},{12,14},{14,12},{16,18},{18,... | collective-permute-start | bytes 786440 | tf_op jit(solution)/shard_map/ppermute | solution.py:19
  12.0 10.9 %collective-permute-start.1 = (bf16[1,128,1024]{2,1,0:T(8,128)(2,1)S(1)}, bf16[1,128,1024]{2,1,0:T(8,128)(2,1)}, u32[]{:S(2)}, u32[]{:S(2)}) collective-permute-start(bf16[1,128,1024]{2,1,0:T(8,128)(2,1)S(1)} %pad_maximum_fusion.refs_0_.refs_5_), channel_id=1, source_target_pairs={{0,4},{2,6},{4,0},{6,2},{8,12},{10,14},{12,8},{14,10},{16,20},{18,... | collective-permute-start | bytes 786440 | tf_op jit(solution)/shard_map/ppermute | solution.py:19
  14.6 14.0 %collective-permute-start.2 = (bf16[1,128,1024]{2,1,0:T(8,128)(2,1)S(1)}, bf16[1,128,1024]{2,1,0:T(8,128)(2,1)}, u32[]{:S(2)}, u32[]{:S(2)}) collective-permute-start(bf16[1,128,1024]{2,1,0:T(8,128)(2,1)S(1)} %pad_maximum_fusion.refs_0_.refs_5_), channel_id=1, source_target_pairs={{0,8},{2,10},{4,12},{6,14},{8,0},{10,2},{12,4},{14,6},{16,24},{18,... | collective-permute-start | bytes 786440 | tf_op jit(solution)/shard_map/ppermute | solution.py:19
  16.2 14.8 %collective-permute-start.3 = (bf16[1,128,1024]{2,1,0:T(8,128)(2,1)S(1)}, bf16[1,128,1024]{2,1,0:T(8,128)(2,1)}, u32[]{:S(2)}, u32[]{:S(2)}) collective-permute-start(bf16[1,128,1024]{2,1,0:T(8,128)(2,1)S(1)} %pad_maximum_fusion.refs_0_.refs_5_), channel_id=1, source_target_pairs={{0,16},{2,18},{4,20},{6,22},{8,24},{10,26},{12,28},{14,30},{16,0},... | collective-permute-start | bytes 786440 | tf_op jit(solution)/shard_map/ppermute | solution.py:19
  42.0 8.9 %collective-permute-start.6 = (bf16[1,128,1024]{2,1,0:T(8,128)(2,1)}, bf16[1,128,1024]{2,1,0:T(8,128)(2,1)S(1)}, u32[]{:S(2)}, u32[]{:S(2)}) collective-permute-start(bf16[1,128,1024]{2,1,0:T(8,128)(2,1)} %get-tuple-element.30), channel_id=1, source_target_pairs={{0,4},{2,6},{4,0},{6,2},{8,12},{10,14},{12,8},{14,10},{16,20},{18,... | collective-permute-start | bytes 786440 | tf_op jit(solution)/shard_map/ppermute | solution.py:19
  42.6 13.9 %collective-permute-start.7 = (bf16[1,128,1024]{2,1,0:T(8,128)(2,1)}, bf16[1,128,1024]{2,1,0:T(8,128)(2,1)S(1)}, u32[]{:S(2)}, u32[]{:S(2)}) collective-permute-start(bf16[1,128,1024]{2,1,0:T(8,128)(2,1)} %get-tuple-element.31), channel_id=1, source_target_pairs={{0,8},{2,10},{4,12},{6,14},{8,0},{10,2},{12,4},{14,6},{16,24},{18,... | collective-permute-start | bytes 786440 | tf_op jit(solution)/shard_map/ppermute | solution.py:19
  43.0 14.9 %collective-permute-start.8 = (bf16[1,128,1024]{2,1,0:T(8,128)(2,1)}, bf16[1,128,1024]{2,1,0:T(8,128)(2,1)S(1)}, u32[]{:S(2)}, u32[]{:S(2)}) collective-permute-start(bf16[1,128,1024]{2,1,0:T(8,128)(2,1)} %get-tuple-element.32), channel_id=1, source_target_pairs={{0,16},{2,18},{4,20},{6,22},{8,24},{10,26},{12,28},{14,30},{16,0},... | collective-permute-start | bytes 786440 | tf_op jit(solution)/shard_map/ppermute | solution.py:19
  48.1 18.6 %collective-permute-start.10 = (bf16[512,512]{0,1:T(8,128)(2,1)S(1)}, bf16[512,512]{0,1:T(8,128)(2,1)S(1)}, u32[]{:S(2)}, u32[]{:S(2)}) collective-permute-start(bf16[512,512]{0,1:T(8,128)(2,1)S(1)} %fusion.19), channel_id=1, source_target_pairs={{0,2},{2,0},{4,6},{6,4},{8,10},{10,8},{12,14},{14,12},{16,18},{18,... | collective-permute-start | bytes 1572872 | tf_op jit(solution)/shard_map/ppermute | solution.py:19
  49.0 20.5 %collective-permute-start.14 = (bf16[512,512]{0,1:T(8,128)(2,1)S(1)}, bf16[512,512]{0,1:T(8,128)(2,1)S(1)}, u32[]{:S(2)}, u32[]{:S(2)}) collective-permute-start(bf16[512,512]{0,1:T(8,128)(2,1)S(1)} %fusion.15), channel_id=1, source_target_pairs={{0,2},{2,0},{4,6},{6,4},{8,10},{10,8},{12,14},{14,12},{16,18},{18,... | collective-permute-start | bytes 1572872 | tf_op jit(solution)/shard_map/ppermute | solution.py:19
  50.9 13.6 %collective-permute-start.4 = (f32[128,512]{1,0:T(8,128)S(1)}, f32[128,512]{1,0:T(8,128)S(1)}, u32[]{:S(2)}, u32[]{:S(2)}) collective-permute-start(f32[128,512]{1,0:T(8,128)S(1)} %constant_dynamic-slice_fusion), channel_id=1, source_target_pairs={{0,1},{1,0},{2,3},{3,2},{4,5},{5,4},{6,7},{7,6},{8,9},{9,8},{10,11... | collective-permute-start | bytes 786440 | tf_op jit(solution)/shard_map/ppermute | solution.py:83
  62.6 130.5 %collective-permute-start.18 = (bf16[512,512]{0,1:T(8,128)(2,1)}, bf16[512,512]{0,1:T(8,128)(2,1)}, u32[]{:S(2)}, u32[]{:S(2)}) collective-permute-start(bf16[512,512]{0,1:T(8,128)(2,1)} %fusion.11), channel_id=1, source_target_pairs={{0,2},{2,0},{4,6},{6,4},{8,10},{10,8},{12,14},{14,12},{16,18},{18,... | collective-permute-start | bytes 1572872 | tf_op jit(solution)/shard_map/ppermute | solution.py:19
  63.5 133.5 %collective-permute-start.22 = (bf16[512,512]{0,1:T(8,128)(2,1)}, bf16[512,512]{0,1:T(8,128)(2,1)}, u32[]{:S(2)}, u32[]{:S(2)}) collective-permute-start(bf16[512,512]{0,1:T(8,128)(2,1)} %fusion.7), channel_id=1, source_target_pairs={{0,2},{2,0},{4,6},{6,4},{8,10},{10,8},{12,14},{14,12},{16,18},{18,... | collective-permute-start | bytes 1572872 | tf_op jit(solution)/shard_map/ppermute | solution.py:19
  64.5 8.2 %collective-permute-start.9 = (bf16[128,1024]{1,0:T(8,128)(2,1)S(1)}, bf16[128,1024]{1,0:T(8,128)(2,1)S(1)}, u32[]{:S(2)}, u32[]{:S(2)}) collective-permute-start(bf16[128,1024]{1,0:T(8,128)(2,1)S(1)} %fusion.1), channel_id=1, source_target_pairs={{0,1},{1,0},{2,3},{3,2},{4,5},{5,4},{6,7},{7,6},{8,9},{9,8},{10,11... | collective-permute-start | bytes 786440 | tf_op jit(solution)/shard_map/ppermute | solution.py:83
  68.0 133.7 %collective-permute-start.11 = (bf16[256,512]{0,1:T(8,128)(2,1)}, bf16[256,512]{0,1:T(8,128)(2,1)}, u32[]{:S(2)}, u32[]{:S(2)}) collective-permute-start(bf16[256,512]{0,1:T(8,128)(2,1)} %dynamic-slice_convert_fusion.3), channel_id=1, source_target_pairs={{0,4},{2,6},{4,0},{6,2},{8,12},{10,14},{12,8},{14,10},{16,20},{18,... | collective-permute-start | bytes 786440 | tf_op jit(solution)/shard_map/ppermute | solution.py:19
  70.9 132.0 %collective-permute-start.15 = (bf16[256,512]{0,1:T(8,128)(2,1)}, bf16[256,512]{0,1:T(8,128)(2,1)}, u32[]{:S(2)}, u32[]{:S(2)}) collective-permute-start(bf16[256,512]{0,1:T(8,128)(2,1)} %dynamic-slice_convert_fusion.2), channel_id=1, source_target_pairs={{0,8},{2,10},{4,12},{6,14},{8,0},{10,2},{12,4},{14,6},{16,24},{18,... | collective-permute-start | bytes 786440 | tf_op jit(solution)/shard_map/ppermute | solution.py:19
  195.5 32.4 %collective-permute-start.19 = (bf16[256,512]{0,1:T(8,128)(2,1)}, bf16[256,512]{0,1:T(8,128)(2,1)}, u32[]{:S(2)}, u32[]{:S(2)}) collective-permute-start(bf16[256,512]{0,1:T(8,128)(2,1)} %dynamic-slice_convert_fusion.1), channel_id=1, source_target_pairs={{0,4},{2,6},{4,0},{6,2},{8,12},{10,14},{12,8},{14,10},{16,20},{18,... | collective-permute-start | bytes 786440 | tf_op jit(solution)/shard_map/ppermute | solution.py:19
  199.0 30.0 %collective-permute-start.23 = (bf16[256,512]{0,1:T(8,128)(2,1)}, bf16[256,512]{0,1:T(8,128)(2,1)}, u32[]{:S(2)}, u32[]{:S(2)}) collective-permute-start(bf16[256,512]{0,1:T(8,128)(2,1)} %dynamic-slice_convert_fusion), channel_id=1, source_target_pairs={{0,8},{2,10},{4,12},{6,14},{8,0},{10,2},{12,4},{14,6},{16,24},{18,... | collective-permute-start | bytes 786440 | tf_op jit(solution)/shard_map/ppermute | solution.py:19
  202.8 8.7 %collective-permute-start.12 = (bf16[128,512]{0,1:T(8,128)(2,1)S(1)}, bf16[128,512]{0,1:T(8,128)(2,1)S(1)}, u32[]{:S(2)}, u32[]{:S(2)}) collective-permute-start(bf16[128,512]{0,1:T(8,128)(2,1)S(1)} %dynamic-slice_convert_fusion.11), channel_id=1, source_target_pairs={{0,8},{2,10},{4,12},{6,14},{8,0},{10,2},{12,4},{14,6},{16,24},{18,... | collective-permute-start | bytes 393224 | tf_op jit(solution)/shard_map/ppermute | solution.py:19
  204.0 8.8 %collective-permute-start.16 = (bf16[128,512]{0,1:T(8,128)(2,1)S(1)}, bf16[128,512]{0,1:T(8,128)(2,1)S(1)}, u32[]{:S(2)}, u32[]{:S(2)}) collective-permute-start(bf16[128,512]{0,1:T(8,128)(2,1)S(1)} %dynamic-slice_convert_fusion.9), channel_id=1, source_target_pairs={{0,4},{2,6},{4,0},{6,2},{8,12},{10,14},{12,8},{14,10},{16,20},{18,... | collective-permute-start | bytes 393224 | tf_op jit(solution)/shard_map/ppermute | solution.py:19
  211.7 11.7 %collective-permute-start.13 = (bf16[64,512]{0,1:T(8,128)(2,1)S(1)}, bf16[64,512]{0,1:T(8,128)(2,1)S(1)}, u32[]{:S(2)}, u32[]{:S(2)}) collective-permute-start(bf16[64,512]{0,1:T(8,128)(2,1)S(1)} %dynamic-slice_convert_fusion.10), channel_id=1, source_target_pairs={{0,16},{2,18},{4,20},{6,22},{8,24},{10,26},{12,28},{14,30},{16,0},... | collective-permute-start | bytes 196616 | tf_op jit(solution)/shard_map/ppermute | solution.py:19
  212.9 13.2 %collective-permute-start.17 = (bf16[64,512]{0,1:T(8,128)(2,1)S(1)}, bf16[64,512]{0,1:T(8,128)(2,1)S(1)}, u32[]{:S(2)}, u32[]{:S(2)}) collective-permute-start(bf16[64,512]{0,1:T(8,128)(2,1)S(1)} %dynamic-slice_convert_fusion.8), channel_id=1, source_target_pairs={{0,16},{2,18},{4,20},{6,22},{8,24},{10,26},{12,28},{14,30},{16,0},... | collective-permute-start | bytes 196616 | tf_op jit(solution)/shard_map/ppermute | solution.py:19
  234.5 11.3 %collective-permute-start.21 = (bf16[64,512]{0,1:T(8,128)(2,1)S(1)}, bf16[64,512]{0,1:T(8,128)(2,1)S(1)}, u32[]{:S(2)}, u32[]{:S(2)}) collective-permute-start(bf16[64,512]{0,1:T(8,128)(2,1)S(1)} %dynamic-slice_convert_fusion.6), channel_id=1, source_target_pairs={{0,16},{2,18},{4,20},{6,22},{8,24},{10,26},{12,28},{14,30},{16,0},... | collective-permute-start | bytes 196616 | tf_op jit(solution)/shard_map/ppermute | solution.py:19
  235.7 12.8 %collective-permute-start.25 = (bf16[64,512]{0,1:T(8,128)(2,1)S(1)}, bf16[64,512]{0,1:T(8,128)(2,1)S(1)}, u32[]{:S(2)}, u32[]{:S(2)}) collective-permute-start(bf16[64,512]{0,1:T(8,128)(2,1)S(1)} %dynamic-slice_convert_fusion.4), channel_id=1, source_target_pairs={{0,16},{2,18},{4,20},{6,22},{8,24},{10,26},{12,28},{14,30},{16,0},... | collective-permute-start | bytes 196616 | tf_op jit(solution)/shard_map/ppermute | solution.py:19
  (30 other events, 131.4 us)
Sparse Core Ops, SparseCore 0:
  74.3 117.4 all-reduce.2

commit v9 on v7

--- a/solution.py
+++ b/solution.py
@@ -28,7 +28,7 @@
     return shaped.transpose(axes).reshape(rows, width)
 
 
-def halving_sum(partial, axis, order):
+def halving_sum(partial, axis, order, extra=None):
     me = lax.axis_index(axis)
     for bit in order:
         half = partial.shape[0] // 2
@@ -37,7 +37,10 @@
         send = lax.dynamic_slice_in_dim(partial, (1 - mine) * half, half, 0)
         got = from_partner(send.astype(jnp.bfloat16), axis, bit)
         partial = keep + got.astype(jnp.float32)
-    return partial
+        if extra is not None:
+            extra = extra + from_partner(extra, axis, bit)
+            partial, extra = lax.optimization_barrier((partial, extra))
+    return partial, extra
 
 
 def split_orders(levels):
@@ -47,7 +50,7 @@
     return first, (0, 2, 1) + first[3:]
 
 
-def scatter_rows(pairs, axis, levels):
+def scatter_rows(pairs, axis, levels, extra=None):
     contract = (((0,), (0,)), ((), ()))
     chunks = []
     for index, order in enumerate(split_orders(levels)):
@@ -61,7 +64,12 @@
                     preferred_element_type=jnp.float32,
                 )
             )
-        chunks.append(halving_sum(jnp.concatenate(pieces, axis=1), axis, order))
+        chunk, summed = halving_sum(
+            jnp.concatenate(pieces, axis=1), axis, order, extra if index == 0 else None
+        )
+        chunks.append(chunk)
+        if index == 0:
+            extra = summed
     results = []
     offset = 0
     for left, right in pairs:
@@ -70,7 +78,7 @@
             jnp.concatenate([chunk[:, offset : offset + cut] for chunk in chunks], axis=1)
         )
         offset += cut
-    return results
+    return results, extra
 
 
 def doubling_sum(value, axis, levels):
@@ -240,22 +248,22 @@
         grad_value = grad_value + returned[bit][1].astype(jnp.float32)
     grad_key = grad_key.astype(jnp.bfloat16).reshape(node_rows, columns)
     grad_value = grad_value.astype(jnp.bfloat16).reshape(node_rows, columns)
-    w_out_rows, w_query_grad = scatter_rows(
+    (w_out_rows, w_query_grad), _ = scatter_rows(
         [(cotangent, attended), (normed, grad_query)], "graph", graph_levels
     )
     w_out_grad = w_out_rows.T
-    w_key_grad, w_value_grad = scatter_rows(
-        [(normed, grad_key), (normed, grad_value)], "graph", graph_levels
-    )
     feature_terms = (
         jnp.dot(grad_query, w_query.T, preferred_element_type=jnp.float32)
         + jnp.dot(grad_key, w_key.T, preferred_element_type=jnp.float32)
         + jnp.dot(grad_value, w_value.T, preferred_element_type=jnp.float32)
     )
     low_terms = feature_terms.astype(jnp.bfloat16)
+    gain_terms = jnp.sum(low_terms.astype(jnp.float32) * wide_nodes * inverse, axis=0)
+    (w_key_grad, w_value_grad), gain_part = scatter_rows(
+        [(normed, grad_key), (normed, grad_value)], "graph", graph_levels, gain_terms
+    )
+    gain_grad = gain_part + head_swap(gain_part)
     grad_normed = low_terms.astype(jnp.float32) + head_swap(low_terms).astype(jnp.float32)
-    gain_terms = jnp.sum(low_terms.astype(jnp.float32) * wide_nodes * inverse, axis=0)
-    gain_grad = doubling_sum(gain_terms + head_swap(gain_terms), "graph", graph_levels)
     scaled = grad_normed * gain
     nodes_grad = (
         inverse

time: 132 us -> 127 us (0.962)
  waiting for transfers between devices: 49.4 us -> 44.6 us
    ppermute x28, waiting for transfers between devices: 43 us -> 37.9 us  [from_partner(): return lax.ppermute(value, axis, pairs)]
  transfers between devices with their start and end apart: 31 -> 31, of which waited for: 16 -> 14; matrix products, arithmetic and copies ran while one was open for 21% -> 22% of each run, Pallas kernels for 0% -> 0%
where the time goes in v9:
time: 127 us
  waiting for transfers between devices  44.6 us (35%)
  starting transfers between devices  33.6 us (26%)
  local copies, waits for them, and re-layouts  15.3 us (12%)
  other arithmetic  11.1 us (9%)
  Pallas kernels  11 us (9%)
  matrix products  10.2 us (8%)
    ppermute x28, waiting for transfers between devices, from_partner(): return lax.ppermute(value, axis, pairs)  37.9 us
    ppermute x28, starting transfers between devices, from_partner(): return lax.ppermute(value, axis, pairs)  29 us
    pallas_call x1, Pallas kernels, block_attention(): pl.pallas_call(functools.partial(attention_kernel, slots, pairs), grid_sp...  11 us
    unnamed x33, local copies, waits for them, and re-layouts  8.14 us
    ppermute x3, waiting for transfers between devices, head_swap(): return lax.ppermute(value, 'head', [(0, 1), (1, 0)])  6.69 us
    ppermute x3, starting transfers between devices, head_swap(): return lax.ppermute(value, 'head', [(0, 1), (1, 0)])  4.59 us
    transpose x4, local copies, waits for them, and re-layouts, bit_major_rows(): return shaped.transpose(axes).reshape(rows, width)  4.1 us
    add x16, other arithmetic, halving_sum(): partial = keep + got.astype(jnp.float32)  3.55 us
  transfers between devices with their start and end apart: 31, of which 14 were waited for; matrix products, arithmetic and copies ran while one was open for 22% of the time, Pallas kernels for 0%

profile of v9, /device:TPU:0, one launch (start us, length us, event | category | flops | bytes accessed | tf_op | source)
XLA Modules:
  0.0 127.0 jit_solution(11290088153343438217)
XLA Ops:
  6.1 2.5 %collective-permute-start.1 = (bf16[1,128,1024]{2,1,0:T(8,128)(2,1)}, bf16[1,128,1024]{2,1,0:T(8,128)(2,1)}, u32[]{:S(2)}, u32[]{:S(2)}) collective-permute-start(bf16[1,128,1024]{2,1,0:T(8,128)(2,1)} %pad_maximum_fusion.refs_0_.refs_5_), channel_id=1, source_target_pairs={{0,4},{2,6},{4,0},{6,2},{8,12},{10,14},{12,8},{14,10},{16,20},{18,... | collective-permute-start | bytes 786440 | tf_op jit(solution)/shard_map/ppermute | solution.py:19
  8.6 1.6 %collective-permute-start.2 = (bf16[1,128,1024]{2,1,0:T(8,128)(2,1)}, bf16[1,128,1024]{2,1,0:T(8,128)(2,1)}, u32[]{:S(2)}, u32[]{:S(2)}) collective-permute-start(bf16[1,128,1024]{2,1,0:T(8,128)(2,1)} %pad_maximum_fusion.refs_0_.refs_5_), channel_id=1, source_target_pairs={{0,8},{2,10},{4,12},{6,14},{8,0},{10,2},{12,4},{14,6},{16,24},{18,... | collective-permute-start | bytes 786440 | tf_op jit(solution)/shard_map/ppermute | solution.py:19
  10.2 2.6 %collective-permute-start.3 = (bf16[1,128,1024]{2,1,0:T(8,128)(2,1)}, bf16[1,128,1024]{2,1,0:T(8,128)(2,1)}, u32[]{:S(2)}, u32[]{:S(2)}) collective-permute-start(bf16[1,128,1024]{2,1,0:T(8,128)(2,1)} %pad_maximum_fusion.refs_0_.refs_5_), channel_id=1, source_target_pairs={{0,16},{2,18},{4,20},{6,22},{8,24},{10,26},{12,28},{14,30},{16,0},... | collective-permute-start | bytes 786440 | tf_op jit(solution)/shard_map/ppermute | solution.py:19
  15.3 1.8 %copy.21 = bf16[128,1024]{0,1:T(8,128)(2,1)} copy(bf16[128,1024]{1,0:T(8,128)(2,1)} %param.15) | data formatting | bytes 524288 | tf_op args[7]
  17.1 1.7 %copy.22 = bf16[128,2,2,2,2,64]{0,5,4,3,2,1:T(8,128)(2,1)} copy(bf16[128,2,2,2,2,64]{0,5,1,2,3,4:T(8,128)(2,1)} %bitcast.70) | data formatting | bytes 524288 | tf_op jit(solution)/shard_map/transpose | solution.py:28
  18.8 1.7 %copy.23 = bf16[128,2,2,2,2,64]{0,5,4,3,2,1:T(8,128)(2,1)} copy(bf16[128,2,2,2,2,64]{0,5,1,3,2,4:T(8,128)(2,1)} %bitcast.71) | data formatting | bytes 524288 | tf_op jit(solution)/shard_map/transpose | solution.py:28
  21.1 2.1 %fusion.3.g_ref = bf16[1,128,512]{2,1,0:T(8,128)(2,1)} fusion(bf16[128,1024]{1,0:T(8,128)(2,1)} %param.15, bf16[512,1024]{1,0:T(8,128)(2,1)S(1)} %copy-done), kind=kOutput, calls=%fused_computation.26 | convolution fusion | flops 134283264 | bytes 1441792 | tf_op jit(solution)/shard_map/dot_general | solution.py:223
  23.2 2.1 %collective-permute-done.3.refs_4_.refs_9_ = bf16[1,128,1024]{2,1,0:T(8,128)(2,1)} collective-permute-done((bf16[1,128,1024]{2,1,0:T(8,128)(2,1)}, bf16[1,128,1024]{2,1,0:T(8,128)(2,1)}, u32[]{:S(2)}, u32[]{:S(2)}) %collective-permute-start.3) | collective-permute-done | bytes 262176 | tf_op jit(solution)/shard_map/ppermute | solution.py:19
  25.2 11.0 %shard_map.135 = (bf16[1,128,512]{2,1,0:T(8,128)(2,1)}, bf16[1,128,512]{2,1,0:T(8,128)(2,1)}, bf16[1,128,1024]{2,1,0:T(8,128)(2,1)}, bf16[1,128,1024]{2,1,0:T(8,...) custom-call(s32[5]{0:T(128)} %add_bitcast_fusion.active_ref, ...), custom_call_target="tpu_custom_call" | custom-call | tf_op jit(solution)/shard_map/pallas_call | solution.py:181
  37.3 2.6 %collective-permute-start.8 = (bf16[1,128,1024]{2,1,0:T(8,128)(2,1)}, bf16[1,128,1024]{2,1,0:T(8,128)(2,1)S(1)}, u32[]{:S(2)}, u32[]{:S(2)}) collective-permute-start(bf16[1,128,1024]{2,1,0:T(8,128)(2,1)} %get-tuple-element.28), channel_id=1, source_target_pairs={{0,16},{2,18},{4,20},{6,22},{8,24},{10,26},{12,28},{14,30},{16,0},... | collective-permute-start | bytes 786440 | tf_op jit(solution)/shard_map/ppermute | solution.py:19
  46.7 4.1 %collective-permute-done.7 = bf16[1,128,1024]{2,1,0:T(8,128)(2,1)S(1)} collective-permute-done((bf16[1,128,1024]{2,1,0:T(8,128)(2,1)}, bf16[1,128,1024]{2,1,0:T(8,128)(2,1)S(1)}, u32[]{:S(2)}, u32[]{:S(2)}) %collective-permute-start.7) | collective-permute-done | bytes 262176 | tf_op jit(solution)/shard_map/ppermute | solution.py:19
  58.8 6.2 %collective-permute-done.9 = bf16[128,1024]{1,0:T(8,128)(2,1)S(1)} collective-permute-done((bf16[128,1024]{1,0:T(8,128)(2,1)S(1)}, bf16[128,1024]{1,0:T(8,128)(2,1)S(1)}, u32[]{:S(2)}, u32[]{:S(2)}) %collective-permute-start.9) | collective-permute-done | bytes 262176 | tf_op jit(solution)/shard_map/ppermute | solution.py:91
  65.7 1.6 %collective-permute-start.20 = (bf16[256,512]{0,1:T(8,128)(2,1)S(1)}, bf16[256,512]{0,1:T(8,128)(2,1)S(1)}, u32[]{:S(2)}, u32[]{:S(2)}) collective-permute-start(bf16[256,512]{0,1:T(8,128)(2,1)S(1)} %dynamic-slice_convert_fusion.2), channel_id=1, source_target_pairs={{0,4},{2,6},{4,0},{6,2},{8,12},{10,14},{12,8},{14,10},{16,20},{18,... | collective-permute-start | bytes 786440 | tf_op jit(solution)/shard_map/ppermute | solution.py:19
  69.8 1.7 %collective-permute-start.28 = (bf16[256,512]{0,1:T(8,128)(2,1)}, bf16[256,512]{0,1:T(8,128)(2,1)}, u32[]{:S(2)}, u32[]{:S(2)}) collective-permute-start(bf16[256,512]{0,1:T(8,128)(2,1)} %dynamic-slice_convert_fusion), channel_id=1, source_target_pairs={{0,8},{2,10},{4,12},{6,14},{8,0},{10,2},{12,4},{14,6},{16,24},{18,... | collective-permute-start | bytes 786440 | tf_op jit(solution)/shard_map/ppermute | solution.py:19
  75.0 1.8 %collective-permute-done.24 = bf16[256,512]{0,1:T(8,128)(2,1)S(1)} collective-permute-done((bf16[256,512]{0,1:T(8,128)(2,1)S(1)}, bf16[256,512]{0,1:T(8,128)(2,1)S(1)}, u32[]{:S(2)}, u32[]{:S(2)}) %collective-permute-start.24) | collective-permute-done | bytes 262176 | tf_op jit(solution)/shard_map/ppermute | solution.py:19
  77.5 7.0 %collective-permute-done.21 = bf16[128,512]{0,1:T(8,128)(2,1)S(1)} collective-permute-done((bf16[128,512]{0,1:T(8,128)(2,1)S(1)}, bf16[128,512]{0,1:T(8,128)(2,1)S(1)}, u32[]{:S(2)}, u32[]{:S(2)}) %collective-permute-start.21) | collective-permute-done | bytes 131104 | tf_op jit(solution)/shard_map/ppermute | solution.py:19
  85.9 1.9 %collective-permute-start.26 = (bf16[64,512]{0,1:T(8,128)(2,1)S(1)}, bf16[64,512]{0,1:T(8,128)(2,1)S(1)}, u32[]{:S(2)}, u32[]{:S(2)}) collective-permute-start(bf16[64,512]{0,1:T(8,128)(2,1)S(1)} %dynamic-slice_convert_fusion.6), channel_id=1, source_target_pairs={{0,16},{2,18},{4,20},{6,22},{8,24},{10,26},{12,28},{14,30},{16,0},... | collective-permute-start | bytes 196616 | tf_op jit(solution)/shard_map/ppermute | solution.py:19
  87.8 8.1 %collective-permute-done.22 = bf16[64,512]{0,1:T(8,128)(2,1)S(1)} collective-permute-done((bf16[64,512]{0,1:T(8,128)(2,1)S(1)}, bf16[64,512]{0,1:T(8,128)(2,1)S(1)}, u32[]{:S(2)}, u32[]{:S(2)}) %collective-permute-start.22) | collective-permute-done | bytes 65568 | tf_op jit(solution)/shard_map/ppermute | solution.py:19
  96.0 2.5 %collective-permute-done.26 = bf16[64,512]{0,1:T(8,128)(2,1)S(1)} collective-permute-done((bf16[64,512]{0,1:T(8,128)(2,1)S(1)}, bf16[64,512]{0,1:T(8,128)(2,1)S(1)}, u32[]{:S(2)}, u32[]{:S(2)}) %collective-permute-start.26) | collective-permute-done | bytes 65568 | tf_op jit(solution)/shard_map/ppermute | solution.py:19
  99.4 1.7 %copy.25 = f32[64,512]{1,0:T(8,128)} copy(f32[64,512]{0,1:T(8,128)} %get-tuple-element.63) | data formatting | bytes 262144
  104.7 2.1 %collective-permute-start.14 = (bf16[128,512]{0,1:T(8,128)(2,1)S(1)}, bf16[128,512]{0,1:T(8,128)(2,1)S(1)}, u32[]{:S(2)}, u32[]{:S(2)}) collective-permute-start(bf16[128,512]{0,1:T(8,128)(2,1)S(1)} %dynamic-slice_convert_fusion.11), channel_id=1, source_target_pairs={{0,8},{2,10},{4,12},{6,14},{8,0},{10,2},{12,4},{14,6},{16,24},{18,... | collective-permute-start | bytes 393224 | tf_op jit(solution)/shard_map/ppermute | solution.py:19
  110.0 4.1 %collective-permute-start.17 = (f32[1024]{0:T(1024)S(1)}, f32[1024]{0:T(1024)S(1)}, u32[]{:S(2)}, u32[]{:S(2)}) collective-permute-start(f32[1024]{0:T(1024)S(1)} %add.199), channel_id=1, source_target_pairs={{0,16},{2,18},{4,20},{6,22},{8,24},{10,26},{12,28},{14,30},{16,0},... | collective-permute-start | bytes 12296 | tf_op jit(solution)/shard_map/ppermute | solution.py:19
  114.2 6.5 %collective-permute-done.17 = f32[1024]{0:T(1024)S(1)} collective-permute-done((f32[1024]{0:T(1024)S(1)}, f32[1024]{0:T(1024)S(1)}, u32[]{:S(2)}, u32[]{:S(2)}) %collective-permute-start.17) | collective-permute-done | bytes 4128 | tf_op jit(solution)/shard_map/ppermute | solution.py:19
  120.9 1.6 %collective-permute-done.16 = bf16[64,512]{0,1:T(8,128)(2,1)S(1)} collective-permute-done((bf16[64,512]{0,1:T(8,128)(2,1)S(1)}, bf16[64,512]{0,1:T(8,128)(2,1)S(1)}, u32[]{:S(2)}, u32[]{:S(2)}) %collective-permute-start.16) | collective-permute-done | bytes 65568 | tf_op jit(solution)/shard_map/ppermute | solution.py:19
  (147 shorter events, 45.6 us)
Async XLA Ops:
  5.6 17.5 %collective-permute-start = (bf16[1,128,1024]{2,1,0:T(8,128)(2,1)}, bf16[1,128,1024]{2,1,0:T(8,128)(2,1)}, u32[]{:S(2)}, u32[]{:S(2)}) collective-permute-start(bf16[1,128,1024]{2,1,0:T(8,128)(2,1)} %pad_maximum_fusion.refs_0_.refs_5_), channel_id=1, source_target_pairs={{0,2},{2,0},{4,6},{6,4},{8,10},{10,8},{12,14},{14,12},{16,18},{18,... | collective-permute-start | bytes 786440 | tf_op jit(solution)/shard_map/ppermute | solution.py:19
  6.1 17.1 %collective-permute-start.1 = (bf16[1,128,1024]{2,1,0:T(8,128)(2,1)}, bf16[1,128,1024]{2,1,0:T(8,128)(2,1)}, u32[]{:S(2)}, u32[]{:S(2)}) collective-permute-start(bf16[1,128,1024]{2,1,0:T(8,128)(2,1)} %pad_maximum_fusion.refs_0_.refs_5_), channel_id=1, source_target_pairs={{0,4},{2,6},{4,0},{6,2},{8,12},{10,14},{12,8},{14,10},{16,20},{18,... | collective-permute-start | bytes 786440 | tf_op jit(solution)/shard_map/ppermute | solution.py:19
  8.6 14.6 %collective-permute-start.2 = (bf16[1,128,1024]{2,1,0:T(8,128)(2,1)}, bf16[1,128,1024]{2,1,0:T(8,128)(2,1)}, u32[]{:S(2)}, u32[]{:S(2)}) collective-permute-start(bf16[1,128,1024]{2,1,0:T(8,128)(2,1)} %pad_maximum_fusion.refs_0_.refs_5_), channel_id=1, source_target_pairs={{0,8},{2,10},{4,12},{6,14},{8,0},{10,2},{12,4},{14,6},{16,24},{18,... | collective-permute-start | bytes 786440 | tf_op jit(solution)/shard_map/ppermute | solution.py:19
  10.2 15.1 %collective-permute-start.3 = (bf16[1,128,1024]{2,1,0:T(8,128)(2,1)}, bf16[1,128,1024]{2,1,0:T(8,128)(2,1)}, u32[]{:S(2)}, u32[]{:S(2)}) collective-permute-start(bf16[1,128,1024]{2,1,0:T(8,128)(2,1)} %pad_maximum_fusion.refs_0_.refs_5_), channel_id=1, source_target_pairs={{0,16},{2,18},{4,20},{6,22},{8,24},{10,26},{12,28},{14,30},{16,0},... | collective-permute-start | bytes 786440 | tf_op jit(solution)/shard_map/ppermute | solution.py:19
  36.3 8.9 %collective-permute-start.6 = (bf16[1,128,1024]{2,1,0:T(8,128)(2,1)}, bf16[1,128,1024]{2,1,0:T(8,128)(2,1)S(1)}, u32[]{:S(2)}, u32[]{:S(2)}) collective-permute-start(bf16[1,128,1024]{2,1,0:T(8,128)(2,1)} %get-tuple-element.26), channel_id=1, source_target_pairs={{0,4},{2,6},{4,0},{6,2},{8,12},{10,14},{12,8},{14,10},{16,20},{18,... | collective-permute-start | bytes 786440 | tf_op jit(solution)/shard_map/ppermute | solution.py:19
  36.8 13.9 %collective-permute-start.7 = (bf16[1,128,1024]{2,1,0:T(8,128)(2,1)}, bf16[1,128,1024]{2,1,0:T(8,128)(2,1)S(1)}, u32[]{:S(2)}, u32[]{:S(2)}) collective-permute-start(bf16[1,128,1024]{2,1,0:T(8,128)(2,1)} %get-tuple-element.27), channel_id=1, source_target_pairs={{0,8},{2,10},{4,12},{6,14},{8,0},{10,2},{12,4},{14,6},{16,24},{18,... | collective-permute-start | bytes 786440 | tf_op jit(solution)/shard_map/ppermute | solution.py:19
  37.3 14.9 %collective-permute-start.8 = (bf16[1,128,1024]{2,1,0:T(8,128)(2,1)}, bf16[1,128,1024]{2,1,0:T(8,128)(2,1)S(1)}, u32[]{:S(2)}, u32[]{:S(2)}) collective-permute-start(bf16[1,128,1024]{2,1,0:T(8,128)(2,1)} %get-tuple-element.28), channel_id=1, source_target_pairs={{0,16},{2,18},{4,20},{6,22},{8,24},{10,26},{12,28},{14,30},{16,0},... | collective-permute-start | bytes 786440 | tf_op jit(solution)/shard_map/ppermute | solution.py:19
  42.5 23.0 %collective-permute-start.19 = (bf16[512,512]{0,1:T(8,128)(2,1)S(1)}, bf16[512,512]{0,1:T(8,128)(2,1)S(1)}, u32[]{:S(2)}, u32[]{:S(2)}) collective-permute-start(bf16[512,512]{0,1:T(8,128)(2,1)S(1)} %fusion.15), channel_id=1, source_target_pairs={{0,2},{2,0},{4,6},{6,4},{8,10},{10,8},{12,14},{14,12},{16,18},{18,... | collective-permute-start | bytes 1572872 | tf_op jit(solution)/shard_map/ppermute | solution.py:19
  44.2 23.1 %collective-permute-start.23 = (bf16[512,512]{0,1:T(8,128)(2,1)S(1)}, bf16[512,512]{0,1:T(8,128)(2,1)S(1)}, u32[]{:S(2)}, u32[]{:S(2)}) collective-permute-start(bf16[512,512]{0,1:T(8,128)(2,1)S(1)} %fusion.11), channel_id=1, source_target_pairs={{0,2},{2,0},{4,6},{6,4},{8,10},{10,8},{12,14},{14,12},{16,18},{18,... | collective-permute-start | bytes 1572872 | tf_op jit(solution)/shard_map/ppermute | solution.py:19
  45.2 12.6 %collective-permute-start.4 = (f32[128,512]{1,0:T(8,128)S(1)}, f32[128,512]{1,0:T(8,128)S(1)}, u32[]{:S(2)}, u32[]{:S(2)}) collective-permute-start(f32[128,512]{1,0:T(8,128)S(1)} %constant_dynamic-slice_fusion), channel_id=1, source_target_pairs={{0,1},{1,0},{2,3},{3,2},{4,5},{5,4},{6,7},{7,6},{8,9},{9,8},{10,11... | collective-permute-start | bytes 786440 | tf_op jit(solution)/shard_map/ppermute | solution.py:91
  55.6 13.2 %collective-permute-start.27 = (bf16[512,512]{0,1:T(8,128)(2,1)S(1)}, bf16[512,512]{0,1:T(8,128)(2,1)S(1)}, u32[]{:S(2)}, u32[]{:S(2)}) collective-permute-start(bf16[512,512]{0,1:T(8,128)(2,1)S(1)} %fusion.7), channel_id=1, source_target_pairs={{0,2},{2,0},{4,6},{6,4},{8,10},{10,8},{12,14},{14,12},{16,18},{18,... | collective-permute-start | bytes 1572872 | tf_op jit(solution)/shard_map/ppermute | solution.py:19
  56.2 8.8 %collective-permute-start.9 = (bf16[128,1024]{1,0:T(8,128)(2,1)S(1)}, bf16[128,1024]{1,0:T(8,128)(2,1)S(1)}, u32[]{:S(2)}, u32[]{:S(2)}) collective-permute-start(bf16[128,1024]{1,0:T(8,128)(2,1)S(1)} %fusion.1), channel_id=1, source_target_pairs={{0,1},{1,0},{2,3},{3,2},{4,5},{5,4},{6,7},{7,6},{8,9},{9,8},{10,11... | collective-permute-start | bytes 786440 | tf_op jit(solution)/shard_map/ppermute | solution.py:91
  57.8 13.7 %collective-permute-start.10 = (bf16[512,512]{0,1:T(8,128)(2,1)S(1)}, bf16[512,512]{0,1:T(8,128)(2,1)S(1)}, u32[]{:S(2)}, u32[]{:S(2)}) collective-permute-start(bf16[512,512]{0,1:T(8,128)(2,1)S(1)} %fusion.19), channel_id=1, source_target_pairs={{0,2},{2,0},{4,6},{6,4},{8,10},{10,8},{12,14},{14,12},{16,18},{18,... | collective-permute-start | bytes 1572872 | tf_op jit(solution)/shard_map/ppermute | solution.py:19
  65.7 8.8 %collective-permute-start.20 = (bf16[256,512]{0,1:T(8,128)(2,1)S(1)}, bf16[256,512]{0,1:T(8,128)(2,1)S(1)}, u32[]{:S(2)}, u32[]{:S(2)}) collective-permute-start(bf16[256,512]{0,1:T(8,128)(2,1)S(1)} %dynamic-slice_convert_fusion.2), channel_id=1, source_target_pairs={{0,4},{2,6},{4,0},{6,2},{8,12},{10,14},{12,8},{14,10},{16,20},{18,... | collective-permute-start | bytes 786440 | tf_op jit(solution)/shard_map/ppermute | solution.py:19
  67.5 9.2 %collective-permute-start.24 = (bf16[256,512]{0,1:T(8,128)(2,1)S(1)}, bf16[256,512]{0,1:T(8,128)(2,1)S(1)}, u32[]{:S(2)}, u32[]{:S(2)}) collective-permute-start(bf16[256,512]{0,1:T(8,128)(2,1)S(1)} %dynamic-slice_convert_fusion.1), channel_id=1, source_target_pairs={{0,8},{2,10},{4,12},{6,14},{8,0},{10,2},{12,4},{14,6},{16,24},{18,... | collective-permute-start | bytes 786440 | tf_op jit(solution)/shard_map/ppermute | solution.py:19
  69.8 32.1 %collective-permute-start.28 = (bf16[256,512]{0,1:T(8,128)(2,1)}, bf16[256,512]{0,1:T(8,128)(2,1)}, u32[]{:S(2)}, u32[]{:S(2)}) collective-permute-start(bf16[256,512]{0,1:T(8,128)(2,1)} %dynamic-slice_convert_fusion), channel_id=1, source_target_pairs={{0,8},{2,10},{4,12},{6,14},{8,0},{10,2},{12,4},{14,6},{16,24},{18,... | collective-permute-start | bytes 786440 | tf_op jit(solution)/shard_map/ppermute | solution.py:19
  73.0 30.5 %collective-permute-start.12 = (bf16[256,512]{0,1:T(8,128)(2,1)}, bf16[256,512]{0,1:T(8,128)(2,1)}, u32[]{:S(2)}, u32[]{:S(2)}) collective-permute-start(bf16[256,512]{0,1:T(8,128)(2,1)} %dynamic-slice_convert_fusion.3), channel_id=1, source_target_pairs={{0,4},{2,6},{4,0},{6,2},{8,12},{10,14},{12,8},{14,10},{16,20},{18,... | collective-permute-start | bytes 786440 | tf_op jit(solution)/shard_map/ppermute | solution.py:19
  74.6 9.8 %collective-permute-start.21 = (bf16[128,512]{0,1:T(8,128)(2,1)S(1)}, bf16[128,512]{0,1:T(8,128)(2,1)S(1)}, u32[]{:S(2)}, u32[]{:S(2)}) collective-permute-start(bf16[128,512]{0,1:T(8,128)(2,1)S(1)} %dynamic-slice_convert_fusion.9), channel_id=1, source_target_pairs={{0,8},{2,10},{4,12},{6,14},{8,0},{10,2},{12,4},{14,6},{16,24},{18,... | collective-permute-start | bytes 393224 | tf_op jit(solution)/shard_map/ppermute | solution.py:19
  76.9 8.9 %collective-permute-start.25 = (bf16[128,512]{0,1:T(8,128)(2,1)S(1)}, bf16[128,512]{0,1:T(8,128)(2,1)S(1)}, u32[]{:S(2)}, u32[]{:S(2)}) collective-permute-start(bf16[128,512]{0,1:T(8,128)(2,1)S(1)} %dynamic-slice_convert_fusion.7), channel_id=1, source_target_pairs={{0,4},{2,6},{4,0},{6,2},{8,12},{10,14},{12,8},{14,10},{16,20},{18,... | collective-permute-start | bytes 393224 | tf_op jit(solution)/shard_map/ppermute | solution.py:19
  84.6 11.3 %collective-permute-start.22 = (bf16[64,512]{0,1:T(8,128)(2,1)S(1)}, bf16[64,512]{0,1:T(8,128)(2,1)S(1)}, u32[]{:S(2)}, u32[]{:S(2)}) collective-permute-start(bf16[64,512]{0,1:T(8,128)(2,1)S(1)} %dynamic-slice_convert_fusion.8), channel_id=1, source_target_pairs={{0,16},{2,18},{4,20},{6,22},{8,24},{10,26},{12,28},{14,30},{16,0},... | collective-permute-start | bytes 196616 | tf_op jit(solution)/shard_map/ppermute | solution.py:19
  85.9 12.6 %collective-permute-start.26 = (bf16[64,512]{0,1:T(8,128)(2,1)S(1)}, bf16[64,512]{0,1:T(8,128)(2,1)S(1)}, u32[]{:S(2)}, u32[]{:S(2)}) collective-permute-start(bf16[64,512]{0,1:T(8,128)(2,1)S(1)} %dynamic-slice_convert_fusion.6), channel_id=1, source_target_pairs={{0,16},{2,18},{4,20},{6,22},{8,24},{10,26},{12,28},{14,30},{16,0},... | collective-permute-start | bytes 196616 | tf_op jit(solution)/shard_map/ppermute | solution.py:19
  108.5 12.3 %collective-permute-start.30 = (bf16[64,512]{0,1:T(8,128)(2,1)S(1)}, bf16[64,512]{0,1:T(8,128)(2,1)S(1)}, u32[]{:S(2)}, u32[]{:S(2)}) collective-permute-start(bf16[64,512]{0,1:T(8,128)(2,1)S(1)} %dynamic-slice_convert_fusion.4), channel_id=1, source_target_pairs={{0,16},{2,18},{4,20},{6,22},{8,24},{10,26},{12,28},{14,30},{16,0},... | collective-permute-start | bytes 196616 | tf_op jit(solution)/shard_map/ppermute | solution.py:19
  110.0 10.8 %collective-permute-start.17 = (f32[1024]{0:T(1024)S(1)}, f32[1024]{0:T(1024)S(1)}, u32[]{:S(2)}, u32[]{:S(2)}) collective-permute-start(f32[1024]{0:T(1024)S(1)} %add.199), channel_id=1, source_target_pairs={{0,16},{2,18},{4,20},{6,22},{8,24},{10,26},{12,28},{14,30},{16,0},... | collective-permute-start | bytes 12296 | tf_op jit(solution)/shard_map/ppermute | solution.py:19
  114.2 8.4 %collective-permute-start.16 = (bf16[64,512]{0,1:T(8,128)(2,1)S(1)}, bf16[64,512]{0,1:T(8,128)(2,1)S(1)}, u32[]{:S(2)}, u32[]{:S(2)}) collective-permute-start(bf16[64,512]{0,1:T(8,128)(2,1)S(1)} %dynamic-slice_convert_fusion.10), channel_id=1, source_target_pairs={{0,16},{2,18},{4,20},{6,22},{8,24},{10,26},{12,28},{14,30},{16,0},... | collective-permute-start | bytes 196616 | tf_op jit(solution)/shard_map/ppermute | solution.py:19
  (21 other events, 109.5 us)

commit v10 on v9

--- a/solution.py
+++ b/solution.py
@@ -28,19 +28,14 @@
     return shaped.transpose(axes).reshape(rows, width)
 
 
-def halving_sum(partial, axis, order, extra=None):
+def halving_step(partial, axis, bit):
     me = lax.axis_index(axis)
-    for bit in order:
-        half = partial.shape[0] // 2
-        mine = (me >> bit) & 1
-        keep = lax.dynamic_slice_in_dim(partial, mine * half, half, 0)
-        send = lax.dynamic_slice_in_dim(partial, (1 - mine) * half, half, 0)
-        got = from_partner(send.astype(jnp.bfloat16), axis, bit)
-        partial = keep + got.astype(jnp.float32)
-        if extra is not None:
-            extra = extra + from_partner(extra, axis, bit)
-            partial, extra = lax.optimization_barrier((partial, extra))
-    return partial, extra
+    half = partial.shape[0] // 2
+    mine = (me >> bit) & 1
+    keep = lax.dynamic_slice_in_dim(partial, mine * half, half, 0)
+    send = lax.dynamic_slice_in_dim(partial, (1 - mine) * half, half, 0)
+    got = from_partner(send.astype(jnp.bfloat16), axis, bit)
+    return keep + got.astype(jnp.float32)
 
 
 def split_orders(levels):
@@ -52,33 +47,54 @@
 
 def scatter_rows(pairs, axis, levels, extra=None):
     contract = (((0,), (0,)), ((), ()))
+    orders = split_orders(levels)
     chunks = []
-    for index, order in enumerate(split_orders(levels)):
-        pieces = []
+    for index, order in enumerate(orders):
         for left, right in pairs:
             cut = right.shape[1] // 2
             piece = right[:, index * cut : (index + 1) * cut]
-            pieces.append(
+            chunks.append(
                 lax.dot_general(
                     bit_major_rows(left, order), piece, contract,
                     preferred_element_type=jnp.float32,
                 )
             )
-        chunk, summed = halving_sum(
-            jnp.concatenate(pieces, axis=1), axis, order, extra if index == 0 else None
-        )
-        chunks.append(chunk)
-        if index == 0:
-            extra = summed
+    first = sum(right.shape[1] // 2 for left, right in pairs)
+    joined = jnp.concatenate(chunks, axis=1)
+    parts = None
+    for step in range(levels):
+        bit_a, bit_b = orders[0][step], orders[1][step]
+        if bit_a == bit_b:
+            if parts is not None:
+                joined = jnp.concatenate(parts, axis=1)
+                parts = None
+            (joined,), extra = halving_many([joined], [bit_a], axis, extra)
+        else:
+            if parts is None:
+                parts = [joined[:, :first], joined[:, first:]]
+            parts, extra = halving_many(parts, [bit_a, bit_b], axis, extra)
+    if parts is not None:
+        joined = jnp.concatenate(parts, axis=1)
     results = []
     offset = 0
     for left, right in pairs:
         cut = right.shape[1] // 2
         results.append(
-            jnp.concatenate([chunk[:, offset : offset + cut] for chunk in chunks], axis=1)
+            jnp.concatenate(
+                [joined[:, offset : offset + cut], joined[:, first + offset : first + offset + cut]],
+                axis=1,
+            )
         )
         offset += cut
     return results, extra
+
+
+def halving_many(parts, bits, axis, extra):
+    parts = [halving_step(part, axis, bit) for part, bit in zip(parts, bits)]
+    if extra is not None:
+        extra = extra + from_partner(extra, axis, bits[0])
+        parts, extra = lax.optimization_barrier((parts, extra))
+    return parts, extra
 
 
 def doubling_sum(value, axis, levels):

time: 127 us -> 116 us (0.913)
  local copies, waits for them, and re-layouts: 15.3 us -> 7.32 us
  waiting for transfers between devices: 44.6 us -> 40.4 us
  matrix products: 10.2 us -> 13.2 us
  other arithmetic: 11.1 us -> 8.45 us
    unnamed x33 -> x32, local copies, waits for them, and re-layouts: 8.14 us -> 4.3 us
    ppermute x3, waiting for transfers between devices: 6.69 us -> 3.69 us  [head_swap(): return lax.ppermute(value, 'head', [(0, 1), (1, 0)])]
    dot_general x8, matrix products: 2.64 us -> 5.3 us  [scatter_rows(): lax.dot_general(bit_major_rows(left, order), piece, contract, preferred_e...]
    transpose x4, local copies, waits for them, and re-layouts: 4.1 us -> 1.49 us  [bit_major_rows(): return shaped.transpose(axes).reshape(rows, width)]
    add x20 -> x16, other arithmetic: 3.56 us -> 1.54 us  [the longest x12 1.52 us: halving_step(): return keep + got.astype(jnp.float32)]
    ppermute x28 -> x24, waiting for transfers between devices: 37.9 us -> 36.7 us  [from_partner(): return lax.ppermute(value, axis, pairs)]
    ppermute x28 -> x24, starting transfers between devices: 29 us -> 29.4 us  [from_partner(): return lax.ppermute(value, axis, pairs)]
  transfers between devices with their start and end apart: 31 -> 27, of which waited for: 14 -> 13; matrix products, arithmetic and copies ran while one was open for 22% -> 19% of each run, Pallas kernels for 0% -> 0%
where the time goes in v10:
time: 116 us
  waiting for transfers between devices  40.4 us (35%)
  starting transfers between devices  34.1 us (29%)
  matrix products  13.2 us (11%)
  Pallas kernels  11 us (9%)
  other arithmetic  8.45 us (7%)
  local copies, waits for them, and re-layouts  7.32 us (6%)
  between operations  1.25 us (1%)
    ppermute x24, waiting for transfers between devices, from_partner(): return lax.ppermute(value, axis, pairs)  36.7 us
    ppermute x24, starting transfers between devices, from_partner(): return lax.ppermute(value, axis, pairs)  29.4 us
    pallas_call x1, Pallas kernels, block_attention(): pl.pallas_call(functools.partial(attention_kernel, slots, pairs), grid_sp...  11 us
    dot_general x8, matrix products, scatter_rows(): lax.dot_general(bit_major_rows(left, order), piece, contract, preferred_e...  5.3 us
    ppermute x3, starting transfers between devices, head_swap(): return lax.ppermute(value, 'head', [(0, 1), (1, 0)])  4.68 us
    unnamed x32, local copies, waits for them, and re-layouts  4.3 us
    ppermute x3, waiting for transfers between devices, head_swap(): return lax.ppermute(value, 'head', [(0, 1), (1, 0)])  3.69 us
  transfers between devices with their start and end apart: 27, of which 13 were waited for; matrix products, arithmetic and copies ran while one was open for 19% of the time, Pallas kernels for 0%

profile of v10, /device:TPU:0, one launch (start us, length us, event | category | flops | bytes accessed | tf_op | source)
XLA Modules:
  0.0 115.7 jit_solution(4482775883634279354)
XLA Ops:
  6.6 2.6 %collective-permute-start.1 = (bf16[1,128,1024]{2,1,0:T(8,128)(2,1)S(1)}, bf16[1,128,1024]{2,1,0:T(8,128)(2,1)}, u32[]{:S(2)}, u32[]{:S(2)}) collective-permute-start(bf16[1,128,1024]{2,1,0:T(8,128)(2,1)S(1)} %pad_maximum_fusion.2.refs_0_.refs_5_), channel_id=1, source_target_pairs={{0,4},{2,6},{4,0},{6,2},{8,12},{10,14},{12,8},{14,10},{16,20},{18,... | collective-permute-start | bytes 786440 | tf_op jit(solution)/shard_map/ppermute | solution.py:19
  9.2 1.6 %collective-permute-start.2 = (bf16[1,128,1024]{2,1,0:T(8,128)(2,1)S(1)}, bf16[1,128,1024]{2,1,0:T(8,128)(2,1)}, u32[]{:S(2)}, u32[]{:S(2)}) collective-permute-start(bf16[1,128,1024]{2,1,0:T(8,128)(2,1)S(1)} %pad_maximum_fusion.2.refs_0_.refs_5_), channel_id=1, source_target_pairs={{0,8},{2,10},{4,12},{6,14},{8,0},{10,2},{12,4},{14,6},{16,24},{18,... | collective-permute-start | bytes 786440 | tf_op jit(solution)/shard_map/ppermute | solution.py:19
  10.8 2.6 %collective-permute-start.3 = (bf16[1,128,1024]{2,1,0:T(8,128)(2,1)S(1)}, bf16[1,128,1024]{2,1,0:T(8,128)(2,1)}, u32[]{:S(2)}, u32[]{:S(2)}) collective-permute-start(bf16[1,128,1024]{2,1,0:T(8,128)(2,1)S(1)} %pad_maximum_fusion.2.refs_0_.refs_5_), channel_id=1, source_target_pairs={{0,16},{2,18},{4,20},{6,22},{8,24},{10,26},{12,28},{14,30},{16,0},... | collective-permute-start | bytes 786440 | tf_op jit(solution)/shard_map/ppermute | solution.py:19
  17.8 2.1 %fusion.3.g_ref = bf16[1,128,512]{2,1,0:T(8,128)(2,1)} fusion(bf16[128,1024]{1,0:T(8,128)(2,1)} %param.15, bf16[512,1024]{1,0:T(8,128)(2,1)S(1)} %copy-done), kind=kOutput, calls=%fused_computation.16 | convolution fusion | flops 134283264 | bytes 1441792 | tf_op jit(solution)/shard_map/dot_general | solution.py:239
  19.9 3.3 %collective-permute-done.2.refs_3_.refs_8_ = bf16[1,128,1024]{2,1,0:T(8,128)(2,1)} collective-permute-done((bf16[1,128,1024]{2,1,0:T(8,128)(2,1)S(1)}, bf16[1,128,1024]{2,1,0:T(8,128)(2,1)}, u32[]{:S(2)}, u32[]{:S(2)}) %collective-permute-start.2) | collective-permute-done | bytes 262176 | tf_op jit(solution)/shard_map/ppermute | solution.py:19
  23.2 2.4 %collective-permute-done.3.refs_4_.refs_9_ = bf16[1,128,1024]{2,1,0:T(8,128)(2,1)} collective-permute-done((bf16[1,128,1024]{2,1,0:T(8,128)(2,1)S(1)}, bf16[1,128,1024]{2,1,0:T(8,128)(2,1)}, u32[]{:S(2)}, u32[]{:S(2)}) %collective-permute-start.3) | collective-permute-done | bytes 262176 | tf_op jit(solution)/shard_map/ppermute | solution.py:19
  25.6 11.0 %shard_map.135 = (bf16[1,128,512]{2,1,0:T(8,128)(2,1)}, bf16[1,128,512]{2,1,0:T(8,128)(2,1)}, bf16[1,128,1024]{2,1,0:T(8,128)(2,1)}, bf16[1,128,1024]{2,1,0:T(8,...) custom-call(s32[5]{0:T(128)} %add_bitcast_fusion.active_ref, ...), custom_call_target="tpu_custom_call" | custom-call | tf_op jit(solution)/shard_map/pallas_call | solution.py:197
  37.7 2.6 %collective-permute-start.8 = (bf16[1,128,1024]{2,1,0:T(8,128)(2,1)}, bf16[1,128,1024]{2,1,0:T(8,128)(2,1)S(1)}, u32[]{:S(2)}, u32[]{:S(2)}) collective-permute-start(bf16[1,128,1024]{2,1,0:T(8,128)(2,1)} %get-tuple-element.30), channel_id=1, source_target_pairs={{0,16},{2,18},{4,20},{6,22},{8,24},{10,26},{12,28},{14,30},{16,0},... | collective-permute-start | bytes 786440 | tf_op jit(solution)/shard_map/ppermute | solution.py:19
  45.5 1.6 %collective-permute-start.4 = (f32[128,512]{1,0:T(8,128)S(1)}, f32[128,512]{1,0:T(8,128)S(1)}, u32[]{:S(2)}, u32[]{:S(2)}) collective-permute-start(f32[128,512]{1,0:T(8,128)S(1)} %constant_dynamic-slice_fusion), channel_id=1, source_target_pairs={{0,1},{1,0},{2,3},{3,2},{4,5},{5,4},{6,7},{7,6},{8,9},{9,8},{10,11... | collective-permute-start | bytes 786440 | tf_op jit(solution)/shard_map/ppermute | solution.py:107
  47.0 4.1 %collective-permute-done.7 = bf16[1,128,1024]{2,1,0:T(8,128)(2,1)S(1)} collective-permute-done((bf16[1,128,1024]{2,1,0:T(8,128)(2,1)}, bf16[1,128,1024]{2,1,0:T(8,128)(2,1)S(1)}, u32[]{:S(2)}, u32[]{:S(2)}) %collective-permute-start.7) | collective-permute-done | bytes 262176 | tf_op jit(solution)/shard_map/ppermute | solution.py:19
  58.8 3.2 %collective-permute-done.9 = bf16[128,1024]{1,0:T(8,128)(2,1)S(1)} collective-permute-done((bf16[128,1024]{1,0:T(8,128)(2,1)S(1)}, bf16[128,1024]{1,0:T(8,128)(2,1)S(1)}, u32[]{:S(2)}, u32[]{:S(2)}) %collective-permute-start.9) | collective-permute-done | bytes 262176 | tf_op jit(solution)/shard_map/ppermute | solution.py:107
  64.0 1.8 %collective-permute-start.24 = (bf16[256,512]{0,1:T(8,128)(2,1)S(1)}, bf16[256,512]{0,1:T(8,128)(2,1)S(1)}, u32[]{:S(2)}, u32[]{:S(2)}) collective-permute-start(bf16[256,512]{0,1:T(8,128)(2,1)S(1)} %dynamic-slice_convert_fusion.2), channel_id=1, source_target_pairs={{0,8},{2,10},{4,12},{6,14},{8,0},{10,2},{12,4},{14,6},{16,24},{18,... | collective-permute-start | bytes 786440 | tf_op jit(solution)/shard_map/ppermute | solution.py:19
  65.9 1.6 %collective-permute-start.22 = (bf16[256,512]{0,1:T(8,128)(2,1)S(1)}, bf16[256,512]{0,1:T(8,128)(2,1)S(1)}, u32[]{:S(2)}, u32[]{:S(2)}) collective-permute-start(bf16[256,512]{0,1:T(8,128)(2,1)S(1)} %dynamic-slice_convert_fusion.3), channel_id=1, source_target_pairs={{0,4},{2,6},{4,0},{6,2},{8,12},{10,14},{12,8},{14,10},{16,20},{18,... | collective-permute-start | bytes 786440 | tf_op jit(solution)/shard_map/ppermute | solution.py:19
  69.0 1.6 %collective-permute-start.12 = (bf16[256,512]{0,1:T(8,128)(2,1)S(1)}, bf16[256,512]{0,1:T(8,128)(2,1)S(1)}, u32[]{:S(2)}, u32[]{:S(2)}) collective-permute-start(bf16[256,512]{0,1:T(8,128)(2,1)S(1)} %dynamic-slice_convert_fusion.6), channel_id=1, source_target_pairs={{0,4},{2,6},{4,0},{6,2},{8,12},{10,14},{12,8},{14,10},{16,20},{18,... | collective-permute-start | bytes 786440 | tf_op jit(solution)/shard_map/ppermute | solution.py:19
  70.6 2.6 %collective-permute-done.24 = bf16[256,512]{0,1:T(8,128)(2,1)S(1)} collective-permute-done((bf16[256,512]{0,1:T(8,128)(2,1)S(1)}, bf16[256,512]{0,1:T(8,128)(2,1)S(1)}, u32[]{:S(2)}, u32[]{:S(2)}) %collective-permute-start.24) | collective-permute-done | bytes 262176 | tf_op jit(solution)/shard_map/ppermute | solution.py:19
  73.4 1.6 %collective-permute-start.25 = (bf16[128,512]{0,1:T(8,128)(2,1)S(1)}, bf16[128,512]{0,1:T(8,128)(2,1)S(1)}, u32[]{:S(2)}, u32[]{:S(2)}) collective-permute-start(bf16[128,512]{0,1:T(8,128)(2,1)S(1)} %dynamic-slice_convert_fusion.7), channel_id=1, source_target_pairs={{0,4},{2,6},{4,0},{6,2},{8,12},{10,14},{12,8},{14,10},{16,20},{18,... | collective-permute-start | bytes 393224 | tf_op jit(solution)/shard_map/ppermute | solution.py:19
  75.2 1.6 %collective-permute-start.23 = (bf16[128,512]{0,1:T(8,128)(2,1)S(1)}, bf16[128,512]{0,1:T(8,128)(2,1)S(1)}, u32[]{:S(2)}, u32[]{:S(2)}) collective-permute-start(bf16[128,512]{0,1:T(8,128)(2,1)S(1)} %dynamic-slice_convert_fusion.8), channel_id=1, source_target_pairs={{0,8},{2,10},{4,12},{6,14},{8,0},{10,2},{12,4},{14,6},{16,24},{18,... | collective-permute-start | bytes 393224 | tf_op jit(solution)/shard_map/ppermute | solution.py:19
  76.9 5.8 %collective-permute-done.25 = bf16[128,512]{0,1:T(8,128)(2,1)S(1)} collective-permute-done((bf16[128,512]{0,1:T(8,128)(2,1)S(1)}, bf16[128,512]{0,1:T(8,128)(2,1)S(1)}, u32[]{:S(2)}, u32[]{:S(2)}) %collective-permute-start.25) | collective-permute-done | bytes 131104 | tf_op jit(solution)/shard_map/ppermute | solution.py:19
  82.9 2.4 %collective-permute-start.26 = (bf16[64,1024]{0,1:T(8,128)(2,1)S(1)}, bf16[64,1024]{0,1:T(8,128)(2,1)S(1)}, u32[]{:S(2)}, u32[]{:S(2)}) collective-permute-start(bf16[64,1024]{0,1:T(8,128)(2,1)S(1)} %fusion.9), channel_id=1, source_target_pairs={{0,16},{2,18},{4,20},{6,22},{8,24},{10,26},{12,28},{14,30},{16,0},... | collective-permute-start | bytes 393224 | tf_op jit(solution)/shard_map/ppermute | solution.py:19
  85.8 1.6 %collective-permute-start.16 = (bf16[128,512]{0,1:T(8,128)(2,1)S(1)}, bf16[128,512]{0,1:T(8,128)(2,1)S(1)}, u32[]{:S(2)}, u32[]{:S(2)}) collective-permute-start(bf16[128,512]{0,1:T(8,128)(2,1)S(1)} %dynamic-slice_convert_fusion.9), channel_id=1, source_target_pairs={{0,4},{2,6},{4,0},{6,2},{8,12},{10,14},{12,8},{14,10},{16,20},{18,... | collective-permute-start | bytes 393224 | tf_op jit(solution)/shard_map/ppermute | solution.py:19
  87.4 1.8 %collective-permute-start.15 = (bf16[128,512]{0,1:T(8,128)(2,1)S(1)}, bf16[128,512]{0,1:T(8,128)(2,1)S(1)}, u32[]{:S(2)}, u32[]{:S(2)}) collective-permute-start(bf16[128,512]{0,1:T(8,128)(2,1)S(1)} %dynamic-slice_convert_fusion.10), channel_id=1, source_target_pairs={{0,8},{2,10},{4,12},{6,14},{8,0},{10,2},{12,4},{14,6},{16,24},{18,... | collective-permute-start | bytes 393224 | tf_op jit(solution)/shard_map/ppermute | solution.py:19
  89.2 7.5 %collective-permute-done.26 = bf16[64,1024]{0,1:T(8,128)(2,1)S(1)} collective-permute-done((bf16[64,1024]{0,1:T(8,128)(2,1)S(1)}, bf16[64,1024]{0,1:T(8,128)(2,1)S(1)}, u32[]{:S(2)}, u32[]{:S(2)}) %collective-permute-start.26) | collective-permute-done | bytes 131104 | tf_op jit(solution)/shard_map/ppermute | solution.py:19
  97.5 3.0 %collective-permute-start.19 = (f32[1024]{0:T(1024)S(1)}, f32[1024]{0:T(1024)S(1)}, u32[]{:S(2)}, u32[]{:S(2)}) collective-permute-start(f32[1024]{0:T(1024)S(1)} %add.185), channel_id=1, source_target_pairs={{0,16},{2,18},{4,20},{6,22},{8,24},{10,26},{12,28},{14,30},{16,0},... | collective-permute-start | bytes 12296 | tf_op jit(solution)/shard_map/ppermute | solution.py:19
  102.0 9.1 %collective-permute-done.19 = f32[1024]{0:T(1024)S(1)} collective-permute-done((f32[1024]{0:T(1024)S(1)}, f32[1024]{0:T(1024)S(1)}, u32[]{:S(2)}, u32[]{:S(2)}) %collective-permute-start.19) | collective-permute-done | bytes 4128 | tf_op jit(solution)/shard_map/ppermute | solution.py:19
  (133 shorter events, 35.6 us)
Async XLA Ops:
  6.1 13.8 %collective-permute-start = (bf16[1,128,1024]{2,1,0:T(8,128)(2,1)S(1)}, bf16[1,128,1024]{2,1,0:T(8,128)(2,1)S(1)}, u32[]{:S(2)}, u32[]{:S(2)}) collective-permute-start(bf16[1,128,1024]{2,1,0:T(8,128)(2,1)S(1)} %pad_maximum_fusion.2.refs_0_.refs_5_), channel_id=1, source_target_pairs={{0,2},{2,0},{4,6},{6,4},{8,10},{10,8},{12,14},{14,12},{16,18},{18,... | collective-permute-start | bytes 786440 | tf_op jit(solution)/shard_map/ppermute | solution.py:19
  6.6 13.3 %collective-permute-start.1 = (bf16[1,128,1024]{2,1,0:T(8,128)(2,1)S(1)}, bf16[1,128,1024]{2,1,0:T(8,128)(2,1)}, u32[]{:S(2)}, u32[]{:S(2)}) collective-permute-start(bf16[1,128,1024]{2,1,0:T(8,128)(2,1)S(1)} %pad_maximum_fusion.2.refs_0_.refs_5_), channel_id=1, source_target_pairs={{0,4},{2,6},{4,0},{6,2},{8,12},{10,14},{12,8},{14,10},{16,20},{18,... | collective-permute-start | bytes 786440 | tf_op jit(solution)/shard_map/ppermute | solution.py:19
  9.2 14.0 %collective-permute-start.2 = (bf16[1,128,1024]{2,1,0:T(8,128)(2,1)S(1)}, bf16[1,128,1024]{2,1,0:T(8,128)(2,1)}, u32[]{:S(2)}, u32[]{:S(2)}) collective-permute-start(bf16[1,128,1024]{2,1,0:T(8,128)(2,1)S(1)} %pad_maximum_fusion.2.refs_0_.refs_5_), channel_id=1, source_target_pairs={{0,8},{2,10},{4,12},{6,14},{8,0},{10,2},{12,4},{14,6},{16,24},{18,... | collective-permute-start | bytes 786440 | tf_op jit(solution)/shard_map/ppermute | solution.py:19
  10.8 14.8 %collective-permute-start.3 = (bf16[1,128,1024]{2,1,0:T(8,128)(2,1)S(1)}, bf16[1,128,1024]{2,1,0:T(8,128)(2,1)}, u32[]{:S(2)}, u32[]{:S(2)}) collective-permute-start(bf16[1,128,1024]{2,1,0:T(8,128)(2,1)S(1)} %pad_maximum_fusion.2.refs_0_.refs_5_), channel_id=1, source_target_pairs={{0,16},{2,18},{4,20},{6,22},{8,24},{10,26},{12,28},{14,30},{16,0},... | collective-permute-start | bytes 786440 | tf_op jit(solution)/shard_map/ppermute | solution.py:19
  36.6 8.9 %collective-permute-start.5 = (bf16[1,128,1024]{2,1,0:T(8,128)(2,1)}, bf16[1,128,1024]{2,1,0:T(8,128)(2,1)S(1)}, u32[]{:S(2)}, u32[]{:S(2)}) collective-permute-start(bf16[1,128,1024]{2,1,0:T(8,128)(2,1)} %get-tuple-element.27), channel_id=1, source_target_pairs={{0,2},{2,0},{4,6},{6,4},{8,10},{10,8},{12,14},{14,12},{16,18},{18,... | collective-permute-start | bytes 786440 | tf_op jit(solution)/shard_map/ppermute | solution.py:19
  36.6 10.4 %collective-permute-start.6 = (bf16[1,128,1024]{2,1,0:T(8,128)(2,1)}, bf16[1,128,1024]{2,1,0:T(8,128)(2,1)S(1)}, u32[]{:S(2)}, u32[]{:S(2)}) collective-permute-start(bf16[1,128,1024]{2,1,0:T(8,128)(2,1)} %get-tuple-element.28), channel_id=1, source_target_pairs={{0,4},{2,6},{4,0},{6,2},{8,12},{10,14},{12,8},{14,10},{16,20},{18,... | collective-permute-start | bytes 786440 | tf_op jit(solution)/shard_map/ppermute | solution.py:19
  37.2 13.9 %collective-permute-start.7 = (bf16[1,128,1024]{2,1,0:T(8,128)(2,1)}, bf16[1,128,1024]{2,1,0:T(8,128)(2,1)S(1)}, u32[]{:S(2)}, u32[]{:S(2)}) collective-permute-start(bf16[1,128,1024]{2,1,0:T(8,128)(2,1)} %get-tuple-element.29), channel_id=1, source_target_pairs={{0,8},{2,10},{4,12},{6,14},{8,0},{10,2},{12,4},{14,6},{16,24},{18,... | collective-permute-start | bytes 786440 | tf_op jit(solution)/shard_map/ppermute | solution.py:19
  37.7 14.9 %collective-permute-start.8 = (bf16[1,128,1024]{2,1,0:T(8,128)(2,1)}, bf16[1,128,1024]{2,1,0:T(8,128)(2,1)S(1)}, u32[]{:S(2)}, u32[]{:S(2)}) collective-permute-start(bf16[1,128,1024]{2,1,0:T(8,128)(2,1)} %get-tuple-element.30), channel_id=1, source_target_pairs={{0,16},{2,18},{4,20},{6,22},{8,24},{10,26},{12,28},{14,30},{16,0},... | collective-permute-start | bytes 786440 | tf_op jit(solution)/shard_map/ppermute | solution.py:19
  45.0 18.5 %collective-permute-start.21 = (bf16[512,1024]{0,1:T(8,128)(2,1)S(1)}, bf16[512,1024]{0,1:T(8,128)(2,1)S(1)}, u32[]{:S(2)}, u32[]{:S(2)}) collective-permute-start(bf16[512,1024]{0,1:T(8,128)(2,1)S(1)} %dynamic-slice_convert_fusion), channel_id=1, source_target_pairs={{0,2},{2,0},{4,6},{6,4},{8,10},{10,8},{12,14},{14,12},{16,18},{18,... | collective-permute-start | bytes 3145736 | tf_op jit(solution)/shard_map/ppermute | solution.py:19
  45.5 12.7 %collective-permute-start.4 = (f32[128,512]{1,0:T(8,128)S(1)}, f32[128,512]{1,0:T(8,128)S(1)}, u32[]{:S(2)}, u32[]{:S(2)}) collective-permute-start(f32[128,512]{1,0:T(8,128)S(1)} %constant_dynamic-slice_fusion), channel_id=1, source_target_pairs={{0,1},{1,0},{2,3},{3,2},{4,5},{5,4},{6,7},{7,6},{8,9},{9,8},{10,11... | collective-permute-start | bytes 786440 | tf_op jit(solution)/shard_map/ppermute | solution.py:107
  58.0 9.4 %collective-permute-start.10 = (bf16[512,1024]{0,1:T(8,128)(2,1)S(1)}, bf16[512,1024]{0,1:T(8,128)(2,1)S(1)}, u32[]{:S(2)}, u32[]{:S(2)}) collective-permute-start(bf16[512,1024]{0,1:T(8,128)(2,1)S(1)} %dynamic-slice_convert_fusion.1), channel_id=1, source_target_pairs={{0,2},{2,0},{4,6},{6,4},{8,10},{10,8},{12,14},{14,12},{16,18},{18,... | collective-permute-start | bytes 3145736 | tf_op jit(solution)/shard_map/ppermute | solution.py:19
  64.0 9.2 %collective-permute-start.24 = (bf16[256,512]{0,1:T(8,128)(2,1)S(1)}, bf16[256,512]{0,1:T(8,128)(2,1)S(1)}, u32[]{:S(2)}, u32[]{:S(2)}) collective-permute-start(bf16[256,512]{0,1:T(8,128)(2,1)S(1)} %dynamic-slice_convert_fusion.2), channel_id=1, source_target_pairs={{0,8},{2,10},{4,12},{6,14},{8,0},{10,2},{12,4},{14,6},{16,24},{18,... | collective-permute-start | bytes 786440 | tf_op jit(solution)/shard_map/ppermute | solution.py:19
  65.9 9.2 %collective-permute-start.22 = (bf16[256,512]{0,1:T(8,128)(2,1)S(1)}, bf16[256,512]{0,1:T(8,128)(2,1)S(1)}, u32[]{:S(2)}, u32[]{:S(2)}) collective-permute-start(bf16[256,512]{0,1:T(8,128)(2,1)S(1)} %dynamic-slice_convert_fusion.3), channel_id=1, source_target_pairs={{0,4},{2,6},{4,0},{6,2},{8,12},{10,14},{12,8},{14,10},{16,20},{18,... | collective-permute-start | bytes 786440 | tf_op jit(solution)/shard_map/ppermute | solution.py:19
  67.8 9.0 %collective-permute-start.14 = (f32[1024]{0:T(1024)S(1)}, f32[1024]{0:T(1024)S(1)}, u32[]{:S(2)}, u32[]{:S(2)}) collective-permute-start(f32[1024]{0:T(1024)S(1)} %add.171), channel_id=1, source_target_pairs={{0,4},{2,6},{4,0},{6,2},{8,12},{10,14},{12,8},{14,10},{16,20},{18,... | collective-permute-start | bytes 12296 | tf_op jit(solution)/shard_map/ppermute | solution.py:19
  68.6 16.6 %collective-permute-start.13 = (bf16[256,512]{0,1:T(8,128)(2,1)S(1)}, bf16[256,512]{0,1:T(8,128)(2,1)S(1)}, u32[]{:S(2)}, u32[]{:S(2)}) collective-permute-start(bf16[256,512]{0,1:T(8,128)(2,1)S(1)} %dynamic-slice_convert_fusion.5), channel_id=1, source_target_pairs={{0,8},{2,10},{4,12},{6,14},{8,0},{10,2},{12,4},{14,6},{16,24},{18,... | collective-permute-start | bytes 786440 | tf_op jit(solution)/shard_map/ppermute | solution.py:19
  69.0 16.3 %collective-permute-start.12 = (bf16[256,512]{0,1:T(8,128)(2,1)S(1)}, bf16[256,512]{0,1:T(8,128)(2,1)S(1)}, u32[]{:S(2)}, u32[]{:S(2)}) collective-permute-start(bf16[256,512]{0,1:T(8,128)(2,1)S(1)} %dynamic-slice_convert_fusion.6), channel_id=1, source_target_pairs={{0,4},{2,6},{4,0},{6,2},{8,12},{10,14},{12,8},{14,10},{16,20},{18,... | collective-permute-start | bytes 786440 | tf_op jit(solution)/shard_map/ppermute | solution.py:19
  73.4 9.3 %collective-permute-start.25 = (bf16[128,512]{0,1:T(8,128)(2,1)S(1)}, bf16[128,512]{0,1:T(8,128)(2,1)S(1)}, u32[]{:S(2)}, u32[]{:S(2)}) collective-permute-start(bf16[128,512]{0,1:T(8,128)(2,1)S(1)} %dynamic-slice_convert_fusion.7), channel_id=1, source_target_pairs={{0,4},{2,6},{4,0},{6,2},{8,12},{10,14},{12,8},{14,10},{16,20},{18,... | collective-permute-start | bytes 393224 | tf_op jit(solution)/shard_map/ppermute | solution.py:19
  75.2 7.5 %collective-permute-start.23 = (bf16[128,512]{0,1:T(8,128)(2,1)S(1)}, bf16[128,512]{0,1:T(8,128)(2,1)S(1)}, u32[]{:S(2)}, u32[]{:S(2)}) collective-permute-start(bf16[128,512]{0,1:T(8,128)(2,1)S(1)} %dynamic-slice_convert_fusion.8), channel_id=1, source_target_pairs={{0,8},{2,10},{4,12},{6,14},{8,0},{10,2},{12,4},{14,6},{16,24},{18,... | collective-permute-start | bytes 393224 | tf_op jit(solution)/shard_map/ppermute | solution.py:19
  82.9 13.8 %collective-permute-start.26 = (bf16[64,1024]{0,1:T(8,128)(2,1)S(1)}, bf16[64,1024]{0,1:T(8,128)(2,1)S(1)}, u32[]{:S(2)}, u32[]{:S(2)}) collective-permute-start(bf16[64,1024]{0,1:T(8,128)(2,1)S(1)} %fusion.9), channel_id=1, source_target_pairs={{0,16},{2,18},{4,20},{6,22},{8,24},{10,26},{12,28},{14,30},{16,0},... | collective-permute-start | bytes 393224 | tf_op jit(solution)/shard_map/ppermute | solution.py:19
  85.4 11.5 %collective-permute-start.17 = (f32[1024]{0:T(1024)S(1)}, f32[1024]{0:T(1024)S(1)}, u32[]{:S(2)}, u32[]{:S(2)}) collective-permute-start(f32[1024]{0:T(1024)S(1)} %add.178), channel_id=1, source_target_pairs={{0,8},{2,10},{4,12},{6,14},{8,0},{10,2},{12,4},{14,6},{16,24},{18,... | collective-permute-start | bytes 12296 | tf_op jit(solution)/shard_map/ppermute | solution.py:19
  85.8 11.1 %collective-permute-start.16 = (bf16[128,512]{0,1:T(8,128)(2,1)S(1)}, bf16[128,512]{0,1:T(8,128)(2,1)S(1)}, u32[]{:S(2)}, u32[]{:S(2)}) collective-permute-start(bf16[128,512]{0,1:T(8,128)(2,1)S(1)} %dynamic-slice_convert_fusion.9), channel_id=1, source_target_pairs={{0,4},{2,6},{4,0},{6,2},{8,12},{10,14},{12,8},{14,10},{16,20},{18,... | collective-permute-start | bytes 393224 | tf_op jit(solution)/shard_map/ppermute | solution.py:19
  87.4 9.7 %collective-permute-start.15 = (bf16[128,512]{0,1:T(8,128)(2,1)S(1)}, bf16[128,512]{0,1:T(8,128)(2,1)S(1)}, u32[]{:S(2)}, u32[]{:S(2)}) collective-permute-start(bf16[128,512]{0,1:T(8,128)(2,1)S(1)} %dynamic-slice_convert_fusion.10), channel_id=1, source_target_pairs={{0,8},{2,10},{4,12},{6,14},{8,0},{10,2},{12,4},{14,6},{16,24},{18,... | collective-permute-start | bytes 393224 | tf_op jit(solution)/shard_map/ppermute | solution.py:19
  97.3 13.8 %collective-permute-start.18 = (bf16[64,1024]{0,1:T(8,128)(2,1)S(1)}, bf16[64,1024]{0,1:T(8,128)(2,1)S(1)}, u32[]{:S(2)}, u32[]{:S(2)}) collective-permute-start(bf16[64,1024]{0,1:T(8,128)(2,1)S(1)} %dynamic-slice_convert_fusion.4), channel_id=1, source_target_pairs={{0,16},{2,18},{4,20},{6,22},{8,24},{10,26},{12,28},{14,30},{16,0},... | collective-permute-start | bytes 393224 | tf_op jit(solution)/shard_map/ppermute | solution.py:19
  97.5 13.7 %collective-permute-start.19 = (f32[1024]{0:T(1024)S(1)}, f32[1024]{0:T(1024)S(1)}, u32[]{:S(2)}, u32[]{:S(2)}) collective-permute-start(f32[1024]{0:T(1024)S(1)} %add.185), channel_id=1, source_target_pairs={{0,16},{2,18},{4,20},{6,22},{8,24},{10,26},{12,28},{14,30},{16,0},... | collective-permute-start | bytes 12296 | tf_op jit(solution)/shard_map/ppermute | solution.py:19
  (16 other events, 147.9 us)

commit v11 on v10

--- a/solution.py
+++ b/solution.py
@@ -264,10 +264,6 @@
         grad_value = grad_value + returned[bit][1].astype(jnp.float32)
     grad_key = grad_key.astype(jnp.bfloat16).reshape(node_rows, columns)
     grad_value = grad_value.astype(jnp.bfloat16).reshape(node_rows, columns)
-    (w_out_rows, w_query_grad), _ = scatter_rows(
-        [(cotangent, attended), (normed, grad_query)], "graph", graph_levels
-    )
-    w_out_grad = w_out_rows.T
     feature_terms = (
         jnp.dot(grad_query, w_query.T, preferred_element_type=jnp.float32)
         + jnp.dot(grad_key, w_key.T, preferred_element_type=jnp.float32)
@@ -275,9 +271,11 @@
     )
     low_terms = feature_terms.astype(jnp.bfloat16)
     gain_terms = jnp.sum(low_terms.astype(jnp.float32) * wide_nodes * inverse, axis=0)
-    (w_key_grad, w_value_grad), gain_part = scatter_rows(
-        [(normed, grad_key), (normed, grad_value)], "graph", graph_levels, gain_terms
-    )
+    (w_out_rows, w_query_grad, w_key_grad, w_value_grad), gain_part = scatter_rows(
+        [(cotangent, attended), (normed, grad_query), (normed, grad_key), (normed, grad_value)],
+        "graph", graph_levels, gain_terms,
+    )
+    w_out_grad = w_out_rows.T
     gain_grad = gain_part + head_swap(gain_part)
     grad_normed = low_terms.astype(jnp.float32) + head_swap(low_terms).astype(jnp.float32)
     scaled = grad_normed * gain

time: 116 us -> 134 us (1.16)
  waiting for transfers between devices: 40.4 us -> 57.6 us
  starting transfers between devices: 34.1 us -> 24.9 us
  local copies, waits for them, and re-layouts: 7.32 us -> 13.1 us
  other arithmetic: 8.45 us -> 12.6 us
    ppermute x24 -> x18, waiting for transfers between devices: 36.7 us -> 50.3 us  [from_partner(): return lax.ppermute(value, axis, pairs)]
    ppermute x24 -> x18, starting transfers between devices: 29.4 us -> 20.2 us  [from_partner(): return lax.ppermute(value, axis, pairs)]
    unnamed x32 -> x42, local copies, waits for them, and re-layouts: 4.3 us -> 9.39 us
    add x12 -> x6, other arithmetic: 1.52 us -> 5.86 us  [halving_step(): return keep + got.astype(jnp.float32)]
    ppermute x3, waiting for transfers between devices: 3.69 us -> 7.21 us  [head_swap(): return lax.ppermute(value, 'head', [(0, 1), (1, 0)])]
  transfers between devices with their start and end apart: 27 -> 21, of which waited for: 13 -> 12; matrix products, arithmetic and copies ran while one was open for 19% -> 14% of each run, Pallas kernels for 0% -> 0%
where the time goes in v11:
time: 134 us
  waiting for transfers between devices  57.6 us (43%)
  starting transfers between devices  24.9 us (19%)
  matrix products  13.5 us (10%)
  local copies, waits for them, and re-layouts  13.1 us (10%)
  other arithmetic  12.6 us (9%)
  Pallas kernels  11 us (8%)
    ppermute x18, waiting for transfers between devices, from_partner(): return lax.ppermute(value, axis, pairs)  50.3 us
    ppermute x18, starting transfers between devices, from_partner(): return lax.ppermute(value, axis, pairs)  20.2 us
    pallas_call x1, Pallas kernels, block_attention(): pl.pallas_call(functools.partial(attention_kernel, slots, pairs), grid_sp...  11 us
    unnamed x42, local copies, waits for them, and re-layouts  9.39 us
    ppermute x3, waiting for transfers between devices, head_swap(): return lax.ppermute(value, 'head', [(0, 1), (1, 0)])  7.21 us
    add x6, other arithmetic, halving_step(): return keep + got.astype(jnp.float32)  5.86 us
    dot_general x8, matrix products, scatter_rows(): lax.dot_general(bit_major_rows(left, order), piece, contract, preferred_e...  5.39 us
    ppermute x3, starting transfers between devices, head_swap(): return lax.ppermute(value, 'head', [(0, 1), (1, 0)])  4.65 us
  transfers between devices with their start and end apart: 21, of which 12 were waited for; matrix products, arithmetic and copies ran while one was open for 14% of the time, Pallas kernels for 0%

profile of v11, /device:TPU:0, one launch (start us, length us, event | category | flops | bytes accessed | tf_op | source)
XLA Modules:
  0.0 133.7 jit_solution(2570763194553763092)
XLA Ops:
  3.3 1.5 %fusion.7 = bf16[1,128,512]{2,1,0:T(8,128)(2,1)S(1)} fusion(bf16[128,1024]{1,0:T(8,128)(2,1)S(1)} %fusion.10, bf16[1024,512]{1,0:T(8,128)(2,1)} %param.12), kind=kOutput, calls=%fused_computation.22 | convolution fusion | flops 134283264 | bytes 1441792 | tf_op jit(solution)/shard_map/dot_general | solution.py:225
  5.4 2.6 %collective-permute-start.1 = (bf16[1,128,1024]{2,1,0:T(8,128)(2,1)S(1)}, bf16[1,128,1024]{2,1,0:T(8,128)(2,1)}, u32[]{:S(2)}, u32[]{:S(2)}) collective-permute-start(bf16[1,128,1024]{2,1,0:T(8,128)(2,1)S(1)} %pad_maximum_fusion.refs_0_.refs_5_), channel_id=1, source_target_pairs={{0,4},{2,6},{4,0},{6,2},{8,12},{10,14},{12,8},{14,10},{16,20},{18,... | collective-permute-start | bytes 786440 | tf_op jit(solution)/shard_map/ppermute | solution.py:19
  8.0 1.6 %collective-permute-start.2 = (bf16[1,128,1024]{2,1,0:T(8,128)(2,1)S(1)}, bf16[1,128,1024]{2,1,0:T(8,128)(2,1)}, u32[]{:S(2)}, u32[]{:S(2)}) collective-permute-start(bf16[1,128,1024]{2,1,0:T(8,128)(2,1)S(1)} %pad_maximum_fusion.refs_0_.refs_5_), channel_id=1, source_target_pairs={{0,8},{2,10},{4,12},{6,14},{8,0},{10,2},{12,4},{14,6},{16,24},{18,... | collective-permute-start | bytes 786440 | tf_op jit(solution)/shard_map/ppermute | solution.py:19
  9.6 2.6 %collective-permute-start.3 = (bf16[1,128,1024]{2,1,0:T(8,128)(2,1)S(1)}, bf16[1,128,1024]{2,1,0:T(8,128)(2,1)}, u32[]{:S(2)}, u32[]{:S(2)}) collective-permute-start(bf16[1,128,1024]{2,1,0:T(8,128)(2,1)S(1)} %pad_maximum_fusion.refs_0_.refs_5_), channel_id=1, source_target_pairs={{0,16},{2,18},{4,20},{6,22},{8,24},{10,26},{12,28},{14,30},{16,0},... | collective-permute-start | bytes 786440 | tf_op jit(solution)/shard_map/ppermute | solution.py:19
  12.4 2.2 %fusion.4.q_ref = bf16[1,128,512]{2,1,0:T(8,128)(2,1)} fusion(bf16[128,1024]{1,0:T(8,128)(2,1)S(1)} %fusion.10, bf16[1024,512]{1,0:T(8,128)(2,1)} %param.10), kind=kOutput, calls=%fused_computation.19 | convolution fusion | flops 134283264 | bytes 1441792 | tf_op jit(solution)/shard_map/dot_general | solution.py:223
  18.9 3.1 %collective-permute-done.2.refs_3_.refs_8_ = bf16[1,128,1024]{2,1,0:T(8,128)(2,1)} collective-permute-done((bf16[1,128,1024]{2,1,0:T(8,128)(2,1)S(1)}, bf16[1,128,1024]{2,1,0:T(8,128)(2,1)}, u32[]{:S(2)}, u32[]{:S(2)}) %collective-permute-start.2) | collective-permute-done | bytes 262176 | tf_op jit(solution)/shard_map/ppermute | solution.py:19
  22.0 2.4 %collective-permute-done.3.refs_4_.refs_9_ = bf16[1,128,1024]{2,1,0:T(8,128)(2,1)} collective-permute-done((bf16[1,128,1024]{2,1,0:T(8,128)(2,1)S(1)}, bf16[1,128,1024]{2,1,0:T(8,128)(2,1)}, u32[]{:S(2)}, u32[]{:S(2)}) %collective-permute-start.3) | collective-permute-done | bytes 262176 | tf_op jit(solution)/shard_map/ppermute | solution.py:19
  24.4 11.0 %shard_map.135 = (bf16[1,128,512]{2,1,0:T(8,128)(2,1)}, bf16[1,128,512]{2,1,0:T(8,128)(2,1)}, bf16[1,128,1024]{2,1,0:T(8,128)(2,1)}, bf16[1,128,1024]{2,1,0:T(8,...) custom-call(s32[5]{0:T(128)} %add_bitcast_fusion.active_ref, ...), custom_call_target="tpu_custom_call" | custom-call | tf_op jit(solution)/shard_map/pallas_call | solution.py:197
  36.4 2.6 %collective-permute-start.8 = (bf16[1,128,1024]{2,1,0:T(8,128)(2,1)}, bf16[1,128,1024]{2,1,0:T(8,128)(2,1)S(1)}, u32[]{:S(2)}, u32[]{:S(2)}) collective-permute-start(bf16[1,128,1024]{2,1,0:T(8,128)(2,1)} %get-tuple-element.30), channel_id=1, source_target_pairs={{0,16},{2,18},{4,20},{6,22},{8,24},{10,26},{12,28},{14,30},{16,0},... | collective-permute-start | bytes 786440 | tf_op jit(solution)/shard_map/ppermute | solution.py:19
  41.6 2.7 %collective-permute-done.6 = bf16[1,128,1024]{2,1,0:T(8,128)(2,1)S(1)} collective-permute-done((bf16[1,128,1024]{2,1,0:T(8,128)(2,1)}, bf16[1,128,1024]{2,1,0:T(8,128)(2,1)S(1)}, u32[]{:S(2)}, u32[]{:S(2)}) %collective-permute-start.6) | collective-permute-done | bytes 262176 | tf_op jit(solution)/shard_map/ppermute | solution.py:19
  44.4 5.6 %collective-permute-done.7 = bf16[1,128,1024]{2,1,0:T(8,128)(2,1)S(1)} collective-permute-done((bf16[1,128,1024]{2,1,0:T(8,128)(2,1)}, bf16[1,128,1024]{2,1,0:T(8,128)(2,1)S(1)}, u32[]{:S(2)}, u32[]{:S(2)}) %collective-permute-start.7) | collective-permute-done | bytes 262176 | tf_op jit(solution)/shard_map/ppermute | solution.py:19
  55.4 3.3 %copy-done.1 = f32[1024,2048]{0,1:T(8,128)} copy-done((f32[1024,2048]{0,1:T(8,128)}, f32[1024,2048]{0,1:T(8,128)S(1)}, u32[]{:S(2)}) %copy-start.1) | copy-done | bytes 8388632
  60.6 1.6 %collective-permute-start.9 = (bf16[128,1024]{1,0:T(8,128)(2,1)S(1)}, bf16[128,1024]{1,0:T(8,128)(2,1)S(1)}, u32[]{:S(2)}, u32[]{:S(2)}) collective-permute-start(bf16[128,1024]{1,0:T(8,128)(2,1)S(1)} %fusion.3), channel_id=1, source_target_pairs={{0,1},{1,0},{2,3},{3,2},{4,5},{5,4},{6,7},{7,6},{8,9},{9,8},{10,11... | collective-permute-start | bytes 786440 | tf_op jit(solution)/shard_map/ppermute | solution.py:107
  62.1 7.2 %collective-permute-done.9 = bf16[128,1024]{1,0:T(8,128)(2,1)S(1)} collective-permute-done((bf16[128,1024]{1,0:T(8,128)(2,1)S(1)}, bf16[128,1024]{1,0:T(8,128)(2,1)S(1)}, u32[]{:S(2)}, u32[]{:S(2)}) %collective-permute-start.9) | collective-permute-done | bytes 262176 | tf_op jit(solution)/shard_map/ppermute | solution.py:107
  71.2 3.7 %convert_add_fusion = f32[512,2048]{0,1:T(8,128)S(1)} fusion(bf16[512,2048]{0,1:T(8,128)(2,1)} %collective-permute-done.10, f32[1024,2048]{0,1:T(8,128)} %copy-done.1, s32[]{:T(128)S(6)} %select_n.44), kind=kLoop, calls=%fused_computation | loop fusion | flops 2097152 | bytes 10485764 | tf_op jit(solution)/shard_map/add | solution.py:38
  78.0 1.6 %collective-permute-start.12 = (bf16[256,1024]{0,1:T(8,128)(2,1)S(1)}, bf16[256,1024]{0,1:T(8,128)(2,1)S(1)}, u32[]{:S(2)}, u32[]{:S(2)}) collective-permute-start(bf16[256,1024]{0,1:T(8,128)(2,1)S(1)} %dynamic-slice_convert_fusion.3), channel_id=1, source_target_pairs={{0,4},{2,6},{4,0},{6,2},{8,12},{10,14},{12,8},{14,10},{16,20},{18,... | collective-permute-start | bytes 1572872 | tf_op jit(solution)/shard_map/ppermute | solution.py:19
  81.8 1.6 %collective-permute-start.4 = (f32[128,512]{1,0:T(8,128)S(1)}, f32[128,512]{1,0:T(8,128)S(1)}, u32[]{:S(2)}, u32[]{:S(2)}) collective-permute-start(f32[128,512]{1,0:T(8,128)S(1)} %constant_dynamic-slice_fusion), channel_id=1, source_target_pairs={{0,1},{1,0},{2,3},{3,2},{4,5},{5,4},{6,7},{7,6},{8,9},{9,8},{10,11... | collective-permute-start | bytes 786440 | tf_op jit(solution)/shard_map/ppermute | solution.py:107
  83.3 8.6 %collective-permute-done.14 = f32[1024]{0:T(1024)S(1)} collective-permute-done((f32[1024]{0:T(1024)S(1)}, f32[1024]{0:T(1024)S(1)}, u32[]{:S(2)}, u32[]{:S(2)}) %collective-permute-start.14) | collective-permute-done | bytes 4128 | tf_op jit(solution)/shard_map/ppermute | solution.py:19
  93.7 1.7 %collective-permute-start.17 = (f32[1024]{0:T(1024)S(1)}, f32[1024]{0:T(1024)S(1)}, u32[]{:S(2)}, u32[]{:S(2)}) collective-permute-start(f32[1024]{0:T(1024)S(1)} %add.148), channel_id=1, source_target_pairs={{0,8},{2,10},{4,12},{6,14},{8,0},{10,2},{12,4},{14,6},{16,24},{18,... | collective-permute-start | bytes 12296 | tf_op jit(solution)/shard_map/ppermute | solution.py:19
  95.4 1.6 %collective-permute-start.16 = (bf16[128,1024]{0,1:T(8,128)(2,1)S(1)}, bf16[128,1024]{0,1:T(8,128)(2,1)S(1)}, u32[]{:S(2)}, u32[]{:S(2)}) collective-permute-start(bf16[128,1024]{0,1:T(8,128)(2,1)S(1)} %dynamic-slice_convert_fusion.4), channel_id=1, source_target_pairs={{0,4},{2,6},{4,0},{6,2},{8,12},{10,14},{12,8},{14,10},{16,20},{18,... | collective-permute-start | bytes 786440 | tf_op jit(solution)/shard_map/ppermute | solution.py:19
  98.2 4.2 %collective-permute-done.16 = bf16[128,1024]{0,1:T(8,128)(2,1)S(1)} collective-permute-done((bf16[128,1024]{0,1:T(8,128)(2,1)S(1)}, bf16[128,1024]{0,1:T(8,128)(2,1)S(1)}, u32[]{:S(2)}, u32[]{:S(2)}) %collective-permute-start.16) | collective-permute-done | bytes 262176 | tf_op jit(solution)/shard_map/ppermute | solution.py:19
  104.2 1.6 %collective-permute-start.18 = (bf16[64,2048]{0,1:T(8,128)(2,1)S(1)}, bf16[64,2048]{0,1:T(8,128)(2,1)S(1)}, u32[]{:S(2)}, u32[]{:S(2)}) collective-permute-start(bf16[64,2048]{0,1:T(8,128)(2,1)S(1)} %dynamic-slice_convert_fusion.1), channel_id=1, source_target_pairs={{0,16},{2,18},{4,20},{6,22},{8,24},{10,26},{12,28},{14,30},{16,0},... | collective-permute-start | bytes 786440 | tf_op jit(solution)/shard_map/ppermute | solution.py:19
  108.1 19.8 %collective-permute-done.19 = f32[1024]{0:T(1024)S(1)} collective-permute-done((f32[1024]{0:T(1024)S(1)}, f32[1024]{0:T(1024)S(1)}, u32[]{:S(2)}, u32[]{:S(2)}) %collective-permute-start.19) | collective-permute-done | bytes 4128 | tf_op jit(solution)/shard_map/ppermute | solution.py:19
  128.4 1.5 %collective-permute-start.20 = (f32[1024]{0:T(1024)S(1)}, f32[1024]{0:T(1024)S(1)}, u32[]{:S(2)}, u32[]{:S(2)}) collective-permute-start(f32[1024]{0:T(1024)S(1)} %add.159), channel_id=1, source_target_pairs={{0,1},{1,0},{2,3},{3,2},{4,5},{5,4},{6,7},{7,6},{8,9},{9,8},{10,11... | collective-permute-start | bytes 12296 | tf_op jit(solution)/shard_map/ppermute | solution.py:107
  (115 shorter events, 36.7 us)
Async XLA Ops:
  4.9 14.0 %collective-permute-start = (bf16[1,128,1024]{2,1,0:T(8,128)(2,1)S(1)}, bf16[1,128,1024]{2,1,0:T(8,128)(2,1)}, u32[]{:S(2)}, u32[]{:S(2)}) collective-permute-start(bf16[1,128,1024]{2,1,0:T(8,128)(2,1)S(1)} %pad_maximum_fusion.refs_0_.refs_5_), channel_id=1, source_target_pairs={{0,2},{2,0},{4,6},{6,4},{8,10},{10,8},{12,14},{14,12},{16,18},{18,... | collective-permute-start | bytes 786440 | tf_op jit(solution)/shard_map/ppermute | solution.py:19
  5.4 13.5 %collective-permute-start.1 = (bf16[1,128,1024]{2,1,0:T(8,128)(2,1)S(1)}, bf16[1,128,1024]{2,1,0:T(8,128)(2,1)}, u32[]{:S(2)}, u32[]{:S(2)}) collective-permute-start(bf16[1,128,1024]{2,1,0:T(8,128)(2,1)S(1)} %pad_maximum_fusion.refs_0_.refs_5_), channel_id=1, source_target_pairs={{0,4},{2,6},{4,0},{6,2},{8,12},{10,14},{12,8},{14,10},{16,20},{18,... | collective-permute-start | bytes 786440 | tf_op jit(solution)/shard_map/ppermute | solution.py:19
  8.0 14.0 %collective-permute-start.2 = (bf16[1,128,1024]{2,1,0:T(8,128)(2,1)S(1)}, bf16[1,128,1024]{2,1,0:T(8,128)(2,1)}, u32[]{:S(2)}, u32[]{:S(2)}) collective-permute-start(bf16[1,128,1024]{2,1,0:T(8,128)(2,1)S(1)} %pad_maximum_fusion.refs_0_.refs_5_), channel_id=1, source_target_pairs={{0,8},{2,10},{4,12},{6,14},{8,0},{10,2},{12,4},{14,6},{16,24},{18,... | collective-permute-start | bytes 786440 | tf_op jit(solution)/shard_map/ppermute | solution.py:19
  9.6 14.8 %collective-permute-start.3 = (bf16[1,128,1024]{2,1,0:T(8,128)(2,1)S(1)}, bf16[1,128,1024]{2,1,0:T(8,128)(2,1)}, u32[]{:S(2)}, u32[]{:S(2)}) collective-permute-start(bf16[1,128,1024]{2,1,0:T(8,128)(2,1)S(1)} %pad_maximum_fusion.refs_0_.refs_5_), channel_id=1, source_target_pairs={{0,16},{2,18},{4,20},{6,22},{8,24},{10,26},{12,28},{14,30},{16,0},... | collective-permute-start | bytes 786440 | tf_op jit(solution)/shard_map/ppermute | solution.py:19
  17.2 36.1 %copy-start.13 = (bf16[128,2,2,2,2,64]{0,5,4,3,2,1:T(8,128)(2,1)S(1)}, bf16[128,2,2,2,2,64]{0,5,4,3,2,1:T(8,128)(2,1)}, u32[]{:S(2)}) copy-start(bf16[128,2,2,2,2,64]{0,5,4,3,2,1:T(8,128)(2,1)} %copy.23) | copy-start | bytes 786436
  35.4 6.2 %collective-permute-start.5 = (bf16[1,128,1024]{2,1,0:T(8,128)(2,1)}, bf16[1,128,1024]{2,1,0:T(8,128)(2,1)S(1)}, u32[]{:S(2)}, u32[]{:S(2)}) collective-permute-start(bf16[1,128,1024]{2,1,0:T(8,128)(2,1)} %get-tuple-element.27), channel_id=1, source_target_pairs={{0,2},{2,0},{4,6},{6,4},{8,10},{10,8},{12,14},{14,12},{16,18},{18,... | collective-permute-start | bytes 786440 | tf_op jit(solution)/shard_map/ppermute | solution.py:19
  35.4 8.9 %collective-permute-start.6 = (bf16[1,128,1024]{2,1,0:T(8,128)(2,1)}, bf16[1,128,1024]{2,1,0:T(8,128)(2,1)S(1)}, u32[]{:S(2)}, u32[]{:S(2)}) collective-permute-start(bf16[1,128,1024]{2,1,0:T(8,128)(2,1)} %get-tuple-element.28), channel_id=1, source_target_pairs={{0,4},{2,6},{4,0},{6,2},{8,12},{10,14},{12,8},{14,10},{16,20},{18,... | collective-permute-start | bytes 786440 | tf_op jit(solution)/shard_map/ppermute | solution.py:19
  36.0 13.9 %collective-permute-start.7 = (bf16[1,128,1024]{2,1,0:T(8,128)(2,1)}, bf16[1,128,1024]{2,1,0:T(8,128)(2,1)S(1)}, u32[]{:S(2)}, u32[]{:S(2)}) collective-permute-start(bf16[1,128,1024]{2,1,0:T(8,128)(2,1)} %get-tuple-element.29), channel_id=1, source_target_pairs={{0,8},{2,10},{4,12},{6,14},{8,0},{10,2},{12,4},{14,6},{16,24},{18,... | collective-permute-start | bytes 786440 | tf_op jit(solution)/shard_map/ppermute | solution.py:19
  36.4 14.9 %collective-permute-start.8 = (bf16[1,128,1024]{2,1,0:T(8,128)(2,1)}, bf16[1,128,1024]{2,1,0:T(8,128)(2,1)S(1)}, u32[]{:S(2)}, u32[]{:S(2)}) collective-permute-start(bf16[1,128,1024]{2,1,0:T(8,128)(2,1)} %get-tuple-element.30), channel_id=1, source_target_pairs={{0,16},{2,18},{4,20},{6,22},{8,24},{10,26},{12,28},{14,30},{16,0},... | collective-permute-start | bytes 786440 | tf_op jit(solution)/shard_map/ppermute | solution.py:19
  59.0 12.2 %collective-permute-start.10 = (bf16[512,2048]{0,1:T(8,128)(2,1)S(1)}, bf16[512,2048]{0,1:T(8,128)(2,1)}, u32[]{:S(2)}, u32[]{:S(2)}) collective-permute-start(bf16[512,2048]{0,1:T(8,128)(2,1)S(1)} %dynamic-slice_convert_fusion), channel_id=1, source_target_pairs={{0,2},{2,0},{4,6},{6,4},{8,10},{10,8},{12,14},{14,12},{16,18},{18,... | collective-permute-start | bytes 6291464 | tf_op jit(solution)/shard_map/ppermute | solution.py:19
  60.6 8.8 %collective-permute-start.9 = (bf16[128,1024]{1,0:T(8,128)(2,1)S(1)}, bf16[128,1024]{1,0:T(8,128)(2,1)S(1)}, u32[]{:S(2)}, u32[]{:S(2)}) collective-permute-start(bf16[128,1024]{1,0:T(8,128)(2,1)S(1)} %fusion.3), channel_id=1, source_target_pairs={{0,1},{1,0},{2,3},{3,2},{4,5},{5,4},{6,7},{7,6},{8,9},{9,8},{10,11... | collective-permute-start | bytes 786440 | tf_op jit(solution)/shard_map/ppermute | solution.py:107
  70.1 1.2 collective-permute-start.11
  77.7 14.3 %collective-permute-start.13 = (bf16[256,1024]{0,1:T(8,128)(2,1)}, bf16[256,1024]{0,1:T(8,128)(2,1)}, u32[]{:S(2)}, u32[]{:S(2)}) collective-permute-start(bf16[256,1024]{0,1:T(8,128)(2,1)} %dynamic-slice_convert_fusion.2), channel_id=1, source_target_pairs={{0,8},{2,10},{4,12},{6,14},{8,0},{10,2},{12,4},{14,6},{16,24},{18,... | collective-permute-start | bytes 1572872 | tf_op jit(solution)/shard_map/ppermute | solution.py:19
  78.0 29.2 %copy-start.8 = (bf16[128,1024]{1,0:T(8,128)(2,1)S(1)}, bf16[128,1024]{1,0:T(8,128)(2,1)}, u32[]{:S(2)}) copy-start(bf16[128,1024]{1,0:T(8,128)(2,1)} %copy-done.7) | copy-start | bytes 786436
  78.0 29.2 %copy-start.11 = (bf16[128,1024]{1,0:T(8,128)(2,1)S(1)}, bf16[128,1024]{1,0:T(8,128)(2,1)}, u32[]{:S(2)}) copy-start(bf16[128,1024]{1,0:T(8,128)(2,1)} %copy-done.10) | copy-start | bytes 786436
  78.0 15.4 %collective-permute-start.12 = (bf16[256,1024]{0,1:T(8,128)(2,1)S(1)}, bf16[256,1024]{0,1:T(8,128)(2,1)S(1)}, u32[]{:S(2)}, u32[]{:S(2)}) collective-permute-start(bf16[256,1024]{0,1:T(8,128)(2,1)S(1)} %dynamic-slice_convert_fusion.3), channel_id=1, source_target_pairs={{0,4},{2,6},{4,0},{6,2},{8,12},{10,14},{12,8},{14,10},{16,20},{18,... | collective-permute-start | bytes 1572872 | tf_op jit(solution)/shard_map/ppermute | solution.py:19
  81.2 10.7 %collective-permute-start.14 = (f32[1024]{0:T(1024)S(1)}, f32[1024]{0:T(1024)S(1)}, u32[]{:S(2)}, u32[]{:S(2)}) collective-permute-start(f32[1024]{0:T(1024)S(1)} %add.141), channel_id=1, source_target_pairs={{0,4},{2,6},{4,0},{6,2},{8,12},{10,14},{12,8},{14,10},{16,20},{18,... | collective-permute-start | bytes 12296 | tf_op jit(solution)/shard_map/ppermute | solution.py:19
  81.8 15.8 %collective-permute-start.4 = (f32[128,512]{1,0:T(8,128)S(1)}, f32[128,512]{1,0:T(8,128)S(1)}, u32[]{:S(2)}, u32[]{:S(2)}) collective-permute-start(f32[128,512]{1,0:T(8,128)S(1)} %constant_dynamic-slice_fusion), channel_id=1, source_target_pairs={{0,1},{1,0},{2,3},{3,2},{4,5},{5,4},{6,7},{7,6},{8,9},{9,8},{10,11... | collective-permute-start | bytes 786440 | tf_op jit(solution)/shard_map/ppermute | solution.py:107
  93.7 4.6 %collective-permute-start.17 = (f32[1024]{0:T(1024)S(1)}, f32[1024]{0:T(1024)S(1)}, u32[]{:S(2)}, u32[]{:S(2)}) collective-permute-start(f32[1024]{0:T(1024)S(1)} %add.148), channel_id=1, source_target_pairs={{0,8},{2,10},{4,12},{6,14},{8,0},{10,2},{12,4},{14,6},{16,24},{18,... | collective-permute-start | bytes 12296 | tf_op jit(solution)/shard_map/ppermute | solution.py:19
  95.4 7.0 %collective-permute-start.16 = (bf16[128,1024]{0,1:T(8,128)(2,1)S(1)}, bf16[128,1024]{0,1:T(8,128)(2,1)S(1)}, u32[]{:S(2)}, u32[]{:S(2)}) collective-permute-start(bf16[128,1024]{0,1:T(8,128)(2,1)S(1)} %dynamic-slice_convert_fusion.4), channel_id=1, source_target_pairs={{0,4},{2,6},{4,0},{6,2},{8,12},{10,14},{12,8},{14,10},{16,20},{18,... | collective-permute-start | bytes 786440 | tf_op jit(solution)/shard_map/ppermute | solution.py:19
  97.1 6.7 %collective-permute-start.15 = (bf16[128,1024]{0,1:T(8,128)(2,1)S(1)}, bf16[128,1024]{0,1:T(8,128)(2,1)S(1)}, u32[]{:S(2)}, u32[]{:S(2)}) collective-permute-start(bf16[128,1024]{0,1:T(8,128)(2,1)S(1)} %dynamic-slice_convert_fusion.5), channel_id=1, source_target_pairs={{0,8},{2,10},{4,12},{6,14},{8,0},{10,2},{12,4},{14,6},{16,24},{18,... | collective-permute-start | bytes 786440 | tf_op jit(solution)/shard_map/ppermute | solution.py:19
  104.2 23.7 %collective-permute-start.18 = (bf16[64,2048]{0,1:T(8,128)(2,1)S(1)}, bf16[64,2048]{0,1:T(8,128)(2,1)S(1)}, u32[]{:S(2)}, u32[]{:S(2)}) collective-permute-start(bf16[64,2048]{0,1:T(8,128)(2,1)S(1)} %dynamic-slice_convert_fusion.1), channel_id=1, source_target_pairs={{0,16},{2,18},{4,20},{6,22},{8,24},{10,26},{12,28},{14,30},{16,0},... | collective-permute-start | bytes 786440 | tf_op jit(solution)/shard_map/ppermute | solution.py:19
  105.8 22.1 %collective-permute-start.19 = (f32[1024]{0:T(1024)S(1)}, f32[1024]{0:T(1024)S(1)}, u32[]{:S(2)}, u32[]{:S(2)}) collective-permute-start(f32[1024]{0:T(1024)S(1)} %add.155), channel_id=1, source_target_pairs={{0,16},{2,18},{4,20},{6,22},{8,24},{10,26},{12,28},{14,30},{16,0},... | collective-permute-start | bytes 12296 | tf_op jit(solution)/shard_map/ppermute | solution.py:19
  128.4 4.7 %collective-permute-start.20 = (f32[1024]{0:T(1024)S(1)}, f32[1024]{0:T(1024)S(1)}, u32[]{:S(2)}, u32[]{:S(2)}) collective-permute-start(f32[1024]{0:T(1024)S(1)} %add.159), channel_id=1, source_target_pairs={{0,1},{1,0},{2,3},{3,2},{4,5},{5,4},{6,7},{7,6},{8,9},{9,8},{10,11... | collective-permute-start | bytes 12296 | tf_op jit(solution)/shard_map/ppermute | solution.py:107
  (15 other events, 175.2 us)

commit v12 on v10

--- a/solution.py
+++ b/solution.py
@@ -68,11 +68,11 @@
             if parts is not None:
                 joined = jnp.concatenate(parts, axis=1)
                 parts = None
-            (joined,), extra = halving_many([joined], [bit_a], axis, extra)
+            (joined,), extra = halving_many([joined], [bit_a], axis, extra, step + 1 < levels)
         else:
             if parts is None:
                 parts = [joined[:, :first], joined[:, first:]]
-            parts, extra = halving_many(parts, [bit_a, bit_b], axis, extra)
+            parts, extra = halving_many(parts, [bit_a, bit_b], axis, extra, step + 1 < levels)
     if parts is not None:
         joined = jnp.concatenate(parts, axis=1)
     results = []
@@ -89,11 +89,12 @@
     return results, extra
 
 
-def halving_many(parts, bits, axis, extra):
+def halving_many(parts, bits, axis, extra, tie):
     parts = [halving_step(part, axis, bit) for part, bit in zip(parts, bits)]
     if extra is not None:
         extra = extra + from_partner(extra, axis, bits[0])
-        parts, extra = lax.optimization_barrier((parts, extra))
+        if tie:
+            parts, extra = lax.optimization_barrier((parts, extra))
     return parts, extra
 
 
@@ -274,12 +275,12 @@
         + jnp.dot(grad_value, w_value.T, preferred_element_type=jnp.float32)
     )
     low_terms = feature_terms.astype(jnp.bfloat16)
-    gain_terms = jnp.sum(low_terms.astype(jnp.float32) * wide_nodes * inverse, axis=0)
+    grad_normed = low_terms.astype(jnp.float32) + head_swap(low_terms).astype(jnp.float32)
+    gain_terms = jnp.sum(grad_normed * wide_nodes * inverse, axis=0)
     (w_key_grad, w_value_grad), gain_part = scatter_rows(
         [(normed, grad_key), (normed, grad_value)], "graph", graph_levels, gain_terms
     )
-    gain_grad = gain_part + head_swap(gain_part)
-    grad_normed = low_terms.astype(jnp.float32) + head_swap(low_terms).astype(jnp.float32)
+    gain_grad = gain_part
     scaled = grad_normed * gain
     nodes_grad = (
         inverse

time: 116 us -> 113 us (0.974)
  starting transfers between devices: 34.1 us -> 29.8 us
  waiting for transfers between devices: 40.4 us -> 42 us
    ppermute x3 -> x2, waiting for transfers between devices: 3.69 us -> 6.27 us  [head_swap(): return lax.ppermute(value, 'head', [(0, 1), (1, 0)])]
    ppermute x3 -> x2, starting transfers between devices: 4.68 us -> 2.15 us  [head_swap(): return lax.ppermute(value, 'head', [(0, 1), (1, 0)])]
    ppermute x24, starting transfers between devices: 29.4 us -> 27.6 us  [from_partner(): return lax.ppermute(value, axis, pairs)]
    unnamed x32 -> x34, local copies, waits for them, and re-layouts: 4.3 us -> 4.31 us
  transfers between devices with their start and end apart: 27 -> 26, of which waited for: 13 -> 12; matrix products, arithmetic and copies ran while one was open for 19% -> 16% of each run, Pallas kernels for 0% -> 0%
where the time goes in v12:
time: 113 us
  waiting for transfers between devices  42 us (37%)
  starting transfers between devices  29.8 us (26%)
  matrix products  13.2 us (12%)
  Pallas kernels  11 us (10%)
  other arithmetic  8.59 us (8%)
  local copies, waits for them, and re-layouts  7.14 us (6%)
  between operations  1.23 us (1%)
    ppermute x24, waiting for transfers between devices, from_partner(): return lax.ppermute(value, axis, pairs)  35.7 us
    ppermute x24, starting transfers between devices, from_partner(): return lax.ppermute(value, axis, pairs)  27.6 us
    pallas_call x1, Pallas kernels, block_attention(): pl.pallas_call(functools.partial(attention_kernel, slots, pairs), grid_sp...  11 us
    ppermute x2, waiting for transfers between devices, head_swap(): return lax.ppermute(value, 'head', [(0, 1), (1, 0)])  6.27 us
    dot_general x8, matrix products, scatter_rows(): lax.dot_general(bit_major_rows(left, order), piece, contract, preferred_e...  4.32 us
    unnamed x34, local copies, waits for them, and re-layouts  4.31 us
  transfers between devices with their start and end apart: 26, of which 12 were waited for; matrix products, arithmetic and copies ran while one was open for 16% of the time, Pallas kernels for 0%

profile of v12, /device:TPU:0, one launch (start us, length us, event | category | flops | bytes accessed | tf_op | source)
XLA Modules:
  0.0 112.9 jit_solution(11778060530285251176)
XLA Ops:
  3.0 1.5 %fusion.5 = bf16[1,128,512]{2,1,0:T(8,128)(2,1)S(1)} fusion(bf16[128,1024]{1,0:T(8,128)(2,1)S(1)} %fusion.12, bf16[1024,512]{1,0:T(8,128)(2,1)} %param.12), kind=kOutput, calls=%fused_computation.18 | convolution fusion | flops 134283264 | bytes 1441792 | tf_op jit(solution)/shard_map/dot_general | solution.py:226
  4.6 1.5 %fusion.4 = bf16[1,128,512]{2,1,0:T(8,128)(2,1)S(1)} fusion(bf16[128,1024]{1,0:T(8,128)(2,1)S(1)} %fusion.12, bf16[1024,512]{1,0:T(8,128)(2,1)} %param.11), kind=kOutput, calls=%fused_computation.17 | convolution fusion | flops 134283264 | bytes 1441792 | tf_op jit(solution)/shard_map/dot_general | solution.py:225
  6.7 2.6 %collective-permute-start.1 = (bf16[1,128,1024]{2,1,0:T(8,128)(2,1)S(1)}, bf16[1,128,1024]{2,1,0:T(8,128)(2,1)}, u32[]{:S(2)}, u32[]{:S(2)}) collective-permute-start(bf16[1,128,1024]{2,1,0:T(8,128)(2,1)S(1)} %pad_maximum_fusion.2.refs_0_.refs_5_), channel_id=1, source_target_pairs={{0,4},{2,6},{4,0},{6,2},{8,12},{10,14},{12,8},{14,10},{16,20},{18,... | collective-permute-start | bytes 786440 | tf_op jit(solution)/shard_map/ppermute | solution.py:19
  9.3 1.6 %collective-permute-start.2 = (bf16[1,128,1024]{2,1,0:T(8,128)(2,1)S(1)}, bf16[1,128,1024]{2,1,0:T(8,128)(2,1)}, u32[]{:S(2)}, u32[]{:S(2)}) collective-permute-start(bf16[1,128,1024]{2,1,0:T(8,128)(2,1)S(1)} %pad_maximum_fusion.2.refs_0_.refs_5_), channel_id=1, source_target_pairs={{0,8},{2,10},{4,12},{6,14},{8,0},{10,2},{12,4},{14,6},{16,24},{18,... | collective-permute-start | bytes 786440 | tf_op jit(solution)/shard_map/ppermute | solution.py:19
  10.8 2.6 %collective-permute-start.3 = (bf16[1,128,1024]{2,1,0:T(8,128)(2,1)S(1)}, bf16[1,128,1024]{2,1,0:T(8,128)(2,1)}, u32[]{:S(2)}, u32[]{:S(2)}) collective-permute-start(bf16[1,128,1024]{2,1,0:T(8,128)(2,1)S(1)} %pad_maximum_fusion.2.refs_0_.refs_5_), channel_id=1, source_target_pairs={{0,16},{2,18},{4,20},{6,22},{8,24},{10,26},{12,28},{14,30},{16,0},... | collective-permute-start | bytes 786440 | tf_op jit(solution)/shard_map/ppermute | solution.py:19
  17.8 2.1 %fusion.3.g_ref = bf16[1,128,512]{2,1,0:T(8,128)(2,1)} fusion(bf16[128,1024]{1,0:T(8,128)(2,1)} %param.15, bf16[512,1024]{1,0:T(8,128)(2,1)S(1)} %copy-done), kind=kOutput, calls=%fused_computation.16 | convolution fusion | flops 134283264 | bytes 1441792 | tf_op jit(solution)/shard_map/dot_general | solution.py:240
  19.9 3.3 %collective-permute-done.2.refs_3_.refs_8_ = bf16[1,128,1024]{2,1,0:T(8,128)(2,1)} collective-permute-done((bf16[1,128,1024]{2,1,0:T(8,128)(2,1)S(1)}, bf16[1,128,1024]{2,1,0:T(8,128)(2,1)}, u32[]{:S(2)}, u32[]{:S(2)}) %collective-permute-start.2) | collective-permute-done | bytes 262176 | tf_op jit(solution)/shard_map/ppermute | solution.py:19
  23.2 2.4 %collective-permute-done.3.refs_4_.refs_9_ = bf16[1,128,1024]{2,1,0:T(8,128)(2,1)} collective-permute-done((bf16[1,128,1024]{2,1,0:T(8,128)(2,1)S(1)}, bf16[1,128,1024]{2,1,0:T(8,128)(2,1)}, u32[]{:S(2)}, u32[]{:S(2)}) %collective-permute-start.3) | collective-permute-done | bytes 262176 | tf_op jit(solution)/shard_map/ppermute | solution.py:19
  25.6 11.0 %shard_map.135 = (bf16[1,128,512]{2,1,0:T(8,128)(2,1)}, bf16[1,128,512]{2,1,0:T(8,128)(2,1)}, bf16[1,128,1024]{2,1,0:T(8,128)(2,1)}, bf16[1,128,1024]{2,1,0:T(8,...) custom-call(s32[5]{0:T(128)} %add_bitcast_fusion.active_ref, ...), custom_call_target="tpu_custom_call" | custom-call | tf_op jit(solution)/shard_map/pallas_call | solution.py:198
  36.6 1.3 %fusion.39 = f32[128,1024]{1,0:T(8,128)S(1)} fusion(bf16[512,1024]{1,0:T(8,128)(2,1)S(1)} %copy-done, bf16[1,128,512]{2,1,0:T(8,128)(2,1)} %get-tuple-element.22), kind=kOutput, calls=%fused_computation.93 | convolution fusion | flops 134217728 | bytes 1703936 | tf_op jit(solution)/shard_map/dot_general | solution.py:252
  37.9 1.6 %collective-permute-start.4 = (f32[128,512]{1,0:T(8,128)S(1)}, f32[128,512]{1,0:T(8,128)S(1)}, u32[]{:S(2)}, u32[]{:S(2)}) collective-permute-start(f32[128,512]{1,0:T(8,128)S(1)} %constant_dynamic-slice_fusion), channel_id=1, source_target_pairs={{0,1},{1,0},{2,3},{3,2},{4,5},{5,4},{6,7},{7,6},{8,9},{9,8},{10,11... | collective-permute-start | bytes 786440 | tf_op jit(solution)/shard_map/ppermute | solution.py:108
  39.8 2.7 %collective-permute-start.7 = (bf16[1,128,1024]{2,1,0:T(8,128)(2,1)}, bf16[1,128,1024]{2,1,0:T(8,128)(2,1)S(1)}, u32[]{:S(2)}, u32[]{:S(2)}) collective-permute-start(bf16[1,128,1024]{2,1,0:T(8,128)(2,1)} %get-tuple-element.27), channel_id=1, source_target_pairs={{0,8},{2,10},{4,12},{6,14},{8,0},{10,2},{12,4},{14,6},{16,24},{18,... | collective-permute-start | bytes 786440 | tf_op jit(solution)/shard_map/ppermute | solution.py:19
  46.9 4.3 %collective-permute-done.8 = bf16[1,128,1024]{2,1,0:T(8,128)(2,1)S(1)} collective-permute-done((bf16[1,128,1024]{2,1,0:T(8,128)(2,1)}, bf16[1,128,1024]{2,1,0:T(8,128)(2,1)S(1)}, u32[]{:S(2)}, u32[]{:S(2)}) %collective-permute-start.8) | collective-permute-done | bytes 262176 | tf_op jit(solution)/shard_map/ppermute | solution.py:19
  56.7 6.3 %collective-permute-done.9 = bf16[128,1024]{1,0:T(8,128)(2,1)S(1)} collective-permute-done((bf16[128,1024]{1,0:T(8,128)(2,1)S(1)}, bf16[128,1024]{1,0:T(8,128)(2,1)S(1)}, u32[]{:S(2)}, u32[]{:S(2)}) %collective-permute-start.9) | collective-permute-done | bytes 262176 | tf_op jit(solution)/shard_map/ppermute | solution.py:108
  67.2 1.6 %collective-permute-start.12 = (bf16[256,512]{0,1:T(8,128)(2,1)S(1)}, bf16[256,512]{0,1:T(8,128)(2,1)S(1)}, u32[]{:S(2)}, u32[]{:S(2)}) collective-permute-start(bf16[256,512]{0,1:T(8,128)(2,1)S(1)} %dynamic-slice_convert_fusion.6), channel_id=1, source_target_pairs={{0,4},{2,6},{4,0},{6,2},{8,12},{10,14},{12,8},{14,10},{16,20},{18,... | collective-permute-start | bytes 786440 | tf_op jit(solution)/shard_map/ppermute | solution.py:19
  70.6 3.7 %collective-permute-done.20 = bf16[256,512]{0,1:T(8,128)(2,1)S(1)} collective-permute-done((bf16[256,512]{0,1:T(8,128)(2,1)S(1)}, bf16[256,512]{0,1:T(8,128)(2,1)S(1)}, u32[]{:S(2)}, u32[]{:S(2)}) %collective-permute-start.20) | collective-permute-done | bytes 262176 | tf_op jit(solution)/shard_map/ppermute | solution.py:19
  76.6 3.4 %collective-permute-done.14 = f32[1024]{0:T(1024)S(1)} collective-permute-done((f32[1024]{0:T(1024)S(1)}, f32[1024]{0:T(1024)S(1)}, u32[]{:S(2)}, u32[]{:S(2)}) %collective-permute-start.14) | collective-permute-done | bytes 4128 | tf_op jit(solution)/shard_map/ppermute | solution.py:19
  80.0 2.3 %collective-permute-done.21 = bf16[128,512]{0,1:T(8,128)(2,1)S(1)} collective-permute-done((bf16[128,512]{0,1:T(8,128)(2,1)S(1)}, bf16[128,512]{0,1:T(8,128)(2,1)S(1)}, u32[]{:S(2)}, u32[]{:S(2)}) %collective-permute-start.21) | collective-permute-done | bytes 131104 | tf_op jit(solution)/shard_map/ppermute | solution.py:19
  83.6 3.4 %collective-permute-start.24 = (bf16[64,1024]{0,1:T(8,128)(2,1)S(1)}, bf16[64,1024]{0,1:T(8,128)(2,1)S(1)}, u32[]{:S(2)}, u32[]{:S(2)}) collective-permute-start(bf16[64,1024]{0,1:T(8,128)(2,1)S(1)} %fusion.9), channel_id=1, source_target_pairs={{0,16},{2,18},{4,20},{6,22},{8,24},{10,26},{12,28},{14,30},{16,0},... | collective-permute-start | bytes 393224 | tf_op jit(solution)/shard_map/ppermute | solution.py:19
  87.3 1.6 %collective-permute-start.16 = (bf16[128,512]{0,1:T(8,128)(2,1)S(1)}, bf16[128,512]{0,1:T(8,128)(2,1)S(1)}, u32[]{:S(2)}, u32[]{:S(2)}) collective-permute-start(bf16[128,512]{0,1:T(8,128)(2,1)S(1)} %dynamic-slice_convert_fusion.9), channel_id=1, source_target_pairs={{0,4},{2,6},{4,0},{6,2},{8,12},{10,14},{12,8},{14,10},{16,20},{18,... | collective-permute-start | bytes 393224 | tf_op jit(solution)/shard_map/ppermute | solution.py:19
  88.9 2.8 %collective-permute-done.17 = f32[1024]{0:T(1024)S(1)} collective-permute-done((f32[1024]{0:T(1024)S(1)}, f32[1024]{0:T(1024)S(1)}, u32[]{:S(2)}, u32[]{:S(2)}) %collective-permute-start.17) | collective-permute-done | bytes 4128 | tf_op jit(solution)/shard_map/ppermute | solution.py:19
  92.4 3.3 %collective-permute-start.18 = (f32[1024]{0:T(1024)S(1)}, f32[1024]{0:T(1024)S(1)}, u32[]{:S(2)}, u32[]{:S(2)}) collective-permute-start(f32[1024]{0:T(1024)S(1)} %add.182), channel_id=1, source_target_pairs={{0,16},{2,18},{4,20},{6,22},{8,24},{10,26},{12,28},{14,30},{16,0},... | collective-permute-start | bytes 12296 | tf_op jit(solution)/shard_map/ppermute | solution.py:19
  96.8 8.2 %collective-permute-done.18 = f32[1024]{0:T(1024)S(1)} collective-permute-done((f32[1024]{0:T(1024)S(1)}, f32[1024]{0:T(1024)S(1)}, u32[]{:S(2)}, u32[]{:S(2)}) %collective-permute-start.18) | collective-permute-done | bytes 4128 | tf_op jit(solution)/shard_map/ppermute | solution.py:19
  105.6 3.7 %collective-permute-done.25 = bf16[64,1024]{0,1:T(8,128)(2,1)S(1)} collective-permute-done((bf16[64,1024]{0,1:T(8,128)(2,1)S(1)}, bf16[64,1024]{0,1:T(8,128)(2,1)S(1)}, u32[]{:S(2)}, u32[]{:S(2)}) %collective-permute-start.25) | collective-permute-done | bytes 131104 | tf_op jit(solution)/shard_map/ppermute | solution.py:19
  (133 shorter events, 33.1 us)
Async XLA Ops:
  6.1 13.7 %collective-permute-start = (bf16[1,128,1024]{2,1,0:T(8,128)(2,1)S(1)}, bf16[1,128,1024]{2,1,0:T(8,128)(2,1)S(1)}, u32[]{:S(2)}, u32[]{:S(2)}) collective-permute-start(bf16[1,128,1024]{2,1,0:T(8,128)(2,1)S(1)} %pad_maximum_fusion.2.refs_0_.refs_5_), channel_id=1, source_target_pairs={{0,2},{2,0},{4,6},{6,4},{8,10},{10,8},{12,14},{14,12},{16,18},{18,... | collective-permute-start | bytes 786440 | tf_op jit(solution)/shard_map/ppermute | solution.py:19
  6.7 13.2 %collective-permute-start.1 = (bf16[1,128,1024]{2,1,0:T(8,128)(2,1)S(1)}, bf16[1,128,1024]{2,1,0:T(8,128)(2,1)}, u32[]{:S(2)}, u32[]{:S(2)}) collective-permute-start(bf16[1,128,1024]{2,1,0:T(8,128)(2,1)S(1)} %pad_maximum_fusion.2.refs_0_.refs_5_), channel_id=1, source_target_pairs={{0,4},{2,6},{4,0},{6,2},{8,12},{10,14},{12,8},{14,10},{16,20},{18,... | collective-permute-start | bytes 786440 | tf_op jit(solution)/shard_map/ppermute | solution.py:19
  9.3 14.0 %collective-permute-start.2 = (bf16[1,128,1024]{2,1,0:T(8,128)(2,1)S(1)}, bf16[1,128,1024]{2,1,0:T(8,128)(2,1)}, u32[]{:S(2)}, u32[]{:S(2)}) collective-permute-start(bf16[1,128,1024]{2,1,0:T(8,128)(2,1)S(1)} %pad_maximum_fusion.2.refs_0_.refs_5_), channel_id=1, source_target_pairs={{0,8},{2,10},{4,12},{6,14},{8,0},{10,2},{12,4},{14,6},{16,24},{18,... | collective-permute-start | bytes 786440 | tf_op jit(solution)/shard_map/ppermute | solution.py:19
  10.8 14.8 %collective-permute-start.3 = (bf16[1,128,1024]{2,1,0:T(8,128)(2,1)S(1)}, bf16[1,128,1024]{2,1,0:T(8,128)(2,1)}, u32[]{:S(2)}, u32[]{:S(2)}) collective-permute-start(bf16[1,128,1024]{2,1,0:T(8,128)(2,1)S(1)} %pad_maximum_fusion.2.refs_0_.refs_5_), channel_id=1, source_target_pairs={{0,16},{2,18},{4,20},{6,22},{8,24},{10,26},{12,28},{14,30},{16,0},... | collective-permute-start | bytes 786440 | tf_op jit(solution)/shard_map/ppermute | solution.py:19
  37.9 18.1 %collective-permute-start.4 = (f32[128,512]{1,0:T(8,128)S(1)}, f32[128,512]{1,0:T(8,128)S(1)}, u32[]{:S(2)}, u32[]{:S(2)}) collective-permute-start(f32[128,512]{1,0:T(8,128)S(1)} %constant_dynamic-slice_fusion), channel_id=1, source_target_pairs={{0,1},{1,0},{2,3},{3,2},{4,5},{5,4},{6,7},{7,6},{8,9},{9,8},{10,11... | collective-permute-start | bytes 786440 | tf_op jit(solution)/shard_map/ppermute | solution.py:108
  39.5 11.7 %collective-permute-start.8 = (bf16[1,128,1024]{2,1,0:T(8,128)(2,1)}, bf16[1,128,1024]{2,1,0:T(8,128)(2,1)S(1)}, u32[]{:S(2)}, u32[]{:S(2)}) collective-permute-start(bf16[1,128,1024]{2,1,0:T(8,128)(2,1)} %get-tuple-element.28), channel_id=1, source_target_pairs={{0,16},{2,18},{4,20},{6,22},{8,24},{10,26},{12,28},{14,30},{16,0},... | collective-permute-start | bytes 786440 | tf_op jit(solution)/shard_map/ppermute | solution.py:19
  39.8 11.3 %collective-permute-start.7 = (bf16[1,128,1024]{2,1,0:T(8,128)(2,1)}, bf16[1,128,1024]{2,1,0:T(8,128)(2,1)S(1)}, u32[]{:S(2)}, u32[]{:S(2)}) collective-permute-start(bf16[1,128,1024]{2,1,0:T(8,128)(2,1)} %get-tuple-element.27), channel_id=1, source_target_pairs={{0,8},{2,10},{4,12},{6,14},{8,0},{10,2},{12,4},{14,6},{16,24},{18,... | collective-permute-start | bytes 786440 | tf_op jit(solution)/shard_map/ppermute | solution.py:19
  42.5 8.6 %collective-permute-start.6 = (bf16[1,128,1024]{2,1,0:T(8,128)(2,1)}, bf16[1,128,1024]{2,1,0:T(8,128)(2,1)S(1)}, u32[]{:S(2)}, u32[]{:S(2)}) collective-permute-start(bf16[1,128,1024]{2,1,0:T(8,128)(2,1)} %get-tuple-element.26), channel_id=1, source_target_pairs={{0,4},{2,6},{4,0},{6,2},{8,12},{10,14},{12,8},{14,10},{16,20},{18,... | collective-permute-start | bytes 786440 | tf_op jit(solution)/shard_map/ppermute | solution.py:19
  43.0 8.1 %collective-permute-start.5 = (bf16[1,128,1024]{2,1,0:T(8,128)(2,1)}, bf16[1,128,1024]{2,1,0:T(8,128)(2,1)S(1)}, u32[]{:S(2)}, u32[]{:S(2)}) collective-permute-start(bf16[1,128,1024]{2,1,0:T(8,128)(2,1)} %get-tuple-element.25), channel_id=1, source_target_pairs={{0,2},{2,0},{4,6},{6,4},{8,10},{10,8},{12,14},{14,12},{16,18},{18,... | collective-permute-start | bytes 786440 | tf_op jit(solution)/shard_map/ppermute | solution.py:19
  51.2 13.3 %collective-permute-start.19 = (bf16[512,1024]{0,1:T(8,128)(2,1)S(1)}, bf16[512,1024]{0,1:T(8,128)(2,1)S(1)}, u32[]{:S(2)}, u32[]{:S(2)}) collective-permute-start(bf16[512,1024]{0,1:T(8,128)(2,1)S(1)} %dynamic-slice_convert_fusion), channel_id=1, source_target_pairs={{0,2},{2,0},{4,6},{6,4},{8,10},{10,8},{12,14},{14,12},{16,18},{18,... | collective-permute-start | bytes 3145736 | tf_op jit(solution)/shard_map/ppermute | solution.py:19
  54.2 8.8 %collective-permute-start.9 = (bf16[128,1024]{1,0:T(8,128)(2,1)S(1)}, bf16[128,1024]{1,0:T(8,128)(2,1)S(1)}, u32[]{:S(2)}, u32[]{:S(2)}) collective-permute-start(bf16[128,1024]{1,0:T(8,128)(2,1)S(1)} %fusion.1), channel_id=1, source_target_pairs={{0,1},{1,0},{2,3},{3,2},{4,5},{5,4},{6,7},{7,6},{8,9},{9,8},{10,11... | collective-permute-start | bytes 786440 | tf_op jit(solution)/shard_map/ppermute | solution.py:108
  55.7 10.8 %collective-permute-start.10 = (bf16[512,1024]{0,1:T(8,128)(2,1)S(1)}, bf16[512,1024]{0,1:T(8,128)(2,1)S(1)}, u32[]{:S(2)}, u32[]{:S(2)}) collective-permute-start(bf16[512,1024]{0,1:T(8,128)(2,1)S(1)} %dynamic-slice_convert_fusion.1), channel_id=1, source_target_pairs={{0,2},{2,0},{4,6},{6,4},{8,10},{10,8},{12,14},{14,12},{16,18},{18,... | collective-permute-start | bytes 3145736 | tf_op jit(solution)/shard_map/ppermute | solution.py:19
  65.0 9.2 %collective-permute-start.20 = (bf16[256,512]{0,1:T(8,128)(2,1)S(1)}, bf16[256,512]{0,1:T(8,128)(2,1)S(1)}, u32[]{:S(2)}, u32[]{:S(2)}) collective-permute-start(bf16[256,512]{0,1:T(8,128)(2,1)S(1)} %dynamic-slice_convert_fusion.4), channel_id=1, source_target_pairs={{0,4},{2,6},{4,0},{6,2},{8,12},{10,14},{12,8},{14,10},{16,20},{18,... | collective-permute-start | bytes 786440 | tf_op jit(solution)/shard_map/ppermute | solution.py:19
  65.6 9.6 %collective-permute-start.22 = (bf16[256,512]{0,1:T(8,128)(2,1)S(1)}, bf16[256,512]{0,1:T(8,128)(2,1)S(1)}, u32[]{:S(2)}, u32[]{:S(2)}) collective-permute-start(bf16[256,512]{0,1:T(8,128)(2,1)S(1)} %dynamic-slice_convert_fusion.3), channel_id=1, source_target_pairs={{0,8},{2,10},{4,12},{6,14},{8,0},{10,2},{12,4},{14,6},{16,24},{18,... | collective-permute-start | bytes 786440 | tf_op jit(solution)/shard_map/ppermute | solution.py:19
  67.2 15.1 %collective-permute-start.12 = (bf16[256,512]{0,1:T(8,128)(2,1)S(1)}, bf16[256,512]{0,1:T(8,128)(2,1)S(1)}, u32[]{:S(2)}, u32[]{:S(2)}) collective-permute-start(bf16[256,512]{0,1:T(8,128)(2,1)S(1)} %dynamic-slice_convert_fusion.6), channel_id=1, source_target_pairs={{0,4},{2,6},{4,0},{6,2},{8,12},{10,14},{12,8},{14,10},{16,20},{18,... | collective-permute-start | bytes 786440 | tf_op jit(solution)/shard_map/ppermute | solution.py:19
  68.8 13.6 %collective-permute-start.13 = (bf16[256,512]{0,1:T(8,128)(2,1)S(1)}, bf16[256,512]{0,1:T(8,128)(2,1)S(1)}, u32[]{:S(2)}, u32[]{:S(2)}) collective-permute-start(bf16[256,512]{0,1:T(8,128)(2,1)S(1)} %dynamic-slice_convert_fusion.5), channel_id=1, source_target_pairs={{0,8},{2,10},{4,12},{6,14},{8,0},{10,2},{12,4},{14,6},{16,24},{18,... | collective-permute-start | bytes 786440 | tf_op jit(solution)/shard_map/ppermute | solution.py:19
  70.1 9.9 %collective-permute-start.14 = (f32[1024]{0:T(1024)S(1)}, f32[1024]{0:T(1024)S(1)}, u32[]{:S(2)}, u32[]{:S(2)}) collective-permute-start(f32[1024]{0:T(1024)S(1)} %add.168), channel_id=1, source_target_pairs={{0,4},{2,6},{4,0},{6,2},{8,12},{10,14},{12,8},{14,10},{16,20},{18,... | collective-permute-start | bytes 12296 | tf_op jit(solution)/shard_map/ppermute | solution.py:19
  74.4 7.9 %collective-permute-start.21 = (bf16[128,512]{0,1:T(8,128)(2,1)S(1)}, bf16[128,512]{0,1:T(8,128)(2,1)S(1)}, u32[]{:S(2)}, u32[]{:S(2)}) collective-permute-start(bf16[128,512]{0,1:T(8,128)(2,1)S(1)} %dynamic-slice_convert_fusion.8), channel_id=1, source_target_pairs={{0,8},{2,10},{4,12},{6,14},{8,0},{10,2},{12,4},{14,6},{16,24},{18,... | collective-permute-start | bytes 393224 | tf_op jit(solution)/shard_map/ppermute | solution.py:19
  75.4 6.9 %collective-permute-start.23 = (bf16[128,512]{0,1:T(8,128)(2,1)S(1)}, bf16[128,512]{0,1:T(8,128)(2,1)S(1)}, u32[]{:S(2)}, u32[]{:S(2)}) collective-permute-start(bf16[128,512]{0,1:T(8,128)(2,1)S(1)} %dynamic-slice_convert_fusion.7), channel_id=1, source_target_pairs={{0,4},{2,6},{4,0},{6,2},{8,12},{10,14},{12,8},{14,10},{16,20},{18,... | collective-permute-start | bytes 393224 | tf_op jit(solution)/shard_map/ppermute | solution.py:19
  82.5 9.2 %collective-permute-start.15 = (bf16[128,512]{0,1:T(8,128)(2,1)S(1)}, bf16[128,512]{0,1:T(8,128)(2,1)S(1)}, u32[]{:S(2)}, u32[]{:S(2)}) collective-permute-start(bf16[128,512]{0,1:T(8,128)(2,1)S(1)} %dynamic-slice_convert_fusion.10), channel_id=1, source_target_pairs={{0,8},{2,10},{4,12},{6,14},{8,0},{10,2},{12,4},{14,6},{16,24},{18,... | collective-permute-start | bytes 393224 | tf_op jit(solution)/shard_map/ppermute | solution.py:19
  83.6 22.0 %collective-permute-start.24 = (bf16[64,1024]{0,1:T(8,128)(2,1)S(1)}, bf16[64,1024]{0,1:T(8,128)(2,1)S(1)}, u32[]{:S(2)}, u32[]{:S(2)}) collective-permute-start(bf16[64,1024]{0,1:T(8,128)(2,1)S(1)} %fusion.9), channel_id=1, source_target_pairs={{0,16},{2,18},{4,20},{6,22},{8,24},{10,26},{12,28},{14,30},{16,0},... | collective-permute-start | bytes 393224 | tf_op jit(solution)/shard_map/ppermute | solution.py:19
  87.3 5.0 %collective-permute-start.16 = (bf16[128,512]{0,1:T(8,128)(2,1)S(1)}, bf16[128,512]{0,1:T(8,128)(2,1)S(1)}, u32[]{:S(2)}, u32[]{:S(2)}) collective-permute-start(bf16[128,512]{0,1:T(8,128)(2,1)S(1)} %dynamic-slice_convert_fusion.9), channel_id=1, source_target_pairs={{0,4},{2,6},{4,0},{6,2},{8,12},{10,14},{12,8},{14,10},{16,20},{18,... | collective-permute-start | bytes 393224 | tf_op jit(solution)/shard_map/ppermute | solution.py:19
  92.4 12.7 %collective-permute-start.18 = (f32[1024]{0:T(1024)S(1)}, f32[1024]{0:T(1024)S(1)}, u32[]{:S(2)}, u32[]{:S(2)}) collective-permute-start(f32[1024]{0:T(1024)S(1)} %add.182), channel_id=1, source_target_pairs={{0,16},{2,18},{4,20},{6,22},{8,24},{10,26},{12,28},{14,30},{16,0},... | collective-permute-start | bytes 12296 | tf_op jit(solution)/shard_map/ppermute | solution.py:19
  95.8 13.5 %collective-permute-start.25 = (bf16[64,1024]{0,1:T(8,128)(2,1)S(1)}, bf16[64,1024]{0,1:T(8,128)(2,1)S(1)}, u32[]{:S(2)}, u32[]{:S(2)}) collective-permute-start(bf16[64,1024]{0,1:T(8,128)(2,1)S(1)} %dynamic-slice_convert_fusion.2), channel_id=1, source_target_pairs={{0,16},{2,18},{4,20},{6,22},{8,24},{10,26},{12,28},{14,30},{16,0},... | collective-permute-start | bytes 393224 | tf_op jit(solution)/shard_map/ppermute | solution.py:19
  (16 other events, 154.6 us)

commit v13 on v12

--- a/solution.py
+++ b/solution.py
@@ -252,7 +252,6 @@
     mixed_terms = jnp.dot(attended, w_out, preferred_element_type=jnp.float32)
     own_mixed = lax.dynamic_slice_in_dim(mixed_terms, head_me * columns, columns, 1)
     other_mixed = lax.dynamic_slice_in_dim(mixed_terms, (1 - head_me) * columns, columns, 1)
-    mixed = (own_mixed + head_swap(other_mixed)).astype(jnp.bfloat16)
     grad_key = term_slots[0][:, :, :columns].astype(jnp.float32)
     grad_value = term_slots[0][:, :, columns:].astype(jnp.float32)
     returned = {}
@@ -275,7 +274,9 @@
         + jnp.dot(grad_value, w_value.T, preferred_element_type=jnp.float32)
     )
     low_terms = feature_terms.astype(jnp.bfloat16)
-    grad_normed = low_terms.astype(jnp.float32) + head_swap(low_terms).astype(jnp.float32)
+    swapped = head_swap(jnp.concatenate([low_terms, other_mixed.astype(jnp.bfloat16)], axis=1))
+    mixed = (own_mixed + swapped[:, width:].astype(jnp.float32)).astype(jnp.bfloat16)
+    grad_normed = low_terms.astype(jnp.float32) + swapped[:, :width].astype(jnp.float32)
     gain_terms = jnp.sum(grad_normed * wide_nodes * inverse, axis=0)
     (w_key_grad, w_value_grad), gain_part = scatter_rows(
         [(normed, grad_key), (normed, grad_value)], "graph", graph_levels, gain_terms

time: 113 us -> 113 us (level)
  waiting for transfers between devices: 42 us -> 37.9 us
  starting transfers between devices: 29.8 us -> 33.4 us
    ppermute x24, starting transfers between devices: 27.6 us -> 31.8 us  [from_partner(): return lax.ppermute(value, axis, pairs)]
    ppermute x24, waiting for transfers between devices: 35.7 us -> 32 us  [from_partner(): return lax.ppermute(value, axis, pairs)]
    ppermute x2 -> x1, waiting for transfers between devices: 6.27 us -> 5.9 us  [head_swap(): return lax.ppermute(value, 'head', [(0, 1), (1, 0)])]
    unnamed x34 -> x32, local copies, waits for them, and re-layouts: 4.31 us -> 4.31 us
  transfers between devices with their start and end apart: 26 -> 25, of which waited for: 12 -> 12; matrix products, arithmetic and copies ran while one was open for 16% -> 18% of each run, Pallas kernels for 0% -> 0%
where the time goes in v13:
time: 113 us
  waiting for transfers between devices  37.9 us (34%)
  starting transfers between devices  33.4 us (30%)
  matrix products  13.2 us (12%)
  Pallas kernels  11 us (10%)
  other arithmetic  8.45 us (7%)
  local copies, waits for them, and re-layouts  7.32 us (6%)
  between operations  1.23 us (1%)
    ppermute x24, waiting for transfers between devices, from_partner(): return lax.ppermute(value, axis, pairs)  32 us
    ppermute x24, starting transfers between devices, from_partner(): return lax.ppermute(value, axis, pairs)  31.8 us
    pallas_call x1, Pallas kernels, block_attention(): pl.pallas_call(functools.partial(attention_kernel, slots, pairs), grid_sp...  11 us
    ppermute x1, waiting for transfers between devices, head_swap(): return lax.ppermute(value, 'head', [(0, 1), (1, 0)])  5.9 us
    dot_general x8, matrix products, scatter_rows(): lax.dot_general(bit_major_rows(left, order), piece, contract, preferred_e...  5.33 us
    unnamed x32, local copies, waits for them, and re-layouts  4.31 us
  transfers between devices with their start and end apart: 25, of which 12 were waited for; matrix products, arithmetic and copies ran while one was open for 18% of the time, Pallas kernels for 0%

profile of v13, /device:TPU:0, one launch (start us, length us, event | category | flops | bytes accessed | tf_op | source)
XLA Modules:
  0.0 112.5 jit_solution(1773039759034832074)
XLA Ops:
  6.7 2.6 %collective-permute-start.1 = (bf16[1,128,1024]{2,1,0:T(8,128)(2,1)S(1)}, bf16[1,128,1024]{2,1,0:T(8,128)(2,1)}, u32[]{:S(2)}, u32[]{:S(2)}) collective-permute-start(bf16[1,128,1024]{2,1,0:T(8,128)(2,1)S(1)} %pad_maximum_fusion.3.refs_0_.refs_5_), channel_id=1, source_target_pairs={{0,4},{2,6},{4,0},{6,2},{8,12},{10,14},{12,8},{14,10},{16,20},{18,... | collective-permute-start | bytes 786440 | tf_op jit(solution)/shard_map/ppermute | solution.py:19
  9.3 1.6 %collective-permute-start.2 = (bf16[1,128,1024]{2,1,0:T(8,128)(2,1)S(1)}, bf16[1,128,1024]{2,1,0:T(8,128)(2,1)}, u32[]{:S(2)}, u32[]{:S(2)}) collective-permute-start(bf16[1,128,1024]{2,1,0:T(8,128)(2,1)S(1)} %pad_maximum_fusion.3.refs_0_.refs_5_), channel_id=1, source_target_pairs={{0,8},{2,10},{4,12},{6,14},{8,0},{10,2},{12,4},{14,6},{16,24},{18,... | collective-permute-start | bytes 786440 | tf_op jit(solution)/shard_map/ppermute | solution.py:19
  10.8 2.6 %collective-permute-start.3 = (bf16[1,128,1024]{2,1,0:T(8,128)(2,1)S(1)}, bf16[1,128,1024]{2,1,0:T(8,128)(2,1)}, u32[]{:S(2)}, u32[]{:S(2)}) collective-permute-start(bf16[1,128,1024]{2,1,0:T(8,128)(2,1)S(1)} %pad_maximum_fusion.3.refs_0_.refs_5_), channel_id=1, source_target_pairs={{0,16},{2,18},{4,20},{6,22},{8,24},{10,26},{12,28},{14,30},{16,0},... | collective-permute-start | bytes 786440 | tf_op jit(solution)/shard_map/ppermute | solution.py:19
  17.8 2.1 %fusion.3.g_ref = bf16[1,128,512]{2,1,0:T(8,128)(2,1)} fusion(bf16[128,1024]{1,0:T(8,128)(2,1)} %param.15, bf16[512,1024]{1,0:T(8,128)(2,1)S(1)} %copy-done), kind=kOutput, calls=%fused_computation.16 | convolution fusion | flops 134283264 | bytes 1441792 | tf_op jit(solution)/shard_map/dot_general | solution.py:240
  20.0 3.3 %collective-permute-done.2.refs_3_.refs_8_ = bf16[1,128,1024]{2,1,0:T(8,128)(2,1)} collective-permute-done((bf16[1,128,1024]{2,1,0:T(8,128)(2,1)S(1)}, bf16[1,128,1024]{2,1,0:T(8,128)(2,1)}, u32[]{:S(2)}, u32[]{:S(2)}) %collective-permute-start.2) | collective-permute-done | bytes 262176 | tf_op jit(solution)/shard_map/ppermute | solution.py:19
  23.2 2.4 %collective-permute-done.3.refs_4_.refs_9_ = bf16[1,128,1024]{2,1,0:T(8,128)(2,1)} collective-permute-done((bf16[1,128,1024]{2,1,0:T(8,128)(2,1)S(1)}, bf16[1,128,1024]{2,1,0:T(8,128)(2,1)}, u32[]{:S(2)}, u32[]{:S(2)}) %collective-permute-start.3) | collective-permute-done | bytes 262176 | tf_op jit(solution)/shard_map/ppermute | solution.py:19
  25.6 11.0 %shard_map.135 = (bf16[1,128,512]{2,1,0:T(8,128)(2,1)}, bf16[1,128,512]{2,1,0:T(8,128)(2,1)}, bf16[1,128,1024]{2,1,0:T(8,128)(2,1)}, bf16[1,128,1024]{2,1,0:T(8,...) custom-call(s32[5]{0:T(128)} %add_bitcast_fusion.active_ref, ...), custom_call_target="tpu_custom_call" | custom-call | tf_op jit(solution)/shard_map/pallas_call | solution.py:198
  37.0 2.7 %collective-permute-start.6 = (bf16[1,128,1024]{2,1,0:T(8,128)(2,1)}, bf16[1,128,1024]{2,1,0:T(8,128)(2,1)S(1)}, u32[]{:S(2)}, u32[]{:S(2)}) collective-permute-start(bf16[1,128,1024]{2,1,0:T(8,128)(2,1)} %get-tuple-element.27), channel_id=1, source_target_pairs={{0,8},{2,10},{4,12},{6,14},{8,0},{10,2},{12,4},{14,6},{16,24},{18,... | collective-permute-start | bytes 786440 | tf_op jit(solution)/shard_map/ppermute | solution.py:19
  45.9 2.7 %collective-permute-done.7 = bf16[1,128,1024]{2,1,0:T(8,128)(2,1)S(1)} collective-permute-done((bf16[1,128,1024]{2,1,0:T(8,128)(2,1)}, bf16[1,128,1024]{2,1,0:T(8,128)(2,1)S(1)}, u32[]{:S(2)}, u32[]{:S(2)}) %collective-permute-start.7) | collective-permute-done | bytes 262176 | tf_op jit(solution)/shard_map/ppermute | solution.py:19
  51.3 1.6 %collective-permute-start.8 = (bf16[128,1536]{1,0:T(8,128)(2,1)S(1)}, bf16[128,1536]{1,0:T(8,128)(2,1)S(1)}, u32[]{:S(2)}, u32[]{:S(2)}) collective-permute-start(bf16[128,1536]{1,0:T(8,128)(2,1)S(1)} %pad_maximum_fusion.2), channel_id=1, source_target_pairs={{0,1},{1,0},{2,3},{3,2},{4,5},{5,4},{6,7},{7,6},{8,9},{9,8},{10,11... | collective-permute-start | bytes 1179656 | tf_op jit(solution)/shard_map/ppermute | solution.py:108
  54.3 5.9 %collective-permute-done.8 = bf16[128,1536]{1,0:T(8,128)(2,1)S(1)} collective-permute-done((bf16[128,1536]{1,0:T(8,128)(2,1)S(1)}, bf16[128,1536]{1,0:T(8,128)(2,1)S(1)}, u32[]{:S(2)}, u32[]{:S(2)}) %collective-permute-start.8) | collective-permute-done | bytes 393248 | tf_op jit(solution)/shard_map/ppermute | solution.py:108
  62.2 1.6 %collective-permute-start.19 = (bf16[256,512]{0,1:T(8,128)(2,1)S(1)}, bf16[256,512]{0,1:T(8,128)(2,1)S(1)}, u32[]{:S(2)}, u32[]{:S(2)}) collective-permute-start(bf16[256,512]{0,1:T(8,128)(2,1)S(1)} %dynamic-slice_convert_fusion.4), channel_id=1, source_target_pairs={{0,4},{2,6},{4,0},{6,2},{8,12},{10,14},{12,8},{14,10},{16,20},{18,... | collective-permute-start | bytes 786440 | tf_op jit(solution)/shard_map/ppermute | solution.py:19
  63.8 2.2 %collective-permute-start.21 = (bf16[256,512]{0,1:T(8,128)(2,1)S(1)}, bf16[256,512]{0,1:T(8,128)(2,1)S(1)}, u32[]{:S(2)}, u32[]{:S(2)}) collective-permute-start(bf16[256,512]{0,1:T(8,128)(2,1)S(1)} %dynamic-slice_convert_fusion.3), channel_id=1, source_target_pairs={{0,8},{2,10},{4,12},{6,14},{8,0},{10,2},{12,4},{14,6},{16,24},{18,... | collective-permute-start | bytes 786440 | tf_op jit(solution)/shard_map/ppermute | solution.py:19
  66.7 1.6 %collective-permute-start.11 = (bf16[256,512]{0,1:T(8,128)(2,1)S(1)}, bf16[256,512]{0,1:T(8,128)(2,1)S(1)}, u32[]{:S(2)}, u32[]{:S(2)}) collective-permute-start(bf16[256,512]{0,1:T(8,128)(2,1)S(1)} %dynamic-slice_convert_fusion.6), channel_id=1, source_target_pairs={{0,4},{2,6},{4,0},{6,2},{8,12},{10,14},{12,8},{14,10},{16,20},{18,... | collective-permute-start | bytes 786440 | tf_op jit(solution)/shard_map/ppermute | solution.py:19
  68.9 2.5 %collective-permute-done.19 = bf16[256,512]{0,1:T(8,128)(2,1)S(1)} collective-permute-done((bf16[256,512]{0,1:T(8,128)(2,1)S(1)}, bf16[256,512]{0,1:T(8,128)(2,1)S(1)}, u32[]{:S(2)}, u32[]{:S(2)}) %collective-permute-start.19) | collective-permute-done | bytes 262176 | tf_op jit(solution)/shard_map/ppermute | solution.py:19
  71.5 3.2 %collective-permute-start.20 = (bf16[128,512]{0,1:T(8,128)(2,1)S(1)}, bf16[128,512]{0,1:T(8,128)(2,1)S(1)}, u32[]{:S(2)}, u32[]{:S(2)}) collective-permute-start(bf16[128,512]{0,1:T(8,128)(2,1)S(1)} %dynamic-slice_convert_fusion.8), channel_id=1, source_target_pairs={{0,8},{2,10},{4,12},{6,14},{8,0},{10,2},{12,4},{14,6},{16,24},{18,... | collective-permute-start | bytes 393224 | tf_op jit(solution)/shard_map/ppermute | solution.py:19
  76.9 4.0 %collective-permute-done.20 = bf16[128,512]{0,1:T(8,128)(2,1)S(1)} collective-permute-done((bf16[128,512]{0,1:T(8,128)(2,1)S(1)}, bf16[128,512]{0,1:T(8,128)(2,1)S(1)}, u32[]{:S(2)}, u32[]{:S(2)}) %collective-permute-start.20) | collective-permute-done | bytes 131104 | tf_op jit(solution)/shard_map/ppermute | solution.py:19
  81.2 1.8 %collective-permute-start.14 = (bf16[128,512]{0,1:T(8,128)(2,1)S(1)}, bf16[128,512]{0,1:T(8,128)(2,1)S(1)}, u32[]{:S(2)}, u32[]{:S(2)}) collective-permute-start(bf16[128,512]{0,1:T(8,128)(2,1)S(1)} %dynamic-slice_convert_fusion.10), channel_id=1, source_target_pairs={{0,8},{2,10},{4,12},{6,14},{8,0},{10,2},{12,4},{14,6},{16,24},{18,... | collective-permute-start | bytes 393224 | tf_op jit(solution)/shard_map/ppermute | solution.py:19
  83.2 3.3 %collective-permute-start.23 = (bf16[64,1024]{0,1:T(8,128)(2,1)S(1)}, bf16[64,1024]{0,1:T(8,128)(2,1)S(1)}, u32[]{:S(2)}, u32[]{:S(2)}) collective-permute-start(bf16[64,1024]{0,1:T(8,128)(2,1)S(1)} %fusion.9), channel_id=1, source_target_pairs={{0,16},{2,18},{4,20},{6,22},{8,24},{10,26},{12,28},{14,30},{16,0},... | collective-permute-start | bytes 393224 | tf_op jit(solution)/shard_map/ppermute | solution.py:19
  86.8 1.6 %collective-permute-start.15 = (bf16[128,512]{0,1:T(8,128)(2,1)S(1)}, bf16[128,512]{0,1:T(8,128)(2,1)S(1)}, u32[]{:S(2)}, u32[]{:S(2)}) collective-permute-start(bf16[128,512]{0,1:T(8,128)(2,1)S(1)} %dynamic-slice_convert_fusion.9), channel_id=1, source_target_pairs={{0,4},{2,6},{4,0},{6,2},{8,12},{10,14},{12,8},{14,10},{16,20},{18,... | collective-permute-start | bytes 393224 | tf_op jit(solution)/shard_map/ppermute | solution.py:19
  88.4 2.9 %collective-permute-done.16 = f32[1024]{0:T(1024)S(1)} collective-permute-done((f32[1024]{0:T(1024)S(1)}, f32[1024]{0:T(1024)S(1)}, u32[]{:S(2)}, u32[]{:S(2)}) %collective-permute-start.16) | collective-permute-done | bytes 4128 | tf_op jit(solution)/shard_map/ppermute | solution.py:19
  91.9 3.4 %collective-permute-start.17 = (f32[1024]{0:T(1024)S(1)}, f32[1024]{0:T(1024)S(1)}, u32[]{:S(2)}, u32[]{:S(2)}) collective-permute-start(f32[1024]{0:T(1024)S(1)} %add.182), channel_id=1, source_target_pairs={{0,16},{2,18},{4,20},{6,22},{8,24},{10,26},{12,28},{14,30},{16,0},... | collective-permute-start | bytes 12296 | tf_op jit(solution)/shard_map/ppermute | solution.py:19
  96.2 8.2 %collective-permute-done.17 = f32[1024]{0:T(1024)S(1)} collective-permute-done((f32[1024]{0:T(1024)S(1)}, f32[1024]{0:T(1024)S(1)}, u32[]{:S(2)}, u32[]{:S(2)}) %collective-permute-start.17) | collective-permute-done | bytes 4128 | tf_op jit(solution)/shard_map/ppermute | solution.py:19
  105.0 3.8 %collective-permute-done.24 = bf16[64,1024]{0,1:T(8,128)(2,1)S(1)} collective-permute-done((bf16[64,1024]{0,1:T(8,128)(2,1)S(1)}, bf16[64,1024]{0,1:T(8,128)(2,1)S(1)}, u32[]{:S(2)}, u32[]{:S(2)}) %collective-permute-start.24) | collective-permute-done | bytes 131104 | tf_op jit(solution)/shard_map/ppermute | solution.py:19
  (130 shorter events, 32.8 us)
Async XLA Ops:
  6.1 13.8 %collective-permute-start = (bf16[1,128,1024]{2,1,0:T(8,128)(2,1)S(1)}, bf16[1,128,1024]{2,1,0:T(8,128)(2,1)S(1)}, u32[]{:S(2)}, u32[]{:S(2)}) collective-permute-start(bf16[1,128,1024]{2,1,0:T(8,128)(2,1)S(1)} %pad_maximum_fusion.3.refs_0_.refs_5_), channel_id=1, source_target_pairs={{0,2},{2,0},{4,6},{6,4},{8,10},{10,8},{12,14},{14,12},{16,18},{18,... | collective-permute-start | bytes 786440 | tf_op jit(solution)/shard_map/ppermute | solution.py:19
  6.7 13.3 %collective-permute-start.1 = (bf16[1,128,1024]{2,1,0:T(8,128)(2,1)S(1)}, bf16[1,128,1024]{2,1,0:T(8,128)(2,1)}, u32[]{:S(2)}, u32[]{:S(2)}) collective-permute-start(bf16[1,128,1024]{2,1,0:T(8,128)(2,1)S(1)} %pad_maximum_fusion.3.refs_0_.refs_5_), channel_id=1, source_target_pairs={{0,4},{2,6},{4,0},{6,2},{8,12},{10,14},{12,8},{14,10},{16,20},{18,... | collective-permute-start | bytes 786440 | tf_op jit(solution)/shard_map/ppermute | solution.py:19
  9.3 14.0 %collective-permute-start.2 = (bf16[1,128,1024]{2,1,0:T(8,128)(2,1)S(1)}, bf16[1,128,1024]{2,1,0:T(8,128)(2,1)}, u32[]{:S(2)}, u32[]{:S(2)}) collective-permute-start(bf16[1,128,1024]{2,1,0:T(8,128)(2,1)S(1)} %pad_maximum_fusion.3.refs_0_.refs_5_), channel_id=1, source_target_pairs={{0,8},{2,10},{4,12},{6,14},{8,0},{10,2},{12,4},{14,6},{16,24},{18,... | collective-permute-start | bytes 786440 | tf_op jit(solution)/shard_map/ppermute | solution.py:19
  10.8 14.8 %collective-permute-start.3 = (bf16[1,128,1024]{2,1,0:T(8,128)(2,1)S(1)}, bf16[1,128,1024]{2,1,0:T(8,128)(2,1)}, u32[]{:S(2)}, u32[]{:S(2)}) collective-permute-start(bf16[1,128,1024]{2,1,0:T(8,128)(2,1)S(1)} %pad_maximum_fusion.3.refs_0_.refs_5_), channel_id=1, source_target_pairs={{0,16},{2,18},{4,20},{6,22},{8,24},{10,26},{12,28},{14,30},{16,0},... | collective-permute-start | bytes 786440 | tf_op jit(solution)/shard_map/ppermute | solution.py:19
  36.6 12.0 %collective-permute-start.7 = (bf16[1,128,1024]{2,1,0:T(8,128)(2,1)}, bf16[1,128,1024]{2,1,0:T(8,128)(2,1)S(1)}, u32[]{:S(2)}, u32[]{:S(2)}) collective-permute-start(bf16[1,128,1024]{2,1,0:T(8,128)(2,1)} %get-tuple-element.28), channel_id=1, source_target_pairs={{0,16},{2,18},{4,20},{6,22},{8,24},{10,26},{12,28},{14,30},{16,0},... | collective-permute-start | bytes 786440 | tf_op jit(solution)/shard_map/ppermute | solution.py:19
  37.0 11.6 %collective-permute-start.6 = (bf16[1,128,1024]{2,1,0:T(8,128)(2,1)}, bf16[1,128,1024]{2,1,0:T(8,128)(2,1)S(1)}, u32[]{:S(2)}, u32[]{:S(2)}) collective-permute-start(bf16[1,128,1024]{2,1,0:T(8,128)(2,1)} %get-tuple-element.27), channel_id=1, source_target_pairs={{0,8},{2,10},{4,12},{6,14},{8,0},{10,2},{12,4},{14,6},{16,24},{18,... | collective-permute-start | bytes 786440 | tf_op jit(solution)/shard_map/ppermute | solution.py:19
  39.7 8.9 %collective-permute-start.5 = (bf16[1,128,1024]{2,1,0:T(8,128)(2,1)}, bf16[1,128,1024]{2,1,0:T(8,128)(2,1)S(1)}, u32[]{:S(2)}, u32[]{:S(2)}) collective-permute-start(bf16[1,128,1024]{2,1,0:T(8,128)(2,1)} %get-tuple-element.26), channel_id=1, source_target_pairs={{0,4},{2,6},{4,0},{6,2},{8,12},{10,14},{12,8},{14,10},{16,20},{18,... | collective-permute-start | bytes 786440 | tf_op jit(solution)/shard_map/ppermute | solution.py:19
  40.2 8.4 %collective-permute-start.4 = (bf16[1,128,1024]{2,1,0:T(8,128)(2,1)}, bf16[1,128,1024]{2,1,0:T(8,128)(2,1)S(1)}, u32[]{:S(2)}, u32[]{:S(2)}) collective-permute-start(bf16[1,128,1024]{2,1,0:T(8,128)(2,1)} %get-tuple-element.25), channel_id=1, source_target_pairs={{0,2},{2,0},{4,6},{6,4},{8,10},{10,8},{12,14},{14,12},{16,18},{18,... | collective-permute-start | bytes 786440 | tf_op jit(solution)/shard_map/ppermute | solution.py:19
  45.0 16.6 %collective-permute-start.18 = (bf16[512,1024]{0,1:T(8,128)(2,1)S(1)}, bf16[512,1024]{0,1:T(8,128)(2,1)S(1)}, u32[]{:S(2)}, u32[]{:S(2)}) collective-permute-start(bf16[512,1024]{0,1:T(8,128)(2,1)S(1)} %dynamic-slice_convert_fusion), channel_id=1, source_target_pairs={{0,2},{2,0},{4,6},{6,4},{8,10},{10,8},{12,14},{14,12},{16,18},{18,... | collective-permute-start | bytes 3145736 | tf_op jit(solution)/shard_map/ppermute | solution.py:19
  51.3 8.8 %collective-permute-start.8 = (bf16[128,1536]{1,0:T(8,128)(2,1)S(1)}, bf16[128,1536]{1,0:T(8,128)(2,1)S(1)}, u32[]{:S(2)}, u32[]{:S(2)}) collective-permute-start(bf16[128,1536]{1,0:T(8,128)(2,1)S(1)} %pad_maximum_fusion.2), channel_id=1, source_target_pairs={{0,1},{1,0},{2,3},{3,2},{4,5},{5,4},{6,7},{7,6},{8,9},{9,8},{10,11... | collective-permute-start | bytes 1179656 | tf_op jit(solution)/shard_map/ppermute | solution.py:108
  54.2 11.8 %collective-permute-start.9 = (bf16[512,1024]{0,1:T(8,128)(2,1)S(1)}, bf16[512,1024]{0,1:T(8,128)(2,1)S(1)}, u32[]{:S(2)}, u32[]{:S(2)}) collective-permute-start(bf16[512,1024]{0,1:T(8,128)(2,1)S(1)} %dynamic-slice_convert_fusion.1), channel_id=1, source_target_pairs={{0,2},{2,0},{4,6},{6,4},{8,10},{10,8},{12,14},{14,12},{16,18},{18,... | collective-permute-start | bytes 3145736 | tf_op jit(solution)/shard_map/ppermute | solution.py:19
  62.2 9.2 %collective-permute-start.19 = (bf16[256,512]{0,1:T(8,128)(2,1)S(1)}, bf16[256,512]{0,1:T(8,128)(2,1)S(1)}, u32[]{:S(2)}, u32[]{:S(2)}) collective-permute-start(bf16[256,512]{0,1:T(8,128)(2,1)S(1)} %dynamic-slice_convert_fusion.4), channel_id=1, source_target_pairs={{0,4},{2,6},{4,0},{6,2},{8,12},{10,14},{12,8},{14,10},{16,20},{18,... | collective-permute-start | bytes 786440 | tf_op jit(solution)/shard_map/ppermute | solution.py:19
  63.8 10.9 %collective-permute-start.21 = (bf16[256,512]{0,1:T(8,128)(2,1)S(1)}, bf16[256,512]{0,1:T(8,128)(2,1)S(1)}, u32[]{:S(2)}, u32[]{:S(2)}) collective-permute-start(bf16[256,512]{0,1:T(8,128)(2,1)S(1)} %dynamic-slice_convert_fusion.3), channel_id=1, source_target_pairs={{0,8},{2,10},{4,12},{6,14},{8,0},{10,2},{12,4},{14,6},{16,24},{18,... | collective-permute-start | bytes 786440 | tf_op jit(solution)/shard_map/ppermute | solution.py:19
  66.7 14.3 %collective-permute-start.11 = (bf16[256,512]{0,1:T(8,128)(2,1)S(1)}, bf16[256,512]{0,1:T(8,128)(2,1)S(1)}, u32[]{:S(2)}, u32[]{:S(2)}) collective-permute-start(bf16[256,512]{0,1:T(8,128)(2,1)S(1)} %dynamic-slice_convert_fusion.6), channel_id=1, source_target_pairs={{0,4},{2,6},{4,0},{6,2},{8,12},{10,14},{12,8},{14,10},{16,20},{18,... | collective-permute-start | bytes 786440 | tf_op jit(solution)/shard_map/ppermute | solution.py:19
  68.3 12.8 %collective-permute-start.12 = (bf16[256,512]{0,1:T(8,128)(2,1)S(1)}, bf16[256,512]{0,1:T(8,128)(2,1)S(1)}, u32[]{:S(2)}, u32[]{:S(2)}) collective-permute-start(bf16[256,512]{0,1:T(8,128)(2,1)S(1)} %dynamic-slice_convert_fusion.5), channel_id=1, source_target_pairs={{0,8},{2,10},{4,12},{6,14},{8,0},{10,2},{12,4},{14,6},{16,24},{18,... | collective-permute-start | bytes 786440 | tf_op jit(solution)/shard_map/ppermute | solution.py:19
  68.4 8.5 %collective-permute-start.13 = (f32[1024]{0:T(1024)S(1)}, f32[1024]{0:T(1024)S(1)}, u32[]{:S(2)}, u32[]{:S(2)}) collective-permute-start(f32[1024]{0:T(1024)S(1)} %add.168), channel_id=1, source_target_pairs={{0,4},{2,6},{4,0},{6,2},{8,12},{10,14},{12,8},{14,10},{16,20},{18,... | collective-permute-start | bytes 12296 | tf_op jit(solution)/shard_map/ppermute | solution.py:19
  71.5 9.4 %collective-permute-start.20 = (bf16[128,512]{0,1:T(8,128)(2,1)S(1)}, bf16[128,512]{0,1:T(8,128)(2,1)S(1)}, u32[]{:S(2)}, u32[]{:S(2)}) collective-permute-start(bf16[128,512]{0,1:T(8,128)(2,1)S(1)} %dynamic-slice_convert_fusion.8), channel_id=1, source_target_pairs={{0,8},{2,10},{4,12},{6,14},{8,0},{10,2},{12,4},{14,6},{16,24},{18,... | collective-permute-start | bytes 393224 | tf_op jit(solution)/shard_map/ppermute | solution.py:19
  74.8 6.1 %collective-permute-start.22 = (bf16[128,512]{0,1:T(8,128)(2,1)S(1)}, bf16[128,512]{0,1:T(8,128)(2,1)S(1)}, u32[]{:S(2)}, u32[]{:S(2)}) collective-permute-start(bf16[128,512]{0,1:T(8,128)(2,1)S(1)} %dynamic-slice_convert_fusion.7), channel_id=1, source_target_pairs={{0,4},{2,6},{4,0},{6,2},{8,12},{10,14},{12,8},{14,10},{16,20},{18,... | collective-permute-start | bytes 393224 | tf_op jit(solution)/shard_map/ppermute | solution.py:19
  81.2 10.1 %collective-permute-start.14 = (bf16[128,512]{0,1:T(8,128)(2,1)S(1)}, bf16[128,512]{0,1:T(8,128)(2,1)S(1)}, u32[]{:S(2)}, u32[]{:S(2)}) collective-permute-start(bf16[128,512]{0,1:T(8,128)(2,1)S(1)} %dynamic-slice_convert_fusion.10), channel_id=1, source_target_pairs={{0,8},{2,10},{4,12},{6,14},{8,0},{10,2},{12,4},{14,6},{16,24},{18,... | collective-permute-start | bytes 393224 | tf_op jit(solution)/shard_map/ppermute | solution.py:19
  83.2 21.9 %collective-permute-start.23 = (bf16[64,1024]{0,1:T(8,128)(2,1)S(1)}, bf16[64,1024]{0,1:T(8,128)(2,1)S(1)}, u32[]{:S(2)}, u32[]{:S(2)}) collective-permute-start(bf16[64,1024]{0,1:T(8,128)(2,1)S(1)} %fusion.9), channel_id=1, source_target_pairs={{0,16},{2,18},{4,20},{6,22},{8,24},{10,26},{12,28},{14,30},{16,0},... | collective-permute-start | bytes 393224 | tf_op jit(solution)/shard_map/ppermute | solution.py:19
  86.5 4.8 %collective-permute-start.16 = (f32[1024]{0:T(1024)S(1)}, f32[1024]{0:T(1024)S(1)}, u32[]{:S(2)}, u32[]{:S(2)}) collective-permute-start(f32[1024]{0:T(1024)S(1)} %add.175), channel_id=1, source_target_pairs={{0,8},{2,10},{4,12},{6,14},{8,0},{10,2},{12,4},{14,6},{16,24},{18,... | collective-permute-start | bytes 12296 | tf_op jit(solution)/shard_map/ppermute | solution.py:19
  86.8 5.0 %collective-permute-start.15 = (bf16[128,512]{0,1:T(8,128)(2,1)S(1)}, bf16[128,512]{0,1:T(8,128)(2,1)S(1)}, u32[]{:S(2)}, u32[]{:S(2)}) collective-permute-start(bf16[128,512]{0,1:T(8,128)(2,1)S(1)} %dynamic-slice_convert_fusion.9), channel_id=1, source_target_pairs={{0,4},{2,6},{4,0},{6,2},{8,12},{10,14},{12,8},{14,10},{16,20},{18,... | collective-permute-start | bytes 393224 | tf_op jit(solution)/shard_map/ppermute | solution.py:19
  91.9 12.6 %collective-permute-start.17 = (f32[1024]{0:T(1024)S(1)}, f32[1024]{0:T(1024)S(1)}, u32[]{:S(2)}, u32[]{:S(2)}) collective-permute-start(f32[1024]{0:T(1024)S(1)} %add.182), channel_id=1, source_target_pairs={{0,16},{2,18},{4,20},{6,22},{8,24},{10,26},{12,28},{14,30},{16,0},... | collective-permute-start | bytes 12296 | tf_op jit(solution)/shard_map/ppermute | solution.py:19
  95.5 13.4 %collective-permute-start.24 = (bf16[64,1024]{0,1:T(8,128)(2,1)S(1)}, bf16[64,1024]{0,1:T(8,128)(2,1)S(1)}, u32[]{:S(2)}, u32[]{:S(2)}) collective-permute-start(bf16[64,1024]{0,1:T(8,128)(2,1)S(1)} %dynamic-slice_convert_fusion.2), channel_id=1, source_target_pairs={{0,16},{2,18},{4,20},{6,22},{8,24},{10,26},{12,28},{14,30},{16,0},... | collective-permute-start | bytes 393224 | tf_op jit(solution)/shard_map/ppermute | solution.py:19
  (14 other events, 133.3 us)

commit v14 on v13

--- a/solution.py
+++ b/solution.py
@@ -28,14 +28,27 @@
     return shaped.transpose(axes).reshape(rows, width)
 
 
-def halving_step(partial, axis, bit):
+def halving_step(partial, axis, bit, code=None):
     me = lax.axis_index(axis)
     half = partial.shape[0] // 2
     mine = (me >> bit) & 1
     keep = lax.dynamic_slice_in_dim(partial, mine * half, half, 0)
-    send = lax.dynamic_slice_in_dim(partial, (1 - mine) * half, half, 0)
-    got = from_partner(send.astype(jnp.bfloat16), axis, bit)
-    return keep + got.astype(jnp.float32)
+    send = lax.dynamic_slice_in_dim(partial, (1 - mine) * half, half, 0).astype(jnp.bfloat16)
+    if code is not None:
+        send = jnp.concatenate([send, code], axis=0)
+    got = from_partner(send, axis, bit)
+    return keep + got[:half].astype(jnp.float32), got[half:]
+
+
+def as_pairs(vector):
+    high = vector.astype(jnp.bfloat16)
+    low = (vector - high.astype(jnp.float32)).astype(jnp.bfloat16)
+    return jnp.concatenate([high, low])
+
+
+def from_pairs(pairs):
+    high, low = pairs.reshape(2, -1)
+    return high.astype(jnp.float32) + low.astype(jnp.float32)
 
 
 def split_orders(levels):
@@ -90,11 +103,12 @@
 
 
 def halving_many(parts, bits, axis, extra, tie):
-    parts = [halving_step(part, axis, bit) for part, bit in zip(parts, bits)]
-    if extra is not None:
-        extra = extra + from_partner(extra, axis, bits[0])
-        if tie:
-            parts, extra = lax.optimization_barrier((parts, extra))
+    if extra is None:
+        return [halving_step(part, axis, bit)[0] for part, bit in zip(parts, bits)], None
+    pairs = as_pairs(extra)
+    first, got = halving_step(parts[0], axis, bits[0], pairs.reshape(-1, parts[0].shape[1]))
+    extra = from_pairs(pairs) + from_pairs(got.reshape(-1))
+    parts = [first] + [halving_step(part, axis, bit)[0] for part, bit in zip(parts[1:], bits[1:])]
     return parts, extra
 
 

time: 113 us -> 126 us (1.12)
  other arithmetic: 8.45 us -> 16.4 us
  waiting for transfers between devices: 37.9 us -> 44.7 us
  starting transfers between devices: 33.4 us -> 29.5 us
  local copies, waits for them, and re-layouts: 7.32 us -> 9.69 us
    ppermute x24 -> x20, waiting for transfers between devices: 32 us -> 39.5 us  [from_partner(): return lax.ppermute(value, axis, pairs)]
    add x15, other arithmetic: 2.11 us -> 7.13 us  [the longest x12 5.07 us: halving_step(): return (keep + got[:half].astype(jnp.float32), got[half:])]
    ppermute x24 -> x20, starting transfers between devices: 31.8 us -> 27.9 us  [from_partner(): return lax.ppermute(value, axis, pairs)]
    unnamed x32 -> x39, local copies, waits for them, and re-layouts: 4.31 us -> 4.8 us
  transfers between devices with their start and end apart: 25 -> 21, of which waited for: 12 -> 12; matrix products, arithmetic and copies ran while one was open for 18% -> 20% of each run, Pallas kernels for 0% -> 0%
where the time goes in v14:
time: 126 us; the launch traced here: 125 us
  waiting for transfers between devices  44.7 us (35%)
  starting transfers between devices  29.5 us (23%)
  other arithmetic  16.4 us (13%)
  matrix products  13 us (10%)
  Pallas kernels  11 us (9%)
  local copies, waits for them, and re-layouts  9.69 us (8%)
  between operations  1.27 us (1%)
    ppermute x20, waiting for transfers between devices, from_partner(): return lax.ppermute(value, axis, pairs)  39.5 us
    ppermute x20, starting transfers between devices, from_partner(): return lax.ppermute(value, axis, pairs)  27.9 us
    pallas_call x1, Pallas kernels, block_attention(): pl.pallas_call(functools.partial(attention_kernel, slots, pairs), grid_sp...  11 us
    ppermute x1, waiting for transfers between devices, head_swap(): return lax.ppermute(value, 'head', [(0, 1), (1, 0)])  5.18 us
    add x12, other arithmetic, halving_step(): return (keep + got[:half].astype(jnp.float32), got[half:])  5.07 us
    dot_general x8, matrix products, scatter_rows(): lax.dot_general(bit_major_rows(left, order), piece, contract, preferred_e...  5.06 us
    unnamed x39, local copies, waits for them, and re-layouts  4.8 us
  transfers between devices with their start and end apart: 21, of which 12 were waited for; matrix products, arithmetic and copies ran while one was open for 20% of the time, Pallas kernels for 0%

profile of v14, /device:TPU:0, one launch (start us, length us, event | category | flops | bytes accessed | tf_op | source)
XLA Modules:
  0.0 125.4 jit_solution(13284872773353106478)
XLA Ops:
  6.7 2.6 %collective-permute-start.1 = (bf16[1,128,1024]{2,1,0:T(8,128)(2,1)S(1)}, bf16[1,128,1024]{2,1,0:T(8,128)(2,1)}, u32[]{:S(2)}, u32[]{:S(2)}) collective-permute-start(bf16[1,128,1024]{2,1,0:T(8,128)(2,1)S(1)} %pad_maximum_fusion.5.refs_0_.refs_5_), channel_id=1, source_target_pairs={{0,4},{2,6},{4,0},{6,2},{8,12},{10,14},{12,8},{14,10},{16,20},{18,... | collective-permute-start | bytes 786440 | tf_op jit(solution)/shard_map/ppermute | solution.py:19
  10.8 2.6 %collective-permute-start.3 = (bf16[1,128,1024]{2,1,0:T(8,128)(2,1)S(1)}, bf16[1,128,1024]{2,1,0:T(8,128)(2,1)}, u32[]{:S(2)}, u32[]{:S(2)}) collective-permute-start(bf16[1,128,1024]{2,1,0:T(8,128)(2,1)S(1)} %pad_maximum_fusion.5.refs_0_.refs_5_), channel_id=1, source_target_pairs={{0,16},{2,18},{4,20},{6,22},{8,24},{10,26},{12,28},{14,30},{16,0},... | collective-permute-start | bytes 786440 | tf_op jit(solution)/shard_map/ppermute | solution.py:19
  17.8 2.1 %fusion.3.g_ref = bf16[1,128,512]{2,1,0:T(8,128)(2,1)} fusion(bf16[128,1024]{1,0:T(8,128)(2,1)} %param.15, bf16[512,1024]{1,0:T(8,128)(2,1)S(1)} %copy-done), kind=kOutput, calls=%fused_computation.16 | convolution fusion | flops 134283264 | bytes 1441792 | tf_op jit(solution)/shard_map/dot_general | solution.py:254
  19.9 3.3 %collective-permute-done.2.refs_3_.refs_8_ = bf16[1,128,1024]{2,1,0:T(8,128)(2,1)} collective-permute-done((bf16[1,128,1024]{2,1,0:T(8,128)(2,1)S(1)}, bf16[1,128,1024]{2,1,0:T(8,128)(2,1)}, u32[]{:S(2)}, u32[]{:S(2)}) %collective-permute-start.2) | collective-permute-done | bytes 262176 | tf_op jit(solution)/shard_map/ppermute | solution.py:19
  23.2 2.4 %collective-permute-done.3.refs_4_.refs_9_ = bf16[1,128,1024]{2,1,0:T(8,128)(2,1)} collective-permute-done((bf16[1,128,1024]{2,1,0:T(8,128)(2,1)S(1)}, bf16[1,128,1024]{2,1,0:T(8,128)(2,1)}, u32[]{:S(2)}, u32[]{:S(2)}) %collective-permute-start.3) | collective-permute-done | bytes 262176 | tf_op jit(solution)/shard_map/ppermute | solution.py:19
  25.6 11.0 %shard_map.135 = (bf16[1,128,512]{2,1,0:T(8,128)(2,1)}, bf16[1,128,512]{2,1,0:T(8,128)(2,1)}, bf16[1,128,1024]{2,1,0:T(8,128)(2,1)}, bf16[1,128,1024]{2,1,0:T(8,...) custom-call(s32[5]{0:T(128)} %add_bitcast_fusion.1.active_ref, ...), custom_call_target="tpu_custom_call" | custom-call | tf_op jit(solution)/shard_map/pallas_call | solution.py:212
  37.0 2.7 %collective-permute-start.6 = (bf16[1,128,1024]{2,1,0:T(8,128)(2,1)}, bf16[1,128,1024]{2,1,0:T(8,128)(2,1)S(1)}, u32[]{:S(2)}, u32[]{:S(2)}) collective-permute-start(bf16[1,128,1024]{2,1,0:T(8,128)(2,1)} %get-tuple-element.19), channel_id=1, source_target_pairs={{0,8},{2,10},{4,12},{6,14},{8,0},{10,2},{12,4},{14,6},{16,24},{18,... | collective-permute-start | bytes 786440 | tf_op jit(solution)/shard_map/ppermute | solution.py:19
  46.8 1.8 %collective-permute-done.7 = bf16[1,128,1024]{2,1,0:T(8,128)(2,1)S(1)} collective-permute-done((bf16[1,128,1024]{2,1,0:T(8,128)(2,1)}, bf16[1,128,1024]{2,1,0:T(8,128)(2,1)S(1)}, u32[]{:S(2)}, u32[]{:S(2)}) %collective-permute-start.7) | collective-permute-done | bytes 262176 | tf_op jit(solution)/shard_map/ppermute | solution.py:19
  53.6 2.0 %copy-done.1 = f32[1024,1024]{1,0:T(8,128)} copy-done((f32[1024,1024]{1,0:T(8,128)}, f32[1024,1024]{1,0:T(8,128)S(1)}, u32[]{:S(2)}) %copy-start.1) | copy-done | bytes 4194328
  55.8 5.2 %collective-permute-done.8 = bf16[128,1536]{1,0:T(8,128)(2,1)S(1)} collective-permute-done((bf16[128,1536]{1,0:T(8,128)(2,1)S(1)}, bf16[128,1536]{1,0:T(8,128)(2,1)S(1)}, u32[]{:S(2)}, u32[]{:S(2)}) %collective-permute-start.8) | collective-permute-done | bytes 393248 | tf_op jit(solution)/shard_map/ppermute | solution.py:122
  64.1 2.2 %convert_add_fusion = f32[512,1024]{0,1:T(8,128)S(1)} fusion(bf16[512,1024]{0,1:T(8,128)(2,1)} %collective-permute-done.15, f32[1024,1024]{0,1:T(8,128)} %copy-done.2, s32[]{:T(128)S(6)} %select_n.57), kind=kLoop, calls=%fused_computation.2 | loop fusion | flops 1048576 | bytes 5242884 | tf_op jit(solution)/shard_map/add | solution.py:40
  70.2 5.1 %collective-permute-done.16 = bf16[256,512]{0,1:T(8,128)(2,1)S(1)} collective-permute-done((bf16[256,512]{0,1:T(8,128)(2,1)S(1)}, bf16[256,512]{0,1:T(8,128)(2,1)S(1)}, u32[]{:S(2)}, u32[]{:S(2)}) %collective-permute-start.16) | collective-permute-done | bytes 262176 | tf_op jit(solution)/shard_map/ppermute | solution.py:19
  75.5 2.1 %collective-permute-start.17 = (bf16[128,512]{0,1:T(8,128)(2,1)S(1)}, bf16[128,512]{0,1:T(8,128)(2,1)S(1)}, u32[]{:S(2)}, u32[]{:S(2)}) collective-permute-start(bf16[128,512]{0,1:T(8,128)(2,1)S(1)} %dynamic-slice_convert_fusion.7), channel_id=1, source_target_pairs={{0,8},{2,10},{4,12},{6,14},{8,0},{10,2},{12,4},{14,6},{16,24},{18,... | collective-permute-start | bytes 393224 | tf_op jit(solution)/shard_map/ppermute | solution.py:19
  78.6 2.3 %collective-permute-done.17 = bf16[128,512]{0,1:T(8,128)(2,1)S(1)} collective-permute-done((bf16[128,512]{0,1:T(8,128)(2,1)S(1)}, bf16[128,512]{0,1:T(8,128)(2,1)S(1)}, u32[]{:S(2)}, u32[]{:S(2)}) %collective-permute-start.17) | collective-permute-done | bytes 131104 | tf_op jit(solution)/shard_map/ppermute | solution.py:19
  81.0 1.8 %collective-permute-done.19 = bf16[128,512]{0,1:T(8,128)(2,1)S(1)} collective-permute-done((bf16[128,512]{0,1:T(8,128)(2,1)S(1)}, bf16[128,512]{0,1:T(8,128)(2,1)S(1)}, u32[]{:S(2)}, u32[]{:S(2)}) %collective-permute-start.19) | collective-permute-done | bytes 131104 | tf_op jit(solution)/shard_map/ppermute | solution.py:19
  82.9 3.3 %collective-permute-start.20 = (bf16[64,1024]{0,1:T(8,128)(2,1)S(1)}, bf16[64,1024]{0,1:T(8,128)(2,1)S(1)}, u32[]{:S(2)}, u32[]{:S(2)}) collective-permute-start(bf16[64,1024]{0,1:T(8,128)(2,1)S(1)} %fusion.9), channel_id=1, source_target_pairs={{0,16},{2,18},{4,20},{6,22},{8,24},{10,26},{12,28},{14,30},{16,0},... | collective-permute-start | bytes 393224 | tf_op jit(solution)/shard_map/ppermute | solution.py:19
  86.9 9.7 %collective-permute-done.20 = bf16[64,1024]{0,1:T(8,128)(2,1)S(1)} collective-permute-done((bf16[64,1024]{0,1:T(8,128)(2,1)S(1)}, bf16[64,1024]{0,1:T(8,128)(2,1)S(1)}, u32[]{:S(2)}, u32[]{:S(2)}) %collective-permute-start.20) | collective-permute-done | bytes 131104 | tf_op jit(solution)/shard_map/ppermute | solution.py:19
  98.9 2.2 %convert_add_fusion.1 = f32[512,1024]{1,0:T(8,128)S(1)} fusion(f32[1024,1024]{1,0:T(8,128)} %copy-done.1, s32[]{:T(128)S(6)} %select_n.57, bf16[514,1024]{1,0:T(8,128)(2,1)} %collective-permute-done.9), kind=kLoop, calls=%fused_computation.4 | loop fusion | flops 1048576 | bytes 5242884 | tf_op jit(solution)/shard_map/add | solution.py:40
  103.3 5.6 %collective-permute-done.12 = bf16[256,512]{1,0:T(8,128)(2,1)S(1)} collective-permute-done((bf16[256,512]{1,0:T(8,128)(2,1)S(1)}, bf16[256,512]{1,0:T(8,128)(2,1)S(1)}, u32[]{:S(2)}, u32[]{:S(2)}) %collective-permute-start.12) | collective-permute-done | bytes 262176 | tf_op jit(solution)/shard_map/ppermute | solution.py:19
  108.9 1.8 %collective-permute-start.13 = (bf16[128,512]{1,0:T(8,128)(2,1)S(1)}, bf16[128,512]{1,0:T(8,128)(2,1)S(1)}, u32[]{:S(2)}, u32[]{:S(2)}) collective-permute-start(bf16[128,512]{1,0:T(8,128)(2,1)S(1)} %dynamic-slice_convert_fusion.8), channel_id=1, source_target_pairs={{0,4},{2,6},{4,0},{6,2},{8,12},{10,14},{12,8},{14,10},{16,20},{18,... | collective-permute-start | bytes 393224 | tf_op jit(solution)/shard_map/ppermute | solution.py:19
  111.3 2.7 %collective-permute-done.13 = bf16[128,512]{1,0:T(8,128)(2,1)S(1)} collective-permute-done((bf16[128,512]{1,0:T(8,128)(2,1)S(1)}, bf16[128,512]{1,0:T(8,128)(2,1)S(1)}, u32[]{:S(2)}, u32[]{:S(2)}) %collective-permute-start.13) | collective-permute-done | bytes 131104 | tf_op jit(solution)/shard_map/ppermute | solution.py:19
  114.0 2.0 %collective-permute-done.11 = bf16[132,512]{1,0:T(8,128)(2,1)S(1)} collective-permute-done((bf16[132,512]{1,0:T(8,128)(2,1)S(1)}, bf16[132,512]{1,0:T(8,128)(2,1)S(1)}, u32[]{:S(2)}, u32[]{:S(2)}) %collective-permute-start.11) | collective-permute-done | bytes 135200 | tf_op jit(solution)/shard_map/ppermute | solution.py:19
  116.2 3.4 %collective-permute-start.14 = (bf16[66,1024]{1,0:T(8,128)(2,1)S(1)}, bf16[66,1024]{1,0:T(8,128)(2,1)S(1)}, u32[]{:S(2)}, u32[]{:S(2)}) collective-permute-start(bf16[66,1024]{1,0:T(8,128)(2,1)S(1)} %pad_maximum_fusion.7), channel_id=1, source_target_pairs={{0,16},{2,18},{4,20},{6,22},{8,24},{10,26},{12,28},{14,30},{16,0},... | collective-permute-start | bytes 405512 | tf_op jit(solution)/shard_map/ppermute | solution.py:19
  121.2 2.8 %collective-permute-done.14 = bf16[66,1024]{1,0:T(8,128)(2,1)S(1)} collective-permute-done((bf16[66,1024]{1,0:T(8,128)(2,1)S(1)}, bf16[66,1024]{1,0:T(8,128)(2,1)S(1)}, u32[]{:S(2)}, u32[]{:S(2)}) %collective-permute-start.14) | collective-permute-done | bytes 135200 | tf_op jit(solution)/shard_map/ppermute | solution.py:19
  (144 shorter events, 41.4 us)
Async XLA Ops:
  1.9 59.1 %copy-start.14 = (f32[128]{0:T(128)}, f32[128]{0:T(128)S(1)}, u32[]{:S(2)}) copy-start(f32[128]{0:T(128)S(1)} %add_rsqrt_fusion) | copy-start | bytes 1540
  6.1 19.5 %copy-start.7 = (bf16[1,128,1024]{2,1,0:T(8,128)(2,1)}, bf16[1,128,1024]{2,1,0:T(8,128)(2,1)S(1)}, u32[]{:S(2)}) copy-start(bf16[1,128,1024]{2,1,0:T(8,128)(2,1)S(1)} %pad_maximum_fusion.5.refs_0_.refs_5_) | copy-start | bytes 786436
  6.1 13.8 %collective-permute-start = (bf16[1,128,1024]{2,1,0:T(8,128)(2,1)S(1)}, bf16[1,128,1024]{2,1,0:T(8,128)(2,1)S(1)}, u32[]{:S(2)}, u32[]{:S(2)}) collective-permute-start(bf16[1,128,1024]{2,1,0:T(8,128)(2,1)S(1)} %pad_maximum_fusion.5.refs_0_.refs_5_), channel_id=1, source_target_pairs={{0,2},{2,0},{4,6},{6,4},{8,10},{10,8},{12,14},{14,12},{16,18},{18,... | collective-permute-start | bytes 786440 | tf_op jit(solution)/shard_map/ppermute | solution.py:19
  6.7 13.3 %collective-permute-start.1 = (bf16[1,128,1024]{2,1,0:T(8,128)(2,1)S(1)}, bf16[1,128,1024]{2,1,0:T(8,128)(2,1)}, u32[]{:S(2)}, u32[]{:S(2)}) collective-permute-start(bf16[1,128,1024]{2,1,0:T(8,128)(2,1)S(1)} %pad_maximum_fusion.5.refs_0_.refs_5_), channel_id=1, source_target_pairs={{0,4},{2,6},{4,0},{6,2},{8,12},{10,14},{12,8},{14,10},{16,20},{18,... | collective-permute-start | bytes 786440 | tf_op jit(solution)/shard_map/ppermute | solution.py:19
  9.2 14.0 %collective-permute-start.2 = (bf16[1,128,1024]{2,1,0:T(8,128)(2,1)S(1)}, bf16[1,128,1024]{2,1,0:T(8,128)(2,1)}, u32[]{:S(2)}, u32[]{:S(2)}) collective-permute-start(bf16[1,128,1024]{2,1,0:T(8,128)(2,1)S(1)} %pad_maximum_fusion.5.refs_0_.refs_5_), channel_id=1, source_target_pairs={{0,8},{2,10},{4,12},{6,14},{8,0},{10,2},{12,4},{14,6},{16,24},{18,... | collective-permute-start | bytes 786440 | tf_op jit(solution)/shard_map/ppermute | solution.py:19
  10.8 14.8 %collective-permute-start.3 = (bf16[1,128,1024]{2,1,0:T(8,128)(2,1)S(1)}, bf16[1,128,1024]{2,1,0:T(8,128)(2,1)}, u32[]{:S(2)}, u32[]{:S(2)}) collective-permute-start(bf16[1,128,1024]{2,1,0:T(8,128)(2,1)S(1)} %pad_maximum_fusion.5.refs_0_.refs_5_), channel_id=1, source_target_pairs={{0,16},{2,18},{4,20},{6,22},{8,24},{10,26},{12,28},{14,30},{16,0},... | collective-permute-start | bytes 786440 | tf_op jit(solution)/shard_map/ppermute | solution.py:19
  17.8 26.1 %copy-start.9 = (bf16[128,2,2,2,2,64]{0,5,4,3,2,1:T(8,128)(2,1)S(1)}, bf16[128,2,2,2,2,64]{0,5,4,3,2,1:T(8,128)(2,1)}, u32[]{:S(2)}) copy-start(bf16[128,2,2,2,2,64]{0,5,4,3,2,1:T(8,128)(2,1)} %copy.63) | copy-start | bytes 786436
  36.6 12.0 %collective-permute-start.7 = (bf16[1,128,1024]{2,1,0:T(8,128)(2,1)}, bf16[1,128,1024]{2,1,0:T(8,128)(2,1)S(1)}, u32[]{:S(2)}, u32[]{:S(2)}) collective-permute-start(bf16[1,128,1024]{2,1,0:T(8,128)(2,1)} %get-tuple-element.20), channel_id=1, source_target_pairs={{0,16},{2,18},{4,20},{6,22},{8,24},{10,26},{12,28},{14,30},{16,0},... | collective-permute-start | bytes 786440 | tf_op jit(solution)/shard_map/ppermute | solution.py:19
  37.0 11.6 %collective-permute-start.6 = (bf16[1,128,1024]{2,1,0:T(8,128)(2,1)}, bf16[1,128,1024]{2,1,0:T(8,128)(2,1)S(1)}, u32[]{:S(2)}, u32[]{:S(2)}) collective-permute-start(bf16[1,128,1024]{2,1,0:T(8,128)(2,1)} %get-tuple-element.19), channel_id=1, source_target_pairs={{0,8},{2,10},{4,12},{6,14},{8,0},{10,2},{12,4},{14,6},{16,24},{18,... | collective-permute-start | bytes 786440 | tf_op jit(solution)/shard_map/ppermute | solution.py:19
  39.7 8.9 %collective-permute-start.5 = (bf16[1,128,1024]{2,1,0:T(8,128)(2,1)}, bf16[1,128,1024]{2,1,0:T(8,128)(2,1)S(1)}, u32[]{:S(2)}, u32[]{:S(2)}) collective-permute-start(bf16[1,128,1024]{2,1,0:T(8,128)(2,1)} %get-tuple-element.18), channel_id=1, source_target_pairs={{0,4},{2,6},{4,0},{6,2},{8,12},{10,14},{12,8},{14,10},{16,20},{18,... | collective-permute-start | bytes 786440 | tf_op jit(solution)/shard_map/ppermute | solution.py:19
  40.2 8.4 %collective-permute-start.4 = (bf16[1,128,1024]{2,1,0:T(8,128)(2,1)}, bf16[1,128,1024]{2,1,0:T(8,128)(2,1)S(1)}, u32[]{:S(2)}, u32[]{:S(2)}) collective-permute-start(bf16[1,128,1024]{2,1,0:T(8,128)(2,1)} %get-tuple-element.17), channel_id=1, source_target_pairs={{0,2},{2,0},{4,6},{6,4},{8,10},{10,8},{12,14},{14,12},{16,18},{18,... | collective-permute-start | bytes 786440 | tf_op jit(solution)/shard_map/ppermute | solution.py:19
  45.9 18.1 %collective-permute-start.15 = (bf16[512,1024]{0,1:T(8,128)(2,1)}, bf16[512,1024]{0,1:T(8,128)(2,1)}, u32[]{:S(2)}, u32[]{:S(2)}) collective-permute-start(bf16[512,1024]{0,1:T(8,128)(2,1)} %dynamic-slice_convert_fusion), channel_id=1, source_target_pairs={{0,2},{2,0},{4,6},{6,4},{8,10},{10,8},{12,14},{14,12},{16,18},{18,... | collective-permute-start | bytes 3145736 | tf_op jit(solution)/shard_map/ppermute | solution.py:19
  51.1 9.9 %collective-permute-start.8 = (bf16[128,1536]{1,0:T(8,128)(2,1)S(1)}, bf16[128,1536]{1,0:T(8,128)(2,1)S(1)}, u32[]{:S(2)}, u32[]{:S(2)}) collective-permute-start(bf16[128,1536]{1,0:T(8,128)(2,1)S(1)} %pad_maximum_fusion.3), channel_id=1, source_target_pairs={{0,1},{1,0},{2,3},{3,2},{4,5},{5,4},{6,7},{7,6},{8,9},{9,8},{10,11... | collective-permute-start | bytes 1179656 | tf_op jit(solution)/shard_map/ppermute | solution.py:122
  63.3 33.5 %collective-permute-start.9 = (bf16[514,1024]{1,0:T(8,128)(2,1)S(1)}, bf16[514,1024]{1,0:T(8,128)(2,1)}, u32[]{:S(2)}, u32[]{:S(2)}) collective-permute-start(bf16[514,1024]{1,0:T(8,128)(2,1)S(1)} %pad_maximum_fusion.2), channel_id=1, source_target_pairs={{0,2},{2,0},{4,6},{6,4},{8,10},{10,8},{12,14},{14,12},{16,18},{18,... | collective-permute-start | bytes 3158024 | tf_op jit(solution)/shard_map/ppermute | solution.py:19
  66.6 8.8 %collective-permute-start.16 = (bf16[256,512]{0,1:T(8,128)(2,1)S(1)}, bf16[256,512]{0,1:T(8,128)(2,1)S(1)}, u32[]{:S(2)}, u32[]{:S(2)}) collective-permute-start(bf16[256,512]{0,1:T(8,128)(2,1)S(1)} %dynamic-slice_convert_fusion.3), channel_id=1, source_target_pairs={{0,4},{2,6},{4,0},{6,2},{8,12},{10,14},{12,8},{14,10},{16,20},{18,... | collective-permute-start | bytes 786440 | tf_op jit(solution)/shard_map/ppermute | solution.py:19
  69.1 8.5 %collective-permute-start.18 = (bf16[256,512]{0,1:T(8,128)(2,1)S(1)}, bf16[256,512]{0,1:T(8,128)(2,1)S(1)}, u32[]{:S(2)}, u32[]{:S(2)}) collective-permute-start(bf16[256,512]{0,1:T(8,128)(2,1)S(1)} %dynamic-slice_convert_fusion.2), channel_id=1, source_target_pairs={{0,8},{2,10},{4,12},{6,14},{8,0},{10,2},{12,4},{14,6},{16,24},{18,... | collective-permute-start | bytes 786440 | tf_op jit(solution)/shard_map/ppermute | solution.py:19
  75.5 5.5 %collective-permute-start.17 = (bf16[128,512]{0,1:T(8,128)(2,1)S(1)}, bf16[128,512]{0,1:T(8,128)(2,1)S(1)}, u32[]{:S(2)}, u32[]{:S(2)}) collective-permute-start(bf16[128,512]{0,1:T(8,128)(2,1)S(1)} %dynamic-slice_convert_fusion.7), channel_id=1, source_target_pairs={{0,8},{2,10},{4,12},{6,14},{8,0},{10,2},{12,4},{14,6},{16,24},{18,... | collective-permute-start | bytes 393224 | tf_op jit(solution)/shard_map/ppermute | solution.py:19
  77.7 5.0 %collective-permute-start.19 = (bf16[128,512]{0,1:T(8,128)(2,1)S(1)}, bf16[128,512]{0,1:T(8,128)(2,1)S(1)}, u32[]{:S(2)}, u32[]{:S(2)}) collective-permute-start(bf16[128,512]{0,1:T(8,128)(2,1)S(1)} %dynamic-slice_convert_fusion.6), channel_id=1, source_target_pairs={{0,4},{2,6},{4,0},{6,2},{8,12},{10,14},{12,8},{14,10},{16,20},{18,... | collective-permute-start | bytes 393224 | tf_op jit(solution)/shard_map/ppermute | solution.py:19
  82.9 13.8 %collective-permute-start.20 = (bf16[64,1024]{0,1:T(8,128)(2,1)S(1)}, bf16[64,1024]{0,1:T(8,128)(2,1)S(1)}, u32[]{:S(2)}, u32[]{:S(2)}) collective-permute-start(bf16[64,1024]{0,1:T(8,128)(2,1)S(1)} %fusion.9), channel_id=1, source_target_pairs={{0,16},{2,18},{4,20},{6,22},{8,24},{10,26},{12,28},{14,30},{16,0},... | collective-permute-start | bytes 393224 | tf_op jit(solution)/shard_map/ppermute | solution.py:19
  101.3 7.5 %collective-permute-start.12 = (bf16[256,512]{1,0:T(8,128)(2,1)S(1)}, bf16[256,512]{1,0:T(8,128)(2,1)S(1)}, u32[]{:S(2)}, u32[]{:S(2)}) collective-permute-start(bf16[256,512]{1,0:T(8,128)(2,1)S(1)} %dynamic-slice_convert_fusion.4), channel_id=1, source_target_pairs={{0,8},{2,10},{4,12},{6,14},{8,0},{10,2},{12,4},{14,6},{16,24},{18,... | collective-permute-start | bytes 786440 | tf_op jit(solution)/shard_map/ppermute | solution.py:19
  102.0 8.8 %collective-permute-start.10 = (bf16[260,512]{1,0:T(8,128)(2,1)S(1)}, bf16[260,512]{1,0:T(8,128)(2,1)S(1)}, u32[]{:S(2)}, u32[]{:S(2)}) collective-permute-start(bf16[260,512]{1,0:T(8,128)(2,1)S(1)} %pad_maximum_fusion.4), channel_id=1, source_target_pairs={{0,4},{2,6},{4,0},{6,2},{8,12},{10,14},{12,8},{14,10},{16,20},{18,... | collective-permute-start | bytes 798728 | tf_op jit(solution)/shard_map/ppermute | solution.py:19
  108.9 5.0 %collective-permute-start.13 = (bf16[128,512]{1,0:T(8,128)(2,1)S(1)}, bf16[128,512]{1,0:T(8,128)(2,1)S(1)}, u32[]{:S(2)}, u32[]{:S(2)}) collective-permute-start(bf16[128,512]{1,0:T(8,128)(2,1)S(1)} %dynamic-slice_convert_fusion.8), channel_id=1, source_target_pairs={{0,4},{2,6},{4,0},{6,2},{8,12},{10,14},{12,8},{14,10},{16,20},{18,... | collective-permute-start | bytes 393224 | tf_op jit(solution)/shard_map/ppermute | solution.py:19
  110.9 5.1 %collective-permute-start.11 = (bf16[132,512]{1,0:T(8,128)(2,1)S(1)}, bf16[132,512]{1,0:T(8,128)(2,1)S(1)}, u32[]{:S(2)}, u32[]{:S(2)}) collective-permute-start(bf16[132,512]{1,0:T(8,128)(2,1)S(1)} %pad_maximum_fusion.8), channel_id=1, source_target_pairs={{0,8},{2,10},{4,12},{6,14},{8,0},{10,2},{12,4},{14,6},{16,24},{18,... | collective-permute-start | bytes 405512 | tf_op jit(solution)/shard_map/ppermute | solution.py:19
  116.2 7.8 %collective-permute-start.14 = (bf16[66,1024]{1,0:T(8,128)(2,1)S(1)}, bf16[66,1024]{1,0:T(8,128)(2,1)S(1)}, u32[]{:S(2)}, u32[]{:S(2)}) collective-permute-start(bf16[66,1024]{1,0:T(8,128)(2,1)S(1)} %pad_maximum_fusion.7), channel_id=1, source_target_pairs={{0,16},{2,18},{4,20},{6,22},{8,24},{10,26},{12,28},{14,30},{16,0},... | collective-permute-start | bytes 405512 | tf_op jit(solution)/shard_map/ppermute | solution.py:19
  (14 other events, 99.4 us)

commit v15 on v13

--- a/solution.py
+++ b/solution.py
@@ -2,6 +2,7 @@
 import jax.numpy as jnp
 from jax import lax
 from jax.sharding import PartitionSpec as P
+from jax.experimental.layout import Layout, with_layout_constraint
 import functools
 from jax.experimental import pallas as pl
 from jax.experimental.pallas import tpu as pltpu
@@ -60,7 +61,7 @@
                 )
             )
     first = sum(right.shape[1] // 2 for left, right in pairs)
-    joined = jnp.concatenate(chunks, axis=1)
+    joined = with_layout_constraint(jnp.concatenate(chunks, axis=1), Layout((0, 1)))
     parts = None
     for step in range(levels):
         bit_a, bit_b = orders[0][step], orders[1][step]

time: 113 us -> 103 us (0.912)
  waiting for transfers between devices: 37.9 us -> 30.1 us
  local copies, waits for them, and re-layouts: 7.32 us -> 3.93 us
  other arithmetic: 8.45 us -> 10.9 us
    ppermute x24, waiting for transfers between devices: 32 us -> 24 us  [from_partner(): return lax.ppermute(value, axis, pairs)]
    unnamed x32 -> x28, local copies, waits for them, and re-layouts: 4.31 us -> 1.22 us
    concatenate x3, other arithmetic: 0.06 us -> 1.99 us  [scatter_rows(): jnp.concatenate([joined[:, offset:offset + cut], joined[:, first + offset...]
  transfers between devices with their start and end apart: 25 -> 25, of which waited for: 12 -> 11; matrix products, arithmetic and copies ran while one was open for 18% -> 19% of each run, Pallas kernels for 0% -> 0%
where the time goes in v15:
time: 103 us
  starting transfers between devices  33 us (32%)
  waiting for transfers between devices  30.1 us (29%)
  matrix products  12.8 us (12%)
  Pallas kernels  11 us (11%)
  other arithmetic  10.9 us (11%)
  local copies, waits for them, and re-layouts  3.93 us (4%)
  between operations  1.21 us (1%)
    ppermute x24, starting transfers between devices, from_partner(): return lax.ppermute(value, axis, pairs)  31.4 us
    ppermute x24, waiting for transfers between devices, from_partner(): return lax.ppermute(value, axis, pairs)  24 us
    pallas_call x1, Pallas kernels, block_attention(): pl.pallas_call(functools.partial(attention_kernel, slots, pairs), grid_sp...  11 us
    ppermute x1, waiting for transfers between devices, head_swap(): return lax.ppermute(value, 'head', [(0, 1), (1, 0)])  6.05 us
    dot_general x8, matrix products, scatter_rows(): lax.dot_general(bit_major_rows(left, order), piece, contract, preferred_e...  4.86 us
    dot_general x1, matrix products, shards(): jnp.dot(cotangent, w_out.T, preferred_element_type=jnp.float32)  2.14 us
  transfers between devices with their start and end apart: 25, of which 11 were waited for; matrix products, arithmetic and copies ran while one was open for 19% of the time, Pallas kernels for 0%

profile of v15, /device:TPU:0, one launch (start us, length us, event | category | flops | bytes accessed | tf_op | source)
XLA Modules:
  0.0 102.9 jit_solution(14882195492535624823)
XLA Ops:
  3.0 1.5 %fusion.5 = bf16[1,128,512]{2,1,0:T(8,128)(2,1)S(1)} fusion(bf16[128,1024]{1,0:T(8,128)(2,1)S(1)} %fusion.8, bf16[1024,512]{1,0:T(8,128)(2,1)} %param.12), kind=kOutput, calls=%fused_computation.18 | convolution fusion | flops 134283264 | bytes 1441792 | tf_op jit(solution)/shard_map/dot_general | solution.py:227
  6.7 2.6 %collective-permute-start.1 = (bf16[1,128,1024]{2,1,0:T(8,128)(2,1)S(1)}, bf16[1,128,1024]{2,1,0:T(8,128)(2,1)}, u32[]{:S(2)}, u32[]{:S(2)}) collective-permute-start(bf16[1,128,1024]{2,1,0:T(8,128)(2,1)S(1)} %pad_maximum_fusion.3.refs_0_.refs_5_), channel_id=1, source_target_pairs={{0,4},{2,6},{4,0},{6,2},{8,12},{10,14},{12,8},{14,10},{16,20},{18,... | collective-permute-start | bytes 786440 | tf_op jit(solution)/shard_map/ppermute | solution.py:20
  9.3 1.6 %collective-permute-start.2 = (bf16[1,128,1024]{2,1,0:T(8,128)(2,1)S(1)}, bf16[1,128,1024]{2,1,0:T(8,128)(2,1)}, u32[]{:S(2)}, u32[]{:S(2)}) collective-permute-start(bf16[1,128,1024]{2,1,0:T(8,128)(2,1)S(1)} %pad_maximum_fusion.3.refs_0_.refs_5_), channel_id=1, source_target_pairs={{0,8},{2,10},{4,12},{6,14},{8,0},{10,2},{12,4},{14,6},{16,24},{18,... | collective-permute-start | bytes 786440 | tf_op jit(solution)/shard_map/ppermute | solution.py:20
  10.8 2.6 %collective-permute-start.3 = (bf16[1,128,1024]{2,1,0:T(8,128)(2,1)S(1)}, bf16[1,128,1024]{2,1,0:T(8,128)(2,1)}, u32[]{:S(2)}, u32[]{:S(2)}) collective-permute-start(bf16[1,128,1024]{2,1,0:T(8,128)(2,1)S(1)} %pad_maximum_fusion.3.refs_0_.refs_5_), channel_id=1, source_target_pairs={{0,16},{2,18},{4,20},{6,22},{8,24},{10,26},{12,28},{14,30},{16,0},... | collective-permute-start | bytes 786440 | tf_op jit(solution)/shard_map/ppermute | solution.py:20
  17.8 2.1 %fusion.3.g_ref = bf16[1,128,512]{2,1,0:T(8,128)(2,1)} fusion(bf16[128,1024]{1,0:T(8,128)(2,1)} %param.15, bf16[512,1024]{1,0:T(8,128)(2,1)S(1)} %copy-done), kind=kOutput, calls=%fused_computation.16 | convolution fusion | flops 134283264 | bytes 1441792 | tf_op jit(solution)/shard_map/dot_general | solution.py:241
  20.0 3.3 %collective-permute-done.2.refs_3_.refs_8_ = bf16[1,128,1024]{2,1,0:T(8,128)(2,1)} collective-permute-done((bf16[1,128,1024]{2,1,0:T(8,128)(2,1)S(1)}, bf16[1,128,1024]{2,1,0:T(8,128)(2,1)}, u32[]{:S(2)}, u32[]{:S(2)}) %collective-permute-start.2) | collective-permute-done | bytes 262176 | tf_op jit(solution)/shard_map/ppermute | solution.py:20
  23.2 2.4 %collective-permute-done.3.refs_4_.refs_9_ = bf16[1,128,1024]{2,1,0:T(8,128)(2,1)} collective-permute-done((bf16[1,128,1024]{2,1,0:T(8,128)(2,1)S(1)}, bf16[1,128,1024]{2,1,0:T(8,128)(2,1)}, u32[]{:S(2)}, u32[]{:S(2)}) %collective-permute-start.3) | collective-permute-done | bytes 262176 | tf_op jit(solution)/shard_map/ppermute | solution.py:20
  25.6 11.0 %shard_map.135 = (bf16[1,128,512]{2,1,0:T(8,128)(2,1)}, bf16[1,128,512]{2,1,0:T(8,128)(2,1)}, bf16[1,128,1024]{2,1,0:T(8,128)(2,1)}, bf16[1,128,1024]{2,1,0:T(8,...) custom-call(s32[5]{0:T(128)} %add_bitcast_fusion.active_ref, ...), custom_call_target="tpu_custom_call" | custom-call | tf_op jit(solution)/shard_map/pallas_call | solution.py:199
  37.0 2.7 %collective-permute-start.6 = (bf16[1,128,1024]{2,1,0:T(8,128)(2,1)}, bf16[1,128,1024]{2,1,0:T(8,128)(2,1)S(1)}, u32[]{:S(2)}, u32[]{:S(2)}) collective-permute-start(bf16[1,128,1024]{2,1,0:T(8,128)(2,1)} %get-tuple-element.27), channel_id=1, source_target_pairs={{0,8},{2,10},{4,12},{6,14},{8,0},{10,2},{12,4},{14,6},{16,24},{18,... | collective-permute-start | bytes 786440 | tf_op jit(solution)/shard_map/ppermute | solution.py:20
  45.7 2.9 %collective-permute-done.7 = bf16[1,128,1024]{2,1,0:T(8,128)(2,1)S(1)} collective-permute-done((bf16[1,128,1024]{2,1,0:T(8,128)(2,1)}, bf16[1,128,1024]{2,1,0:T(8,128)(2,1)S(1)}, u32[]{:S(2)}, u32[]{:S(2)}) %collective-permute-start.7) | collective-permute-done | bytes 262176 | tf_op jit(solution)/shard_map/ppermute | solution.py:20
  51.1 1.6 %collective-permute-start.8 = (bf16[128,1536]{1,0:T(8,128)(2,1)S(1)}, bf16[128,1536]{1,0:T(8,128)(2,1)S(1)}, u32[]{:S(2)}, u32[]{:S(2)}) collective-permute-start(bf16[128,1536]{1,0:T(8,128)(2,1)S(1)} %pad_maximum_fusion.2), channel_id=1, source_target_pairs={{0,1},{1,0},{2,3},{3,2},{4,5},{5,4},{6,7},{7,6},{8,9},{9,8},{10,11... | collective-permute-start | bytes 1179656 | tf_op jit(solution)/shard_map/ppermute | solution.py:109
  53.9 6.0 %collective-permute-done.8 = bf16[128,1536]{1,0:T(8,128)(2,1)S(1)} collective-permute-done((bf16[128,1536]{1,0:T(8,128)(2,1)S(1)}, bf16[128,1536]{1,0:T(8,128)(2,1)S(1)}, u32[]{:S(2)}, u32[]{:S(2)}) %collective-permute-start.8) | collective-permute-done | bytes 393248 | tf_op jit(solution)/shard_map/ppermute | solution.py:109
  63.5 2.3 %collective-permute-start.21 = (bf16[256,512]{1,0:T(8,128)(2,1)S(1)}, bf16[256,512]{1,0:T(8,128)(2,1)S(1)}, u32[]{:S(2)}, u32[]{:S(2)}) collective-permute-start(bf16[256,512]{1,0:T(8,128)(2,1)S(1)} %dynamic-slice_convert_fusion.2), channel_id=1, source_target_pairs={{0,8},{2,10},{4,12},{6,14},{8,0},{10,2},{12,4},{14,6},{16,24},{18,... | collective-permute-start | bytes 786440 | tf_op jit(solution)/shard_map/ppermute | solution.py:20
  66.5 1.6 %collective-permute-start.11 = (bf16[256,512]{1,0:T(8,128)(2,1)S(1)}, bf16[256,512]{1,0:T(8,128)(2,1)S(1)}, u32[]{:S(2)}, u32[]{:S(2)}) collective-permute-start(bf16[256,512]{1,0:T(8,128)(2,1)S(1)} %dynamic-slice_convert_fusion.5), channel_id=1, source_target_pairs={{0,4},{2,6},{4,0},{6,2},{8,12},{10,14},{12,8},{14,10},{16,20},{18,... | collective-permute-start | bytes 786440 | tf_op jit(solution)/shard_map/ppermute | solution.py:20
  68.8 2.4 %collective-permute-done.19 = bf16[256,512]{1,0:T(8,128)(2,1)S(1)} collective-permute-done((bf16[256,512]{1,0:T(8,128)(2,1)S(1)}, bf16[256,512]{1,0:T(8,128)(2,1)S(1)}, u32[]{:S(2)}, u32[]{:S(2)}) %collective-permute-start.19) | collective-permute-done | bytes 262176 | tf_op jit(solution)/shard_map/ppermute | solution.py:20
  71.3 3.2 %collective-permute-start.20 = (bf16[128,512]{1,0:T(8,128)(2,1)S(1)}, bf16[128,512]{1,0:T(8,128)(2,1)S(1)}, u32[]{:S(2)}, u32[]{:S(2)}) collective-permute-start(bf16[128,512]{1,0:T(8,128)(2,1)S(1)} %dynamic-slice_convert_fusion.8), channel_id=1, source_target_pairs={{0,8},{2,10},{4,12},{6,14},{8,0},{10,2},{12,4},{14,6},{16,24},{18,... | collective-permute-start | bytes 393224 | tf_op jit(solution)/shard_map/ppermute | solution.py:20
  76.6 4.3 %collective-permute-done.20 = bf16[128,512]{1,0:T(8,128)(2,1)S(1)} collective-permute-done((bf16[128,512]{1,0:T(8,128)(2,1)S(1)}, bf16[128,512]{1,0:T(8,128)(2,1)S(1)}, u32[]{:S(2)}, u32[]{:S(2)}) %collective-permute-start.20) | collective-permute-done | bytes 131104 | tf_op jit(solution)/shard_map/ppermute | solution.py:20
  81.2 1.8 %collective-permute-start.14 = (bf16[128,512]{1,0:T(8,128)(2,1)S(1)}, bf16[128,512]{1,0:T(8,128)(2,1)S(1)}, u32[]{:S(2)}, u32[]{:S(2)}) collective-permute-start(bf16[128,512]{1,0:T(8,128)(2,1)S(1)} %dynamic-slice_convert_fusion.10), channel_id=1, source_target_pairs={{0,8},{2,10},{4,12},{6,14},{8,0},{10,2},{12,4},{14,6},{16,24},{18,... | collective-permute-start | bytes 393224 | tf_op jit(solution)/shard_map/ppermute | solution.py:20
  83.0 3.3 %collective-permute-start.23 = (bf16[64,1024]{1,0:T(8,128)(2,1)S(1)}, bf16[64,1024]{1,0:T(8,128)(2,1)S(1)}, u32[]{:S(2)}, u32[]{:S(2)}) collective-permute-start(bf16[64,1024]{1,0:T(8,128)(2,1)S(1)} %fusion.19), channel_id=1, source_target_pairs={{0,16},{2,18},{4,20},{6,22},{8,24},{10,26},{12,28},{14,30},{16,0},... | collective-permute-start | bytes 393224 | tf_op jit(solution)/shard_map/ppermute | solution.py:20
  86.6 1.6 %collective-permute-start.15 = (bf16[128,512]{1,0:T(8,128)(2,1)S(1)}, bf16[128,512]{1,0:T(8,128)(2,1)S(1)}, u32[]{:S(2)}, u32[]{:S(2)}) collective-permute-start(bf16[128,512]{1,0:T(8,128)(2,1)S(1)} %dynamic-slice_convert_fusion.9), channel_id=1, source_target_pairs={{0,4},{2,6},{4,0},{6,2},{8,12},{10,14},{12,8},{14,10},{16,20},{18,... | collective-permute-start | bytes 393224 | tf_op jit(solution)/shard_map/ppermute | solution.py:20
  88.2 1.8 %collective-permute-done.16 = f32[1024]{0:T(1024)S(1)} collective-permute-done((f32[1024]{0:T(1024)S(1)}, f32[1024]{0:T(1024)S(1)}, u32[]{:S(2)}, u32[]{:S(2)}) %collective-permute-start.16) | collective-permute-done | bytes 4128 | tf_op jit(solution)/shard_map/ppermute | solution.py:20
  90.0 1.6 %collective-permute-done.15 = bf16[128,512]{1,0:T(8,128)(2,1)S(1)} collective-permute-done((bf16[128,512]{1,0:T(8,128)(2,1)S(1)}, bf16[128,512]{1,0:T(8,128)(2,1)S(1)}, u32[]{:S(2)}, u32[]{:S(2)}) %collective-permute-start.15) | collective-permute-done | bytes 131104 | tf_op jit(solution)/shard_map/ppermute | solution.py:20
  92.7 2.1 %collective-permute-start.24 = (bf16[64,1024]{1,0:T(8,128)(2,1)S(1)}, bf16[64,1024]{1,0:T(8,128)(2,1)S(1)}, u32[]{:S(2)}, u32[]{:S(2)}) collective-permute-start(bf16[64,1024]{1,0:T(8,128)(2,1)S(1)} %dynamic-slice_convert_fusion.6), channel_id=1, source_target_pairs={{0,16},{2,18},{4,20},{6,22},{8,24},{10,26},{12,28},{14,30},{16,0},... | collective-permute-start | bytes 393224 | tf_op jit(solution)/shard_map/ppermute | solution.py:20
  97.0 3.1 %collective-permute-done.24 = bf16[64,1024]{1,0:T(8,128)(2,1)S(1)} collective-permute-done((bf16[64,1024]{1,0:T(8,128)(2,1)S(1)}, bf16[64,1024]{1,0:T(8,128)(2,1)S(1)}, u32[]{:S(2)}, u32[]{:S(2)}) %collective-permute-start.24) | collective-permute-done | bytes 131104 | tf_op jit(solution)/shard_map/ppermute | solution.py:20
  (126 shorter events, 32.3 us)
Async XLA Ops:
  6.1 13.8 %collective-permute-start = (bf16[1,128,1024]{2,1,0:T(8,128)(2,1)S(1)}, bf16[1,128,1024]{2,1,0:T(8,128)(2,1)S(1)}, u32[]{:S(2)}, u32[]{:S(2)}) collective-permute-start(bf16[1,128,1024]{2,1,0:T(8,128)(2,1)S(1)} %pad_maximum_fusion.3.refs_0_.refs_5_), channel_id=1, source_target_pairs={{0,2},{2,0},{4,6},{6,4},{8,10},{10,8},{12,14},{14,12},{16,18},{18,... | collective-permute-start | bytes 786440 | tf_op jit(solution)/shard_map/ppermute | solution.py:20
  6.7 13.3 %collective-permute-start.1 = (bf16[1,128,1024]{2,1,0:T(8,128)(2,1)S(1)}, bf16[1,128,1024]{2,1,0:T(8,128)(2,1)}, u32[]{:S(2)}, u32[]{:S(2)}) collective-permute-start(bf16[1,128,1024]{2,1,0:T(8,128)(2,1)S(1)} %pad_maximum_fusion.3.refs_0_.refs_5_), channel_id=1, source_target_pairs={{0,4},{2,6},{4,0},{6,2},{8,12},{10,14},{12,8},{14,10},{16,20},{18,... | collective-permute-start | bytes 786440 | tf_op jit(solution)/shard_map/ppermute | solution.py:20
  9.3 14.0 %collective-permute-start.2 = (bf16[1,128,1024]{2,1,0:T(8,128)(2,1)S(1)}, bf16[1,128,1024]{2,1,0:T(8,128)(2,1)}, u32[]{:S(2)}, u32[]{:S(2)}) collective-permute-start(bf16[1,128,1024]{2,1,0:T(8,128)(2,1)S(1)} %pad_maximum_fusion.3.refs_0_.refs_5_), channel_id=1, source_target_pairs={{0,8},{2,10},{4,12},{6,14},{8,0},{10,2},{12,4},{14,6},{16,24},{18,... | collective-permute-start | bytes 786440 | tf_op jit(solution)/shard_map/ppermute | solution.py:20
  10.8 14.8 %collective-permute-start.3 = (bf16[1,128,1024]{2,1,0:T(8,128)(2,1)S(1)}, bf16[1,128,1024]{2,1,0:T(8,128)(2,1)}, u32[]{:S(2)}, u32[]{:S(2)}) collective-permute-start(bf16[1,128,1024]{2,1,0:T(8,128)(2,1)S(1)} %pad_maximum_fusion.3.refs_0_.refs_5_), channel_id=1, source_target_pairs={{0,16},{2,18},{4,20},{6,22},{8,24},{10,26},{12,28},{14,30},{16,0},... | collective-permute-start | bytes 786440 | tf_op jit(solution)/shard_map/ppermute | solution.py:20
  36.6 12.0 %collective-permute-start.7 = (bf16[1,128,1024]{2,1,0:T(8,128)(2,1)}, bf16[1,128,1024]{2,1,0:T(8,128)(2,1)S(1)}, u32[]{:S(2)}, u32[]{:S(2)}) collective-permute-start(bf16[1,128,1024]{2,1,0:T(8,128)(2,1)} %get-tuple-element.28), channel_id=1, source_target_pairs={{0,16},{2,18},{4,20},{6,22},{8,24},{10,26},{12,28},{14,30},{16,0},... | collective-permute-start | bytes 786440 | tf_op jit(solution)/shard_map/ppermute | solution.py:20
  37.0 11.6 %collective-permute-start.6 = (bf16[1,128,1024]{2,1,0:T(8,128)(2,1)}, bf16[1,128,1024]{2,1,0:T(8,128)(2,1)S(1)}, u32[]{:S(2)}, u32[]{:S(2)}) collective-permute-start(bf16[1,128,1024]{2,1,0:T(8,128)(2,1)} %get-tuple-element.27), channel_id=1, source_target_pairs={{0,8},{2,10},{4,12},{6,14},{8,0},{10,2},{12,4},{14,6},{16,24},{18,... | collective-permute-start | bytes 786440 | tf_op jit(solution)/shard_map/ppermute | solution.py:20
  39.7 8.9 %collective-permute-start.5 = (bf16[1,128,1024]{2,1,0:T(8,128)(2,1)}, bf16[1,128,1024]{2,1,0:T(8,128)(2,1)S(1)}, u32[]{:S(2)}, u32[]{:S(2)}) collective-permute-start(bf16[1,128,1024]{2,1,0:T(8,128)(2,1)} %get-tuple-element.26), channel_id=1, source_target_pairs={{0,4},{2,6},{4,0},{6,2},{8,12},{10,14},{12,8},{14,10},{16,20},{18,... | collective-permute-start | bytes 786440 | tf_op jit(solution)/shard_map/ppermute | solution.py:20
  40.2 8.4 %collective-permute-start.4 = (bf16[1,128,1024]{2,1,0:T(8,128)(2,1)}, bf16[1,128,1024]{2,1,0:T(8,128)(2,1)S(1)}, u32[]{:S(2)}, u32[]{:S(2)}) collective-permute-start(bf16[1,128,1024]{2,1,0:T(8,128)(2,1)} %get-tuple-element.25), channel_id=1, source_target_pairs={{0,2},{2,0},{4,6},{6,4},{8,10},{10,8},{12,14},{14,12},{16,18},{18,... | collective-permute-start | bytes 786440 | tf_op jit(solution)/shard_map/ppermute | solution.py:20
  44.8 16.6 %collective-permute-start.18 = (bf16[512,1024]{1,0:T(8,128)(2,1)S(1)}, bf16[512,1024]{1,0:T(8,128)(2,1)S(1)}, u32[]{:S(2)}, u32[]{:S(2)}) collective-permute-start(bf16[512,1024]{1,0:T(8,128)(2,1)S(1)} %dynamic-slice_convert_fusion), channel_id=1, source_target_pairs={{0,2},{2,0},{4,6},{6,4},{8,10},{10,8},{12,14},{14,12},{16,18},{18,... | collective-permute-start | bytes 3145736 | tf_op jit(solution)/shard_map/ppermute | solution.py:20
  51.1 8.8 %collective-permute-start.8 = (bf16[128,1536]{1,0:T(8,128)(2,1)S(1)}, bf16[128,1536]{1,0:T(8,128)(2,1)S(1)}, u32[]{:S(2)}, u32[]{:S(2)}) collective-permute-start(bf16[128,1536]{1,0:T(8,128)(2,1)S(1)} %pad_maximum_fusion.2), channel_id=1, source_target_pairs={{0,1},{1,0},{2,3},{3,2},{4,5},{5,4},{6,7},{7,6},{8,9},{9,8},{10,11... | collective-permute-start | bytes 1179656 | tf_op jit(solution)/shard_map/ppermute | solution.py:109
  53.8 12.0 %collective-permute-start.9 = (bf16[512,1024]{1,0:T(8,128)(2,1)S(1)}, bf16[512,1024]{1,0:T(8,128)(2,1)S(1)}, u32[]{:S(2)}, u32[]{:S(2)}) collective-permute-start(bf16[512,1024]{1,0:T(8,128)(2,1)S(1)} %dynamic-slice_convert_fusion.1), channel_id=1, source_target_pairs={{0,2},{2,0},{4,6},{6,4},{8,10},{10,8},{12,14},{14,12},{16,18},{18,... | collective-permute-start | bytes 3145736 | tf_op jit(solution)/shard_map/ppermute | solution.py:20
  62.0 9.2 %collective-permute-start.19 = (bf16[256,512]{1,0:T(8,128)(2,1)S(1)}, bf16[256,512]{1,0:T(8,128)(2,1)S(1)}, u32[]{:S(2)}, u32[]{:S(2)}) collective-permute-start(bf16[256,512]{1,0:T(8,128)(2,1)S(1)} %dynamic-slice_convert_fusion.3), channel_id=1, source_target_pairs={{0,4},{2,6},{4,0},{6,2},{8,12},{10,14},{12,8},{14,10},{16,20},{18,... | collective-permute-start | bytes 786440 | tf_op jit(solution)/shard_map/ppermute | solution.py:20
  63.5 11.0 %collective-permute-start.21 = (bf16[256,512]{1,0:T(8,128)(2,1)S(1)}, bf16[256,512]{1,0:T(8,128)(2,1)S(1)}, u32[]{:S(2)}, u32[]{:S(2)}) collective-permute-start(bf16[256,512]{1,0:T(8,128)(2,1)S(1)} %dynamic-slice_convert_fusion.2), channel_id=1, source_target_pairs={{0,8},{2,10},{4,12},{6,14},{8,0},{10,2},{12,4},{14,6},{16,24},{18,... | collective-permute-start | bytes 786440 | tf_op jit(solution)/shard_map/ppermute | solution.py:20
  66.5 14.4 %collective-permute-start.11 = (bf16[256,512]{1,0:T(8,128)(2,1)S(1)}, bf16[256,512]{1,0:T(8,128)(2,1)S(1)}, u32[]{:S(2)}, u32[]{:S(2)}) collective-permute-start(bf16[256,512]{1,0:T(8,128)(2,1)S(1)} %dynamic-slice_convert_fusion.5), channel_id=1, source_target_pairs={{0,4},{2,6},{4,0},{6,2},{8,12},{10,14},{12,8},{14,10},{16,20},{18,... | collective-permute-start | bytes 786440 | tf_op jit(solution)/shard_map/ppermute | solution.py:20
  68.1 12.9 %collective-permute-start.12 = (bf16[256,512]{1,0:T(8,128)(2,1)S(1)}, bf16[256,512]{1,0:T(8,128)(2,1)S(1)}, u32[]{:S(2)}, u32[]{:S(2)}) collective-permute-start(bf16[256,512]{1,0:T(8,128)(2,1)S(1)} %dynamic-slice_convert_fusion.4), channel_id=1, source_target_pairs={{0,8},{2,10},{4,12},{6,14},{8,0},{10,2},{12,4},{14,6},{16,24},{18,... | collective-permute-start | bytes 786440 | tf_op jit(solution)/shard_map/ppermute | solution.py:20
  68.2 8.4 %collective-permute-start.13 = (f32[1024]{0:T(1024)S(1)}, f32[1024]{0:T(1024)S(1)}, u32[]{:S(2)}, u32[]{:S(2)}) collective-permute-start(f32[1024]{0:T(1024)S(1)} %add.168), channel_id=1, source_target_pairs={{0,4},{2,6},{4,0},{6,2},{8,12},{10,14},{12,8},{14,10},{16,20},{18,... | collective-permute-start | bytes 12296 | tf_op jit(solution)/shard_map/ppermute | solution.py:20
  71.3 9.6 %collective-permute-start.20 = (bf16[128,512]{1,0:T(8,128)(2,1)S(1)}, bf16[128,512]{1,0:T(8,128)(2,1)S(1)}, u32[]{:S(2)}, u32[]{:S(2)}) collective-permute-start(bf16[128,512]{1,0:T(8,128)(2,1)S(1)} %dynamic-slice_convert_fusion.8), channel_id=1, source_target_pairs={{0,8},{2,10},{4,12},{6,14},{8,0},{10,2},{12,4},{14,6},{16,24},{18,... | collective-permute-start | bytes 393224 | tf_op jit(solution)/shard_map/ppermute | solution.py:20
  74.6 6.3 %collective-permute-start.22 = (bf16[128,512]{1,0:T(8,128)(2,1)S(1)}, bf16[128,512]{1,0:T(8,128)(2,1)S(1)}, u32[]{:S(2)}, u32[]{:S(2)}) collective-permute-start(bf16[128,512]{1,0:T(8,128)(2,1)S(1)} %dynamic-slice_convert_fusion.7), channel_id=1, source_target_pairs={{0,4},{2,6},{4,0},{6,2},{8,12},{10,14},{12,8},{14,10},{16,20},{18,... | collective-permute-start | bytes 393224 | tf_op jit(solution)/shard_map/ppermute | solution.py:20
  81.2 8.8 %collective-permute-start.14 = (bf16[128,512]{1,0:T(8,128)(2,1)S(1)}, bf16[128,512]{1,0:T(8,128)(2,1)S(1)}, u32[]{:S(2)}, u32[]{:S(2)}) collective-permute-start(bf16[128,512]{1,0:T(8,128)(2,1)S(1)} %dynamic-slice_convert_fusion.10), channel_id=1, source_target_pairs={{0,8},{2,10},{4,12},{6,14},{8,0},{10,2},{12,4},{14,6},{16,24},{18,... | collective-permute-start | bytes 393224 | tf_op jit(solution)/shard_map/ppermute | solution.py:20
  83.0 14.0 %collective-permute-start.23 = (bf16[64,1024]{1,0:T(8,128)(2,1)S(1)}, bf16[64,1024]{1,0:T(8,128)(2,1)S(1)}, u32[]{:S(2)}, u32[]{:S(2)}) collective-permute-start(bf16[64,1024]{1,0:T(8,128)(2,1)S(1)} %fusion.19), channel_id=1, source_target_pairs={{0,16},{2,18},{4,20},{6,22},{8,24},{10,26},{12,28},{14,30},{16,0},... | collective-permute-start | bytes 393224 | tf_op jit(solution)/shard_map/ppermute | solution.py:20
  86.3 3.6 %collective-permute-start.16 = (f32[1024]{0:T(1024)S(1)}, f32[1024]{0:T(1024)S(1)}, u32[]{:S(2)}, u32[]{:S(2)}) collective-permute-start(f32[1024]{0:T(1024)S(1)} %add.175), channel_id=1, source_target_pairs={{0,8},{2,10},{4,12},{6,14},{8,0},{10,2},{12,4},{14,6},{16,24},{18,... | collective-permute-start | bytes 12296 | tf_op jit(solution)/shard_map/ppermute | solution.py:20
  86.6 5.0 %collective-permute-start.15 = (bf16[128,512]{1,0:T(8,128)(2,1)S(1)}, bf16[128,512]{1,0:T(8,128)(2,1)S(1)}, u32[]{:S(2)}, u32[]{:S(2)}) collective-permute-start(bf16[128,512]{1,0:T(8,128)(2,1)S(1)} %dynamic-slice_convert_fusion.9), channel_id=1, source_target_pairs={{0,4},{2,6},{4,0},{6,2},{8,12},{10,14},{12,8},{14,10},{16,20},{18,... | collective-permute-start | bytes 393224 | tf_op jit(solution)/shard_map/ppermute | solution.py:20
  91.7 4.7 %collective-permute-start.17 = (f32[1024]{0:T(1024)S(1)}, f32[1024]{0:T(1024)S(1)}, u32[]{:S(2)}, u32[]{:S(2)}) collective-permute-start(f32[1024]{0:T(1024)S(1)} %add.182), channel_id=1, source_target_pairs={{0,16},{2,18},{4,20},{6,22},{8,24},{10,26},{12,28},{14,30},{16,0},... | collective-permute-start | bytes 12296 | tf_op jit(solution)/shard_map/ppermute | solution.py:20
  92.7 7.4 %collective-permute-start.24 = (bf16[64,1024]{1,0:T(8,128)(2,1)S(1)}, bf16[64,1024]{1,0:T(8,128)(2,1)S(1)}, u32[]{:S(2)}, u32[]{:S(2)}) collective-permute-start(bf16[64,1024]{1,0:T(8,128)(2,1)S(1)} %dynamic-slice_convert_fusion.6), channel_id=1, source_target_pairs={{0,16},{2,18},{4,20},{6,22},{8,24},{10,26},{12,28},{14,30},{16,0},... | collective-permute-start | bytes 393224 | tf_op jit(solution)/shard_map/ppermute | solution.py:20
  (14 other events, 133.4 us)

commit v16 on v15

--- a/solution.py
+++ b/solution.py
@@ -278,7 +278,8 @@
     swapped = head_swap(jnp.concatenate([low_terms, other_mixed.astype(jnp.bfloat16)], axis=1))
     mixed = (own_mixed + swapped[:, width:].astype(jnp.float32)).astype(jnp.bfloat16)
     grad_normed = low_terms.astype(jnp.float32) + swapped[:, :width].astype(jnp.float32)
-    gain_terms = jnp.sum(grad_normed * wide_nodes * inverse, axis=0)
+    head_gain = jnp.sum(low_terms.astype(jnp.float32) * wide_nodes * inverse, axis=0)
+    gain_terms = head_gain + head_swap(head_gain)
     (w_key_grad, w_value_grad), gain_part = scatter_rows(
         [(normed, grad_key), (normed, grad_value)], "graph", graph_levels, gain_terms
     )

time: 103 us -> 107 us (1.039)
  waiting for transfers between devices: 30.1 us -> 32.3 us
  starting transfers between devices: 33 us -> 34.4 us
    ppermute x1 -> x2, waiting for transfers between devices: 6.05 us -> 8.2 us  [head_swap(): return lax.ppermute(value, 'head', [(0, 1), (1, 0)])]
    ppermute x1 -> x2, starting transfers between devices: 1.55 us -> 3.1 us  [head_swap(): return lax.ppermute(value, 'head', [(0, 1), (1, 0)])]
  transfers between devices with their start and end apart: 25 -> 26, of which waited for: 11 -> 13; matrix products, arithmetic and copies ran while one was open for 19% -> 18% of each run, Pallas kernels for 0% -> 0%
where the time goes in v16:
time: 107 us; the launch traced here: 106 us
  starting transfers between devices  34.4 us (32%)
  waiting for transfers between devices  32.3 us (30%)
  matrix products  12.8 us (12%)
  Pallas kernels  11 us (10%)
  other arithmetic  10.9 us (10%)
  local copies, waits for them, and re-layouts  3.94 us (4%)
  between operations  1.2 us (1%)
    ppermute x24, starting transfers between devices, from_partner(): return lax.ppermute(value, axis, pairs)  31.3 us
    ppermute x24, waiting for transfers between devices, from_partner(): return lax.ppermute(value, axis, pairs)  24.1 us
    pallas_call x1, Pallas kernels, block_attention(): pl.pallas_call(functools.partial(attention_kernel, slots, pairs), grid_sp...  11 us
    ppermute x2, waiting for transfers between devices, head_swap(): return lax.ppermute(value, 'head', [(0, 1), (1, 0)])  8.2 us
    dot_general x8, matrix products, scatter_rows(): lax.dot_general(bit_major_rows(left, order), piece, contract, preferred_e...  4.86 us
    ppermute x2, starting transfers between devices, head_swap(): return lax.ppermute(value, 'head', [(0, 1), (1, 0)])  3.1 us
  transfers between devices with their start and end apart: 26, of which 13 were waited for; matrix products, arithmetic and copies ran while one was open for 18% of the time, Pallas kernels for 0%

profile of v16, /device:TPU:0, one launch (start us, length us, event | category | flops | bytes accessed | tf_op | source)
XLA Modules:
  0.0 106.5 jit_solution(17468415882180321312)
XLA Ops:
  6.7 2.6 %collective-permute-start.1 = (bf16[1,128,1024]{2,1,0:T(8,128)(2,1)S(1)}, bf16[1,128,1024]{2,1,0:T(8,128)(2,1)}, u32[]{:S(2)}, u32[]{:S(2)}) collective-permute-start(bf16[1,128,1024]{2,1,0:T(8,128)(2,1)S(1)} %pad_maximum_fusion.3.refs_0_.refs_5_), channel_id=1, source_target_pairs={{0,4},{2,6},{4,0},{6,2},{8,12},{10,14},{12,8},{14,10},{16,20},{18,... | collective-permute-start | bytes 786440 | tf_op jit(solution)/shard_map/ppermute | solution.py:20
  9.3 1.6 %collective-permute-start.2 = (bf16[1,128,1024]{2,1,0:T(8,128)(2,1)S(1)}, bf16[1,128,1024]{2,1,0:T(8,128)(2,1)}, u32[]{:S(2)}, u32[]{:S(2)}) collective-permute-start(bf16[1,128,1024]{2,1,0:T(8,128)(2,1)S(1)} %pad_maximum_fusion.3.refs_0_.refs_5_), channel_id=1, source_target_pairs={{0,8},{2,10},{4,12},{6,14},{8,0},{10,2},{12,4},{14,6},{16,24},{18,... | collective-permute-start | bytes 786440 | tf_op jit(solution)/shard_map/ppermute | solution.py:20
  10.8 2.6 %collective-permute-start.3 = (bf16[1,128,1024]{2,1,0:T(8,128)(2,1)S(1)}, bf16[1,128,1024]{2,1,0:T(8,128)(2,1)}, u32[]{:S(2)}, u32[]{:S(2)}) collective-permute-start(bf16[1,128,1024]{2,1,0:T(8,128)(2,1)S(1)} %pad_maximum_fusion.3.refs_0_.refs_5_), channel_id=1, source_target_pairs={{0,16},{2,18},{4,20},{6,22},{8,24},{10,26},{12,28},{14,30},{16,0},... | collective-permute-start | bytes 786440 | tf_op jit(solution)/shard_map/ppermute | solution.py:20
  17.8 2.1 %fusion.3.g_ref = bf16[1,128,512]{2,1,0:T(8,128)(2,1)} fusion(bf16[128,1024]{1,0:T(8,128)(2,1)} %param.15, bf16[512,1024]{1,0:T(8,128)(2,1)S(1)} %copy-done), kind=kOutput, calls=%fused_computation.16 | convolution fusion | flops 134283264 | bytes 1441792 | tf_op jit(solution)/shard_map/dot_general | solution.py:241
  20.0 3.3 %collective-permute-done.2.refs_3_.refs_8_ = bf16[1,128,1024]{2,1,0:T(8,128)(2,1)} collective-permute-done((bf16[1,128,1024]{2,1,0:T(8,128)(2,1)S(1)}, bf16[1,128,1024]{2,1,0:T(8,128)(2,1)}, u32[]{:S(2)}, u32[]{:S(2)}) %collective-permute-start.2) | collective-permute-done | bytes 262176 | tf_op jit(solution)/shard_map/ppermute | solution.py:20
  23.2 2.4 %collective-permute-done.3.refs_4_.refs_9_ = bf16[1,128,1024]{2,1,0:T(8,128)(2,1)} collective-permute-done((bf16[1,128,1024]{2,1,0:T(8,128)(2,1)S(1)}, bf16[1,128,1024]{2,1,0:T(8,128)(2,1)}, u32[]{:S(2)}, u32[]{:S(2)}) %collective-permute-start.3) | collective-permute-done | bytes 262176 | tf_op jit(solution)/shard_map/ppermute | solution.py:20
  25.6 11.0 %shard_map.135 = (bf16[1,128,512]{2,1,0:T(8,128)(2,1)}, bf16[1,128,512]{2,1,0:T(8,128)(2,1)}, bf16[1,128,1024]{2,1,0:T(8,128)(2,1)}, bf16[1,128,1024]{2,1,0:T(8,...) custom-call(s32[5]{0:T(128)} %add_bitcast_fusion.active_ref, ...), custom_call_target="tpu_custom_call" | custom-call | tf_op jit(solution)/shard_map/pallas_call | solution.py:199
  37.0 2.7 %collective-permute-start.6 = (bf16[1,128,1024]{2,1,0:T(8,128)(2,1)}, bf16[1,128,1024]{2,1,0:T(8,128)(2,1)S(1)}, u32[]{:S(2)}, u32[]{:S(2)}) collective-permute-start(bf16[1,128,1024]{2,1,0:T(8,128)(2,1)} %get-tuple-element.27), channel_id=1, source_target_pairs={{0,8},{2,10},{4,12},{6,14},{8,0},{10,2},{12,4},{14,6},{16,24},{18,... | collective-permute-start | bytes 786440 | tf_op jit(solution)/shard_map/ppermute | solution.py:20
  45.7 2.9 %collective-permute-done.7 = bf16[1,128,1024]{2,1,0:T(8,128)(2,1)S(1)} collective-permute-done((bf16[1,128,1024]{2,1,0:T(8,128)(2,1)}, bf16[1,128,1024]{2,1,0:T(8,128)(2,1)S(1)}, u32[]{:S(2)}, u32[]{:S(2)}) %collective-permute-start.7) | collective-permute-done | bytes 262176 | tf_op jit(solution)/shard_map/ppermute | solution.py:20
  51.2 1.6 %collective-permute-start.8 = (bf16[128,1536]{1,0:T(8,128)(2,1)S(1)}, bf16[128,1536]{1,0:T(8,128)(2,1)S(1)}, u32[]{:S(2)}, u32[]{:S(2)}) collective-permute-start(bf16[128,1536]{1,0:T(8,128)(2,1)S(1)} %pad_maximum_fusion.2), channel_id=1, source_target_pairs={{0,1},{1,0},{2,3},{3,2},{4,5},{5,4},{6,7},{7,6},{8,9},{9,8},{10,11... | collective-permute-start | bytes 1179656 | tf_op jit(solution)/shard_map/ppermute | solution.py:109
  53.9 6.1 %collective-permute-done.8 = bf16[128,1536]{1,0:T(8,128)(2,1)S(1)} collective-permute-done((bf16[128,1536]{1,0:T(8,128)(2,1)S(1)}, bf16[128,1536]{1,0:T(8,128)(2,1)S(1)}, u32[]{:S(2)}, u32[]{:S(2)}) %collective-permute-start.8) | collective-permute-done | bytes 393248 | tf_op jit(solution)/shard_map/ppermute | solution.py:109
  61.8 2.1 %collective-permute-done.10 = f32[1024]{0:T(1024)S(1)} collective-permute-done((f32[1024]{0:T(1024)S(1)}, f32[1024]{0:T(1024)S(1)}, u32[]{:S(2)}, u32[]{:S(2)}) %collective-permute-start.10) | collective-permute-done | bytes 4128 | tf_op jit(solution)/shard_map/ppermute | solution.py:109
  67.1 2.4 %collective-permute-start.22 = (bf16[256,512]{1,0:T(8,128)(2,1)S(1)}, bf16[256,512]{1,0:T(8,128)(2,1)S(1)}, u32[]{:S(2)}, u32[]{:S(2)}) collective-permute-start(bf16[256,512]{1,0:T(8,128)(2,1)S(1)} %dynamic-slice_convert_fusion.2), channel_id=1, source_target_pairs={{0,8},{2,10},{4,12},{6,14},{8,0},{10,2},{12,4},{14,6},{16,24},{18,... | collective-permute-start | bytes 786440 | tf_op jit(solution)/shard_map/ppermute | solution.py:20
  70.1 1.6 %collective-permute-start.12 = (bf16[256,512]{1,0:T(8,128)(2,1)S(1)}, bf16[256,512]{1,0:T(8,128)(2,1)S(1)}, u32[]{:S(2)}, u32[]{:S(2)}) collective-permute-start(bf16[256,512]{1,0:T(8,128)(2,1)S(1)} %dynamic-slice_convert_fusion.5), channel_id=1, source_target_pairs={{0,4},{2,6},{4,0},{6,2},{8,12},{10,14},{12,8},{14,10},{16,20},{18,... | collective-permute-start | bytes 786440 | tf_op jit(solution)/shard_map/ppermute | solution.py:20
  72.4 2.4 %collective-permute-done.20 = bf16[256,512]{1,0:T(8,128)(2,1)S(1)} collective-permute-done((bf16[256,512]{1,0:T(8,128)(2,1)S(1)}, bf16[256,512]{1,0:T(8,128)(2,1)S(1)}, u32[]{:S(2)}, u32[]{:S(2)}) %collective-permute-start.20) | collective-permute-done | bytes 262176 | tf_op jit(solution)/shard_map/ppermute | solution.py:20
  74.9 3.2 %collective-permute-start.21 = (bf16[128,512]{1,0:T(8,128)(2,1)S(1)}, bf16[128,512]{1,0:T(8,128)(2,1)S(1)}, u32[]{:S(2)}, u32[]{:S(2)}) collective-permute-start(bf16[128,512]{1,0:T(8,128)(2,1)S(1)} %dynamic-slice_convert_fusion.8), channel_id=1, source_target_pairs={{0,8},{2,10},{4,12},{6,14},{8,0},{10,2},{12,4},{14,6},{16,24},{18,... | collective-permute-start | bytes 393224 | tf_op jit(solution)/shard_map/ppermute | solution.py:20
  80.3 4.2 %collective-permute-done.21 = bf16[128,512]{1,0:T(8,128)(2,1)S(1)} collective-permute-done((bf16[128,512]{1,0:T(8,128)(2,1)S(1)}, bf16[128,512]{1,0:T(8,128)(2,1)S(1)}, u32[]{:S(2)}, u32[]{:S(2)}) %collective-permute-start.21) | collective-permute-done | bytes 131104 | tf_op jit(solution)/shard_map/ppermute | solution.py:20
  84.8 1.8 %collective-permute-start.15 = (bf16[128,512]{1,0:T(8,128)(2,1)S(1)}, bf16[128,512]{1,0:T(8,128)(2,1)S(1)}, u32[]{:S(2)}, u32[]{:S(2)}) collective-permute-start(bf16[128,512]{1,0:T(8,128)(2,1)S(1)} %dynamic-slice_convert_fusion.10), channel_id=1, source_target_pairs={{0,8},{2,10},{4,12},{6,14},{8,0},{10,2},{12,4},{14,6},{16,24},{18,... | collective-permute-start | bytes 393224 | tf_op jit(solution)/shard_map/ppermute | solution.py:20
  86.6 3.3 %collective-permute-start.24 = (bf16[64,1024]{1,0:T(8,128)(2,1)S(1)}, bf16[64,1024]{1,0:T(8,128)(2,1)S(1)}, u32[]{:S(2)}, u32[]{:S(2)}) collective-permute-start(bf16[64,1024]{1,0:T(8,128)(2,1)S(1)} %fusion.19), channel_id=1, source_target_pairs={{0,16},{2,18},{4,20},{6,22},{8,24},{10,26},{12,28},{14,30},{16,0},... | collective-permute-start | bytes 393224 | tf_op jit(solution)/shard_map/ppermute | solution.py:20
  90.3 1.6 %collective-permute-start.16 = (bf16[128,512]{1,0:T(8,128)(2,1)S(1)}, bf16[128,512]{1,0:T(8,128)(2,1)S(1)}, u32[]{:S(2)}, u32[]{:S(2)}) collective-permute-start(bf16[128,512]{1,0:T(8,128)(2,1)S(1)} %dynamic-slice_convert_fusion.9), channel_id=1, source_target_pairs={{0,4},{2,6},{4,0},{6,2},{8,12},{10,14},{12,8},{14,10},{16,20},{18,... | collective-permute-start | bytes 393224 | tf_op jit(solution)/shard_map/ppermute | solution.py:20
  91.8 1.8 %collective-permute-done.17 = f32[1024]{0:T(1024)S(1)} collective-permute-done((f32[1024]{0:T(1024)S(1)}, f32[1024]{0:T(1024)S(1)}, u32[]{:S(2)}, u32[]{:S(2)}) %collective-permute-start.17) | collective-permute-done | bytes 4128 | tf_op jit(solution)/shard_map/ppermute | solution.py:20
  93.6 1.6 %collective-permute-done.16 = bf16[128,512]{1,0:T(8,128)(2,1)S(1)} collective-permute-done((bf16[128,512]{1,0:T(8,128)(2,1)S(1)}, bf16[128,512]{1,0:T(8,128)(2,1)S(1)}, u32[]{:S(2)}, u32[]{:S(2)}) %collective-permute-start.16) | collective-permute-done | bytes 131104 | tf_op jit(solution)/shard_map/ppermute | solution.py:20
  96.3 2.1 %collective-permute-start.25 = (bf16[64,1024]{1,0:T(8,128)(2,1)S(1)}, bf16[64,1024]{1,0:T(8,128)(2,1)S(1)}, u32[]{:S(2)}, u32[]{:S(2)}) collective-permute-start(bf16[64,1024]{1,0:T(8,128)(2,1)S(1)} %dynamic-slice_convert_fusion.6), channel_id=1, source_target_pairs={{0,16},{2,18},{4,20},{6,22},{8,24},{10,26},{12,28},{14,30},{16,0},... | collective-permute-start | bytes 393224 | tf_op jit(solution)/shard_map/ppermute | solution.py:20
  100.6 3.1 %collective-permute-done.25 = bf16[64,1024]{1,0:T(8,128)(2,1)S(1)} collective-permute-done((bf16[64,1024]{1,0:T(8,128)(2,1)S(1)}, bf16[64,1024]{1,0:T(8,128)(2,1)S(1)}, u32[]{:S(2)}, u32[]{:S(2)}) %collective-permute-start.25) | collective-permute-done | bytes 131104 | tf_op jit(solution)/shard_map/ppermute | solution.py:20
  (129 shorter events, 35.3 us)
Async XLA Ops:
  6.1 13.8 %collective-permute-start = (bf16[1,128,1024]{2,1,0:T(8,128)(2,1)S(1)}, bf16[1,128,1024]{2,1,0:T(8,128)(2,1)S(1)}, u32[]{:S(2)}, u32[]{:S(2)}) collective-permute-start(bf16[1,128,1024]{2,1,0:T(8,128)(2,1)S(1)} %pad_maximum_fusion.3.refs_0_.refs_5_), channel_id=1, source_target_pairs={{0,2},{2,0},{4,6},{6,4},{8,10},{10,8},{12,14},{14,12},{16,18},{18,... | collective-permute-start | bytes 786440 | tf_op jit(solution)/shard_map/ppermute | solution.py:20
  6.7 13.3 %collective-permute-start.1 = (bf16[1,128,1024]{2,1,0:T(8,128)(2,1)S(1)}, bf16[1,128,1024]{2,1,0:T(8,128)(2,1)}, u32[]{:S(2)}, u32[]{:S(2)}) collective-permute-start(bf16[1,128,1024]{2,1,0:T(8,128)(2,1)S(1)} %pad_maximum_fusion.3.refs_0_.refs_5_), channel_id=1, source_target_pairs={{0,4},{2,6},{4,0},{6,2},{8,12},{10,14},{12,8},{14,10},{16,20},{18,... | collective-permute-start | bytes 786440 | tf_op jit(solution)/shard_map/ppermute | solution.py:20
  9.3 14.0 %collective-permute-start.2 = (bf16[1,128,1024]{2,1,0:T(8,128)(2,1)S(1)}, bf16[1,128,1024]{2,1,0:T(8,128)(2,1)}, u32[]{:S(2)}, u32[]{:S(2)}) collective-permute-start(bf16[1,128,1024]{2,1,0:T(8,128)(2,1)S(1)} %pad_maximum_fusion.3.refs_0_.refs_5_), channel_id=1, source_target_pairs={{0,8},{2,10},{4,12},{6,14},{8,0},{10,2},{12,4},{14,6},{16,24},{18,... | collective-permute-start | bytes 786440 | tf_op jit(solution)/shard_map/ppermute | solution.py:20
  10.8 14.8 %collective-permute-start.3 = (bf16[1,128,1024]{2,1,0:T(8,128)(2,1)S(1)}, bf16[1,128,1024]{2,1,0:T(8,128)(2,1)}, u32[]{:S(2)}, u32[]{:S(2)}) collective-permute-start(bf16[1,128,1024]{2,1,0:T(8,128)(2,1)S(1)} %pad_maximum_fusion.3.refs_0_.refs_5_), channel_id=1, source_target_pairs={{0,16},{2,18},{4,20},{6,22},{8,24},{10,26},{12,28},{14,30},{16,0},... | collective-permute-start | bytes 786440 | tf_op jit(solution)/shard_map/ppermute | solution.py:20
  36.6 12.0 %collective-permute-start.7 = (bf16[1,128,1024]{2,1,0:T(8,128)(2,1)}, bf16[1,128,1024]{2,1,0:T(8,128)(2,1)S(1)}, u32[]{:S(2)}, u32[]{:S(2)}) collective-permute-start(bf16[1,128,1024]{2,1,0:T(8,128)(2,1)} %get-tuple-element.28), channel_id=1, source_target_pairs={{0,16},{2,18},{4,20},{6,22},{8,24},{10,26},{12,28},{14,30},{16,0},... | collective-permute-start | bytes 786440 | tf_op jit(solution)/shard_map/ppermute | solution.py:20
  37.0 11.6 %collective-permute-start.6 = (bf16[1,128,1024]{2,1,0:T(8,128)(2,1)}, bf16[1,128,1024]{2,1,0:T(8,128)(2,1)S(1)}, u32[]{:S(2)}, u32[]{:S(2)}) collective-permute-start(bf16[1,128,1024]{2,1,0:T(8,128)(2,1)} %get-tuple-element.27), channel_id=1, source_target_pairs={{0,8},{2,10},{4,12},{6,14},{8,0},{10,2},{12,4},{14,6},{16,24},{18,... | collective-permute-start | bytes 786440 | tf_op jit(solution)/shard_map/ppermute | solution.py:20
  39.7 8.9 %collective-permute-start.5 = (bf16[1,128,1024]{2,1,0:T(8,128)(2,1)}, bf16[1,128,1024]{2,1,0:T(8,128)(2,1)S(1)}, u32[]{:S(2)}, u32[]{:S(2)}) collective-permute-start(bf16[1,128,1024]{2,1,0:T(8,128)(2,1)} %get-tuple-element.26), channel_id=1, source_target_pairs={{0,4},{2,6},{4,0},{6,2},{8,12},{10,14},{12,8},{14,10},{16,20},{18,... | collective-permute-start | bytes 786440 | tf_op jit(solution)/shard_map/ppermute | solution.py:20
  40.2 8.4 %collective-permute-start.4 = (bf16[1,128,1024]{2,1,0:T(8,128)(2,1)}, bf16[1,128,1024]{2,1,0:T(8,128)(2,1)S(1)}, u32[]{:S(2)}, u32[]{:S(2)}) collective-permute-start(bf16[1,128,1024]{2,1,0:T(8,128)(2,1)} %get-tuple-element.25), channel_id=1, source_target_pairs={{0,2},{2,0},{4,6},{6,4},{8,10},{10,8},{12,14},{14,12},{16,18},{18,... | collective-permute-start | bytes 786440 | tf_op jit(solution)/shard_map/ppermute | solution.py:20
  44.8 20.3 %collective-permute-start.19 = (bf16[512,1024]{1,0:T(8,128)(2,1)S(1)}, bf16[512,1024]{1,0:T(8,128)(2,1)S(1)}, u32[]{:S(2)}, u32[]{:S(2)}) collective-permute-start(bf16[512,1024]{1,0:T(8,128)(2,1)S(1)} %dynamic-slice_convert_fusion), channel_id=1, source_target_pairs={{0,2},{2,0},{4,6},{6,4},{8,10},{10,8},{12,14},{14,12},{16,18},{18,... | collective-permute-start | bytes 3145736 | tf_op jit(solution)/shard_map/ppermute | solution.py:20
  51.2 8.8 %collective-permute-start.8 = (bf16[128,1536]{1,0:T(8,128)(2,1)S(1)}, bf16[128,1536]{1,0:T(8,128)(2,1)S(1)}, u32[]{:S(2)}, u32[]{:S(2)}) collective-permute-start(bf16[128,1536]{1,0:T(8,128)(2,1)S(1)} %pad_maximum_fusion.2), channel_id=1, source_target_pairs={{0,1},{1,0},{2,3},{3,2},{4,5},{5,4},{6,7},{7,6},{8,9},{9,8},{10,11... | collective-permute-start | bytes 1179656 | tf_op jit(solution)/shard_map/ppermute | solution.py:109
  53.8 15.6 %collective-permute-start.9 = (bf16[512,1024]{1,0:T(8,128)(2,1)S(1)}, bf16[512,1024]{1,0:T(8,128)(2,1)S(1)}, u32[]{:S(2)}, u32[]{:S(2)}) collective-permute-start(bf16[512,1024]{1,0:T(8,128)(2,1)S(1)} %dynamic-slice_convert_fusion.1), channel_id=1, source_target_pairs={{0,2},{2,0},{4,6},{6,4},{8,10},{10,8},{12,14},{14,12},{16,18},{18,... | collective-permute-start | bytes 3145736 | tf_op jit(solution)/shard_map/ppermute | solution.py:20
  60.3 3.7 %collective-permute-start.10 = (f32[1024]{0:T(1024)S(1)}, f32[1024]{0:T(1024)S(1)}, u32[]{:S(2)}, u32[]{:S(2)}) collective-permute-start(f32[1024]{0:T(1024)S(1)} %get-tuple-element.37), channel_id=1, source_target_pairs={{0,1},{1,0},{2,3},{3,2},{4,5},{5,4},{6,7},{7,6},{8,9},{9,8},{10,11... | collective-permute-start | bytes 12296 | tf_op jit(solution)/shard_map/ppermute | solution.py:109
  65.7 9.2 %collective-permute-start.20 = (bf16[256,512]{1,0:T(8,128)(2,1)S(1)}, bf16[256,512]{1,0:T(8,128)(2,1)S(1)}, u32[]{:S(2)}, u32[]{:S(2)}) collective-permute-start(bf16[256,512]{1,0:T(8,128)(2,1)S(1)} %dynamic-slice_convert_fusion.3), channel_id=1, source_target_pairs={{0,4},{2,6},{4,0},{6,2},{8,12},{10,14},{12,8},{14,10},{16,20},{18,... | collective-permute-start | bytes 786440 | tf_op jit(solution)/shard_map/ppermute | solution.py:20
  67.1 11.0 %collective-permute-start.22 = (bf16[256,512]{1,0:T(8,128)(2,1)S(1)}, bf16[256,512]{1,0:T(8,128)(2,1)S(1)}, u32[]{:S(2)}, u32[]{:S(2)}) collective-permute-start(bf16[256,512]{1,0:T(8,128)(2,1)S(1)} %dynamic-slice_convert_fusion.2), channel_id=1, source_target_pairs={{0,8},{2,10},{4,12},{6,14},{8,0},{10,2},{12,4},{14,6},{16,24},{18,... | collective-permute-start | bytes 786440 | tf_op jit(solution)/shard_map/ppermute | solution.py:20
  70.1 14.4 %collective-permute-start.12 = (bf16[256,512]{1,0:T(8,128)(2,1)S(1)}, bf16[256,512]{1,0:T(8,128)(2,1)S(1)}, u32[]{:S(2)}, u32[]{:S(2)}) collective-permute-start(bf16[256,512]{1,0:T(8,128)(2,1)S(1)} %dynamic-slice_convert_fusion.5), channel_id=1, source_target_pairs={{0,4},{2,6},{4,0},{6,2},{8,12},{10,14},{12,8},{14,10},{16,20},{18,... | collective-permute-start | bytes 786440 | tf_op jit(solution)/shard_map/ppermute | solution.py:20
  71.8 12.9 %collective-permute-start.13 = (bf16[256,512]{1,0:T(8,128)(2,1)S(1)}, bf16[256,512]{1,0:T(8,128)(2,1)S(1)}, u32[]{:S(2)}, u32[]{:S(2)}) collective-permute-start(bf16[256,512]{1,0:T(8,128)(2,1)S(1)} %dynamic-slice_convert_fusion.4), channel_id=1, source_target_pairs={{0,8},{2,10},{4,12},{6,14},{8,0},{10,2},{12,4},{14,6},{16,24},{18,... | collective-permute-start | bytes 786440 | tf_op jit(solution)/shard_map/ppermute | solution.py:20
  71.9 8.4 %collective-permute-start.14 = (f32[1024]{0:T(1024)S(1)}, f32[1024]{0:T(1024)S(1)}, u32[]{:S(2)}, u32[]{:S(2)}) collective-permute-start(f32[1024]{0:T(1024)S(1)} %add.172), channel_id=1, source_target_pairs={{0,4},{2,6},{4,0},{6,2},{8,12},{10,14},{12,8},{14,10},{16,20},{18,... | collective-permute-start | bytes 12296 | tf_op jit(solution)/shard_map/ppermute | solution.py:20
  74.9 9.5 %collective-permute-start.21 = (bf16[128,512]{1,0:T(8,128)(2,1)S(1)}, bf16[128,512]{1,0:T(8,128)(2,1)S(1)}, u32[]{:S(2)}, u32[]{:S(2)}) collective-permute-start(bf16[128,512]{1,0:T(8,128)(2,1)S(1)} %dynamic-slice_convert_fusion.8), channel_id=1, source_target_pairs={{0,8},{2,10},{4,12},{6,14},{8,0},{10,2},{12,4},{14,6},{16,24},{18,... | collective-permute-start | bytes 393224 | tf_op jit(solution)/shard_map/ppermute | solution.py:20
  78.2 6.3 %collective-permute-start.23 = (bf16[128,512]{1,0:T(8,128)(2,1)S(1)}, bf16[128,512]{1,0:T(8,128)(2,1)S(1)}, u32[]{:S(2)}, u32[]{:S(2)}) collective-permute-start(bf16[128,512]{1,0:T(8,128)(2,1)S(1)} %dynamic-slice_convert_fusion.7), channel_id=1, source_target_pairs={{0,4},{2,6},{4,0},{6,2},{8,12},{10,14},{12,8},{14,10},{16,20},{18,... | collective-permute-start | bytes 393224 | tf_op jit(solution)/shard_map/ppermute | solution.py:20
  84.8 8.8 %collective-permute-start.15 = (bf16[128,512]{1,0:T(8,128)(2,1)S(1)}, bf16[128,512]{1,0:T(8,128)(2,1)S(1)}, u32[]{:S(2)}, u32[]{:S(2)}) collective-permute-start(bf16[128,512]{1,0:T(8,128)(2,1)S(1)} %dynamic-slice_convert_fusion.10), channel_id=1, source_target_pairs={{0,8},{2,10},{4,12},{6,14},{8,0},{10,2},{12,4},{14,6},{16,24},{18,... | collective-permute-start | bytes 393224 | tf_op jit(solution)/shard_map/ppermute | solution.py:20
  86.6 14.0 %collective-permute-start.24 = (bf16[64,1024]{1,0:T(8,128)(2,1)S(1)}, bf16[64,1024]{1,0:T(8,128)(2,1)S(1)}, u32[]{:S(2)}, u32[]{:S(2)}) collective-permute-start(bf16[64,1024]{1,0:T(8,128)(2,1)S(1)} %fusion.19), channel_id=1, source_target_pairs={{0,16},{2,18},{4,20},{6,22},{8,24},{10,26},{12,28},{14,30},{16,0},... | collective-permute-start | bytes 393224 | tf_op jit(solution)/shard_map/ppermute | solution.py:20
  90.3 5.0 %collective-permute-start.16 = (bf16[128,512]{1,0:T(8,128)(2,1)S(1)}, bf16[128,512]{1,0:T(8,128)(2,1)S(1)}, u32[]{:S(2)}, u32[]{:S(2)}) collective-permute-start(bf16[128,512]{1,0:T(8,128)(2,1)S(1)} %dynamic-slice_convert_fusion.9), channel_id=1, source_target_pairs={{0,4},{2,6},{4,0},{6,2},{8,12},{10,14},{12,8},{14,10},{16,20},{18,... | collective-permute-start | bytes 393224 | tf_op jit(solution)/shard_map/ppermute | solution.py:20
  95.3 4.7 %collective-permute-start.18 = (f32[1024]{0:T(1024)S(1)}, f32[1024]{0:T(1024)S(1)}, u32[]{:S(2)}, u32[]{:S(2)}) collective-permute-start(f32[1024]{0:T(1024)S(1)} %add.186), channel_id=1, source_target_pairs={{0,16},{2,18},{4,20},{6,22},{8,24},{10,26},{12,28},{14,30},{16,0},... | collective-permute-start | bytes 12296 | tf_op jit(solution)/shard_map/ppermute | solution.py:20
  96.3 7.4 %collective-permute-start.25 = (bf16[64,1024]{1,0:T(8,128)(2,1)S(1)}, bf16[64,1024]{1,0:T(8,128)(2,1)S(1)}, u32[]{:S(2)}, u32[]{:S(2)}) collective-permute-start(bf16[64,1024]{1,0:T(8,128)(2,1)S(1)} %dynamic-slice_convert_fusion.6), channel_id=1, source_target_pairs={{0,16},{2,18},{4,20},{6,22},{8,24},{10,26},{12,28},{14,30},{16,0},... | collective-permute-start | bytes 393224 | tf_op jit(solution)/shard_map/ppermute | solution.py:20
  (15 other events, 137.1 us)

commit v17 on v12

--- a/solution.py
+++ b/solution.py
@@ -2,6 +2,7 @@
 import jax.numpy as jnp
 from jax import lax
 from jax.sharding import PartitionSpec as P
+from jax.experimental.layout import Layout, with_layout_constraint
 import functools
 from jax.experimental import pallas as pl
 from jax.experimental.pallas import tpu as pltpu
@@ -60,7 +61,7 @@
                 )
             )
     first = sum(right.shape[1] // 2 for left, right in pairs)
-    joined = jnp.concatenate(chunks, axis=1)
+    joined = with_layout_constraint(jnp.concatenate(chunks, axis=1), Layout((0, 1)))
     parts = None
     for step in range(levels):
         bit_a, bit_b = orders[0][step], orders[1][step]

time: 113 us -> 103 us (0.912)
  waiting for transfers between devices: 42 us -> 33.6 us
  local copies, waits for them, and re-layouts: 7.14 us -> 3.9 us
  other arithmetic: 8.59 us -> 10.7 us
    ppermute x24, waiting for transfers between devices: 35.7 us -> 27.2 us  [from_partner(): return lax.ppermute(value, axis, pairs)]
    unnamed x34 -> x30, local copies, waits for them, and re-layouts: 4.31 us -> 1.21 us
    concatenate x3, other arithmetic: 0.06 us -> 1.99 us  [scatter_rows(): jnp.concatenate([joined[:, offset:offset + cut], joined[:, first + offset...]
  transfers between devices with their start and end apart: 26 -> 26, of which waited for: 12 -> 12; matrix products, arithmetic and copies ran while one was open for 16% -> 17% of each run, Pallas kernels for 0% -> 0%
where the time goes in v17:
time: 103 us
  waiting for transfers between devices  33.6 us (33%)
  starting transfers between devices  29.5 us (29%)
  matrix products  12.7 us (12%)
  Pallas kernels  11 us (11%)
  other arithmetic  10.7 us (10%)
  local copies, waits for them, and re-layouts  3.9 us (4%)
  between operations  1.39 us (1%)
    ppermute x24, starting transfers between devices, from_partner(): return lax.ppermute(value, axis, pairs)  27.3 us
    ppermute x24, waiting for transfers between devices, from_partner(): return lax.ppermute(value, axis, pairs)  27.2 us
    pallas_call x1, Pallas kernels, block_attention(): pl.pallas_call(functools.partial(attention_kernel, slots, pairs), grid_sp...  11 us
    ppermute x2, waiting for transfers between devices, head_swap(): return lax.ppermute(value, 'head', [(0, 1), (1, 0)])  6.4 us
    dot_general x8, matrix products, scatter_rows(): lax.dot_general(bit_major_rows(left, order), piece, contract, preferred_e...  3.88 us
    ppermute x2, starting transfers between devices, head_swap(): return lax.ppermute(value, 'head', [(0, 1), (1, 0)])  2.15 us
    dot_general x1, matrix products, shards(): jnp.dot(cotangent, w_out.T, preferred_element_type=jnp.float32)  2.09 us
  transfers between devices with their start and end apart: 26, of which 12 were waited for; matrix products, arithmetic and copies ran while one was open for 17% of the time, Pallas kernels for 0%

profile of v17, /device:TPU:0, one launch (start us, length us, event | category | flops | bytes accessed | tf_op | source)
XLA Modules:
  0.0 102.8 jit_solution(16767754679761685262)
XLA Ops:
  3.0 1.5 %fusion.5 = bf16[1,128,512]{2,1,0:T(8,128)(2,1)S(1)} fusion(bf16[128,1024]{1,0:T(8,128)(2,1)S(1)} %fusion.8, bf16[1024,512]{1,0:T(8,128)(2,1)} %param.12), kind=kOutput, calls=%fused_computation.18 | convolution fusion | flops 134283264 | bytes 1441792 | tf_op jit(solution)/shard_map/dot_general | solution.py:227
  4.6 1.5 %fusion.4 = bf16[1,128,512]{2,1,0:T(8,128)(2,1)S(1)} fusion(bf16[128,1024]{1,0:T(8,128)(2,1)S(1)} %fusion.8, bf16[1024,512]{1,0:T(8,128)(2,1)} %param.11), kind=kOutput, calls=%fused_computation.17 | convolution fusion | flops 134283264 | bytes 1441792 | tf_op jit(solution)/shard_map/dot_general | solution.py:226
  6.7 2.6 %collective-permute-start.1 = (bf16[1,128,1024]{2,1,0:T(8,128)(2,1)S(1)}, bf16[1,128,1024]{2,1,0:T(8,128)(2,1)}, u32[]{:S(2)}, u32[]{:S(2)}) collective-permute-start(bf16[1,128,1024]{2,1,0:T(8,128)(2,1)S(1)} %pad_maximum_fusion.2.refs_0_.refs_5_), channel_id=1, source_target_pairs={{0,4},{2,6},{4,0},{6,2},{8,12},{10,14},{12,8},{14,10},{16,20},{18,... | collective-permute-start | bytes 786440 | tf_op jit(solution)/shard_map/ppermute | solution.py:20
  9.3 1.6 %collective-permute-start.2 = (bf16[1,128,1024]{2,1,0:T(8,128)(2,1)S(1)}, bf16[1,128,1024]{2,1,0:T(8,128)(2,1)}, u32[]{:S(2)}, u32[]{:S(2)}) collective-permute-start(bf16[1,128,1024]{2,1,0:T(8,128)(2,1)S(1)} %pad_maximum_fusion.2.refs_0_.refs_5_), channel_id=1, source_target_pairs={{0,8},{2,10},{4,12},{6,14},{8,0},{10,2},{12,4},{14,6},{16,24},{18,... | collective-permute-start | bytes 786440 | tf_op jit(solution)/shard_map/ppermute | solution.py:20
  10.8 2.6 %collective-permute-start.3 = (bf16[1,128,1024]{2,1,0:T(8,128)(2,1)S(1)}, bf16[1,128,1024]{2,1,0:T(8,128)(2,1)}, u32[]{:S(2)}, u32[]{:S(2)}) collective-permute-start(bf16[1,128,1024]{2,1,0:T(8,128)(2,1)S(1)} %pad_maximum_fusion.2.refs_0_.refs_5_), channel_id=1, source_target_pairs={{0,16},{2,18},{4,20},{6,22},{8,24},{10,26},{12,28},{14,30},{16,0},... | collective-permute-start | bytes 786440 | tf_op jit(solution)/shard_map/ppermute | solution.py:20
  17.8 2.1 %fusion.3.g_ref = bf16[1,128,512]{2,1,0:T(8,128)(2,1)} fusion(bf16[128,1024]{1,0:T(8,128)(2,1)} %param.15, bf16[512,1024]{1,0:T(8,128)(2,1)S(1)} %copy-done), kind=kOutput, calls=%fused_computation.16 | convolution fusion | flops 134283264 | bytes 1441792 | tf_op jit(solution)/shard_map/dot_general | solution.py:241
  19.9 3.3 %collective-permute-done.2.refs_3_.refs_8_ = bf16[1,128,1024]{2,1,0:T(8,128)(2,1)} collective-permute-done((bf16[1,128,1024]{2,1,0:T(8,128)(2,1)S(1)}, bf16[1,128,1024]{2,1,0:T(8,128)(2,1)}, u32[]{:S(2)}, u32[]{:S(2)}) %collective-permute-start.2) | collective-permute-done | bytes 262176 | tf_op jit(solution)/shard_map/ppermute | solution.py:20
  23.2 2.4 %collective-permute-done.3.refs_4_.refs_9_ = bf16[1,128,1024]{2,1,0:T(8,128)(2,1)} collective-permute-done((bf16[1,128,1024]{2,1,0:T(8,128)(2,1)S(1)}, bf16[1,128,1024]{2,1,0:T(8,128)(2,1)}, u32[]{:S(2)}, u32[]{:S(2)}) %collective-permute-start.3) | collective-permute-done | bytes 262176 | tf_op jit(solution)/shard_map/ppermute | solution.py:20
  25.6 11.0 %shard_map.135 = (bf16[1,128,512]{2,1,0:T(8,128)(2,1)}, bf16[1,128,512]{2,1,0:T(8,128)(2,1)}, bf16[1,128,1024]{2,1,0:T(8,128)(2,1)}, bf16[1,128,1024]{2,1,0:T(8,...) custom-call(s32[5]{0:T(128)} %add_bitcast_fusion.active_ref, ...), custom_call_target="tpu_custom_call" | custom-call | tf_op jit(solution)/shard_map/pallas_call | solution.py:199
  36.6 1.3 %fusion.39 = f32[128,1024]{1,0:T(8,128)S(1)} fusion(bf16[512,1024]{1,0:T(8,128)(2,1)S(1)} %copy-done, bf16[1,128,512]{2,1,0:T(8,128)(2,1)} %get-tuple-element.22), kind=kOutput, calls=%fused_computation.93 | convolution fusion | flops 134217728 | bytes 1703936 | tf_op jit(solution)/shard_map/dot_general | solution.py:253
  37.9 1.6 %collective-permute-start.4 = (f32[128,512]{1,0:T(8,128)S(1)}, f32[128,512]{1,0:T(8,128)S(1)}, u32[]{:S(2)}, u32[]{:S(2)}) collective-permute-start(f32[128,512]{1,0:T(8,128)S(1)} %constant_dynamic-slice_fusion), channel_id=1, source_target_pairs={{0,1},{1,0},{2,3},{3,2},{4,5},{5,4},{6,7},{7,6},{8,9},{9,8},{10,11... | collective-permute-start | bytes 786440 | tf_op jit(solution)/shard_map/ppermute | solution.py:109
  39.8 2.7 %collective-permute-start.7 = (bf16[1,128,1024]{2,1,0:T(8,128)(2,1)}, bf16[1,128,1024]{2,1,0:T(8,128)(2,1)S(1)}, u32[]{:S(2)}, u32[]{:S(2)}) collective-permute-start(bf16[1,128,1024]{2,1,0:T(8,128)(2,1)} %get-tuple-element.27), channel_id=1, source_target_pairs={{0,8},{2,10},{4,12},{6,14},{8,0},{10,2},{12,4},{14,6},{16,24},{18,... | collective-permute-start | bytes 786440 | tf_op jit(solution)/shard_map/ppermute | solution.py:20
  46.7 4.4 %collective-permute-done.8 = bf16[1,128,1024]{2,1,0:T(8,128)(2,1)S(1)} collective-permute-done((bf16[1,128,1024]{2,1,0:T(8,128)(2,1)}, bf16[1,128,1024]{2,1,0:T(8,128)(2,1)S(1)}, u32[]{:S(2)}, u32[]{:S(2)}) %collective-permute-start.8) | collective-permute-done | bytes 262176 | tf_op jit(solution)/shard_map/ppermute | solution.py:20
  56.4 6.4 %collective-permute-done.9 = bf16[128,1024]{1,0:T(8,128)(2,1)S(1)} collective-permute-done((bf16[128,1024]{1,0:T(8,128)(2,1)S(1)}, bf16[128,1024]{1,0:T(8,128)(2,1)S(1)}, u32[]{:S(2)}, u32[]{:S(2)}) %collective-permute-start.9) | collective-permute-done | bytes 262176 | tf_op jit(solution)/shard_map/ppermute | solution.py:109
  67.0 1.6 %collective-permute-start.12 = (bf16[256,512]{1,0:T(8,128)(2,1)S(1)}, bf16[256,512]{1,0:T(8,128)(2,1)S(1)}, u32[]{:S(2)}, u32[]{:S(2)}) collective-permute-start(bf16[256,512]{1,0:T(8,128)(2,1)S(1)} %dynamic-slice_convert_fusion.5), channel_id=1, source_target_pairs={{0,4},{2,6},{4,0},{6,2},{8,12},{10,14},{12,8},{14,10},{16,20},{18,... | collective-permute-start | bytes 786440 | tf_op jit(solution)/shard_map/ppermute | solution.py:20
  70.4 3.6 %collective-permute-done.20 = bf16[256,512]{1,0:T(8,128)(2,1)S(1)} collective-permute-done((bf16[256,512]{1,0:T(8,128)(2,1)S(1)}, bf16[256,512]{1,0:T(8,128)(2,1)S(1)}, u32[]{:S(2)}, u32[]{:S(2)}) %collective-permute-start.20) | collective-permute-done | bytes 262176 | tf_op jit(solution)/shard_map/ppermute | solution.py:20
  76.3 3.4 %collective-permute-done.14 = f32[1024]{0:T(1024)S(1)} collective-permute-done((f32[1024]{0:T(1024)S(1)}, f32[1024]{0:T(1024)S(1)}, u32[]{:S(2)}, u32[]{:S(2)}) %collective-permute-start.14) | collective-permute-done | bytes 4128 | tf_op jit(solution)/shard_map/ppermute | solution.py:20
  79.7 2.3 %collective-permute-done.21 = bf16[128,512]{1,0:T(8,128)(2,1)S(1)} collective-permute-done((bf16[128,512]{1,0:T(8,128)(2,1)S(1)}, bf16[128,512]{1,0:T(8,128)(2,1)S(1)}, u32[]{:S(2)}, u32[]{:S(2)}) %collective-permute-start.21) | collective-permute-done | bytes 131104 | tf_op jit(solution)/shard_map/ppermute | solution.py:20
  83.2 3.4 %collective-permute-start.24 = (bf16[64,1024]{1,0:T(8,128)(2,1)S(1)}, bf16[64,1024]{1,0:T(8,128)(2,1)S(1)}, u32[]{:S(2)}, u32[]{:S(2)}) collective-permute-start(bf16[64,1024]{1,0:T(8,128)(2,1)S(1)} %fusion.19), channel_id=1, source_target_pairs={{0,16},{2,18},{4,20},{6,22},{8,24},{10,26},{12,28},{14,30},{16,0},... | collective-permute-start | bytes 393224 | tf_op jit(solution)/shard_map/ppermute | solution.py:20
  86.9 1.6 %collective-permute-start.16 = (bf16[128,512]{1,0:T(8,128)(2,1)S(1)}, bf16[128,512]{1,0:T(8,128)(2,1)S(1)}, u32[]{:S(2)}, u32[]{:S(2)}) collective-permute-start(bf16[128,512]{1,0:T(8,128)(2,1)S(1)} %dynamic-slice_convert_fusion.9), channel_id=1, source_target_pairs={{0,4},{2,6},{4,0},{6,2},{8,12},{10,14},{12,8},{14,10},{16,20},{18,... | collective-permute-start | bytes 393224 | tf_op jit(solution)/shard_map/ppermute | solution.py:20
  88.5 2.0 %collective-permute-done.17 = f32[1024]{0:T(1024)S(1)} collective-permute-done((f32[1024]{0:T(1024)S(1)}, f32[1024]{0:T(1024)S(1)}, u32[]{:S(2)}, u32[]{:S(2)}) %collective-permute-start.17) | collective-permute-done | bytes 4128 | tf_op jit(solution)/shard_map/ppermute | solution.py:20
  90.5 1.5 %collective-permute-done.16 = bf16[128,512]{1,0:T(8,128)(2,1)S(1)} collective-permute-done((bf16[128,512]{1,0:T(8,128)(2,1)S(1)}, bf16[128,512]{1,0:T(8,128)(2,1)S(1)}, u32[]{:S(2)}, u32[]{:S(2)}) %collective-permute-start.16) | collective-permute-done | bytes 131104 | tf_op jit(solution)/shard_map/ppermute | solution.py:20
  92.7 2.5 %collective-permute-start.25 = (bf16[64,1024]{1,0:T(8,128)(2,1)S(1)}, bf16[64,1024]{1,0:T(8,128)(2,1)S(1)}, u32[]{:S(2)}, u32[]{:S(2)}) collective-permute-start(bf16[64,1024]{1,0:T(8,128)(2,1)S(1)} %dynamic-slice_convert_fusion.6), channel_id=1, source_target_pairs={{0,16},{2,18},{4,20},{6,22},{8,24},{10,26},{12,28},{14,30},{16,0},... | collective-permute-start | bytes 393224 | tf_op jit(solution)/shard_map/ppermute | solution.py:20
  97.3 2.8 %collective-permute-done.25 = bf16[64,1024]{1,0:T(8,128)(2,1)S(1)} collective-permute-done((bf16[64,1024]{1,0:T(8,128)(2,1)S(1)}, bf16[64,1024]{1,0:T(8,128)(2,1)S(1)}, u32[]{:S(2)}, u32[]{:S(2)}) %collective-permute-start.25) | collective-permute-done | bytes 131104 | tf_op jit(solution)/shard_map/ppermute | solution.py:20
  (129 shorter events, 32.0 us)
Async XLA Ops:
  6.1 13.7 %collective-permute-start = (bf16[1,128,1024]{2,1,0:T(8,128)(2,1)S(1)}, bf16[1,128,1024]{2,1,0:T(8,128)(2,1)S(1)}, u32[]{:S(2)}, u32[]{:S(2)}) collective-permute-start(bf16[1,128,1024]{2,1,0:T(8,128)(2,1)S(1)} %pad_maximum_fusion.2.refs_0_.refs_5_), channel_id=1, source_target_pairs={{0,2},{2,0},{4,6},{6,4},{8,10},{10,8},{12,14},{14,12},{16,18},{18,... | collective-permute-start | bytes 786440 | tf_op jit(solution)/shard_map/ppermute | solution.py:20
  6.7 13.2 %collective-permute-start.1 = (bf16[1,128,1024]{2,1,0:T(8,128)(2,1)S(1)}, bf16[1,128,1024]{2,1,0:T(8,128)(2,1)}, u32[]{:S(2)}, u32[]{:S(2)}) collective-permute-start(bf16[1,128,1024]{2,1,0:T(8,128)(2,1)S(1)} %pad_maximum_fusion.2.refs_0_.refs_5_), channel_id=1, source_target_pairs={{0,4},{2,6},{4,0},{6,2},{8,12},{10,14},{12,8},{14,10},{16,20},{18,... | collective-permute-start | bytes 786440 | tf_op jit(solution)/shard_map/ppermute | solution.py:20
  9.3 14.0 %collective-permute-start.2 = (bf16[1,128,1024]{2,1,0:T(8,128)(2,1)S(1)}, bf16[1,128,1024]{2,1,0:T(8,128)(2,1)}, u32[]{:S(2)}, u32[]{:S(2)}) collective-permute-start(bf16[1,128,1024]{2,1,0:T(8,128)(2,1)S(1)} %pad_maximum_fusion.2.refs_0_.refs_5_), channel_id=1, source_target_pairs={{0,8},{2,10},{4,12},{6,14},{8,0},{10,2},{12,4},{14,6},{16,24},{18,... | collective-permute-start | bytes 786440 | tf_op jit(solution)/shard_map/ppermute | solution.py:20
  10.8 14.8 %collective-permute-start.3 = (bf16[1,128,1024]{2,1,0:T(8,128)(2,1)S(1)}, bf16[1,128,1024]{2,1,0:T(8,128)(2,1)}, u32[]{:S(2)}, u32[]{:S(2)}) collective-permute-start(bf16[1,128,1024]{2,1,0:T(8,128)(2,1)S(1)} %pad_maximum_fusion.2.refs_0_.refs_5_), channel_id=1, source_target_pairs={{0,16},{2,18},{4,20},{6,22},{8,24},{10,26},{12,28},{14,30},{16,0},... | collective-permute-start | bytes 786440 | tf_op jit(solution)/shard_map/ppermute | solution.py:20
  37.9 17.7 %collective-permute-start.4 = (f32[128,512]{1,0:T(8,128)S(1)}, f32[128,512]{1,0:T(8,128)S(1)}, u32[]{:S(2)}, u32[]{:S(2)}) collective-permute-start(f32[128,512]{1,0:T(8,128)S(1)} %constant_dynamic-slice_fusion), channel_id=1, source_target_pairs={{0,1},{1,0},{2,3},{3,2},{4,5},{5,4},{6,7},{7,6},{8,9},{9,8},{10,11... | collective-permute-start | bytes 786440 | tf_op jit(solution)/shard_map/ppermute | solution.py:109
  39.5 11.7 %collective-permute-start.8 = (bf16[1,128,1024]{2,1,0:T(8,128)(2,1)}, bf16[1,128,1024]{2,1,0:T(8,128)(2,1)S(1)}, u32[]{:S(2)}, u32[]{:S(2)}) collective-permute-start(bf16[1,128,1024]{2,1,0:T(8,128)(2,1)} %get-tuple-element.28), channel_id=1, source_target_pairs={{0,16},{2,18},{4,20},{6,22},{8,24},{10,26},{12,28},{14,30},{16,0},... | collective-permute-start | bytes 786440 | tf_op jit(solution)/shard_map/ppermute | solution.py:20
  39.8 11.3 %collective-permute-start.7 = (bf16[1,128,1024]{2,1,0:T(8,128)(2,1)}, bf16[1,128,1024]{2,1,0:T(8,128)(2,1)S(1)}, u32[]{:S(2)}, u32[]{:S(2)}) collective-permute-start(bf16[1,128,1024]{2,1,0:T(8,128)(2,1)} %get-tuple-element.27), channel_id=1, source_target_pairs={{0,8},{2,10},{4,12},{6,14},{8,0},{10,2},{12,4},{14,6},{16,24},{18,... | collective-permute-start | bytes 786440 | tf_op jit(solution)/shard_map/ppermute | solution.py:20
  42.5 8.6 %collective-permute-start.6 = (bf16[1,128,1024]{2,1,0:T(8,128)(2,1)}, bf16[1,128,1024]{2,1,0:T(8,128)(2,1)S(1)}, u32[]{:S(2)}, u32[]{:S(2)}) collective-permute-start(bf16[1,128,1024]{2,1,0:T(8,128)(2,1)} %get-tuple-element.26), channel_id=1, source_target_pairs={{0,4},{2,6},{4,0},{6,2},{8,12},{10,14},{12,8},{14,10},{16,20},{18,... | collective-permute-start | bytes 786440 | tf_op jit(solution)/shard_map/ppermute | solution.py:20
  43.0 8.1 %collective-permute-start.5 = (bf16[1,128,1024]{2,1,0:T(8,128)(2,1)}, bf16[1,128,1024]{2,1,0:T(8,128)(2,1)S(1)}, u32[]{:S(2)}, u32[]{:S(2)}) collective-permute-start(bf16[1,128,1024]{2,1,0:T(8,128)(2,1)} %get-tuple-element.25), channel_id=1, source_target_pairs={{0,2},{2,0},{4,6},{6,4},{8,10},{10,8},{12,14},{14,12},{16,18},{18,... | collective-permute-start | bytes 786440 | tf_op jit(solution)/shard_map/ppermute | solution.py:20
  51.2 13.1 %collective-permute-start.19 = (bf16[512,1024]{1,0:T(8,128)(2,1)S(1)}, bf16[512,1024]{1,0:T(8,128)(2,1)S(1)}, u32[]{:S(2)}, u32[]{:S(2)}) collective-permute-start(bf16[512,1024]{1,0:T(8,128)(2,1)S(1)} %dynamic-slice_convert_fusion), channel_id=1, source_target_pairs={{0,2},{2,0},{4,6},{6,4},{8,10},{10,8},{12,14},{14,12},{16,18},{18,... | collective-permute-start | bytes 3145736 | tf_op jit(solution)/shard_map/ppermute | solution.py:20
  54.0 8.8 %collective-permute-start.9 = (bf16[128,1024]{1,0:T(8,128)(2,1)S(1)}, bf16[128,1024]{1,0:T(8,128)(2,1)S(1)}, u32[]{:S(2)}, u32[]{:S(2)}) collective-permute-start(bf16[128,1024]{1,0:T(8,128)(2,1)S(1)} %fusion.1), channel_id=1, source_target_pairs={{0,1},{1,0},{2,3},{3,2},{4,5},{5,4},{6,7},{7,6},{8,9},{9,8},{10,11... | collective-permute-start | bytes 786440 | tf_op jit(solution)/shard_map/ppermute | solution.py:109
  55.4 10.9 %collective-permute-start.10 = (bf16[512,1024]{1,0:T(8,128)(2,1)S(1)}, bf16[512,1024]{1,0:T(8,128)(2,1)S(1)}, u32[]{:S(2)}, u32[]{:S(2)}) collective-permute-start(bf16[512,1024]{1,0:T(8,128)(2,1)S(1)} %dynamic-slice_convert_fusion.1), channel_id=1, source_target_pairs={{0,2},{2,0},{4,6},{6,4},{8,10},{10,8},{12,14},{14,12},{16,18},{18,... | collective-permute-start | bytes 3145736 | tf_op jit(solution)/shard_map/ppermute | solution.py:20
  64.8 9.2 %collective-permute-start.20 = (bf16[256,512]{1,0:T(8,128)(2,1)S(1)}, bf16[256,512]{1,0:T(8,128)(2,1)S(1)}, u32[]{:S(2)}, u32[]{:S(2)}) collective-permute-start(bf16[256,512]{1,0:T(8,128)(2,1)S(1)} %dynamic-slice_convert_fusion.3), channel_id=1, source_target_pairs={{0,4},{2,6},{4,0},{6,2},{8,12},{10,14},{12,8},{14,10},{16,20},{18,... | collective-permute-start | bytes 786440 | tf_op jit(solution)/shard_map/ppermute | solution.py:20
  65.4 9.6 %collective-permute-start.22 = (bf16[256,512]{1,0:T(8,128)(2,1)S(1)}, bf16[256,512]{1,0:T(8,128)(2,1)S(1)}, u32[]{:S(2)}, u32[]{:S(2)}) collective-permute-start(bf16[256,512]{1,0:T(8,128)(2,1)S(1)} %dynamic-slice_convert_fusion.2), channel_id=1, source_target_pairs={{0,8},{2,10},{4,12},{6,14},{8,0},{10,2},{12,4},{14,6},{16,24},{18,... | collective-permute-start | bytes 786440 | tf_op jit(solution)/shard_map/ppermute | solution.py:20
  67.0 15.0 %collective-permute-start.12 = (bf16[256,512]{1,0:T(8,128)(2,1)S(1)}, bf16[256,512]{1,0:T(8,128)(2,1)S(1)}, u32[]{:S(2)}, u32[]{:S(2)}) collective-permute-start(bf16[256,512]{1,0:T(8,128)(2,1)S(1)} %dynamic-slice_convert_fusion.5), channel_id=1, source_target_pairs={{0,4},{2,6},{4,0},{6,2},{8,12},{10,14},{12,8},{14,10},{16,20},{18,... | collective-permute-start | bytes 786440 | tf_op jit(solution)/shard_map/ppermute | solution.py:20
  68.6 13.5 %collective-permute-start.13 = (bf16[256,512]{1,0:T(8,128)(2,1)S(1)}, bf16[256,512]{1,0:T(8,128)(2,1)S(1)}, u32[]{:S(2)}, u32[]{:S(2)}) collective-permute-start(bf16[256,512]{1,0:T(8,128)(2,1)S(1)} %dynamic-slice_convert_fusion.4), channel_id=1, source_target_pairs={{0,8},{2,10},{4,12},{6,14},{8,0},{10,2},{12,4},{14,6},{16,24},{18,... | collective-permute-start | bytes 786440 | tf_op jit(solution)/shard_map/ppermute | solution.py:20
  69.9 9.8 %collective-permute-start.14 = (f32[1024]{0:T(1024)S(1)}, f32[1024]{0:T(1024)S(1)}, u32[]{:S(2)}, u32[]{:S(2)}) collective-permute-start(f32[1024]{0:T(1024)S(1)} %add.168), channel_id=1, source_target_pairs={{0,4},{2,6},{4,0},{6,2},{8,12},{10,14},{12,8},{14,10},{16,20},{18,... | collective-permute-start | bytes 12296 | tf_op jit(solution)/shard_map/ppermute | solution.py:20
  74.1 7.9 %collective-permute-start.21 = (bf16[128,512]{1,0:T(8,128)(2,1)S(1)}, bf16[128,512]{1,0:T(8,128)(2,1)S(1)}, u32[]{:S(2)}, u32[]{:S(2)}) collective-permute-start(bf16[128,512]{1,0:T(8,128)(2,1)S(1)} %dynamic-slice_convert_fusion.8), channel_id=1, source_target_pairs={{0,8},{2,10},{4,12},{6,14},{8,0},{10,2},{12,4},{14,6},{16,24},{18,... | collective-permute-start | bytes 393224 | tf_op jit(solution)/shard_map/ppermute | solution.py:20
  75.1 6.9 %collective-permute-start.23 = (bf16[128,512]{1,0:T(8,128)(2,1)S(1)}, bf16[128,512]{1,0:T(8,128)(2,1)S(1)}, u32[]{:S(2)}, u32[]{:S(2)}) collective-permute-start(bf16[128,512]{1,0:T(8,128)(2,1)S(1)} %dynamic-slice_convert_fusion.7), channel_id=1, source_target_pairs={{0,4},{2,6},{4,0},{6,2},{8,12},{10,14},{12,8},{14,10},{16,20},{18,... | collective-permute-start | bytes 393224 | tf_op jit(solution)/shard_map/ppermute | solution.py:20
  82.3 8.2 %collective-permute-start.15 = (bf16[128,512]{1,0:T(8,128)(2,1)S(1)}, bf16[128,512]{1,0:T(8,128)(2,1)S(1)}, u32[]{:S(2)}, u32[]{:S(2)}) collective-permute-start(bf16[128,512]{1,0:T(8,128)(2,1)S(1)} %dynamic-slice_convert_fusion.10), channel_id=1, source_target_pairs={{0,8},{2,10},{4,12},{6,14},{8,0},{10,2},{12,4},{14,6},{16,24},{18,... | collective-permute-start | bytes 393224 | tf_op jit(solution)/shard_map/ppermute | solution.py:20
  83.2 14.1 %collective-permute-start.24 = (bf16[64,1024]{1,0:T(8,128)(2,1)S(1)}, bf16[64,1024]{1,0:T(8,128)(2,1)S(1)}, u32[]{:S(2)}, u32[]{:S(2)}) collective-permute-start(bf16[64,1024]{1,0:T(8,128)(2,1)S(1)} %fusion.19), channel_id=1, source_target_pairs={{0,16},{2,18},{4,20},{6,22},{8,24},{10,26},{12,28},{14,30},{16,0},... | collective-permute-start | bytes 393224 | tf_op jit(solution)/shard_map/ppermute | solution.py:20
  86.9 5.0 %collective-permute-start.16 = (bf16[128,512]{1,0:T(8,128)(2,1)S(1)}, bf16[128,512]{1,0:T(8,128)(2,1)S(1)}, u32[]{:S(2)}, u32[]{:S(2)}) collective-permute-start(bf16[128,512]{1,0:T(8,128)(2,1)S(1)} %dynamic-slice_convert_fusion.9), channel_id=1, source_target_pairs={{0,4},{2,6},{4,0},{6,2},{8,12},{10,14},{12,8},{14,10},{16,20},{18,... | collective-permute-start | bytes 393224 | tf_op jit(solution)/shard_map/ppermute | solution.py:20
  92.0 4.7 %collective-permute-start.18 = (f32[1024]{0:T(1024)S(1)}, f32[1024]{0:T(1024)S(1)}, u32[]{:S(2)}, u32[]{:S(2)}) collective-permute-start(f32[1024]{0:T(1024)S(1)} %add.182), channel_id=1, source_target_pairs={{0,16},{2,18},{4,20},{6,22},{8,24},{10,26},{12,28},{14,30},{16,0},... | collective-permute-start | bytes 12296 | tf_op jit(solution)/shard_map/ppermute | solution.py:20
  92.7 7.4 %collective-permute-start.25 = (bf16[64,1024]{1,0:T(8,128)(2,1)S(1)}, bf16[64,1024]{1,0:T(8,128)(2,1)S(1)}, u32[]{:S(2)}, u32[]{:S(2)}) collective-permute-start(bf16[64,1024]{1,0:T(8,128)(2,1)S(1)} %dynamic-slice_convert_fusion.6), channel_id=1, source_target_pairs={{0,16},{2,18},{4,20},{6,22},{8,24},{10,26},{12,28},{14,30},{16,0},... | collective-permute-start | bytes 393224 | tf_op jit(solution)/shard_map/ppermute | solution.py:20
  (16 other events, 153.7 us)
